TPU v7x, 32 devices: a whole 2x2x4 slice. The times are simulated.
32 devices in a mesh: gx: 4 (over y, x), gy: 8 (over z, core).
Axes of the slice: x: 2, y: 2, z: 4, core: 2. Of those that a mesh axis runs over, the one named last changes fastest.
Arguments:
- stream_in: bfloat16 [64, 1536], P(None, 'gx'), may hold values from -60 to 60
- attention_gain: float32 [2, 1536], P(None, 'gx'), may hold values from 0.5 to 1.5
- feedforward_gain: float32 [2, 1536], P(None, 'gx'), may hold values from 0.5 to 1.5
- final_gain: float32 [1536], P('gx'), may hold values from 0.5 to 1.5
- qkv_weight: bfloat16 [2, 1536, 3072], P(None, 'gx', 'gy'), may hold values from -0.15625 to 0.15625
- forget_weight: bfloat16 [2, 1536, 16], P(None, 'gx', 'gy'), may hold values from -0.15625 to 0.15625
- forget_bias: float32 [2, 16], P(None, 'gy'), may hold values from -2 to 3
- out_weight: bfloat16 [2, 1024, 1536], P(None, 'gy', 'gx'), may hold values from -0.1875 to 0.1875
- gate_weight: bfloat16 [2, 1536, 4096], P(None, 'gx', 'gy'), may hold values from -0.15625 to 0.15625
- up_weight: bfloat16 [2, 1536, 4096], P(None, 'gx', 'gy'), may hold values from -0.15625 to 0.15625
- down_weight: bfloat16 [2, 4096, 1536], P(None, 'gy', 'gx'), may hold values from -0.09375 to 0.09375
- head_weight: bfloat16 [1536, 49152], P('gx', 'gy'), may hold values from -0.15625 to 0.15625
- kv_cache: bfloat16 [2, 512, 128, 16, 128], P(None, 'gx', None, 'gy'), may hold values from -102 to 102
- decay_cache: float32 [2, 512, 16, 128], P(None, 'gx', 'gy'), may hold values from -66 to 0
- lengths: int32 [64], replicated, may hold values from 1 to 32768, as said below
- page_table: int32 [64, 256], replicated, may hold values from -1 to 511, as said below
Outputs:
- final_hidden: bfloat16 [64, 1536], P(None, 'gx')
- row_norms: float32 [64], replicated
- top_logits: float32 [64], replicated
Inputs may be any that keep to these rules, and one draw needn't show every extreme that they name: `lengths`: every request has at least one cached token and one request has exactly 32768. `page_table`: row r names the slots of its first ceil(lengths[r] / 128) pages and holds -1 after them; no slot is named twice; slot s lies in block s // 128 of gx.
All inputs are finite; a program needn't handle non-finite values.
Results may differ from a plain program's by a relative error of at most 0.01.
The roundings to bfloat16 on the way count: a program that leaves them out, or rounds other values in their place, can miss the bound.
Values may be sent and summed in bfloat16 or wider, within the bound.
No kernel may reach another device: no remote copies, remote signals or barrier semaphores. Data moves between devices by JAX's collectives and lax.ppermute only.
A program may use at most 128 MiB of HBM per device.

v0:
```python
import jax
import jax.numpy as jnp
from jax import lax
from jax.sharding import PartitionSpec as P

D = 1536
HEAD = 64
DEPTH_NUMBER = 2
SHEET_ENTRIES = 128


SCORE_SCALE = 0.125
NEGATIVE = -1e30
EPSILON = 1e-06


def merged(value, axis, join):
    pieces = jax.tree.map(lambda part: lax.all_gather(part, axis), value)
    head = jax.tree.map(lambda part: part[0], pieces)
    tail = jax.tree.map(lambda part: part[1:], pieces)
    subtotal, _ = lax.scan(lambda subtotal, piece: (join(subtotal, piece), None), head, tail)
    return subtotal


def slot_layout(lengths, page_table, slot_count):
    request_count, page_count = page_table.shape
    request_ids = jnp.broadcast_to(
        jnp.arange(request_count, dtype=jnp.int32)[:, None], (request_count, page_count)
    )
    page_ids = jnp.broadcast_to(
        jnp.arange(page_count, dtype=jnp.int32)[None, :], (request_count, page_count)
    )
    targets = jnp.where(page_table >= 0, page_table, slot_count).reshape(-1)
    slot_owner = (
        jnp.full((slot_count,), -1, jnp.int32).at[targets].set(request_ids.reshape(-1), mode="drop")
    )
    page_index = (
        jnp.zeros((slot_count,), jnp.int32).at[targets].set(page_ids.reshape(-1), mode="drop")
    )
    safe_owner = jnp.maximum(slot_owner, 0)
    covered = lengths[safe_owner] - page_index * SHEET_ENTRIES
    offsets = jnp.arange(SHEET_ENTRIES, dtype=jnp.int32)
    live_slots = (slot_owner[:, None] >= 0) & (offsets[None, :] < covered[:, None])
    return (slot_owner, live_slots)


def row_rms(stream):
    squares = lax.psum(jnp.sum(stream * stream, axis=1), "gx")
    return jnp.sqrt(squares / D + EPSILON)


def column_total(partial_value):
    return lax.psum(partial_value, "gy")


def join_partials(first, second):
    first_peak, first_sum, first_out = first
    second_peak, second_sum, second_out = second
    joint_peak = jnp.maximum(first_peak, second_peak)
    first_scale = jnp.exp(first_peak - joint_peak)
    second_scale = jnp.exp(second_peak - joint_peak)
    joint_sum = first_scale * first_sum + second_scale * second_sum
    joint_out = first_scale[:, :, None] * first_out + second_scale[:, :, None] * second_out
    return (joint_peak, joint_sum, joint_out)


def local_attention(queries, forget_log, kv_layer, decay_layer, slot_owner, live_slots):
    request_count = queries.shape[0]
    safe_owner = jnp.maximum(slot_owner, 0)
    cache_keys = kv_layer[..., :HEAD]
    cache_values = kv_layer[..., HEAD:]
    scores = (
        jnp.einsum(
            "phd,pthd->pht", queries[safe_owner], cache_keys, preferred_element_type=jnp.float32
        )
        * SCORE_SCALE
    )
    scores = scores + decay_layer + forget_log[safe_owner][:, :, None]
    scores = jnp.where(live_slots[:, None, :], scores, NEGATIVE)
    page_peak = jnp.max(scores, axis=2)
    weights = jnp.where(live_slots[:, None, :], jnp.exp(scores - page_peak[:, :, None]), 0.0)
    page_sum = jnp.sum(weights, axis=2)
    page_out = jnp.einsum(
        "pht,pthd->phd",
        weights.astype(jnp.bfloat16),
        cache_values,
        preferred_element_type=jnp.float32,
    )
    member = slot_owner[None, :] == jnp.arange(request_count, dtype=jnp.int32)[:, None]
    row_peak = jnp.max(jnp.where(member[:, :, None], page_peak[None], NEGATIVE), axis=1)
    factor = jnp.where(member[:, :, None], jnp.exp(page_peak[None] - row_peak[:, None]), 0.0)
    row_sum = jnp.sum(factor * page_sum[None], axis=1)
    row_out = jnp.einsum("bph,phd->bhd", factor, page_out, precision=lax.Precision.HIGHEST)
    return (row_peak, row_sum, row_out)


def local(
    stream_in,
    attention_gain,
    feedforward_gain,
    final_gain,
    qkv_weight,
    forget_weight,
    forget_bias,
    out_weight,
    gate_weight,
    up_weight,
    down_weight,
    head_weight,
    kv_cache,
    decay_cache,
    lengths,
    page_table,
):
    local_pages = kv_cache.shape[1]
    local_heads = kv_cache.shape[3]
    request_count = stream_in.shape[0]
    slot_owner, live_slots = slot_layout(lengths, page_table, local_pages * lax.axis_size("gx"))
    first_slot = lax.axis_index("gx") * local_pages
    slot_owner = lax.dynamic_slice_in_dim(slot_owner, first_slot, local_pages)
    live_slots = lax.dynamic_slice_in_dim(live_slots, first_slot, local_pages)
    stream = stream_in.astype(jnp.float32)
    for layer_id in range(DEPTH_NUMBER):
        rms_value = row_rms(stream)
        normed = (stream / rms_value[:, None] * attention_gain[layer_id][None, :]).astype(
            jnp.bfloat16
        )
        qkv_part = jnp.dot(normed, qkv_weight[layer_id], preferred_element_type=jnp.float32)
        forget_part = jnp.dot(normed, forget_weight[layer_id], preferred_element_type=jnp.float32)
        projected, forget_logit = lax.psum((qkv_part, forget_part), "gx")
        projected = projected.reshape(request_count, local_heads, 3 * HEAD)
        queries = projected[:, :, :HEAD].astype(jnp.bfloat16)
        new_keys = projected[:, :, HEAD : 2 * HEAD].astype(jnp.bfloat16)
        new_values = projected[:, :, 2 * HEAD :].astype(jnp.bfloat16)
        forget_log = jax.nn.log_sigmoid(forget_logit + forget_bias[layer_id][None, :])
        local_peak, local_sum, local_out = local_attention(
            queries, forget_log, kv_cache[layer_id], decay_cache[layer_id], slot_owner, live_slots
        )
        row_peak, row_sum, row_out = merged((local_peak, local_sum, local_out), "gx", join_partials)
        own_score = (
            jnp.sum(queries.astype(jnp.float32) * new_keys.astype(jnp.float32), axis=2)
            * SCORE_SCALE
        )
        full_peak = jnp.maximum(row_peak, own_score)
        cache_scale = jnp.exp(row_peak - full_peak)
        own_weight = jnp.exp(own_score - full_peak)
        own_rounded = lax.optimization_barrier(own_weight.astype(jnp.bfloat16)).astype(jnp.float32)
        numerator = cache_scale[:, :, None] * row_out + own_rounded[:, :, None] * new_values.astype(
            jnp.float32
        )
        denominator = cache_scale * row_sum + own_weight
        attended = (
            (numerator / denominator[:, :, None])
            .reshape(request_count, local_heads * HEAD)
            .astype(jnp.bfloat16)
        )
        stream = stream + column_total(
            jnp.dot(attended, out_weight[layer_id], preferred_element_type=jnp.float32)
        )
        rms_value = row_rms(stream)
        normed = (stream / rms_value[:, None] * feedforward_gain[layer_id][None, :]).astype(
            jnp.bfloat16
        )
        layer_gate = gate_weight[layer_id]
        layer_up = up_weight[layer_id]
        gate_part, up_part = lax.psum(
            (
                jnp.dot(normed, layer_gate, preferred_element_type=jnp.float32),
                jnp.dot(normed, layer_up, preferred_element_type=jnp.float32),
            ),
            "gx",
        )
        hidden = (jax.nn.silu(gate_part) * up_part).astype(jnp.bfloat16)
        stream = stream + column_total(
            jnp.dot(hidden, down_weight[layer_id], preferred_element_type=jnp.float32)
        )
    rms_value = row_rms(stream)
    final_hidden = (stream / rms_value[:, None] * final_gain[None, :]).astype(jnp.bfloat16)
    logits = lax.psum(jnp.dot(final_hidden, head_weight, preferred_element_type=jnp.float32), "gx")
    top_logits = lax.pmax(jnp.max(logits, axis=1), "gy")
    return (final_hidden, rms_value, top_logits)


def solution(mesh):
    placed = (
        P(None, "gx"),
        P(None, "gx"),
        P(None, "gx"),
        P("gx"),
        P(None, "gx", "gy"),
        P(None, "gx", "gy"),
        P(None, "gy"),
        P(None, "gy", "gx"),
        P(None, "gx", "gy"),
        P(None, "gx", "gy"),
        P(None, "gy", "gx"),
        P("gx", "gy"),
        P(None, "gx", None, "gy", None),
        P(None, "gx", "gy", None),
        P(),
        P(),
    )
    return jax.shard_map(
        local, mesh=mesh, in_specs=placed, out_specs=(P(None, "gx"), P(), P()), check_vma=False
    )
```

profile of v0, /device:TPU:0, one launch (start us, length us, event | category | flops | bytes accessed | tf_op | source)
XLA Modules:
  0.0 826.1 jit_solution(14256440611061137002)
XLA Ops:
  7.2 1.6 fusion.106
  8.8 2.1 fusion.103
  10.9 2.1 fusion.104
  12.9 2.1 fusion.105
  16.0 11.4 %psum.126 = f32[64]{0:T(128)S(1)} all-reduce(f32[64]{0:T(128)S(1)} %fusion.44), channel_id=1, replica_groups=mesh['gx'=4,'gy'=8] {'gx'}, use_global_device_ids=true, to_apply=%region_3.4 | all-reduce | flops 64 | bytes 512 | tf_op jit(solution)/shard_map/psum | solution.py:48
  29.1 1.2 fusion.32
  30.5 16.8 %all-reduce.1 = (bf16[64,2,192]{2,1,0:T(2,128)(2,1)S(1)}, f32[64,2]{0,1:T(2,128)S(1)}) all-reduce(f32[64,2,192]{2,1,0:T(2,128)S(1)} %reshape.104, f32[64,2]{0,1:T(2,128)S(1)} %fusion.70), channel_id=1, replica_groups=mesh['gx'=4,'gy'=8] {'gx'}, use_global_device_ids=true, to_apply=%region_4.5 | all-reduce | flops 24704 | bytes 148480 | tf_op jit(solution)/shard_map/psum | solution.py:130
  49.3 60.3 %scatter_custom_fusion = s32[512]{0:T(512)S(1)} fusion(s32[16384]{0:T(1024)S(1)} %bitcast.225, s32[16384]{0:T(1024)S(1)} %bitcast.229, s32[]{:T(128)} %constant.32.clone.1), kind=kCustom, calls=%fused_computation.164 | custom fusion | bytes 2052 | tf_op jit(solution)/shard_map/scatter | solution.py:35
  109.9 60.3 %scatter_custom_fusion.1 = s32[512]{0:T(512)S(1)} fusion(s32[16384]{0:T(1024)S(1)} %bitcast.226, s32[16384]{0:T(1024)S(1)} %bitcast.230, s32[]{:T(128)} %copy.202), kind=kCustom, calls=%fused_computation.161 | custom fusion | bytes 2052 | tf_op jit(solution)/shard_map/scatter | solution.py:38
  170.2 39.8 %select_subtract_fusion = s32[512]{0:T(512)S(1)} fusion(s32[512]{0:T(512)S(1)} %scatter_custom_fusion.1, s32[512]{0:T(512)S(1)} %scatter_custom_fusion, s32[]{:T(128)} %bitcast.72, s32[]{:T(128)} %bitcast.9, s32[]{:T(128)} %bitcast.10, s32[]{:T(128)} %bitcast.11, s32[]{:T(128)} %bitcast.12, s32[]{:T(128)} %bitcast.13, s32[]{:T(128)} %bitcast.14, ...), kind=kLoop, calls=%fused_computation.134 | loop fusion | flops 66048 | bytes 6400 | tf_op jit(solution)/shard_map/sub | solution.py:41
  211.6 13.9 %slice_bitcast_fusion.2 = (bf16[128,128,2,128]{3,2,1,0:T(2,128)(2,1)}, bf16[128,128,2,128]{3,2,1,0:T(2,128)(2,1)S(1)}) fusion(bf16[2,128,128,2,128]{4,3,2,1,0:T(2,128)(2,1)} %param.32), kind=kLoop, calls=%fused_computation.36 | loop fusion | bytes 33554432 | tf_op jit(solution)/shard_map/squeeze | solution.py:137
  225.7 3.1 copy-done
  228.8 4.4 fusion.10
  234.4 7.3 all-gather.7
  241.7 7.8 all-gather.6
  249.5 4.9 copy.127
  254.4 30.3 %multiply_reduce_fusion.1 = f32[128,2,64]{2,1,0:T(2,128)S(1)} fusion(bf16[128,128,2,128]{3,2,1,0:T(2,128)(2,1)} %copy-done, f32[128,2,128]{1,2,0:T(8,128)} %copy.127), kind=kLoop, calls=%fused_computation.29 | loop fusion | flops 6275072 | bytes 4390912
  285.3 8.4 %all-gather.2 = f32[256,2,64]{2,1,0:T(2,128)S(1)} all-gather(f32[64,2,64]{2,1,0:T(2,128)S(1)} %copy.86), channel_id=4, replica_groups=mesh['gx'=4,'gy'=8] {'gx'}, dimensions={0}, use_global_device_ids=true | all-gather | bytes 163840 | tf_op jit(solution)/shard_map/all_gather | solution.py:18
  293.8 2.0 while.28
  297.4 52.0 %all-reduce.12.cloned.1.call-done = f32[64,384]{1,0:T(8,128)} async-done(((f32[64,384]{1,0:T(8,128)}), f32[64,384]{1,0:T(8,128)}) %all-reduce.12.cloned.1.call-update) | async-done | bytes 98320 | tf_op jit(solution)/shard_map/psum | solution.py:53
  349.4 1.0 multiply_reduce_fusion.5
  350.4 9.8 %psum.130 = f32[64]{0:T(128)S(1)} all-reduce(f32[64]{0:T(128)S(1)} %multiply_reduce_fusion.5), channel_id=1, replica_groups=mesh['gx'=4,'gy'=8] {'gx'}, use_global_device_ids=true, to_apply=%region_15.16 | all-reduce | flops 64 | bytes 512 | tf_op jit(solution)/shard_map/psum | solution.py:48
  360.2 1.8 fusion.20
  362.0 1.8 fusion.22
  363.8 42.8 %all-reduce.24.cloned.1.call-done = (f32[64,512]{1,0:T(8,128)}, f32[64,512]{1,0:T(8,128)}) async-done(((f32[64,512]{1,0:T(8,128)}, f32[64,512]{1,0:T(8,128)}), (f32[64,512]{1,0:T(8,128)}, f32[64,512]{1,0:T(8,128)})) %all-reduce.24.cloned.1.call-update) | async-done | bytes 262160 | tf_op jit(solution)/shard_map/psum | solution.py:166
  406.7 2.0 fusion.18
  408.7 51.9 %all-reduce.14.cloned.1.call-done = f32[64,384]{1,0:T(8,128)} async-done(((f32[64,384]{1,0:T(8,128)}), f32[64,384]{1,0:T(8,128)}) %all-reduce.14.cloned.1.call-update) | async-done | bytes 98320 | tf_op jit(solution)/shard_map/psum | solution.py:53
  460.7 1.1 multiply_reduce_fusion.4
  461.7 9.8 %psum.134 = f32[64]{0:T(128)S(1)} all-reduce(f32[64]{0:T(128)S(1)} %get-tuple-element.199), channel_id=1, replica_groups=mesh['gx'=4,'gy'=8] {'gx'}, use_global_device_ids=true, to_apply=%region_20.21 | all-reduce | flops 64 | bytes 512 | tf_op jit(solution)/shard_map/psum | solution.py:48
  472.2 16.4 %all-reduce = (bf16[64,2,192]{2,1,0:T(2,128)(2,1)S(1)}, f32[64,2]{0,1:T(2,128)S(1)}) all-reduce(f32[64,2,192]{2,1,0:T(2,128)S(1)} %reshape.105, f32[64,2]{0,1:T(2,128)S(1)} %fusion.68), channel_id=1, replica_groups=mesh['gx'=4,'gy'=8] {'gx'}, use_global_device_ids=true, to_apply=%region_21.22 | all-reduce | flops 24704 | bytes 148480 | tf_op jit(solution)/shard_map/psum | solution.py:130
  490.4 7.8 fusion.8
  499.4 7.6 all-gather.9
  507.1 7.5 all-gather.8
  514.6 4.9 copy.128
  519.5 30.2 %multiply_reduce_fusion = f32[128,2,64]{2,1,0:T(2,128)S(1)} fusion(bf16[128,128,2,128]{3,2,1,0:T(2,128)(2,1)} %get-tuple-element.207, f32[128,2,128]{1,2,0:T(8,128)} %copy.128), kind=kLoop, calls=%fused_computation.28 | loop fusion | flops 6275072 | bytes 4390912
  550.2 8.6 %all-gather.5 = f32[256,2,64]{2,1,0:T(2,128)S(1)} all-gather(f32[64,2,64]{2,1,0:T(2,128)S(1)} %copy.96), channel_id=7, replica_groups=mesh['gx'=4,'gy'=8] {'gx'}, dimensions={0}, use_global_device_ids=true | all-gather | bytes 163840 | tf_op jit(solution)/shard_map/all_gather | solution.py:18
  558.9 2.0 while.29
  562.4 52.7 %all-reduce.16.cloned.1.call-done = f32[64,384]{1,0:T(8,128)} async-done(((f32[64,384]{1,0:T(8,128)}), f32[64,384]{1,0:T(8,128)}) %all-reduce.16.cloned.1.call-update) | async-done | bytes 98320 | tf_op jit(solution)/shard_map/psum | solution.py:53
  615.1 1.0 multiply_reduce_fusion.3
  616.1 9.8 %psum.138 = f32[64]{0:T(128)S(1)} all-reduce(f32[64]{0:T(128)S(1)} %get-tuple-element.193), channel_id=1, replica_groups=mesh['gx'=4,'gy'=8] {'gx'}, use_global_device_ids=true, to_apply=%region_32.33 | all-reduce | flops 64 | bytes 512 | tf_op jit(solution)/shard_map/psum | solution.py:48
  627.8 42.8 %all-reduce.22.cloned.1.call-done = (f32[64,512]{1,0:T(8,128)}, f32[64,512]{1,0:T(8,128)}) async-done(((f32[64,512]{1,0:T(8,128)}, f32[64,512]{1,0:T(8,128)}), (f32[64,512]{1,0:T(8,128)}, f32[64,512]{1,0:T(8,128)})) %all-reduce.22.cloned.1.call-update) | async-done | bytes 262160 | tf_op jit(solution)/shard_map/psum | solution.py:166
  670.7 2.0 fusion.12
  672.7 51.9 %all-reduce.18.cloned.1.call-done = f32[64,384]{1,0:T(8,128)} async-done(((f32[64,384]{1,0:T(8,128)}), f32[64,384]{1,0:T(8,128)}) %all-reduce.18.cloned.1.call-update) | async-done | bytes 98320 | tf_op jit(solution)/shard_map/psum | solution.py:53
  725.6 9.8 %psum.142 = f32[64]{0:T(128)S(1)} all-reduce(f32[64]{0:T(128)S(1)} %get-tuple-element.191), channel_id=1, replica_groups=mesh['gx'=4,'gy'=8] {'gx'}, use_global_device_ids=true, to_apply=%region_37.38 | all-reduce | flops 64 | bytes 512 | tf_op jit(solution)/shard_map/psum | solution.py:48
  735.6 4.5 fusion.107
  740.1 60.7 %all-reduce.20.cloned.1.call-done = f32[64,6144]{1,0:T(8,128)} async-done(((f32[64,6144]{1,0:T(8,128)}), f32[64,6144]{1,0:T(8,128)}) %all-reduce.20.cloned.1.call-update) | async-done | bytes 1572880 | tf_op jit(solution)/shard_map/psum | solution.py:179
  800.8 1.6 reduce_max.49
  802.4 16.9 %pmax.7 = f32[64]{0:T(128)} all-reduce(f32[64]{0:T(128)S(1)} %reduce_max.49), channel_id=1, replica_groups=mesh['gx'=4,'gy'=8] {'gy'}, use_global_device_ids=true, to_apply=%region_40.41 | all-reduce | flops 64 | bytes 512 | tf_op jit(solution)/shard_map/pmax | solution.py:180
  (158 shorter events, 23.0 us)
Async XLA Ops:
  7.2 342.2 %all-reduce.12.cloned.1.call-start = ((), (), s32[]{:S(2)}) async-start(), calls=%async_computation | async-start | bytes 196608 | tf_op jit(solution)/shard_map/psum | solution.py:53
  225.6 3.2 copy-start
  225.6 7.6 copy-start.2
  254.4 42.1 %copy-start.4 = (bf16[2,128,384]{2,1,0:T(8,128)(2,1)S(1)}, bf16[2,128,384]{2,1,0:T(8,128)(2,1)}, u32[]{:S(2)}) copy-start(bf16[2,128,384]{2,1,0:T(8,128)(2,1)} %param.27) | copy-start | bytes 589828
  254.4 42.9 %copy-start.6 = (f32[2,384]{1,0:T(2,128)S(1)}, f32[2,384]{1,0:T(2,128)}, u32[]{:S(2)}) copy-start(f32[2,384]{1,0:T(2,128)} %param.22) | copy-start | bytes 9220
  254.4 94.9 %copy-start.1 = (bf16[64,384]{1,0:T(8,128)(2,1)S(1)}, bf16[64,384]{1,0:T(8,128)(2,1)}, u32[]{:S(2)}) copy-start(bf16[64,384]{1,0:T(8,128)(2,1)} %param.20) | copy-start | bytes 147460
  254.4 105.8 %copy-start.9 = (bf16[2,384,512]{2,1,0:T(8,128)(2,1)S(1)}, bf16[2,384,512]{2,1,0:T(8,128)(2,1)}, u32[]{:S(2)}) copy-start(bf16[2,384,512]{2,1,0:T(8,128)(2,1)} %param.29) | copy-start | bytes 2359300
  254.4 107.6 %copy-start.10 = (bf16[2,384,512]{2,1,0:T(8,128)(2,1)S(1)}, bf16[2,384,512]{2,1,0:T(8,128)(2,1)}, u32[]{:S(2)}) copy-start(bf16[2,384,512]{2,1,0:T(8,128)(2,1)} %param.28) | copy-start | bytes 2359300
  284.7 187.0 %copy-start.11 = (bf16[2,384,2]{1,2,0:T(2,128)(2,1)S(1)}, bf16[2,384,2]{1,2,0:T(2,128)(2,1)}, u32[]{:S(2)}) copy-start(bf16[2,384,2]{1,2,0:T(2,128)(2,1)} %param.25) | copy-start | bytes 9220
  284.7 187.1 %copy-start.5 = (bf16[2,384,384]{2,1,0:T(8,128)(2,1)S(1)}, bf16[2,384,384]{2,1,0:T(8,128)(2,1)}, u32[]{:S(2)}) copy-start(bf16[2,384,384]{2,1,0:T(8,128)(2,1)} %param.24) | copy-start | bytes 1769476
  297.3 109.4 %all-reduce.24.cloned.1.call-start = ((), (), s32[]{:S(2)}) async-start(), calls=%async_computation.6 | async-start | bytes 524288 | tf_op jit(solution)/shard_map/psum | solution.py:166
  363.8 96.9 %all-reduce.14.cloned.1.call-start = ((), (), s32[]{:S(2)}) async-start(), calls=%async_computation.1 | async-start | bytes 196608 | tf_op jit(solution)/shard_map/psum | solution.py:53
  408.7 206.4 %all-reduce.16.cloned.1.call-start = ((), (), s32[]{:S(2)}) async-start(), calls=%async_computation.2 | async-start | bytes 196608 | tf_op jit(solution)/shard_map/psum | solution.py:53
  549.7 185.8 %copy-start.7 = (f32[384]{0:T(512)S(1)}, f32[384]{0:T(512)}, u32[]{:S(2)}) copy-start(f32[384]{0:T(512)} %param.23) | copy-start | bytes 4612
  562.4 108.3 %all-reduce.22.cloned.1.call-start = ((), (), s32[]{:S(2)}) async-start(), calls=%async_computation.5 | async-start | bytes 524288 | tf_op jit(solution)/shard_map/psum | solution.py:166
  627.8 96.8 %all-reduce.18.cloned.1.call-start = ((), (), s32[]{:S(2)}) async-start(), calls=%async_computation.3 | async-start | bytes 196608 | tf_op jit(solution)/shard_map/psum | solution.py:53
  672.7 128.1 %all-reduce.20.cloned.1.call-start = ((), (), s32[]{:S(2)}) async-start(), calls=%async_computation.4 | async-start | bytes 3145728 | tf_op jit(solution)/shard_map/psum | solution.py:179
  735.5 83.8 %copy-start.8 = (f32[64]{0:T(128)}, f32[64]{0:T(128)S(1)}, u32[]{:S(2)}) copy-start(f32[64]{0:T(128)S(1)} %add_sqrt_fusion) | copy-start | bytes 772
  735.6 83.7 %copy-start.3 = (bf16[64,384]{1,0:T(8,128)(2,1)}, bf16[64,384]{1,0:T(8,128)(2,1)S(1)}, u32[]{:S(2)}) copy-start(bf16[64,384]{1,0:T(8,128)(2,1)S(1)} %multiply_convert_fusion.2) | copy-start | bytes 147460
Sparse Core Ops, SparseCore 0:
  297.4 51.8 all-reduce.11
  363.9 42.7 all-reduce.23
  409.0 51.5 all-reduce.13
  562.5 52.5 all-reduce.15
  627.9 42.7 all-reduce.21
  673.0 51.6 all-reduce.17
  740.2 60.5 all-reduce.19
where the time goes:
time: 828 us; the launch traced here: 826 us
  waiting for transfers between devices  355 us (43%)
  local copies, waits for them, and re-layouts  163 us (20%)
  blocking collectives  148 us (18%)
  other arithmetic  114 us (14%)
  matrix products  30.9 us (4%)
  between operations  14.6 us (2%)
    psum x4, waiting for transfers between devices, column_total(): return lax.psum(partial_value, 'gy')  208 us
    psum x2, waiting for transfers between devices, local(): lax.psum((jnp.dot(normed, layer_gate, preferred_element_type=jnp.float32)...  85.7 us
    unnamed x5, other arithmetic  62.1 us
    psum x1, waiting for transfers between devices, local(): lax.psum(jnp.dot(final_hidden, head_weight, preferred_element_type=jnp.fl...  60.7 us
    scatter x1, local copies, waits for them, and re-layouts, slot_layout(): jnp.full((slot_count,), -1, jnp.int32).at[targets]  60.3 us
    scatter x1, local copies, waits for them, and re-layouts, slot_layout(): jnp.zeros((slot_count,), jnp.int32).at[targets]  60.3 us
    psum x5, blocking collectives, row_rms(): squares = lax.psum(jnp.sum(stream * stream, axis=1), 'gx')  50.7 us
    all_gather x6, blocking collectives, merged(): pieces = jax.tree.map(lambda part: lax.all_gather(part, axis), value)  47.2 us
  transfers between devices with their start and end apart: 7, of which 7 were waited for; matrix products, arithmetic and copies ran while one was open for 0% of the time, Pallas kernels for 0%

commit v1 on v0

v1 whole, which is shorter than its diff:
```python
import jax
import jax.numpy as jnp
from jax import lax
from jax.sharding import PartitionSpec as P

HEAD = 64
DEPTH_NUMBER = 2
SHEET_ENTRIES = 128

SCORE_SCALE = 0.125
NEGATIVE = -1e30
EPSILON = 1e-06
LOW_BLOCK = 16


def gather_sum(value, axis):
    return jnp.sum(lax.all_gather(value, axis), axis=0)


def local_slots(page_table, base, slot_count):
    request_count, page_count = page_table.shape
    flat = page_table.reshape(-1) - base
    valid = (flat >= 0) & (flat < slot_count)
    high = jnp.where(valid, flat // LOW_BLOCK, -1)
    low = flat % LOW_BLOCK
    entry = jnp.arange(request_count * page_count, dtype=jnp.int32)
    owner_code = (entry // page_count + 1).astype(jnp.float32)
    page_code = (entry % page_count).astype(jnp.float32)
    high_count = slot_count // LOW_BLOCK
    high_hot = (high[None, :] == jnp.arange(high_count, dtype=jnp.int32)[:, None]).astype(jnp.float32)
    low_hot = (low[None, :] == jnp.arange(LOW_BLOCK, dtype=jnp.int32)[:, None]).astype(jnp.bfloat16)
    coded = jnp.concatenate(
        [high_hot * owner_code[None, :], high_hot * page_code[None, :]], axis=0
    ).astype(jnp.bfloat16)
    table = lax.dot_general(
        coded, low_hot, (((1,), (1,)), ((), ())), preferred_element_type=jnp.float32
    )
    table = table.reshape(2, slot_count).astype(jnp.int32)
    owner = table[0] - 1
    page = table[1]
    return owner, page


def local_attention(queries, forget_log, kv_layer, decay_layer, owner, live, member):
    slots, tokens, heads, width = kv_layer.shape
    request_count = queries.shape[0]
    safe_owner = jnp.maximum(owner, 0)
    kv_flat = kv_layer.reshape(slots, tokens, heads * width)
    slot_queries = queries[safe_owner]
    padded = jnp.concatenate([slot_queries, jnp.zeros_like(slot_queries)], axis=2)
    diagonal = jnp.eye(heads, dtype=jnp.bfloat16)
    query_block = (diagonal[None, :, :, None] * padded[:, :, None, :]).reshape(
        slots, heads, heads * width
    )
    scores = jnp.einsum(
        "ptc,phc->pht", kv_flat, query_block, preferred_element_type=jnp.float32
    ) * SCORE_SCALE
    scores = scores + decay_layer + forget_log[safe_owner][:, :, None]
    scores = jnp.where(live[:, None, :], scores, NEGATIVE)
    page_peak = jnp.max(scores, axis=2)
    row_peak = jnp.max(jnp.where(member[:, :, None], page_peak[None], NEGATIVE), axis=1)
    slot_peak = row_peak[safe_owner]
    weights = jnp.where(live[:, None, :], jnp.exp(scores - slot_peak[:, :, None]), 0.0)
    page_sum = jnp.sum(weights, axis=2)
    mixed = jnp.einsum(
        "pht,ptc->phc", weights.astype(jnp.bfloat16), kv_flat, preferred_element_type=jnp.float32
    ).reshape(slots, heads, heads, width)
    page_out = jnp.stack([mixed[:, h, h, HEAD:] for h in range(heads)], axis=1)
    member_f = member.astype(jnp.float32)
    row_sum = jnp.einsum("rp,ph->rh", member_f, page_sum, precision=lax.Precision.HIGHEST)
    row_out = jnp.einsum("rp,phd->rhd", member_f, page_out, precision=lax.Precision.HIGHEST)
    return row_peak, row_sum, row_out


def merge_pages(row_peak, row_sum, row_out):
    packed = jnp.concatenate([row_peak[:, :, None], row_sum[:, :, None], row_out], axis=2)
    every = lax.all_gather(packed, "gx")
    peaks = every[:, :, :, 0]
    top = jnp.max(peaks, axis=0)
    scale = jnp.exp(peaks - top[None])
    total = jnp.sum(scale * every[:, :, :, 1], axis=0)
    out = jnp.sum(scale[..., None] * every[:, :, :, 2:], axis=0)
    return top, total, out


def local(
    stream_in,
    attention_gain,
    feedforward_gain,
    final_gain,
    qkv_weight,
    forget_weight,
    forget_bias,
    out_weight,
    gate_weight,
    up_weight,
    down_weight,
    head_weight,
    kv_cache,
    decay_cache,
    lengths,
    page_table,
):
    local_pages = kv_cache.shape[1]
    local_heads = kv_cache.shape[3]
    request_count = stream_in.shape[0]
    width = stream_in.shape[1] * lax.axis_size("gx")
    base = lax.axis_index("gx") * local_pages
    owner, page = local_slots(page_table, base, local_pages)
    member = owner[None, :] == jnp.arange(request_count, dtype=jnp.int32)[:, None]
    slot_length = jnp.sum(jnp.where(member, lengths[:, None], 0), axis=0)
    offsets = jnp.arange(SHEET_ENTRIES, dtype=jnp.int32)
    live = (owner[:, None] >= 0) & (
        page[:, None] * SHEET_ENTRIES + offsets[None, :] < slot_length[:, None]
    )
    stream = stream_in.astype(jnp.float32)
    qkv_cols = qkv_weight.shape[2]
    for layer_id in range(DEPTH_NUMBER):
        squares = jnp.sum(stream * stream, axis=1)
        scaled = (stream * attention_gain[layer_id][None, :]).astype(jnp.bfloat16)
        qkv_part = jnp.dot(scaled, qkv_weight[layer_id], preferred_element_type=jnp.float32)
        forget_part = jnp.dot(scaled, forget_weight[layer_id], preferred_element_type=jnp.float32)
        total = gather_sum(
            jnp.concatenate([qkv_part, forget_part, squares[:, None]], axis=1), "gx"
        )
        rms_value = jnp.sqrt(total[:, -1] / width + EPSILON)
        projected = (total[:, :qkv_cols] / rms_value[:, None]).reshape(
            request_count, local_heads, 3 * HEAD
        )
        forget_logit = total[:, qkv_cols : qkv_cols + local_heads] / rms_value[:, None]
        queries = projected[:, :, :HEAD].astype(jnp.bfloat16)
        new_keys = projected[:, :, HEAD : 2 * HEAD].astype(jnp.bfloat16)
        new_values = projected[:, :, 2 * HEAD :].astype(jnp.bfloat16)
        forget_log = jax.nn.log_sigmoid(forget_logit + forget_bias[layer_id][None, :])
        local_peak, local_sum, local_out = local_attention(
            queries, forget_log, kv_cache[layer_id], decay_cache[layer_id], owner, live, member
        )
        row_peak, row_sum, row_out = merge_pages(local_peak, local_sum, local_out)
        own_score = (
            jnp.sum(queries.astype(jnp.float32) * new_keys.astype(jnp.float32), axis=2)
            * SCORE_SCALE
        )
        full_peak = jnp.maximum(row_peak, own_score)
        cache_scale = jnp.exp(row_peak - full_peak)
        own_weight = jnp.exp(own_score - full_peak)
        own_rounded = lax.optimization_barrier(own_weight.astype(jnp.bfloat16)).astype(jnp.float32)
        numerator = cache_scale[:, :, None] * row_out + own_rounded[:, :, None] * new_values.astype(
            jnp.float32
        )
        denominator = cache_scale * row_sum + own_weight
        attended = (
            (numerator / denominator[:, :, None])
            .reshape(request_count, local_heads * HEAD)
            .astype(jnp.bfloat16)
        )
        stream = stream + gather_sum(
            jnp.dot(attended, out_weight[layer_id], preferred_element_type=jnp.float32), "gy"
        )
        squares = jnp.sum(stream * stream, axis=1)
        scaled = (stream * feedforward_gain[layer_id][None, :]).astype(jnp.bfloat16)
        gate_part = jnp.dot(scaled, gate_weight[layer_id], preferred_element_type=jnp.float32)
        up_part = jnp.dot(scaled, up_weight[layer_id], preferred_element_type=jnp.float32)
        hidden_cols = gate_part.shape[1]
        total = gather_sum(jnp.concatenate([gate_part, squares[:, None]], axis=1), "gx")
        up_total = gather_sum(up_part, "gx")
        rms_value = jnp.sqrt(total[:, -1] / width + EPSILON)
        gate_full = total[:, :hidden_cols] / rms_value[:, None]
        up_full = up_total / rms_value[:, None]
        hidden = (jax.nn.silu(gate_full) * up_full).astype(jnp.bfloat16)
        stream = stream + gather_sum(
            jnp.dot(hidden, down_weight[layer_id], preferred_element_type=jnp.float32), "gy"
        )
    squares = jnp.sum(stream * stream, axis=1)
    scaled = (stream * final_gain[None, :]).astype(jnp.bfloat16)
    logits = jnp.dot(scaled, head_weight, preferred_element_type=jnp.float32)
    parts = lax.axis_size("gx")
    chunk = logits.shape[1] // parts
    pieces = jnp.concatenate(
        [
            logits.reshape(request_count, parts, chunk),
            jnp.broadcast_to(squares[:, None, None], (request_count, parts, 1)),
        ],
        axis=2,
    )
    pieces = jnp.sum(lax.all_to_all(pieces, "gx", 1, 1, tiled=True), axis=1)
    rms_value = jnp.sqrt(pieces[:, chunk] / width + EPSILON)
    final_hidden = (stream / rms_value[:, None] * final_gain[None, :]).astype(jnp.bfloat16)
    local_top = jnp.max(pieces[:, :chunk], axis=1) / rms_value
    top_logits = lax.pmax(local_top, ("gx", "gy"))
    return (final_hidden, rms_value, top_logits)


def solution(mesh):
    placed = (
        P(None, "gx"),
        P(None, "gx"),
        P(None, "gx"),
        P("gx"),
        P(None, "gx", "gy"),
        P(None, "gx", "gy"),
        P(None, "gy"),
        P(None, "gy", "gx"),
        P(None, "gx", "gy"),
        P(None, "gx", "gy"),
        P(None, "gy", "gx"),
        P("gx", "gy"),
        P(None, "gx", None, "gy", None),
        P(None, "gx", "gy", None),
        P(),
        P(),
    )
    return jax.shard_map(
        local, mesh=mesh, in_specs=placed, out_specs=(P(None, "gx"), P(), P()), check_vma=False
    )
```

time: 828 us -> 302 us (0.36)
  waiting for transfers between devices: 355 us -> 0 us
  local copies, waits for them, and re-layouts: 163 us -> 52.2 us
  other arithmetic: 114 us -> 8.18 us
  blocking collectives: 148 us -> 207 us
  between operations: 14.6 us -> 1.48 us
    psum x7 -> x0, waiting for transfers between devices: 355 us -> none  [the longest x4 208 us: column_total(): return lax.psum(partial_value, 'gy')]
    scatter x2 -> x0, local copies, waits for them, and re-layouts: 121 us -> none  [the longest x1 60.3 us: slot_layout(): jnp.full((slot_count,), -1, jnp.int32).at[targets]]
    all_gather x6 -> x12, blocking collectives: 47.2 us -> 144 us  [the longest x10 126 us: gather_sum(): return jnp.sum(lax.all_gather(value, axis), axis=0)]
    psum x7 -> x0, blocking collectives: 83.9 us -> none  [the longest x5 50.7 us: row_rms(): squares = lax.psum(jnp.sum(stream * stream, axis=1), 'gx')]
    unnamed x5 -> x1, other arithmetic: 62.1 us -> 0.85 us
    sub x1 -> x0, other arithmetic: 39.8 us -> none  [slot_layout(): covered = lengths[safe_owner] - page_index * SHEET_ENTRIES]
    another operation x0 -> x6, local copies, waits for them, and re-layouts: none -> 28.5 us  [the longest x2 28.2 us: local_attention(): kv_flat = kv_layer.reshape(slots, tokens, heads * width)]
    all_to_all x0 -> x1, blocking collectives: none -> 24.4 us  [local(): pieces = jnp.sum(lax.all_to_all(pieces, 'gx', 1, 1, tiled=True), axis=1)]
  transfers between devices with their start and end apart: 7 -> 0, of which waited for: 7 -> 0; matrix products, arithmetic and copies ran while one was open for 0% -> 0% of each run, Pallas kernels for 0% -> 0%
where the time goes in v1:
time: 302 us; the launch traced here: 301 us
  blocking collectives  207 us (69%)
  local copies, waits for them, and re-layouts  52.2 us (17%)
  matrix products  31.3 us (10%)
  other arithmetic  8.18 us (3%)
    all_gather x10, blocking collectives, gather_sum(): return jnp.sum(lax.all_gather(value, axis), axis=0)  126 us
    pmax x1, blocking collectives, local(): top_logits = lax.pmax(local_top, ('gx', 'gy'))  38.6 us
    another operation x2, local copies, waits for them, and re-layouts, local_attention(): kv_flat = kv_layer.reshape(slots, tokens, heads * width)  28.2 us
    all_to_all x1, blocking collectives, local(): pieces = jnp.sum(lax.all_to_all(pieces, 'gx', 1, 1, tiled=True), axis=1)  24.4 us
    all_gather x2, blocking collectives, merge_pages(): every = lax.all_gather(packed, 'gx')  18.3 us
    slice x1, local copies, waits for them, and re-layouts, local(): kv_cache[layer_id]  14.9 us
    dot_general x2, matrix products, local_attention(): jnp.einsum('ptc,phc->pht', kv_flat, query_block, preferred_element_type=j...  11.5 us
    dot_general x2, matrix products, local_attention(): jnp.einsum('pht,ptc->phc', weights.astype(jnp.bfloat16), kv_flat, preferr...  9.33 us

profile of v1, /device:TPU:0, one launch (start us, length us, event | category | flops | bytes accessed | tf_op | source)
XLA Modules:
  0.0 300.6 jit_solution(10429559740980360728)
XLA Ops:
  0.6 0.9 fusion.43
  1.6 0.8 slice_reduce_fusion.2
  2.4 0.9 fusion.81
  3.4 1.2 fusion.30
  4.6 11.5 %all-gather = f32[256,387]{1,0:T(8,128)S(1)} all-gather(f32[64,387]{1,0:T(8,128)S(1)} %pad_maximum_fusion.3), channel_id=2, replica_groups=mesh['gx'=4,'gy'=8] {'gx'}, dimensions={0}, use_global_device_ids=true | all-gather | bytes 495360 | tf_op jit(solution)/shard_map/all_gather | solution.py:17
  16.4 0.8 subtract_bitcast_fusion
  17.5 0.3 convolution_convert_fusion
  17.8 14.9 %fusion.135 = (bf16[1,128,128,2,128]{4,3,2,1,0:T(2,128)(2,1)}, bf16[1,128,128,2,128]{4,3,2,1,0:T(2,128)(2,1)}) fusion(bf16[2,128,128,2,128]{4,3,2,1,0:T(2,128)(2,1)} %param.28), kind=kLoop, calls=%fused_computation.233 | loop fusion | bytes 33554432 | tf_op jit(solution)/shard_map/slice | solution.py:136
  32.8 14.1 %reshape_squeeze.6 = bf16[128,128,256]{2,1,0:T(8,128)(2,1)} reshape(bf16[1,128,128,2,128]{4,3,2,1,0:T(2,128)(2,1)} %get-tuple-element.18) | data formatting | bytes 16777216 | tf_op jit(solution)/shard_map/reshape;squeeze | solution.py:48
  47.5 0.6 gather_fusion.1
  48.2 0.7 gather_fusion
  49.8 5.7 %fusion.140 = (f32[128,2]{1,0:T(8,128)S(1)}, f32[128,2,128]{2,1,0:T(2,128)S(1)}) fusion(f32[128,2]{1,0:T(8,128)S(1)} %gather_fusion.1, f32[2,128,2,128]{3,2,1,0:T(2,128)S(1)} %copy-done.13, bf16[128,128,256]{2,1,0:T(8,128)(2,1)} %reshape_squeeze.6, bf16[128,2,256]{2,1,0:T(2,128)(2,1)S(1)} %mul.276, bf16[2,256]{1,0:T(2,128)(2,1)S(1)} %bitcast.152, ...), kind=kOutput, calls=%fused_computation.238 | convolution fusion | flops 17202944 | bytes 8801280 | tf_op jit(solution)/shard_map/ptc,phc->pht/dot_general | solution.py:55
  55.8 0.7 gather_fusion.2
  56.5 4.7 %fusion.73 = f32[128,2,256]{2,1,0:T(2,128)S(1)} fusion(bf16[128,128,256]{2,1,0:T(8,128)(2,1)} %reshape_squeeze.6, f32[128,2,128]{2,1,0:T(2,128)S(1)} %get-tuple-element.47, pred[128,128]{1,0:T(8,128)(4,1)S(1)} %fusion.78, f32[128,2]{1,0:T(8,128)S(1)} %gather_fusion.2), kind=kOutput, calls=%fused_computation.133 | convolution fusion | flops 16875520 | bytes 8799232 | tf_op jit(solution)/shard_map/pht,ptc->phc/dot_general | solution.py:65
  61.2 0.4 fusion.130
  61.6 0.2 multiply_reduce_fusion.5
  61.9 0.2 convolution_bitcast_fusion.1
  62.4 0.2 fusion.59
  62.7 9.0 %all-gather.1 = f32[256,2,66]{2,0,1:T(8,128)S(1)} all-gather(f32[64,2,66]{2,0,1:T(8,128)S(1)} %pad_maximum_fusion.5), channel_id=3, replica_groups=mesh['gx'=4,'gy'=8] {'gx'}, dimensions={0}, use_global_device_ids=true | all-gather | bytes 168960 | tf_op jit(solution)/shard_map/all_gather | solution.py:77
  72.0 0.2 fusion.35
  73.0 16.5 %all-gather.2 = f32[512,384]{1,0:T(8,128)S(1)} all-gather(f32[64,384]{1,0:T(8,128)S(1)} %fusion.48), channel_id=4, replica_groups=mesh['gx'=4,'gy'=8] {'gy'}, dimensions={0}, use_global_device_ids=true | all-gather | bytes 884736 | tf_op jit(solution)/shard_map/all_gather | solution.py:17
  89.8 9.5 %all-gather.4 = f32[256,512]{1,0:T(8,128)S(1)} all-gather(f32[64,512]{1,0:T(8,128)S(1)} %fusion.18), channel_id=6, replica_groups=mesh['gx'=4,'gy'=8] {'gx'}, dimensions={0}, use_global_device_ids=true | all-gather | bytes 655360 | tf_op jit(solution)/shard_map/all_gather | solution.py:17
  99.6 11.2 %all-gather.3 = f32[256,513]{1,0:T(8,128)S(1)} all-gather(f32[64,513]{1,0:T(8,128)S(1)} %pad_maximum_fusion.1), channel_id=5, replica_groups=mesh['gx'=4,'gy'=8] {'gx'}, dimensions={0}, use_global_device_ids=true | all-gather | bytes 656640 | tf_op jit(solution)/shard_map/all_gather | solution.py:17
  111.0 1.3 fusion.16
  112.3 15.7 %all-gather.5 = f32[512,384]{1,0:T(8,128)S(1)} all-gather(f32[64,384]{1,0:T(8,128)S(1)} %fusion.16), channel_id=7, replica_groups=mesh['gx'=4,'gy'=8] {'gy'}, dimensions={0}, use_global_device_ids=true | all-gather | bytes 884736 | tf_op jit(solution)/shard_map/all_gather | solution.py:17
  128.7 9.5 %all-gather.6 = f32[256,387]{1,0:T(8,128)S(1)} all-gather(f32[64,387]{1,0:T(8,128)S(1)} %pad_maximum_fusion.4), channel_id=8, replica_groups=mesh['gx'=4,'gy'=8] {'gx'}, dimensions={0}, use_global_device_ids=true | all-gather | bytes 495360 | tf_op jit(solution)/shard_map/all_gather | solution.py:17
  138.5 14.2 %reshape_squeeze.7 = bf16[128,128,256]{2,1,0:T(8,128)(2,1)} reshape(bf16[1,128,128,2,128]{4,3,2,1,0:T(2,128)(2,1)} %get-tuple-element.17) | data formatting | bytes 16777216 | tf_op jit(solution)/shard_map/reshape;squeeze | solution.py:48
  153.0 0.7 gather_fusion.4
  153.8 0.7 gather_fusion.3
  154.8 5.7 %fusion.141 = (f32[128,2]{1,0:T(8,128)S(1)}, f32[128,2,128]{2,1,0:T(2,128)S(1)}) fusion(f32[128,2]{1,0:T(8,128)S(1)} %gather_fusion.4, f32[2,128,2,128]{3,2,1,0:T(2,128)S(1)} %copy-done.14, bf16[128,128,256]{2,1,0:T(8,128)(2,1)} %reshape_squeeze.7, bf16[128,2,256]{2,1,0:T(2,128)(2,1)S(1)} %mul.301, bf16[2,256]{1,0:T(2,128)(2,1)S(1)} %bitcast.153, ...), kind=kOutput, calls=%fused_computation.239 | convolution fusion | flops 17202944 | bytes 8801280 | tf_op jit(solution)/shard_map/ptc,phc->pht/dot_general | solution.py:55
  160.9 0.7 gather_fusion.5
  161.5 4.6 %fusion.68 = f32[128,2,256]{2,1,0:T(2,128)S(1)} fusion(bf16[128,128,256]{2,1,0:T(8,128)(2,1)} %reshape_squeeze.7, f32[128,2,128]{2,1,0:T(2,128)S(1)} %get-tuple-element.49, pred[128,128]{1,0:T(8,128)(4,1)S(1)} %fusion.78, f32[128,2]{1,0:T(8,128)S(1)} %gather_fusion.5), kind=kOutput, calls=%fused_computation.125 | convolution fusion | flops 16875520 | bytes 8799232 | tf_op jit(solution)/shard_map/pht,ptc->phc/dot_general | solution.py:65
  166.2 0.4 fusion.131
  166.5 0.2 multiply_reduce_fusion.4
  166.9 0.2 convolution_bitcast_fusion
  167.4 0.3 fusion.63
  167.7 9.4 %all-gather.7 = f32[256,2,66]{2,0,1:T(8,128)S(1)} all-gather(f32[64,2,66]{2,0,1:T(8,128)S(1)} %pad_maximum_fusion.6), channel_id=9, replica_groups=mesh['gx'=4,'gy'=8] {'gx'}, dimensions={0}, use_global_device_ids=true | all-gather | bytes 168960 | tf_op jit(solution)/shard_map/all_gather | solution.py:77
  177.4 0.2 fusion.34
  178.3 15.7 %all-gather.8 = f32[512,384]{1,0:T(8,128)S(1)} all-gather(f32[64,384]{1,0:T(8,128)S(1)} %fusion.46), channel_id=10, replica_groups=mesh['gx'=4,'gy'=8] {'gy'}, dimensions={0}, use_global_device_ids=true | all-gather | bytes 884736 | tf_op jit(solution)/shard_map/all_gather | solution.py:17
  194.2 0.2 fusion.12
  194.6 9.3 %all-gather.10 = f32[256,512]{1,0:T(8,128)S(1)} all-gather(f32[64,512]{1,0:T(8,128)S(1)} %fusion.12), channel_id=12, replica_groups=mesh['gx'=4,'gy'=8] {'gx'}, dimensions={0}, use_global_device_ids=true | all-gather | bytes 655360 | tf_op jit(solution)/shard_map/all_gather | solution.py:17
  204.0 11.4 %all-gather.9 = f32[256,513]{1,0:T(8,128)S(1)} all-gather(f32[64,513]{1,0:T(8,128)S(1)} %pad_maximum_fusion.2), channel_id=11, replica_groups=mesh['gx'=4,'gy'=8] {'gx'}, dimensions={0}, use_global_device_ids=true | all-gather | bytes 656640 | tf_op jit(solution)/shard_map/all_gather | solution.py:17
  215.6 1.3 fusion.10
  216.9 15.7 %all-gather.11 = f32[512,384]{1,0:T(8,128)S(1)} all-gather(f32[64,384]{1,0:T(8,128)S(1)} %fusion.10), channel_id=13, replica_groups=mesh['gx'=4,'gy'=8] {'gy'}, dimensions={0}, use_global_device_ids=true | all-gather | bytes 884736 | tf_op jit(solution)/shard_map/all_gather | solution.py:17
  232.8 3.3 %fusion.79 = f32[64,6144]{1,0:T(8,128)S(1)} fusion(bf16[384,6144]{1,0:T(8,128)(2,1)} %param.27, f32[64,384]{1,0:T(8,128)S(1)} %get-tuple-element.8, f32[384]{0:T(512)S(1)} %copy-done.8), kind=kOutput, calls=%fused_computation.143 | convolution fusion | flops 302039040 | bytes 6391296 | tf_op jit(solution)/shard_map/dot_general | solution.py:175
  236.4 24.4 %all_to_all.5 = f32[64,4,1537]{2,0,1:T(8,128)S(1)} all-to-all(f32[64,4,1537]{2,0,1:T(8,128)S(1)} %pad_maximum_fusion), channel_id=1, replica_groups=mesh['gx'=4,'gy'=8] {'gx'}, dimensions={1} | all-to-all | bytes 3147776 | tf_op jit(solution)/shard_map/all_to_all | solution.py:185
  261.2 0.7 multiply_convert_fusion.2
  261.9 38.6 %pmax.7 = f32[64]{0:T(128)} all-reduce(f32[64]{0:T(128)S(1)} %div.175), channel_id=1, replica_groups=mesh['gx'=4,'gy'=8] {'gx','gy'}, use_global_device_ids=true, to_apply=%region_32.33 | all-reduce | flops 64 | bytes 512 | tf_op jit(solution)/shard_map/pmax | solution.py:189
  (150 shorter events, 9.4 us)
Async XLA Ops:
  16.2 16.6 %copy-start.3 = (f32[64,387]{1,0:T(8,128)}, f32[64,387]{1,0:T(8,128)S(1)}, u32[]{:S(2)}) copy-start(f32[64,387]{1,0:T(8,128)S(1)} %reduce_sum.227) | copy-start | bytes 297220
  32.7 14.2 %slice-start = ((f32[64,387]{1,0:T(8,128)}), f32[64,2]{1,0:T(8,128)S(1)}, s32[]{:S(2)}) async-start(f32[64,387]{1,0:T(8,128)} %copy-done.3), calls=%async_computation.1 | async-start | bytes 65536 | tf_op jit(solution)/shard_map/slice | solution.py:130
  32.7 14.2 %copy-start.12 = (f32[2,2]{1,0:T(2,128)S(1)}, f32[2,2]{1,0:T(2,128)}, u32[]{:S(2)}) copy-start(f32[2,2]{1,0:T(2,128)} %param.22) | copy-start | bytes 52
  32.7 14.2 %copy-start.4 = (f32[64,387]{1,0:T(8,128)S(1)}, f32[64,387]{1,0:T(8,128)}, u32[]{:S(2)}) copy-start(f32[64,387]{1,0:T(8,128)} %copy-done.3) | copy-start | bytes 297220
  32.8 16.6 %copy-start.15 = (s32[64]{0:T(128)S(1)}, s32[64]{0:T(128)}, u32[]{:S(2)}) copy-start(s32[64]{0:T(128)} %param.30) | copy-start | bytes 772
  32.8 17.0 %copy-start.13 = (f32[2,128,2,128]{3,2,1,0:T(2,128)S(1)}, f32[2,128,2,128]{3,2,1,0:T(2,128)}, u32[]{:S(2)}) copy-start(f32[2,128,2,128]{3,2,1,0:T(2,128)} %param.29) | copy-start | bytes 786436
  55.5 17.3 %copy-start.6 = (bf16[2,128,384]{2,1,0:T(8,128)(2,1)S(1)}, bf16[2,128,384]{2,1,0:T(8,128)(2,1)}, u32[]{:S(2)}) copy-start(bf16[2,128,384]{2,1,0:T(8,128)(2,1)} %param.23) | copy-start | bytes 589828
  55.5 34.0 %copy-start.10 = (f32[2,384]{1,0:T(2,128)S(1)}, f32[2,384]{1,0:T(2,128)}, u32[]{:S(2)}) copy-start(f32[2,384]{1,0:T(2,128)} %param.18) | copy-start | bytes 9220
  55.5 34.0 %copy-start = (bf16[64,384]{1,0:T(8,128)(2,1)S(1)}, bf16[64,384]{1,0:T(8,128)(2,1)}, u32[]{:S(2)}) copy-start(bf16[64,384]{1,0:T(8,128)(2,1)} %param.16) | copy-start | bytes 147460
  55.5 34.1 %copy-start.1 = (bf16[2,384,512]{2,1,0:T(8,128)(2,1)S(1)}, bf16[2,384,512]{2,1,0:T(8,128)(2,1)}, u32[]{:S(2)}) copy-start(bf16[2,384,512]{2,1,0:T(8,128)(2,1)} %param.25) | copy-start | bytes 2359300
  56.5 43.0 %copy-start.2 = (bf16[2,384,512]{2,1,0:T(8,128)(2,1)S(1)}, bf16[2,384,512]{2,1,0:T(8,128)(2,1)}, u32[]{:S(2)}) copy-start(bf16[2,384,512]{2,1,0:T(8,128)(2,1)} %param.24) | copy-start | bytes 2359300
  61.2 67.0 %copy-start.9 = (bf16[2,384,2]{1,2,0:T(2,128)(2,1)S(1)}, bf16[2,384,2]{1,2,0:T(2,128)(2,1)}, u32[]{:S(2)}) copy-start(bf16[2,384,2]{1,2,0:T(2,128)(2,1)} %param.21) | copy-start | bytes 9220
  61.2 67.2 %copy-start.5 = (bf16[2,384,384]{2,1,0:T(8,128)(2,1)S(1)}, bf16[2,384,384]{2,1,0:T(8,128)(2,1)}, u32[]{:S(2)}) copy-start(bf16[2,384,384]{2,1,0:T(8,128)(2,1)} %param.20) | copy-start | bytes 1769476
  138.5 16.3 %copy-start.14 = (f32[2,128,2,128]{3,2,1,0:T(2,128)S(1)}, f32[2,128,2,128]{3,2,1,0:T(2,128)}, u32[]{:S(2)}) copy-start(f32[2,128,2,128]{3,2,1,0:T(2,128)} %param.29) | copy-start | bytes 786436
  160.6 17.6 %copy-start.7 = (bf16[2,128,384]{2,1,0:T(8,128)(2,1)S(1)}, bf16[2,128,384]{2,1,0:T(8,128)(2,1)}, u32[]{:S(2)}) copy-start(bf16[2,128,384]{2,1,0:T(8,128)(2,1)} %param.23) | copy-start | bytes 589828
  166.1 66.6 %copy-start.8 = (f32[384]{0:T(512)S(1)}, f32[384]{0:T(512)}, u32[]{:S(2)}) copy-start(f32[384]{0:T(512)} %param.19) | copy-start | bytes 4612
  261.1 39.5 %copy-start.11 = (f32[64]{0:T(128)}, f32[64]{0:T(128)S(1)}, u32[]{:S(2)}) copy-start(f32[64]{0:T(128)S(1)} %fusion.88) | copy-start | bytes 772

commit v2 on v1

--- a/solution.py
+++ b/solution.py
@@ -43,17 +43,13 @@
 
 def local_attention(queries, forget_log, kv_layer, decay_layer, owner, live, member):
     slots, tokens, heads, width = kv_layer.shape
-    request_count = queries.shape[0]
     safe_owner = jnp.maximum(owner, 0)
-    kv_flat = kv_layer.reshape(slots, tokens, heads * width)
     slot_queries = queries[safe_owner]
     padded = jnp.concatenate([slot_queries, jnp.zeros_like(slot_queries)], axis=2)
     diagonal = jnp.eye(heads, dtype=jnp.bfloat16)
-    query_block = (diagonal[None, :, :, None] * padded[:, :, None, :]).reshape(
-        slots, heads, heads * width
-    )
+    query_block = diagonal[None, :, :, None] * padded[:, :, None, :]
     scores = jnp.einsum(
-        "ptc,phc->pht", kv_flat, query_block, preferred_element_type=jnp.float32
+        "pthc,pkhc->pkt", kv_layer, query_block, preferred_element_type=jnp.float32
     ) * SCORE_SCALE
     scores = scores + decay_layer + forget_log[safe_owner][:, :, None]
     scores = jnp.where(live[:, None, :], scores, NEGATIVE)
@@ -63,8 +59,8 @@
     weights = jnp.where(live[:, None, :], jnp.exp(scores - slot_peak[:, :, None]), 0.0)
     page_sum = jnp.sum(weights, axis=2)
     mixed = jnp.einsum(
-        "pht,ptc->phc", weights.astype(jnp.bfloat16), kv_flat, preferred_element_type=jnp.float32
-    ).reshape(slots, heads, heads, width)
+        "pkt,pthc->pkhc", weights.astype(jnp.bfloat16), kv_layer, preferred_element_type=jnp.float32
+    )
     page_out = jnp.stack([mixed[:, h, h, HEAD:] for h in range(heads)], axis=1)
     member_f = member.astype(jnp.float32)
     row_sum = jnp.einsum("rp,ph->rh", member_f, page_sum, precision=lax.Precision.HIGHEST)
@@ -186,7 +182,7 @@
     rms_value = jnp.sqrt(pieces[:, chunk] / width + EPSILON)
     final_hidden = (stream / rms_value[:, None] * final_gain[None, :]).astype(jnp.bfloat16)
     local_top = jnp.max(pieces[:, :chunk], axis=1) / rms_value
-    top_logits = lax.pmax(local_top, ("gx", "gy"))
+    top_logits = lax.pmax(lax.pmax(local_top, "gx"), "gy")
     return (final_hidden, rms_value, top_logits)
 
 

time: 302 us -> 257 us (0.85)
  local copies, waits for them, and re-layouts: 52.2 us -> 26.8 us
  blocking collectives: 207 us -> 191 us
  matrix products: 31.3 us -> 27.9 us
    another operation x6 -> x2, local copies, waits for them, and re-layouts: 28.5 us -> 0.2 us  [the longest x2 28.2 us: local_attention(): kv_flat = kv_layer.reshape(slots, tokens, heads * width)]
    pmax x1 -> x2, blocking collectives: 38.6 us -> 22.7 us  [local(): top_logits = lax.pmax(lax.pmax(local_top, 'gx'), 'gy')]
    dot_general x4, matrix products: 20.8 us -> 17.5 us  [the longest x2 9.27 us: local_attention(): jnp.einsum('pkt,pthc->pkhc', weights.astype(jnp.bfloat16), kv_layer, pref...]
where the time goes in v2:
time: 257 us; the launch traced here: 256 us
  blocking collectives  191 us (74%)
  matrix products  27.9 us (11%)
  local copies, waits for them, and re-layouts  26.8 us (10%)
  other arithmetic  8.77 us (3%)
    all_gather x10, blocking collectives, gather_sum(): return jnp.sum(lax.all_gather(value, axis), axis=0)  126 us
    all_to_all x1, blocking collectives, local(): pieces = jnp.sum(lax.all_to_all(pieces, 'gx', 1, 1, tiled=True), axis=1)  24.4 us
    pmax x2, blocking collectives, local(): top_logits = lax.pmax(lax.pmax(local_top, 'gx'), 'gy')  22.7 us
    all_gather x2, blocking collectives, merge_pages(): every = lax.all_gather(packed, 'gx')  18.3 us
    slice x1, local copies, waits for them, and re-layouts, local(): kv_cache[layer_id]  14 us
    dot_general x2, matrix products, local_attention(): jnp.einsum('pkt,pthc->pkhc', weights.astype(jnp.bfloat16), kv_layer, pref...  9.27 us
    dot_general x2, matrix products, local_attention(): jnp.einsum('pthc,pkhc->pkt', kv_layer, query_block, preferred_element_typ...  8.25 us

profile of v2, /device:TPU:0, one launch (start us, length us, event | category | flops | bytes accessed | tf_op | source)
XLA Modules:
  0.0 256.2 jit_solution(4576220176391048034)
XLA Ops:
  0.7 0.9 fusion.59
  1.6 0.8 slice_reduce_fusion.2
  2.5 0.9 fusion.91
  3.4 1.2 fusion.38
  4.6 11.5 %all-gather = f32[256,387]{1,0:T(8,128)S(1)} all-gather(f32[64,387]{1,0:T(8,128)S(1)} %pad_maximum_fusion.3), channel_id=2, replica_groups=mesh['gx'=4,'gy'=8] {'gx'}, dimensions={0}, use_global_device_ids=true | all-gather | bytes 495360 | tf_op jit(solution)/shard_map/all_gather | solution.py:17
  16.6 0.2 multiply_reduce_fusion.5
  16.9 0.8 subtract_bitcast_fusion
  17.9 0.3 convolution_convert_fusion
  18.3 0.8 slice_bitcast_fusion
  19.6 0.7 select_reduce_fusion.2
  20.5 0.6 gather_fusion.1
  21.1 0.7 gather_fusion
  21.9 14.0 %fusion.145 = (bf16[1,128,128,2,128]{4,3,2,1,0:T(2,128)(2,1)}, bf16[1,128,128,2,128]{4,3,2,1,0:T(2,128)(2,1)S(1)}) fusion(bf16[2,128,128,2,128]{4,3,2,1,0:T(2,128)(2,1)} %param.28), kind=kLoop, calls=%fused_computation.237 | loop fusion | bytes 33554432 | tf_op jit(solution)/shard_map/slice | solution.py:132
  36.1 3.0 %copy-done = bf16[1,128,128,2,128]{4,3,2,1,0:T(2,128)(2,1)} copy-done((bf16[1,128,128,2,128]{4,3,2,1,0:T(2,128)(2,1)}, bf16[1,128,128,2,128]{4,3,2,1,0:T(2,128)(2,1)S(1)}, u32[]{:S(2)}) %copy-start) | copy-done | bytes 8388632
  39.1 2.4 fusion.152
  41.8 0.7 gather_fusion.2
  42.5 4.6 %fusion = f32[128,2,2,128]{3,1,2,0:T(2,128)S(1)} fusion(bf16[1,128,128,2,128]{4,3,2,1,0:T(2,128)(2,1)} %copy-done, f32[128,2,128]{2,1,0:T(2,128)S(1)} %get-tuple-element.47, pred[128,128]{1,0:T(8,128)(4,1)S(1)} %fusion.88, f32[128,2]{1,0:T(8,128)S(1)} %gather_fusion.2), kind=kOutput, calls=%fused_computation.8 | convolution fusion | flops 16875520 | bytes 8799232 | tf_op jit(solution)/shard_map/pkt,pthc->pkhc/dot_general | solution.py:61
  47.1 0.4 fusion.140
  47.6 0.3 fusion.149
  47.9 0.2 convolution_bitcast_fusion.1
  48.7 9.0 %all-gather.1 = f32[256,2,66]{2,0,1:T(8,128)S(1)} all-gather(f32[64,2,66]{2,0,1:T(8,128)S(1)} %pad_maximum_fusion.5), channel_id=3, replica_groups=mesh['gx'=4,'gy'=8] {'gx'}, dimensions={0}, use_global_device_ids=true | all-gather | bytes 168960 | tf_op jit(solution)/shard_map/all_gather | solution.py:73
  58.2 0.2 fusion.43
  58.8 16.5 %all-gather.2 = f32[512,384]{1,0:T(8,128)S(1)} all-gather(f32[64,384]{1,0:T(8,128)S(1)} %fusion.64), channel_id=4, replica_groups=mesh['gx'=4,'gy'=8] {'gy'}, dimensions={0}, use_global_device_ids=true | all-gather | bytes 884736 | tf_op jit(solution)/shard_map/all_gather | solution.py:17
  75.9 9.5 %all-gather.4 = f32[256,512]{1,0:T(8,128)S(1)} all-gather(f32[64,512]{1,0:T(8,128)S(1)} %fusion.26), channel_id=6, replica_groups=mesh['gx'=4,'gy'=8] {'gx'}, dimensions={0}, use_global_device_ids=true | all-gather | bytes 655360 | tf_op jit(solution)/shard_map/all_gather | solution.py:17
  85.5 11.2 %all-gather.3 = f32[256,513]{1,0:T(8,128)S(1)} all-gather(f32[64,513]{1,0:T(8,128)S(1)} %pad_maximum_fusion.1), channel_id=5, replica_groups=mesh['gx'=4,'gy'=8] {'gx'}, dimensions={0}, use_global_device_ids=true | all-gather | bytes 656640 | tf_op jit(solution)/shard_map/all_gather | solution.py:17
  96.9 1.3 fusion.24
  98.1 15.7 %all-gather.5 = f32[512,384]{1,0:T(8,128)S(1)} all-gather(f32[64,384]{1,0:T(8,128)S(1)} %fusion.24), channel_id=7, replica_groups=mesh['gx'=4,'gy'=8] {'gy'}, dimensions={0}, use_global_device_ids=true | all-gather | bytes 884736 | tf_op jit(solution)/shard_map/all_gather | solution.py:17
  114.5 9.5 %all-gather.6 = f32[256,387]{1,0:T(8,128)S(1)} all-gather(f32[64,387]{1,0:T(8,128)S(1)} %pad_maximum_fusion.4), channel_id=8, replica_groups=mesh['gx'=4,'gy'=8] {'gx'}, dimensions={0}, use_global_device_ids=true | all-gather | bytes 495360 | tf_op jit(solution)/shard_map/all_gather | solution.py:17
  124.5 0.2 multiply_reduce_fusion.4
  125.0 0.7 gather_fusion.4
  125.6 0.7 gather_fusion.3
  126.5 5.8 %fusion.153 = (f32[128,2]{1,0:T(8,128)S(1)}, f32[128,2,128]{2,1,0:T(2,128)S(1)}) fusion(f32[128,2]{1,0:T(8,128)S(1)} %gather_fusion.4, f32[2,128,2,128]{3,2,1,0:T(2,128)} %param.29, bf16[1,128,128,2,128]{4,3,2,1,0:T(2,128)(2,1)} %get-tuple-element.17, bf16[128,2,128]{2,1,0:T(2,128)(2,1)S(1)} %concatenate.37, bf16[2,2]{0,1:T(2,128)(2,1)S(1)} %compare_convert_fusion, ...), kind=kOutput, calls=%fused_computation.245 | convolution fusion | flops 17202944 | bytes 8734728 | tf_op jit(solution)/shard_map/pthc,pkhc->pkt/dot_general | solution.py:51
  132.6 0.7 gather_fusion.5
  133.2 4.6 %fusion.2 = f32[128,2,2,128]{3,1,2,0:T(2,128)S(1)} fusion(bf16[1,128,128,2,128]{4,3,2,1,0:T(2,128)(2,1)} %get-tuple-element.17, f32[128,2,128]{2,1,0:T(2,128)S(1)} %get-tuple-element.49, pred[128,128]{1,0:T(8,128)(4,1)S(1)} %fusion.88, f32[128,2]{1,0:T(8,128)S(1)} %gather_fusion.5), kind=kOutput, calls=%fused_computation.10 | convolution fusion | flops 16875520 | bytes 8799232 | tf_op jit(solution)/shard_map/pkt,pthc->pkhc/dot_general | solution.py:61
  137.9 0.4 fusion.141
  138.3 0.3 fusion.147
  139.4 9.4 %all-gather.7 = f32[256,2,66]{2,0,1:T(8,128)S(1)} all-gather(f32[64,2,66]{2,0,1:T(8,128)S(1)} %pad_maximum_fusion.6), channel_id=9, replica_groups=mesh['gx'=4,'gy'=8] {'gx'}, dimensions={0}, use_global_device_ids=true | all-gather | bytes 168960 | tf_op jit(solution)/shard_map/all_gather | solution.py:73
  149.3 0.2 fusion.42
  149.9 15.7 %all-gather.8 = f32[512,384]{1,0:T(8,128)S(1)} all-gather(f32[64,384]{1,0:T(8,128)S(1)} %fusion.62), channel_id=10, replica_groups=mesh['gx'=4,'gy'=8] {'gy'}, dimensions={0}, use_global_device_ids=true | all-gather | bytes 884736 | tf_op jit(solution)/shard_map/all_gather | solution.py:17
  166.3 9.3 %all-gather.10 = f32[256,512]{1,0:T(8,128)S(1)} all-gather(f32[64,512]{1,0:T(8,128)S(1)} %fusion.20), channel_id=12, replica_groups=mesh['gx'=4,'gy'=8] {'gx'}, dimensions={0}, use_global_device_ids=true | all-gather | bytes 655360 | tf_op jit(solution)/shard_map/all_gather | solution.py:17
  175.6 11.4 %all-gather.9 = f32[256,513]{1,0:T(8,128)S(1)} all-gather(f32[64,513]{1,0:T(8,128)S(1)} %pad_maximum_fusion.2), channel_id=11, replica_groups=mesh['gx'=4,'gy'=8] {'gx'}, dimensions={0}, use_global_device_ids=true | all-gather | bytes 656640 | tf_op jit(solution)/shard_map/all_gather | solution.py:17
  187.2 1.3 fusion.18
  188.5 15.7 %all-gather.11 = f32[512,384]{1,0:T(8,128)S(1)} all-gather(f32[64,384]{1,0:T(8,128)S(1)} %fusion.18), channel_id=13, replica_groups=mesh['gx'=4,'gy'=8] {'gy'}, dimensions={0}, use_global_device_ids=true | all-gather | bytes 884736 | tf_op jit(solution)/shard_map/all_gather | solution.py:17
  204.4 3.3 %fusion.89 = f32[64,6144]{1,0:T(8,128)S(1)} fusion(bf16[384,6144]{1,0:T(8,128)(2,1)} %param.27, f32[64,384]{1,0:T(8,128)S(1)} %get-tuple-element.8, f32[384]{0:T(512)S(1)} %copy-done.7), kind=kOutput, calls=%fused_computation.153 | convolution fusion | flops 302039040 | bytes 6391296 | tf_op jit(solution)/shard_map/dot_general | solution.py:171
  208.0 24.4 %all_to_all.5 = f32[64,4,1537]{2,0,1:T(8,128)S(1)} all-to-all(f32[64,4,1537]{2,0,1:T(8,128)S(1)} %pad_maximum_fusion), channel_id=1, replica_groups=mesh['gx'=4,'gy'=8] {'gx'}, dimensions={1} | all-to-all | bytes 3147776 | tf_op jit(solution)/shard_map/all_to_all | solution.py:181
  232.8 0.7 multiply_convert_fusion.2
  233.5 8.4 %pmax.14 = f32[64]{0:T(128)S(1)} all-reduce(f32[64]{0:T(128)S(1)} %div.175), channel_id=1, replica_groups=mesh['gx'=4,'gy'=8] {'gx'}, use_global_device_ids=true, to_apply=%region_32.33 | all-reduce | flops 64 | bytes 512 | tf_op jit(solution)/shard_map/pmax | solution.py:185
  241.9 14.3 %pmax.15 = f32[64]{0:T(128)} all-reduce(f32[64]{0:T(128)S(1)} %pmax.14), channel_id=1, replica_groups=mesh['gx'=4,'gy'=8] {'gy'}, use_global_device_ids=true, to_apply=%region_33.34 | all-reduce | flops 64 | bytes 512 | tf_op jit(solution)/shard_map/pmax | solution.py:185
  (132 shorter events, 9.4 us)
Async XLA Ops:
  21.8 17.2 %copy-start.11 = (f32[2,128,2,128]{3,2,1,0:T(2,128)S(1)}, f32[2,128,2,128]{3,2,1,0:T(2,128)}, u32[]{:S(2)}) copy-start(f32[2,128,2,128]{3,2,1,0:T(2,128)} %param.29) | copy-start | bytes 786436
  35.9 3.2 %copy-start = (bf16[1,128,128,2,128]{4,3,2,1,0:T(2,128)(2,1)}, bf16[1,128,128,2,128]{4,3,2,1,0:T(2,128)(2,1)S(1)}, u32[]{:S(2)}) copy-start(bf16[1,128,128,2,128]{4,3,2,1,0:T(2,128)(2,1)S(1)} %get-tuple-element.18) | copy-start | bytes 25165828
  39.1 8.4 %copy-start.9 = (f32[2,384]{1,0:T(2,128)S(1)}, f32[2,384]{1,0:T(2,128)}, u32[]{:S(2)}) copy-start(f32[2,384]{1,0:T(2,128)} %param.18) | copy-start | bytes 9220
  41.5 17.2 %copy-start.5 = (bf16[2,128,384]{2,1,0:T(8,128)(2,1)S(1)}, bf16[2,128,384]{2,1,0:T(8,128)(2,1)}, u32[]{:S(2)}) copy-start(bf16[2,128,384]{2,1,0:T(8,128)(2,1)} %param.23) | copy-start | bytes 589828
  41.5 33.8 %copy-start.1 = (bf16[64,384]{1,0:T(8,128)(2,1)S(1)}, bf16[64,384]{1,0:T(8,128)(2,1)}, u32[]{:S(2)}) copy-start(bf16[64,384]{1,0:T(8,128)(2,1)} %param.16) | copy-start | bytes 147460
  41.5 34.0 %copy-start.2 = (bf16[2,384,512]{2,1,0:T(8,128)(2,1)S(1)}, bf16[2,384,512]{2,1,0:T(8,128)(2,1)}, u32[]{:S(2)}) copy-start(bf16[2,384,512]{2,1,0:T(8,128)(2,1)} %param.25) | copy-start | bytes 2359300
  41.5 34.2 %copy-start.3 = (bf16[2,384,512]{2,1,0:T(8,128)(2,1)S(1)}, bf16[2,384,512]{2,1,0:T(8,128)(2,1)}, u32[]{:S(2)}) copy-start(bf16[2,384,512]{2,1,0:T(8,128)(2,1)} %param.24) | copy-start | bytes 2359300
  47.1 66.9 %copy-start.8 = (bf16[2,384,2]{1,2,0:T(2,128)(2,1)S(1)}, bf16[2,384,2]{1,2,0:T(2,128)(2,1)}, u32[]{:S(2)}) copy-start(bf16[2,384,2]{1,2,0:T(2,128)(2,1)} %param.21) | copy-start | bytes 9220
  47.1 67.0 %copy-start.4 = (bf16[2,384,384]{2,1,0:T(8,128)(2,1)S(1)}, bf16[2,384,384]{2,1,0:T(8,128)(2,1)}, u32[]{:S(2)}) copy-start(bf16[2,384,384]{2,1,0:T(8,128)(2,1)} %param.20) | copy-start | bytes 1769476
  132.3 17.5 %copy-start.6 = (bf16[2,128,384]{2,1,0:T(8,128)(2,1)S(1)}, bf16[2,128,384]{2,1,0:T(8,128)(2,1)}, u32[]{:S(2)}) copy-start(bf16[2,128,384]{2,1,0:T(8,128)(2,1)} %param.23) | copy-start | bytes 589828
  137.9 66.5 %copy-start.7 = (f32[384]{0:T(512)S(1)}, f32[384]{0:T(512)}, u32[]{:S(2)}) copy-start(f32[384]{0:T(512)} %param.19) | copy-start | bytes 4612
  232.7 23.5 %copy-start.10 = (f32[64]{0:T(128)}, f32[64]{0:T(128)S(1)}, u32[]{:S(2)}) copy-start(f32[64]{0:T(128)S(1)} %fusion.98) | copy-start | bytes 772

commit v3 on v2

--- a/solution.py
+++ b/solution.py
@@ -15,6 +15,16 @@
 
 def gather_sum(value, axis):
     return jnp.sum(lax.all_gather(value, axis), axis=0)
+
+
+def xor_sum(value, axis):
+    count = lax.axis_size(axis)
+    parts = [value] + [
+        lax.ppermute(value, axis, [(i, i ^ k) for i in range(count)]) for k in range(1, count)
+    ]
+    while len(parts) > 1:
+        parts = [parts[i] + parts[i + 1] for i in range(0, len(parts), 2)]
+    return parts[0]
 
 
 def local_slots(page_table, base, slot_count):
@@ -116,7 +126,7 @@
         scaled = (stream * attention_gain[layer_id][None, :]).astype(jnp.bfloat16)
         qkv_part = jnp.dot(scaled, qkv_weight[layer_id], preferred_element_type=jnp.float32)
         forget_part = jnp.dot(scaled, forget_weight[layer_id], preferred_element_type=jnp.float32)
-        total = gather_sum(
+        total = xor_sum(
             jnp.concatenate([qkv_part, forget_part, squares[:, None]], axis=1), "gx"
         )
         rms_value = jnp.sqrt(total[:, -1] / width + EPSILON)
@@ -157,11 +167,10 @@
         gate_part = jnp.dot(scaled, gate_weight[layer_id], preferred_element_type=jnp.float32)
         up_part = jnp.dot(scaled, up_weight[layer_id], preferred_element_type=jnp.float32)
         hidden_cols = gate_part.shape[1]
-        total = gather_sum(jnp.concatenate([gate_part, squares[:, None]], axis=1), "gx")
-        up_total = gather_sum(up_part, "gx")
+        total = xor_sum(jnp.concatenate([gate_part, up_part, squares[:, None]], axis=1), "gx")
         rms_value = jnp.sqrt(total[:, -1] / width + EPSILON)
         gate_full = total[:, :hidden_cols] / rms_value[:, None]
-        up_full = up_total / rms_value[:, None]
+        up_full = total[:, hidden_cols : 2 * hidden_cols] / rms_value[:, None]
         hidden = (jax.nn.silu(gate_full) * up_full).astype(jnp.bfloat16)
         stream = stream + gather_sum(
             jnp.dot(hidden, down_weight[layer_id], preferred_element_type=jnp.float32), "gy"
@@ -171,17 +180,22 @@
     logits = jnp.dot(scaled, head_weight, preferred_element_type=jnp.float32)
     parts = lax.axis_size("gx")
     chunk = logits.shape[1] // parts
+    squares_high = squares.astype(jnp.bfloat16)
+    squares_low = (squares - squares_high.astype(jnp.float32)).astype(jnp.bfloat16)
+    squares_pair = jnp.stack([squares_high, squares_low], axis=1)
     pieces = jnp.concatenate(
         [
-            logits.reshape(request_count, parts, chunk),
-            jnp.broadcast_to(squares[:, None, None], (request_count, parts, 1)),
+            logits.astype(jnp.bfloat16).reshape(request_count, parts, chunk),
+            jnp.broadcast_to(squares_pair[:, None, :], (request_count, parts, 2)),
         ],
         axis=2,
     )
-    pieces = jnp.sum(lax.all_to_all(pieces, "gx", 1, 1, tiled=True), axis=1)
-    rms_value = jnp.sqrt(pieces[:, chunk] / width + EPSILON)
+    pieces = lax.all_to_all(pieces, "gx", 1, 1, tiled=True).astype(jnp.float32)
+    top_part = jnp.sum(pieces[:, :, :chunk], axis=1)
+    total_squares = jnp.sum(pieces[:, :, chunk] + pieces[:, :, chunk + 1], axis=1)
+    rms_value = jnp.sqrt(total_squares / width + EPSILON)
     final_hidden = (stream / rms_value[:, None] * final_gain[None, :]).astype(jnp.bfloat16)
-    local_top = jnp.max(pieces[:, :chunk], axis=1) / rms_value
+    local_top = jnp.max(top_part, axis=1) / rms_value
     top_logits = lax.pmax(lax.pmax(local_top, "gx"), "gy")
     return (final_hidden, rms_value, top_logits)
 

time: 257 us -> 243 us (0.946)
  blocking collectives: 191 us -> 121 us
  waiting for transfers between devices: 0 us -> 35.2 us
  starting transfers between devices: 0 us -> 15.3 us
  matrix products: 27.9 us -> 33.1 us
    all_gather x10 -> x4, blocking collectives: 126 us -> 63.2 us  [gather_sum(): return jnp.sum(lax.all_gather(value, axis), axis=0)]
    ppermute x0 -> x12, waiting for transfers between devices: none -> 35.2 us  [xor_sum(): lax.ppermute(value, axis, [(i, i ^ k) for i in range(count)])]
    ppermute x0 -> x12, starting transfers between devices: none -> 15.3 us  [xor_sum(): lax.ppermute(value, axis, [(i, i ^ k) for i in range(count)])]
    all_to_all x1, blocking collectives: 24.4 us -> 15.4 us  [local(): pieces = lax.all_to_all(pieces, 'gx', 1, 1, tiled=True).astype(jnp.float32)]
    dot_general x2, matrix products: 8.25 us -> 11.6 us  [local_attention(): jnp.einsum('pthc,pkhc->pkt', kv_layer, query_block, preferred_element_typ...]
    ppermute x0 -> x6, local copies, waits for them, and re-layouts: none -> 3.1 us  [xor_sum(): lax.ppermute(value, axis, [(i, i ^ k) for i in range(count)])]
  transfers between devices with their start and end apart: 0 -> 12, of which waited for: 0 -> 6; matrix products, arithmetic and copies ran while one was open for 0% -> 9% of each run, Pallas kernels for 0% -> 0%
where the time goes in v3:
time: 243 us
  blocking collectives  121 us (50%)
  waiting for transfers between devices  35.2 us (14%)
  matrix products  33.1 us (14%)
  local copies, waits for them, and re-layouts  28.8 us (12%)
  starting transfers between devices  15.3 us (6%)
  other arithmetic  8.16 us (3%)
    all_gather x4, blocking collectives, gather_sum(): return jnp.sum(lax.all_gather(value, axis), axis=0)  63.2 us
    ppermute x12, waiting for transfers between devices, xor_sum(): lax.ppermute(value, axis, [(i, i ^ k) for i in range(count)])  35.2 us
    pmax x2, blocking collectives, local(): top_logits = lax.pmax(lax.pmax(local_top, 'gx'), 'gy')  23.1 us
    all_gather x2, blocking collectives, merge_pages(): every = lax.all_gather(packed, 'gx')  18.9 us
    all_to_all x1, blocking collectives, local(): pieces = lax.all_to_all(pieces, 'gx', 1, 1, tiled=True).astype(jnp.float32)  15.4 us
    ppermute x12, starting transfers between devices, xor_sum(): lax.ppermute(value, axis, [(i, i ^ k) for i in range(count)])  15.3 us
    slice x1, local copies, waits for them, and re-layouts, local(): kv_cache[layer_id]  14.9 us
    dot_general x2, matrix products, local_attention(): jnp.einsum('pthc,pkhc->pkt', kv_layer, query_block, preferred_element_typ...  11.6 us
  transfers between devices with their start and end apart: 12, of which 6 were waited for; matrix products, arithmetic and copies ran while one was open for 9% of the time, Pallas kernels for 0%

profile of v3, /device:TPU:0, one launch (start us, length us, event | category | flops | bytes accessed | tf_op | source)
XLA Modules:
  0.0 242.5 jit_solution(6078363396337200670)
XLA Ops:
  0.6 0.9 fusion.68
  1.5 0.8 slice_reduce_fusion.2
  2.3 0.9 fusion.93
  3.3 1.3 fusion.38
  4.6 3.0 %collective-permute-start.1 = (f32[64,387]{0,1:T(8,128)S(1)}, f32[64,387]{0,1:T(8,128)S(1)}, u32[]{:S(2)}, u32[]{:S(2)}) collective-permute-start(f32[64,387]{0,1:T(8,128)S(1)} %pad_maximum_fusion.3), channel_id=1, source_target_pairs={{0,16},{8,24},{16,0},{24,8},{1,17},{9,25},{17,1},{25,9},{2,18},{10... | collective-permute-start | bytes 297224 | tf_op jit(solution)/shard_map/ppermute | solution.py:23
  7.6 1.4 collective-permute-start.2
  9.2 0.8 subtract_bitcast_fusion
  10.7 0.8 slice_bitcast_fusion
  11.4 0.8 slice_reduce_fusion.1
  12.5 0.7 select_reduce_fusion.2
  13.3 14.9 %fusion.150 = (bf16[1,128,128,2,128]{4,3,2,1,0:T(2,128)(2,1)}, bf16[1,128,128,2,128]{4,3,2,1,0:T(2,128)(2,1)}) fusion(bf16[2,128,128,2,128]{4,3,2,1,0:T(2,128)(2,1)} %param.28), kind=kLoop, calls=%fused_computation.251 | loop fusion | bytes 33554432 | tf_op jit(solution)/shard_map/slice | solution.py:142
  28.8 0.6 gather_fusion.1
  29.5 0.7 gather_fusion
  30.3 5.8 %fusion.157 = (f32[128,2]{1,0:T(8,128)S(1)}, f32[128,2,128]{2,1,0:T(2,128)S(1)}) fusion(f32[128,2]{1,0:T(8,128)S(1)} %gather_fusion.1, f32[2,128,2,128]{3,2,1,0:T(2,128)S(1)} %copy-done.9, bf16[1,128,128,2,128]{4,3,2,1,0:T(2,128)(2,1)} %get-tuple-element.20, bf16[128,2,128]{2,1,0:T(2,128)(2,1)S(1)} %concatenate.33, ...), kind=kOutput, calls=%fused_computation.258 | convolution fusion | flops 17202944 | bytes 8734728 | tf_op jit(solution)/shard_map/pthc,pkhc->pkt/dot_general | solution.py:61
  36.4 0.7 gather_fusion.2
  37.0 4.6 %fusion = f32[128,2,2,128]{3,1,2,0:T(2,128)S(1)} fusion(bf16[1,128,128,2,128]{4,3,2,1,0:T(2,128)(2,1)} %get-tuple-element.20, f32[128,2,128]{2,1,0:T(2,128)S(1)} %get-tuple-element.51, pred[128,128]{1,0:T(8,128)(4,1)S(1)} %fusion.91, f32[128,2]{1,0:T(8,128)S(1)} %gather_fusion.2), kind=kOutput, calls=%fused_computation.8 | convolution fusion | flops 16875520 | bytes 8799232 | tf_op jit(solution)/shard_map/pkt,pthc->pkhc/dot_general | solution.py:71
  43.6 9.4 %all-gather = f32[256,2,66]{2,0,1:T(8,128)S(1)} all-gather(f32[64,2,66]{2,0,1:T(8,128)S(1)} %pad_maximum_fusion.5), channel_id=2, replica_groups=mesh['gx'=4,'gy'=8] {'gx'}, dimensions={0}, use_global_device_ids=true | all-gather | bytes 168960 | tf_op jit(solution)/shard_map/all_gather | solution.py:83
  54.2 16.3 %all-gather.1 = f32[512,384]{1,0:T(8,128)S(1)} all-gather(f32[64,384]{1,0:T(8,128)S(1)} %fusion.71), channel_id=3, replica_groups=mesh['gx'=4,'gy'=8] {'gy'}, dimensions={0}, use_global_device_ids=true | all-gather | bytes 884736 | tf_op jit(solution)/shard_map/all_gather | solution.py:17
  71.7 1.5 collective-permute-start.5
  73.2 1.9 collective-permute-start.4
  75.2 7.3 %collective-permute-done.5 = f32[64,1025]{1,0:T(8,128)S(1)} collective-permute-done((f32[64,1025]{1,0:T(8,128)S(1)}, f32[64,1025]{1,0:T(8,128)S(1)}, u32[]{:S(2)}, u32[]{:S(2)}) %collective-permute-start.5) | collective-permute-done | bytes 262432 | tf_op jit(solution)/shard_map/ppermute | solution.py:23
  82.7 5.6 %collective-permute-done.4 = f32[64,1025]{1,0:T(8,128)} collective-permute-done((f32[64,1025]{1,0:T(8,128)S(1)}, f32[64,1025]{1,0:T(8,128)}, u32[]{:S(2)}, u32[]{:S(2)}) %collective-permute-start.4) | collective-permute-done | bytes 262432 | tf_op jit(solution)/shard_map/ppermute | solution.py:23
  88.3 1.2 copy.299
  89.5 1.2 copy.296
  90.8 1.3 fusion.24
  92.1 15.4 %all-gather.2 = f32[512,384]{1,0:T(8,128)S(1)} all-gather(f32[64,384]{1,0:T(8,128)S(1)} %fusion.24), channel_id=4, replica_groups=mesh['gx'=4,'gy'=8] {'gy'}, dimensions={0}, use_global_device_ids=true | all-gather | bytes 884736 | tf_op jit(solution)/shard_map/all_gather | solution.py:17
  107.8 1.3 fusion.36
  109.1 2.1 collective-permute-start.7
  111.1 1.5 collective-permute-start.8
  112.7 8.3 %collective-permute-done.7 = f32[64,387]{0,1:T(8,128)S(1)} collective-permute-done((f32[64,387]{0,1:T(8,128)S(1)}, f32[64,387]{0,1:T(8,128)S(1)}, u32[]{:S(2)}, u32[]{:S(2)}) %collective-permute-start.7) | collective-permute-done | bytes 99104 | tf_op jit(solution)/shard_map/ppermute | solution.py:23
  121.0 1.3 collective-permute-done.6
  122.7 0.7 gather_fusion.3
  124.1 5.8 %fusion.158 = (f32[128,2]{1,0:T(8,128)S(1)}, f32[128,2,128]{2,1,0:T(2,128)S(1)}) fusion(f32[128,2]{1,0:T(8,128)S(1)} %gather_fusion.4, f32[2,128,2,128]{3,2,1,0:T(2,128)} %param.29, bf16[1,128,128,2,128]{4,3,2,1,0:T(2,128)(2,1)} %get-tuple-element.19, bf16[128,2,128]{2,1,0:T(2,128)(2,1)S(1)} %concatenate.37, bf16[2,2]{0,1:T(2,128)(2,1)S(1)} %compare_convert_fusion, ...), kind=kOutput, calls=%fused_computation.259 | convolution fusion | flops 17202944 | bytes 8734728 | tf_op jit(solution)/shard_map/pthc,pkhc->pkt/dot_general | solution.py:61
  130.2 0.7 gather_fusion.5
  130.9 4.6 %fusion.2 = f32[128,2,2,128]{3,1,2,0:T(2,128)S(1)} fusion(bf16[1,128,128,2,128]{4,3,2,1,0:T(2,128)(2,1)} %get-tuple-element.19, f32[128,2,128]{2,1,0:T(2,128)S(1)} %get-tuple-element.53, pred[128,128]{1,0:T(8,128)(4,1)S(1)} %fusion.91, f32[128,2]{1,0:T(8,128)S(1)} %gather_fusion.5), kind=kOutput, calls=%fused_computation.10 | convolution fusion | flops 16875520 | bytes 8799232 | tf_op jit(solution)/shard_map/pkt,pthc->pkhc/dot_general | solution.py:71
  137.5 9.5 %all-gather.3 = f32[256,2,66]{2,0,1:T(8,128)S(1)} all-gather(f32[64,2,66]{2,0,1:T(8,128)S(1)} %pad_maximum_fusion.6), channel_id=5, replica_groups=mesh['gx'=4,'gy'=8] {'gx'}, dimensions={0}, use_global_device_ids=true | all-gather | bytes 168960 | tf_op jit(solution)/shard_map/all_gather | solution.py:83
  148.1 16.2 %all-gather.4 = f32[512,384]{1,0:T(8,128)S(1)} all-gather(f32[64,384]{1,0:T(8,128)S(1)} %fusion.69), channel_id=6, replica_groups=mesh['gx'=4,'gy'=8] {'gy'}, dimensions={0}, use_global_device_ids=true | all-gather | bytes 884736 | tf_op jit(solution)/shard_map/all_gather | solution.py:17
  165.4 1.5 collective-permute-start.11
  167.0 2.0 collective-permute-start.9
  169.0 7.3 %collective-permute-done.11 = f32[64,1025]{1,0:T(8,128)S(1)} collective-permute-done((f32[64,1025]{1,0:T(8,128)S(1)}, f32[64,1025]{1,0:T(8,128)S(1)}, u32[]{:S(2)}, u32[]{:S(2)}) %collective-permute-start.11) | collective-permute-done | bytes 262432 | tf_op jit(solution)/shard_map/ppermute | solution.py:23
  176.5 5.5 %collective-permute-done.10 = f32[64,1025]{1,0:T(8,128)S(1)} collective-permute-done((f32[64,1025]{1,0:T(8,128)S(1)}, f32[64,1025]{1,0:T(8,128)S(1)}, u32[]{:S(2)}, u32[]{:S(2)}) %collective-permute-start.10) | collective-permute-done | bytes 262432 | tf_op jit(solution)/shard_map/ppermute | solution.py:23
  182.5 1.3 fusion.18
  183.8 15.2 %all-gather.5 = f32[512,384]{1,0:T(8,128)S(1)} all-gather(f32[64,384]{1,0:T(8,128)S(1)} %fusion.18), channel_id=7, replica_groups=mesh['gx'=4,'gy'=8] {'gy'}, dimensions={0}, use_global_device_ids=true | all-gather | bytes 884736 | tf_op jit(solution)/shard_map/all_gather | solution.py:17
  199.3 3.3 %convolution_convert_fusion = bf16[64,6144]{1,0:T(8,128)(2,1)S(1)} fusion(bf16[384,6144]{1,0:T(8,128)(2,1)} %param.27, f32[64,384]{1,0:T(8,128)S(1)} %get-tuple-element.10, f32[384]{0:T(512)S(1)} %copy-done.6), kind=kOutput, calls=%fused_computation.12 | convolution fusion | flops 302432256 | bytes 5604864 | tf_op jit(solution)/shard_map/dot_general | solution.py:180
  202.8 15.4 %all_to_all.5 = bf16[64,4,1538]{2,0,1:T(8,128)(2,1)S(1)} all-to-all(bf16[64,4,1538]{2,0,1:T(8,128)(2,1)S(1)} %pad_maximum_fusion), channel_id=1, replica_groups=mesh['gx'=4,'gy'=8] {'gx'}, dimensions={1} | all-to-all | bytes 1574912 | tf_op jit(solution)/shard_map/all_to_all | solution.py:193
  218.7 0.7 multiply_convert_fusion
  219.4 8.2 %pmax.14 = f32[64]{0:T(128)S(1)} all-reduce(f32[64]{0:T(128)S(1)} %get-tuple-element.7), channel_id=1, replica_groups=mesh['gx'=4,'gy'=8] {'gx'}, use_global_device_ids=true, to_apply=%region_27.28 | all-reduce | flops 64 | bytes 512 | tf_op jit(solution)/shard_map/pmax | solution.py:199
  227.6 14.9 %pmax.15 = f32[64]{0:T(128)} all-reduce(f32[64]{0:T(128)S(1)} %pmax.14), channel_id=1, replica_groups=mesh['gx'=4,'gy'=8] {'gy'}, use_global_device_ids=true, to_apply=%region_28.29 | all-reduce | flops 64 | bytes 512 | tf_op jit(solution)/shard_map/pmax | solution.py:199
  (153 shorter events, 14.0 us)
Async XLA Ops:
  4.6 23.8 %collective-permute-start.1 = (f32[64,387]{0,1:T(8,128)S(1)}, f32[64,387]{0,1:T(8,128)S(1)}, u32[]{:S(2)}, u32[]{:S(2)}) collective-permute-start(f32[64,387]{0,1:T(8,128)S(1)} %pad_maximum_fusion.3), channel_id=1, source_target_pairs={{0,16},{8,24},{16,0},{24,8},{1,17},{9,25},{17,1},{25,9},{2,18},{10... | collective-permute-start | bytes 297224 | tf_op jit(solution)/shard_map/ppermute | solution.py:23
  7.6 20.7 %collective-permute-start.2 = (f32[64,387]{0,1:T(8,128)S(1)}, f32[64,387]{0,1:T(8,128)S(1)}, u32[]{:S(2)}, u32[]{:S(2)}) collective-permute-start(f32[64,387]{0,1:T(8,128)S(1)} %pad_maximum_fusion.3), channel_id=1, source_target_pairs={{0,24},{8,16},{16,8},{24,0},{1,25},{9,17},{17,9},{25,1},{2,26},{10... | collective-permute-start | bytes 297224 | tf_op jit(solution)/shard_map/ppermute | solution.py:23
  9.1 19.3 %collective-permute-start = (f32[64,387]{0,1:T(8,128)S(1)}, f32[64,387]{0,1:T(8,128)S(1)}, u32[]{:S(2)}, u32[]{:S(2)}) collective-permute-start(f32[64,387]{0,1:T(8,128)S(1)} %pad_maximum_fusion.3), channel_id=1, source_target_pairs={{0,8},{8,0},{16,24},{24,16},{1,9},{9,1},{17,25},{25,17},{2,10},{10... | collective-permute-start | bytes 297224 | tf_op jit(solution)/shard_map/ppermute | solution.py:23
  13.3 17.0 %copy-start.9 = (f32[2,128,2,128]{3,2,1,0:T(2,128)S(1)}, f32[2,128,2,128]{3,2,1,0:T(2,128)}, u32[]{:S(2)}) copy-start(f32[2,128,2,128]{3,2,1,0:T(2,128)} %param.29) | copy-start | bytes 786436
  36.1 17.9 %copy-start.4 = (bf16[2,128,384]{2,1,0:T(8,128)(2,1)S(1)}, bf16[2,128,384]{2,1,0:T(8,128)(2,1)}, u32[]{:S(2)}) copy-start(bf16[2,128,384]{2,1,0:T(8,128)(2,1)} %param.23) | copy-start | bytes 589828
  36.1 34.5 %copy-start.3 = (bf16[64,384]{1,0:T(8,128)(2,1)S(1)}, bf16[64,384]{1,0:T(8,128)(2,1)}, u32[]{:S(2)}) copy-start(bf16[64,384]{1,0:T(8,128)(2,1)} %param.16) | copy-start | bytes 147460
  36.1 34.6 %copy-start = (bf16[2,384,512]{2,1,0:T(8,128)(2,1)S(1)}, bf16[2,384,512]{2,1,0:T(8,128)(2,1)}, u32[]{:S(2)}) copy-start(bf16[2,384,512]{2,1,0:T(8,128)(2,1)} %param.25) | copy-start | bytes 2359300
  36.1 35.0 %copy-start.1 = (bf16[2,384,512]{2,1,0:T(8,128)(2,1)S(1)}, bf16[2,384,512]{2,1,0:T(8,128)(2,1)}, u32[]{:S(2)}) copy-start(bf16[2,384,512]{2,1,0:T(8,128)(2,1)} %param.24) | copy-start | bytes 2359300
  53.5 54.2 %copy-start.8 = (bf16[2,384,2]{1,2,0:T(2,128)(2,1)S(1)}, bf16[2,384,2]{1,2,0:T(2,128)(2,1)}, u32[]{:S(2)}) copy-start(bf16[2,384,2]{1,2,0:T(2,128)(2,1)} %param.21) | copy-start | bytes 9220
  71.7 10.8 %collective-permute-start.5 = (f32[64,1025]{1,0:T(8,128)S(1)}, f32[64,1025]{1,0:T(8,128)S(1)}, u32[]{:S(2)}, u32[]{:S(2)}) collective-permute-start(f32[64,1025]{1,0:T(8,128)S(1)} %copy.295), channel_id=1, source_target_pairs={{0,24},{8,16},{16,8},{24,0},{1,25},{9,17},{17,9},{25,1},{2,26},{10... | collective-permute-start | bytes 787208 | tf_op jit(solution)/shard_map/ppermute | solution.py:23
  73.2 15.1 %collective-permute-start.4 = (f32[64,1025]{1,0:T(8,128)S(1)}, f32[64,1025]{1,0:T(8,128)}, u32[]{:S(2)}, u32[]{:S(2)}) collective-permute-start(f32[64,1025]{1,0:T(8,128)S(1)} %copy.295), channel_id=1, source_target_pairs={{0,16},{8,24},{16,0},{24,8},{1,17},{9,25},{17,1},{25,9},{2,18},{10... | collective-permute-start | bytes 787208 | tf_op jit(solution)/shard_map/ppermute | solution.py:23
  75.0 14.4 %collective-permute-start.3 = (f32[64,1025]{1,0:T(8,128)S(1)}, f32[64,1025]{1,0:T(8,128)}, u32[]{:S(2)}, u32[]{:S(2)}) collective-permute-start(f32[64,1025]{1,0:T(8,128)S(1)} %copy.295), channel_id=1, source_target_pairs={{0,8},{8,0},{16,24},{24,16},{1,9},{9,1},{17,25},{25,17},{2,10},{10... | collective-permute-start | bytes 787208 | tf_op jit(solution)/shard_map/ppermute | solution.py:23
  109.1 11.9 %collective-permute-start.7 = (f32[64,387]{0,1:T(8,128)S(1)}, f32[64,387]{0,1:T(8,128)S(1)}, u32[]{:S(2)}, u32[]{:S(2)}) collective-permute-start(f32[64,387]{0,1:T(8,128)S(1)} %pad_maximum_fusion.4), channel_id=1, source_target_pairs={{0,16},{8,24},{16,0},{24,8},{1,17},{9,25},{17,1},{25,9},{2,18},{10... | collective-permute-start | bytes 297224 | tf_op jit(solution)/shard_map/ppermute | solution.py:23
  111.1 9.8 %collective-permute-start.8 = (f32[64,387]{0,1:T(8,128)S(1)}, f32[64,387]{0,1:T(8,128)S(1)}, u32[]{:S(2)}, u32[]{:S(2)}) collective-permute-start(f32[64,387]{0,1:T(8,128)S(1)} %pad_maximum_fusion.4), channel_id=1, source_target_pairs={{0,24},{8,16},{16,8},{24,0},{1,25},{9,17},{17,9},{25,1},{2,26},{10... | collective-permute-start | bytes 297224 | tf_op jit(solution)/shard_map/ppermute | solution.py:23
  112.6 9.6 %collective-permute-start.6 = (f32[64,387]{0,1:T(8,128)S(1)}, f32[64,387]{0,1:T(8,128)S(1)}, u32[]{:S(2)}, u32[]{:S(2)}) collective-permute-start(f32[64,387]{0,1:T(8,128)S(1)} %pad_maximum_fusion.4), channel_id=1, source_target_pairs={{0,8},{8,0},{16,24},{24,16},{1,9},{9,1},{17,25},{25,17},{2,10},{10... | collective-permute-start | bytes 297224 | tf_op jit(solution)/shard_map/ppermute | solution.py:23
  130.0 18.0 %copy-start.5 = (bf16[2,128,384]{2,1,0:T(8,128)(2,1)S(1)}, bf16[2,128,384]{2,1,0:T(8,128)(2,1)}, u32[]{:S(2)}) copy-start(bf16[2,128,384]{2,1,0:T(8,128)(2,1)} %param.23) | copy-start | bytes 589828
  130.0 34.9 %copy-start.2 = (bf16[2,384,512]{2,1,0:T(8,128)(2,1)S(1)}, bf16[2,384,512]{2,1,0:T(8,128)(2,1)}, u32[]{:S(2)}) copy-start(bf16[2,384,512]{2,1,0:T(8,128)(2,1)} %param.24) | copy-start | bytes 2359300
  147.5 51.9 %copy-start.6 = (f32[384]{0:T(512)S(1)}, f32[384]{0:T(512)}, u32[]{:S(2)}) copy-start(f32[384]{0:T(512)} %param.19) | copy-start | bytes 4612
  165.4 10.8 %collective-permute-start.11 = (f32[64,1025]{1,0:T(8,128)S(1)}, f32[64,1025]{1,0:T(8,128)S(1)}, u32[]{:S(2)}, u32[]{:S(2)}) collective-permute-start(f32[64,1025]{1,0:T(8,128)S(1)} %copy.319), channel_id=1, source_target_pairs={{0,24},{8,16},{16,8},{24,0},{1,25},{9,17},{17,9},{25,1},{2,26},{10... | collective-permute-start | bytes 787208 | tf_op jit(solution)/shard_map/ppermute | solution.py:23
  167.0 15.0 %collective-permute-start.10 = (f32[64,1025]{1,0:T(8,128)S(1)}, f32[64,1025]{1,0:T(8,128)S(1)}, u32[]{:S(2)}, u32[]{:S(2)}) collective-permute-start(f32[64,1025]{1,0:T(8,128)S(1)} %copy.319), channel_id=1, source_target_pairs={{0,16},{8,24},{16,0},{24,8},{1,17},{9,25},{17,1},{25,9},{2,18},{10... | collective-permute-start | bytes 787208 | tf_op jit(solution)/shard_map/ppermute | solution.py:23
  167.0 15.2 %collective-permute-start.9 = (f32[64,1025]{1,0:T(8,128)S(1)}, f32[64,1025]{1,0:T(8,128)S(1)}, u32[]{:S(2)}, u32[]{:S(2)}) collective-permute-start(f32[64,1025]{1,0:T(8,128)S(1)} %copy.319), channel_id=1, source_target_pairs={{0,8},{8,0},{16,24},{24,16},{1,9},{9,1},{17,25},{25,17},{2,10},{10... | collective-permute-start | bytes 787208 | tf_op jit(solution)/shard_map/ppermute | solution.py:23
  218.7 23.8 %copy-start.7 = (f32[64]{0:T(128)}, f32[64]{0:T(128)S(1)}, u32[]{:S(2)}) copy-start(f32[64]{0:T(128)S(1)} %get-tuple-element.8) | copy-start | bytes 772

commit v4 on v3

--- a/solution.py
+++ b/solution.py
@@ -17,13 +17,31 @@
     return jnp.sum(lax.all_gather(value, axis), axis=0)
 
 
-def xor_sum(value, axis):
+def xor_sum(value, axis, kind=None):
+    count = lax.axis_size(axis)
+    parts = [value] + [
+        lax.ppermute(value, axis, [(i, i ^ k) for i in range(count)]) for k in range(1, count)
+    ]
+    if kind is not None:
+        parts = [part.astype(kind) for part in parts]
+    while len(parts) > 1:
+        parts = [parts[i] + parts[i + 1] for i in range(0, len(parts), 2)]
+    return parts[0]
+
+
+def split_pair(value):
+    high = value.astype(jnp.bfloat16)
+    low = (value - high.astype(jnp.float32)).astype(jnp.bfloat16)
+    return jnp.stack([high, low], axis=1)
+
+
+def xor_max(value, axis):
     count = lax.axis_size(axis)
     parts = [value] + [
         lax.ppermute(value, axis, [(i, i ^ k) for i in range(count)]) for k in range(1, count)
     ]
     while len(parts) > 1:
-        parts = [parts[i] + parts[i + 1] for i in range(0, len(parts), 2)]
+        parts = [jnp.maximum(parts[i], parts[i + 1]) for i in range(0, len(parts), 2)]
     return parts[0]
 
 
@@ -127,9 +145,14 @@
         qkv_part = jnp.dot(scaled, qkv_weight[layer_id], preferred_element_type=jnp.float32)
         forget_part = jnp.dot(scaled, forget_weight[layer_id], preferred_element_type=jnp.float32)
         total = xor_sum(
-            jnp.concatenate([qkv_part, forget_part, squares[:, None]], axis=1), "gx"
-        )
-        rms_value = jnp.sqrt(total[:, -1] / width + EPSILON)
+            jnp.concatenate(
+                [qkv_part.astype(jnp.bfloat16), forget_part.astype(jnp.bfloat16), split_pair(squares)],
+                axis=1,
+            ),
+            "gx",
+            jnp.float32,
+        )
+        rms_value = jnp.sqrt((total[:, -2] + total[:, -1]) / width + EPSILON)
         projected = (total[:, :qkv_cols] / rms_value[:, None]).reshape(
             request_count, local_heads, 3 * HEAD
         )
@@ -167,8 +190,15 @@
         gate_part = jnp.dot(scaled, gate_weight[layer_id], preferred_element_type=jnp.float32)
         up_part = jnp.dot(scaled, up_weight[layer_id], preferred_element_type=jnp.float32)
         hidden_cols = gate_part.shape[1]
-        total = xor_sum(jnp.concatenate([gate_part, up_part, squares[:, None]], axis=1), "gx")
-        rms_value = jnp.sqrt(total[:, -1] / width + EPSILON)
+        total = xor_sum(
+            jnp.concatenate(
+                [gate_part.astype(jnp.bfloat16), up_part.astype(jnp.bfloat16), split_pair(squares)],
+                axis=1,
+            ),
+            "gx",
+            jnp.float32,
+        )
+        rms_value = jnp.sqrt((total[:, -2] + total[:, -1]) / width + EPSILON)
         gate_full = total[:, :hidden_cols] / rms_value[:, None]
         up_full = total[:, hidden_cols : 2 * hidden_cols] / rms_value[:, None]
         hidden = (jax.nn.silu(gate_full) * up_full).astype(jnp.bfloat16)
@@ -180,9 +210,7 @@
     logits = jnp.dot(scaled, head_weight, preferred_element_type=jnp.float32)
     parts = lax.axis_size("gx")
     chunk = logits.shape[1] // parts
-    squares_high = squares.astype(jnp.bfloat16)
-    squares_low = (squares - squares_high.astype(jnp.float32)).astype(jnp.bfloat16)
-    squares_pair = jnp.stack([squares_high, squares_low], axis=1)
+    squares_pair = split_pair(squares)
     pieces = jnp.concatenate(
         [
             logits.astype(jnp.bfloat16).reshape(request_count, parts, chunk),
@@ -196,7 +224,7 @@
     rms_value = jnp.sqrt(total_squares / width + EPSILON)
     final_hidden = (stream / rms_value[:, None] * final_gain[None, :]).astype(jnp.bfloat16)
     local_top = jnp.max(top_part, axis=1) / rms_value
-    top_logits = lax.pmax(lax.pmax(local_top, "gx"), "gy")
+    top_logits = xor_max(lax.pmax(local_top, "gx"), "gy")
     return (final_hidden, rms_value, top_logits)
 
 

time: 243 us -> 227 us (0.934)
  blocking collectives: 121 us -> 106 us
  starting transfers between devices: 15.3 us -> 23.3 us
  waiting for transfers between devices: 35.2 us -> 30.6 us
  local copies, waits for them, and re-layouts: 28.8 us -> 25.4 us
    pmax x2 -> x1, blocking collectives: 23.1 us -> 8.21 us  [local(): top_logits = xor_max(lax.pmax(local_top, 'gx'), 'gy')]
    ppermute x0 -> x7, starting transfers between devices: none -> 8.1 us  [xor_max(): lax.ppermute(value, axis, [(i, i ^ k) for i in range(count)])]
    ppermute x12, waiting for transfers between devices: 35.2 us -> 28.7 us  [xor_sum(): lax.ppermute(value, axis, [(i, i ^ k) for i in range(count)])]
    ppermute x6 -> x0, local copies, waits for them, and re-layouts: 3.1 us -> none  [xor_sum(): lax.ppermute(value, axis, [(i, i ^ k) for i in range(count)])]
  transfers between devices with their start and end apart: 12 -> 19, of which waited for: 6 -> 10; matrix products, arithmetic and copies ran while one was open for 9% -> 9% of each run, Pallas kernels for 0% -> 0%
where the time goes in v4:
time: 227 us; the launch traced here: 226 us
  blocking collectives  106 us (47%)
  matrix products  31.2 us (14%)
  waiting for transfers between devices  30.6 us (13%)
  local copies, waits for them, and re-layouts  25.4 us (11%)
  starting transfers between devices  23.3 us (10%)
  other arithmetic  8.68 us (4%)
    all_gather x4, blocking collectives, gather_sum(): return jnp.sum(lax.all_gather(value, axis), axis=0)  63.3 us
    ppermute x12, waiting for transfers between devices, xor_sum(): lax.ppermute(value, axis, [(i, i ^ k) for i in range(count)])  28.7 us
    all_gather x2, blocking collectives, merge_pages(): every = lax.all_gather(packed, 'gx')  18.8 us
    all_to_all x1, blocking collectives, local(): pieces = lax.all_to_all(pieces, 'gx', 1, 1, tiled=True).astype(jnp.float32)  15.4 us
    ppermute x12, starting transfers between devices, xor_sum(): lax.ppermute(value, axis, [(i, i ^ k) for i in range(count)])  15.2 us
    slice x1, local copies, waits for them, and re-layouts, local(): kv_cache[layer_id]  14.9 us
    dot_general x2, matrix products, local_attention(): jnp.einsum('pthc,pkhc->pkt', kv_layer, query_block, preferred_element_typ...  11.6 us
    dot_general x2, matrix products, local_attention(): jnp.einsum('pkt,pthc->pkhc', weights.astype(jnp.bfloat16), kv_layer, pref...  9.36 us
  transfers between devices with their start and end apart: 19, of which 10 were waited for; matrix products, arithmetic and copies ran while one was open for 9% of the time, Pallas kernels for 0%

profile of v4, /device:TPU:0, one launch (start us, length us, event | category | flops | bytes accessed | tf_op | source)
XLA Modules:
  0.0 226.2 jit_solution(2283707261136167372)
XLA Ops:
  0.6 0.9 fusion.62
  1.6 0.8 slice_reduce_fusion.2
  2.3 0.9 convolution_convert_fusion.9
  3.3 1.3 convolution_convert_fusion.6
  4.6 3.0 %collective-permute-start.1 = (bf16[64,388]{0,1:T(8,128)(2,1)S(1)}, bf16[64,388]{0,1:T(8,128)(2,1)S(1)}, u32[]{:S(2)}, u32[]{:S(2)}) collective-permute-start(bf16[64,388]{0,1:T(8,128)(2,1)S(1)} %pad_maximum_fusion.1), channel_id=1, source_target_pairs={{0,16},{8,24},{16,0},{24,8},{1,17},{9,25},{17,1},{25,9},{2,18},{10... | collective-permute-start | bytes 149000 | tf_op jit(solution)/shard_map/ppermute | solution.py:23
  7.7 1.5 collective-permute-start
  9.2 0.8 subtract_bitcast_fusion
  10.7 0.8 slice_bitcast_fusion
  11.4 0.8 slice_reduce_fusion.1
  12.5 0.7 select_reduce_fusion.2
  13.3 14.9 %fusion.138 = (bf16[1,128,128,2,128]{4,3,2,1,0:T(2,128)(2,1)}, bf16[1,128,128,2,128]{4,3,2,1,0:T(2,128)(2,1)}) fusion(bf16[2,128,128,2,128]{4,3,2,1,0:T(2,128)(2,1)} %param.28), kind=kLoop, calls=%fused_computation.258 | loop fusion | bytes 33554432 | tf_op jit(solution)/shard_map/slice | solution.py:165
  29.5 0.7 gather_fusion
  30.3 5.8 %fusion.145 = (f32[128,2]{1,0:T(8,128)S(1)}, f32[128,2,128]{2,1,0:T(2,128)S(1)}) fusion(f32[128,2]{1,0:T(8,128)S(1)} %gather_fusion.1, f32[2,128,2,128]{3,2,1,0:T(2,128)S(1)} %copy-done.9, bf16[1,128,128,2,128]{4,3,2,1,0:T(2,128)(2,1)} %get-tuple-element.20, bf16[128,2,128]{2,1,0:T(2,128)(2,1)S(1)} %concatenate.33, ...), kind=kOutput, calls=%fused_computation.265 | convolution fusion | flops 17202944 | bytes 8734728 | tf_op jit(solution)/shard_map/pthc,pkhc->pkt/dot_general | solution.py:79
  36.4 0.7 gather_fusion.2
  37.1 4.6 %fusion = f32[128,2,2,128]{3,1,2,0:T(2,128)S(1)} fusion(bf16[1,128,128,2,128]{4,3,2,1,0:T(2,128)(2,1)} %get-tuple-element.20, f32[128,2,128]{2,1,0:T(2,128)S(1)} %get-tuple-element.51, pred[128,128]{1,0:T(8,128)(4,1)S(1)} %fusion.85, f32[128,2]{1,0:T(8,128)S(1)} %gather_fusion.2), kind=kOutput, calls=%fused_computation.8 | convolution fusion | flops 16875520 | bytes 8799232 | tf_op jit(solution)/shard_map/pkt,pthc->pkhc/dot_general | solution.py:89
  43.6 9.4 %all-gather = f32[256,2,66]{2,0,1:T(8,128)S(1)} all-gather(f32[64,2,66]{2,0,1:T(8,128)S(1)} %pad_maximum_fusion.3), channel_id=2, replica_groups=mesh['gx'=4,'gy'=8] {'gx'}, dimensions={0}, use_global_device_ids=true | all-gather | bytes 168960 | tf_op jit(solution)/shard_map/all_gather | solution.py:101
  54.2 16.4 %all-gather.1 = f32[512,384]{1,0:T(8,128)S(1)} all-gather(f32[64,384]{1,0:T(8,128)S(1)} %fusion.65), channel_id=3, replica_groups=mesh['gx'=4,'gy'=8] {'gy'}, dimensions={0}, use_global_device_ids=true | all-gather | bytes 884736 | tf_op jit(solution)/shard_map/all_gather | solution.py:17
  71.5 1.5 collective-permute-start.5
  73.1 1.8 collective-permute-start.4
  75.1 6.6 %collective-permute-done.5 = bf16[64,1026]{0,1:T(8,128)(2,1)S(1)} collective-permute-done((bf16[64,1026]{0,1:T(8,128)(2,1)S(1)}, bf16[64,1026]{0,1:T(8,128)(2,1)S(1)}, u32[]{:S(2)}, u32[]{:S(2)}) %collective-permute-start.5) | collective-permute-done | bytes 131360 | tf_op jit(solution)/shard_map/ppermute | solution.py:23
  81.7 5.1 %collective-permute-done.4 = bf16[64,1026]{0,1:T(8,128)(2,1)S(1)} collective-permute-done((bf16[64,1026]{0,1:T(8,128)(2,1)S(1)}, bf16[64,1026]{0,1:T(8,128)(2,1)S(1)}, u32[]{:S(2)}, u32[]{:S(2)}) %collective-permute-start.4) | collective-permute-done | bytes 131360 | tf_op jit(solution)/shard_map/ppermute | solution.py:23
  87.3 1.3 fusion.22
  88.6 15.5 %all-gather.2 = f32[512,384]{1,0:T(8,128)S(1)} all-gather(f32[64,384]{1,0:T(8,128)S(1)} %fusion.22), channel_id=4, replica_groups=mesh['gx'=4,'gy'=8] {'gy'}, dimensions={0}, use_global_device_ids=true | all-gather | bytes 884736 | tf_op jit(solution)/shard_map/all_gather | solution.py:17
  104.8 1.6 collective-permute-start.7
  106.9 1.5 collective-permute-start.8
  108.3 1.6 collective-permute-done.7
  109.9 2.1 collective-permute-done.6
  112.0 1.2 collective-permute-done.8
  113.7 0.7 gather_fusion.3
  115.1 5.8 %fusion.146 = (f32[128,2]{1,0:T(8,128)S(1)}, f32[128,2,128]{2,1,0:T(2,128)S(1)}) fusion(f32[128,2]{1,0:T(8,128)S(1)} %gather_fusion.4, f32[2,128,2,128]{3,2,1,0:T(2,128)} %param.29, bf16[1,128,128,2,128]{4,3,2,1,0:T(2,128)(2,1)} %get-tuple-element.19, bf16[128,2,128]{2,1,0:T(2,128)(2,1)S(1)} %concatenate.37, bf16[2,2]{0,1:T(2,128)(2,1)S(1)} %compare_convert_fusion, ...), kind=kOutput, calls=%fused_computation.266 | convolution fusion | flops 17202944 | bytes 8734728 | tf_op jit(solution)/shard_map/pthc,pkhc->pkt/dot_general | solution.py:79
  121.9 4.7 %fusion.2 = f32[128,2,2,128]{3,1,2,0:T(2,128)S(1)} fusion(bf16[1,128,128,2,128]{4,3,2,1,0:T(2,128)(2,1)} %get-tuple-element.19, f32[128,2,128]{2,1,0:T(2,128)S(1)} %get-tuple-element.53, pred[128,128]{1,0:T(8,128)(4,1)S(1)} %fusion.85, f32[128,2]{1,0:T(8,128)S(1)} %gather_fusion.5), kind=kOutput, calls=%fused_computation.10 | convolution fusion | flops 16875520 | bytes 8799232 | tf_op jit(solution)/shard_map/pkt,pthc->pkhc/dot_general | solution.py:89
  128.5 9.3 %all-gather.3 = f32[256,2,66]{2,0,1:T(8,128)S(1)} all-gather(f32[64,2,66]{2,0,1:T(8,128)S(1)} %pad_maximum_fusion.4), channel_id=5, replica_groups=mesh['gx'=4,'gy'=8] {'gx'}, dimensions={0}, use_global_device_ids=true | all-gather | bytes 168960 | tf_op jit(solution)/shard_map/all_gather | solution.py:101
  139.0 16.2 %all-gather.4 = f32[512,384]{1,0:T(8,128)S(1)} all-gather(f32[64,384]{1,0:T(8,128)S(1)} %fusion.63), channel_id=6, replica_groups=mesh['gx'=4,'gy'=8] {'gy'}, dimensions={0}, use_global_device_ids=true | all-gather | bytes 884736 | tf_op jit(solution)/shard_map/all_gather | solution.py:17
  156.2 1.5 collective-permute-start.11
  157.9 1.8 collective-permute-start.9
  159.7 6.6 %collective-permute-done.11 = bf16[64,1026]{0,1:T(8,128)(2,1)S(1)} collective-permute-done((bf16[64,1026]{0,1:T(8,128)(2,1)S(1)}, bf16[64,1026]{0,1:T(8,128)(2,1)S(1)}, u32[]{:S(2)}, u32[]{:S(2)}) %collective-permute-start.11) | collective-permute-done | bytes 131360 | tf_op jit(solution)/shard_map/ppermute | solution.py:23
  166.3 5.1 %collective-permute-done.10 = bf16[64,1026]{0,1:T(8,128)(2,1)S(1)} collective-permute-done((bf16[64,1026]{0,1:T(8,128)(2,1)S(1)}, bf16[64,1026]{0,1:T(8,128)(2,1)S(1)}, u32[]{:S(2)}, u32[]{:S(2)}) %collective-permute-start.10) | collective-permute-done | bytes 131360 | tf_op jit(solution)/shard_map/ppermute | solution.py:23
  171.8 15.2 %all-gather.5 = f32[512,384]{1,0:T(8,128)S(1)} all-gather(f32[64,384]{1,0:T(8,128)S(1)} %fusion.18), channel_id=7, replica_groups=mesh['gx'=4,'gy'=8] {'gy'}, dimensions={0}, use_global_device_ids=true | all-gather | bytes 884736 | tf_op jit(solution)/shard_map/all_gather | solution.py:17
  187.4 3.3 %convolution_convert_fusion = bf16[64,6144]{1,0:T(8,128)(2,1)S(1)} fusion(bf16[384,6144]{1,0:T(8,128)(2,1)} %param.27, f32[64,384]{1,0:T(8,128)S(1)} %get-tuple-element.10, f32[384]{0:T(512)S(1)} %copy-done.5), kind=kOutput, calls=%fused_computation.12 | convolution fusion | flops 302432256 | bytes 5604864 | tf_op jit(solution)/shard_map/dot_general | solution.py:210
  190.8 15.4 %all_to_all.5 = bf16[64,4,1538]{2,0,1:T(8,128)(2,1)S(1)} all-to-all(bf16[64,4,1538]{2,0,1:T(8,128)(2,1)S(1)} %pad_maximum_fusion), channel_id=1, replica_groups=mesh['gx'=4,'gy'=8] {'gx'}, dimensions={1} | all-to-all | bytes 1574912 | tf_op jit(solution)/shard_map/all_to_all | solution.py:221
  206.8 8.2 %pmax.7 = f32[64]{0:T(128)S(1)} all-reduce(f32[64]{0:T(128)S(1)} %get-tuple-element.7), channel_id=1, replica_groups=mesh['gx'=4,'gy'=8] {'gx'}, use_global_device_ids=true, to_apply=%region_27.28 | all-reduce | flops 64 | bytes 512 | tf_op jit(solution)/shard_map/pmax | solution.py:227
  215.0 0.9 collective-permute-start.18
  215.9 2.7 %collective-permute-start.17 = (f32[64]{0:T(128)S(1)}, f32[64]{0:T(128)S(1)}, u32[]{:S(2)}, u32[]{:S(2)}) collective-permute-start(f32[64]{0:T(128)S(1)} %pmax.7), channel_id=1, source_target_pairs={{0,6},{1,7},{2,4},{3,5},{4,2},{5,3},{6,0},{7,1},{8,14},{9,15},{10,... | collective-permute-start | bytes 776 | tf_op jit(solution)/shard_map/ppermute | solution.py:41
  218.6 2.6 %collective-permute-start.15 = (f32[64]{0:T(128)S(1)}, f32[64]{0:T(128)S(1)}, u32[]{:S(2)}, u32[]{:S(2)}) collective-permute-start(f32[64]{0:T(128)S(1)} %pmax.7), channel_id=1, source_target_pairs={{0,4},{1,5},{2,6},{3,7},{4,0},{5,1},{6,2},{7,3},{8,12},{9,13},{10,... | collective-permute-start | bytes 776 | tf_op jit(solution)/shard_map/ppermute | solution.py:41
  221.2 0.9 collective-permute-start.14
  222.1 0.9 collective-permute-start.13
  223.1 0.7 multiply_convert_fusion
  224.2 1.5 collective-permute-done.13
  (167 shorter events, 16.8 us)
Async XLA Ops:
  4.6 23.8 %collective-permute-start.1 = (bf16[64,388]{0,1:T(8,128)(2,1)S(1)}, bf16[64,388]{0,1:T(8,128)(2,1)S(1)}, u32[]{:S(2)}, u32[]{:S(2)}) collective-permute-start(bf16[64,388]{0,1:T(8,128)(2,1)S(1)} %pad_maximum_fusion.1), channel_id=1, source_target_pairs={{0,16},{8,24},{16,0},{24,8},{1,17},{9,25},{17,1},{25,9},{2,18},{10... | collective-permute-start | bytes 149000 | tf_op jit(solution)/shard_map/ppermute | solution.py:23
  7.7 20.7 %collective-permute-start = (bf16[64,388]{0,1:T(8,128)(2,1)S(1)}, bf16[64,388]{0,1:T(8,128)(2,1)S(1)}, u32[]{:S(2)}, u32[]{:S(2)}) collective-permute-start(bf16[64,388]{0,1:T(8,128)(2,1)S(1)} %pad_maximum_fusion.1), channel_id=1, source_target_pairs={{0,8},{8,0},{16,24},{24,16},{1,9},{9,1},{17,25},{25,17},{2,10},{10... | collective-permute-start | bytes 149000 | tf_op jit(solution)/shard_map/ppermute | solution.py:23
  9.1 19.3 %collective-permute-start.2 = (bf16[64,388]{0,1:T(8,128)(2,1)S(1)}, bf16[64,388]{0,1:T(8,128)(2,1)S(1)}, u32[]{:S(2)}, u32[]{:S(2)}) collective-permute-start(bf16[64,388]{0,1:T(8,128)(2,1)S(1)} %pad_maximum_fusion.1), channel_id=1, source_target_pairs={{0,24},{8,16},{16,8},{24,0},{1,25},{9,17},{17,9},{25,1},{2,26},{10... | collective-permute-start | bytes 149000 | tf_op jit(solution)/shard_map/ppermute | solution.py:23
  13.3 17.0 %copy-start.9 = (f32[2,128,2,128]{3,2,1,0:T(2,128)S(1)}, f32[2,128,2,128]{3,2,1,0:T(2,128)}, u32[]{:S(2)}) copy-start(f32[2,128,2,128]{3,2,1,0:T(2,128)} %param.29) | copy-start | bytes 786436
  36.1 18.0 %copy-start.4 = (bf16[2,128,384]{2,1,0:T(8,128)(2,1)S(1)}, bf16[2,128,384]{2,1,0:T(8,128)(2,1)}, u32[]{:S(2)}) copy-start(bf16[2,128,384]{2,1,0:T(8,128)(2,1)} %param.23) | copy-start | bytes 589828
  36.1 34.5 %copy-start.2 = (bf16[64,384]{1,0:T(8,128)(2,1)S(1)}, bf16[64,384]{1,0:T(8,128)(2,1)}, u32[]{:S(2)}) copy-start(bf16[64,384]{1,0:T(8,128)(2,1)} %param.16) | copy-start | bytes 147460
  36.1 34.7 %copy-start = (bf16[2,384,512]{2,1,0:T(8,128)(2,1)S(1)}, bf16[2,384,512]{2,1,0:T(8,128)(2,1)}, u32[]{:S(2)}) copy-start(bf16[2,384,512]{2,1,0:T(8,128)(2,1)} %param.25) | copy-start | bytes 2359300
  36.1 35.0 %copy-start.1 = (bf16[2,384,512]{2,1,0:T(8,128)(2,1)S(1)}, bf16[2,384,512]{2,1,0:T(8,128)(2,1)}, u32[]{:S(2)}) copy-start(bf16[2,384,512]{2,1,0:T(8,128)(2,1)} %param.24) | copy-start | bytes 2359300
  41.7 62.6 %copy-start.7 = (bf16[2,384,2]{1,2,0:T(2,128)(2,1)S(1)}, bf16[2,384,2]{1,2,0:T(2,128)(2,1)}, u32[]{:S(2)}) copy-start(bf16[2,384,2]{1,2,0:T(2,128)(2,1)} %param.21) | copy-start | bytes 9220
  41.7 62.7 %copy-start.3 = (bf16[2,384,384]{2,1,0:T(8,128)(2,1)S(1)}, bf16[2,384,384]{2,1,0:T(8,128)(2,1)}, u32[]{:S(2)}) copy-start(bf16[2,384,384]{2,1,0:T(8,128)(2,1)} %param.20) | copy-start | bytes 1769476
  71.5 10.2 %collective-permute-start.5 = (bf16[64,1026]{0,1:T(8,128)(2,1)S(1)}, bf16[64,1026]{0,1:T(8,128)(2,1)S(1)}, u32[]{:S(2)}, u32[]{:S(2)}) collective-permute-start(bf16[64,1026]{0,1:T(8,128)(2,1)S(1)} %concatenate.35), channel_id=1, source_target_pairs={{0,24},{8,16},{16,8},{24,0},{1,25},{9,17},{17,9},{25,1},{2,26},{10... | collective-permute-start | bytes 393992 | tf_op jit(solution)/shard_map/ppermute | solution.py:23
  73.1 13.7 %collective-permute-start.4 = (bf16[64,1026]{0,1:T(8,128)(2,1)S(1)}, bf16[64,1026]{0,1:T(8,128)(2,1)S(1)}, u32[]{:S(2)}, u32[]{:S(2)}) collective-permute-start(bf16[64,1026]{0,1:T(8,128)(2,1)S(1)} %concatenate.35), channel_id=1, source_target_pairs={{0,16},{8,24},{16,0},{24,8},{1,17},{9,25},{17,1},{25,9},{2,18},{10... | collective-permute-start | bytes 393992 | tf_op jit(solution)/shard_map/ppermute | solution.py:23
  74.9 12.3 %collective-permute-start.3 = (bf16[64,1026]{0,1:T(8,128)(2,1)S(1)}, bf16[64,1026]{0,1:T(8,128)(2,1)S(1)}, u32[]{:S(2)}, u32[]{:S(2)}) collective-permute-start(bf16[64,1026]{0,1:T(8,128)(2,1)S(1)} %concatenate.35), channel_id=1, source_target_pairs={{0,8},{8,0},{16,24},{24,16},{1,9},{9,1},{17,25},{25,17},{2,10},{10... | collective-permute-start | bytes 393992 | tf_op jit(solution)/shard_map/ppermute | solution.py:23
  104.8 5.2 %collective-permute-start.7 = (bf16[64,388]{0,1:T(8,128)(2,1)S(1)}, bf16[64,388]{0,1:T(8,128)(2,1)S(1)}, u32[]{:S(2)}, u32[]{:S(2)}) collective-permute-start(bf16[64,388]{0,1:T(8,128)(2,1)S(1)} %pad_maximum_fusion.2), channel_id=1, source_target_pairs={{0,16},{8,24},{16,0},{24,8},{1,17},{9,25},{17,1},{25,9},{2,18},{10... | collective-permute-start | bytes 149000 | tf_op jit(solution)/shard_map/ppermute | solution.py:23
  106.4 5.7 %collective-permute-start.6 = (bf16[64,388]{0,1:T(8,128)(2,1)S(1)}, bf16[64,388]{0,1:T(8,128)(2,1)S(1)}, u32[]{:S(2)}, u32[]{:S(2)}) collective-permute-start(bf16[64,388]{0,1:T(8,128)(2,1)S(1)} %pad_maximum_fusion.2), channel_id=1, source_target_pairs={{0,8},{8,0},{16,24},{24,16},{1,9},{9,1},{17,25},{25,17},{2,10},{10... | collective-permute-start | bytes 149000 | tf_op jit(solution)/shard_map/ppermute | solution.py:23
  106.9 6.4 %collective-permute-start.8 = (bf16[64,388]{0,1:T(8,128)(2,1)S(1)}, bf16[64,388]{0,1:T(8,128)(2,1)S(1)}, u32[]{:S(2)}, u32[]{:S(2)}) collective-permute-start(bf16[64,388]{0,1:T(8,128)(2,1)S(1)} %pad_maximum_fusion.2), channel_id=1, source_target_pairs={{0,24},{8,16},{16,8},{24,0},{1,25},{9,17},{17,9},{25,1},{2,26},{10... | collective-permute-start | bytes 149000 | tf_op jit(solution)/shard_map/ppermute | solution.py:23
  121.9 49.6 %copy-start.8 = (bf16[2,512,384]{2,1,0:T(8,128)(2,1)S(1)}, bf16[2,512,384]{2,1,0:T(8,128)(2,1)}, u32[]{:S(2)}) copy-start(bf16[2,512,384]{2,1,0:T(8,128)(2,1)} %param.26) | copy-start | bytes 2359300
  126.6 60.7 %copy-start.5 = (f32[384]{0:T(512)S(1)}, f32[384]{0:T(512)}, u32[]{:S(2)}) copy-start(f32[384]{0:T(512)} %param.19) | copy-start | bytes 4612
  156.2 10.2 %collective-permute-start.11 = (bf16[64,1026]{0,1:T(8,128)(2,1)S(1)}, bf16[64,1026]{0,1:T(8,128)(2,1)S(1)}, u32[]{:S(2)}, u32[]{:S(2)}) collective-permute-start(bf16[64,1026]{0,1:T(8,128)(2,1)S(1)} %concatenate.39), channel_id=1, source_target_pairs={{0,24},{8,16},{16,8},{24,0},{1,25},{9,17},{17,9},{25,1},{2,26},{10... | collective-permute-start | bytes 393992 | tf_op jit(solution)/shard_map/ppermute | solution.py:23
  157.7 13.7 %collective-permute-start.10 = (bf16[64,1026]{0,1:T(8,128)(2,1)S(1)}, bf16[64,1026]{0,1:T(8,128)(2,1)S(1)}, u32[]{:S(2)}, u32[]{:S(2)}) collective-permute-start(bf16[64,1026]{0,1:T(8,128)(2,1)S(1)} %concatenate.39), channel_id=1, source_target_pairs={{0,16},{8,24},{16,0},{24,8},{1,17},{9,25},{17,1},{25,9},{2,18},{10... | collective-permute-start | bytes 393992 | tf_op jit(solution)/shard_map/ppermute | solution.py:23
  157.9 13.5 %collective-permute-start.9 = (bf16[64,1026]{0,1:T(8,128)(2,1)S(1)}, bf16[64,1026]{0,1:T(8,128)(2,1)S(1)}, u32[]{:S(2)}, u32[]{:S(2)}) collective-permute-start(bf16[64,1026]{0,1:T(8,128)(2,1)S(1)} %concatenate.39), channel_id=1, source_target_pairs={{0,8},{8,0},{16,24},{24,16},{1,9},{9,1},{17,25},{25,17},{2,10},{10... | collective-permute-start | bytes 393992 | tf_op jit(solution)/shard_map/ppermute | solution.py:23
  206.8 19.4 %copy-start.6 = (f32[64]{0:T(128)}, f32[64]{0:T(128)S(1)}, u32[]{:S(2)}) copy-start(f32[64]{0:T(128)S(1)} %get-tuple-element.8) | copy-start | bytes 772
  215.0 7.1 %collective-permute-start.18 = (f32[64]{0:T(128)S(1)}, f32[64]{0:T(128)S(1)}, u32[]{:S(2)}, u32[]{:S(2)}) collective-permute-start(f32[64]{0:T(128)S(1)} %pmax.7), channel_id=1, source_target_pairs={{0,7},{1,6},{2,5},{3,4},{4,3},{5,2},{6,1},{7,0},{8,15},{9,14},{10,... | collective-permute-start | bytes 776 | tf_op jit(solution)/shard_map/ppermute | solution.py:41
  215.9 7.1 %collective-permute-start.17 = (f32[64]{0:T(128)S(1)}, f32[64]{0:T(128)S(1)}, u32[]{:S(2)}, u32[]{:S(2)}) collective-permute-start(f32[64]{0:T(128)S(1)} %pmax.7), channel_id=1, source_target_pairs={{0,6},{1,7},{2,4},{3,5},{4,2},{5,3},{6,0},{7,1},{8,14},{9,15},{10,... | collective-permute-start | bytes 776 | tf_op jit(solution)/shard_map/ppermute | solution.py:41
  218.6 5.2 %collective-permute-start.16 = (f32[64]{0:T(128)S(1)}, f32[64]{0:T(128)S(1)}, u32[]{:S(2)}, u32[]{:S(2)}) collective-permute-start(f32[64]{0:T(128)S(1)} %pmax.7), channel_id=1, source_target_pairs={{0,5},{1,4},{2,7},{3,6},{4,1},{5,0},{6,3},{7,2},{8,13},{9,12},{10,... | collective-permute-start | bytes 776 | tf_op jit(solution)/shard_map/ppermute | solution.py:41
  218.6 5.2 %collective-permute-start.15 = (f32[64]{0:T(128)S(1)}, f32[64]{0:T(128)S(1)}, u32[]{:S(2)}, u32[]{:S(2)}) collective-permute-start(f32[64]{0:T(128)S(1)} %pmax.7), channel_id=1, source_target_pairs={{0,4},{1,5},{2,6},{3,7},{4,0},{5,1},{6,2},{7,3},{8,12},{9,13},{10,... | collective-permute-start | bytes 776 | tf_op jit(solution)/shard_map/ppermute | solution.py:41
  221.2 3.0 %collective-permute-start.14 = (f32[64]{0:T(128)S(1)}, f32[64]{0:T(128)S(1)}, u32[]{:S(2)}, u32[]{:S(2)}) collective-permute-start(f32[64]{0:T(128)S(1)} %pmax.7), channel_id=1, source_target_pairs={{0,3},{1,2},{2,1},{3,0},{4,7},{5,6},{6,5},{7,4},{8,11},{9,10},{10,... | collective-permute-start | bytes 776 | tf_op jit(solution)/shard_map/ppermute | solution.py:41
  222.1 3.6 %collective-permute-start.13 = (f32[64]{0:T(128)S(1)}, f32[64]{0:T(128)S(1)}, u32[]{:S(2)}, u32[]{:S(2)}) collective-permute-start(f32[64]{0:T(128)S(1)} %pmax.7), channel_id=1, source_target_pairs={{0,2},{1,3},{2,0},{3,1},{4,6},{5,7},{6,4},{7,5},{8,10},{9,11},{10,... | collective-permute-start | bytes 776 | tf_op jit(solution)/shard_map/ppermute | solution.py:41
  223.0 2.7 %collective-permute-start.12 = (f32[64]{0:T(128)S(1)}, f32[64]{0:T(128)S(1)}, u32[]{:S(2)}, u32[]{:S(2)}) collective-permute-start(f32[64]{0:T(128)S(1)} %pmax.7), channel_id=1, source_target_pairs={{0,1},{1,0},{2,3},{3,2},{4,5},{5,4},{6,7},{7,6},{8,9},{9,8},{10,11... | collective-permute-start | bytes 776 | tf_op jit(solution)/shard_map/ppermute | solution.py:41

commit v5 on v4

--- a/solution.py
+++ b/solution.py
@@ -14,7 +14,7 @@
 
 
 def gather_sum(value, axis):
-    return jnp.sum(lax.all_gather(value, axis), axis=0)
+    return jnp.sum(lax.all_gather(value, axis).astype(jnp.float32), axis=0)
 
 
 def xor_sum(value, axis, kind=None):
@@ -27,6 +27,26 @@
     while len(parts) > 1:
         parts = [parts[i] + parts[i + 1] for i in range(0, len(parts), 2)]
     return parts[0]
+
+
+def butterfly(parts, join):
+    while len(parts) > 1:
+        parts = [join(parts[i], parts[i + 1]) for i in range(0, len(parts), 2)]
+    return parts[0]
+
+
+def exchange(value, axis, partner):
+    count = lax.axis_size(axis)
+    return lax.ppermute(value, axis, [(i, i ^ partner) for i in range(count)])
+
+
+def core_first_sum(value, axis):
+    carried = value.astype(jnp.bfloat16)
+    pair = carried.astype(jnp.float32) + exchange(carried, axis, 1).astype(jnp.float32)
+    pair = pair.astype(jnp.bfloat16)
+    count = lax.axis_size(axis)
+    parts = [pair] + [exchange(pair, axis, k) for k in range(2, count, 2)]
+    return butterfly([part.astype(jnp.float32) for part in parts], jnp.add)
 
 
 def split_pair(value):
@@ -98,12 +118,14 @@
 
 def merge_pages(row_peak, row_sum, row_out):
     packed = jnp.concatenate([row_peak[:, :, None], row_sum[:, :, None], row_out], axis=2)
-    every = lax.all_gather(packed, "gx")
-    peaks = every[:, :, :, 0]
-    top = jnp.max(peaks, axis=0)
-    scale = jnp.exp(peaks - top[None])
-    total = jnp.sum(scale * every[:, :, :, 1], axis=0)
-    out = jnp.sum(scale[..., None] * every[:, :, :, 2:], axis=0)
+    count = lax.axis_size("gx")
+    every = [packed] + [exchange(packed, "gx", k) for k in range(1, count)]
+    top = butterfly([part[:, :, 0] for part in every], jnp.maximum)
+    scales = [jnp.exp(part[:, :, 0] - top) for part in every]
+    total = butterfly([scale * part[:, :, 1] for scale, part in zip(scales, every)], jnp.add)
+    out = butterfly(
+        [scale[..., None] * part[:, :, 2:] for scale, part in zip(scales, every)], jnp.add
+    )
     return top, total, out
 
 
@@ -182,7 +204,7 @@
             .reshape(request_count, local_heads * HEAD)
             .astype(jnp.bfloat16)
         )
-        stream = stream + gather_sum(
+        stream = stream + core_first_sum(
             jnp.dot(attended, out_weight[layer_id], preferred_element_type=jnp.float32), "gy"
         )
         squares = jnp.sum(stream * stream, axis=1)
@@ -190,19 +212,18 @@
         gate_part = jnp.dot(scaled, gate_weight[layer_id], preferred_element_type=jnp.float32)
         up_part = jnp.dot(scaled, up_weight[layer_id], preferred_element_type=jnp.float32)
         hidden_cols = gate_part.shape[1]
-        total = xor_sum(
+        total = gather_sum(
             jnp.concatenate(
                 [gate_part.astype(jnp.bfloat16), up_part.astype(jnp.bfloat16), split_pair(squares)],
                 axis=1,
             ),
             "gx",
-            jnp.float32,
         )
         rms_value = jnp.sqrt((total[:, -2] + total[:, -1]) / width + EPSILON)
         gate_full = total[:, :hidden_cols] / rms_value[:, None]
         up_full = total[:, hidden_cols : 2 * hidden_cols] / rms_value[:, None]
         hidden = (jax.nn.silu(gate_full) * up_full).astype(jnp.bfloat16)
-        stream = stream + gather_sum(
+        stream = stream + core_first_sum(
             jnp.dot(hidden, down_weight[layer_id], preferred_element_type=jnp.float32), "gy"
         )
     squares = jnp.sum(stream * stream, axis=1)

time: 227 us -> 182 us (0.80)
  blocking collectives: 106 us -> 44.7 us
  starting transfers between devices: 23.3 us -> 41.4 us
    all_gather x6 -> x2, blocking collectives: 82 us -> 21.8 us  [gather_sum(): return jnp.sum(lax.all_gather(value, axis).astype(jnp.float32), axis=0)]
    ppermute x0 -> x22, waiting for transfers between devices: none -> 25.7 us  [exchange(): return lax.ppermute(value, axis, [(i, i ^ partner) for i in range(count)])]
    ppermute x0 -> x22, starting transfers between devices: none -> 25.2 us  [exchange(): return lax.ppermute(value, axis, [(i, i ^ partner) for i in range(count)])]
    ppermute x12 -> x6, waiting for transfers between devices: 28.7 us -> 4.44 us  [xor_sum(): lax.ppermute(value, axis, [(i, i ^ k) for i in range(count)])]
    ppermute x12 -> x6, starting transfers between devices: 15.2 us -> 8.13 us  [xor_sum(): lax.ppermute(value, axis, [(i, i ^ k) for i in range(count)])]
  transfers between devices with their start and end apart: 19 -> 35, of which waited for: 10 -> 23; matrix products, arithmetic and copies ran while one was open for 9% -> 11% of each run, Pallas kernels for 0% -> 0%
where the time goes in v5:
time: 182 us
  blocking collectives  44.7 us (25%)
  starting transfers between devices  41.4 us (23%)
  waiting for transfers between devices  31.2 us (17%)
  matrix products  30.8 us (17%)
  local copies, waits for them, and re-layouts  24.7 us (14%)
  other arithmetic  7.7 us (4%)
    ppermute x22, waiting for transfers between devices, exchange(): return lax.ppermute(value, axis, [(i, i ^ partner) for i in range(count)])  25.7 us
    ppermute x22, starting transfers between devices, exchange(): return lax.ppermute(value, axis, [(i, i ^ partner) for i in range(count)])  25.2 us
    all_gather x2, blocking collectives, gather_sum(): return jnp.sum(lax.all_gather(value, axis).astype(jnp.float32), axis=0)  21.8 us
    slice x1, local copies, waits for them, and re-layouts, local(): kv_cache[layer_id]  14.9 us
    all_to_all x1, blocking collectives, local(): pieces = lax.all_to_all(pieces, 'gx', 1, 1, tiled=True).astype(jnp.float32)  14.7 us
    dot_general x2, matrix products, local_attention(): jnp.einsum('pthc,pkhc->pkt', kv_layer, query_block, preferred_element_typ...  11.7 us
    dot_general x2, matrix products, local_attention(): jnp.einsum('pkt,pthc->pkhc', weights.astype(jnp.bfloat16), kv_layer, pref...  9.37 us
    pmax x1, blocking collectives, local(): top_logits = xor_max(lax.pmax(local_top, 'gx'), 'gy')  8.21 us
  transfers between devices with their start and end apart: 35, of which 23 were waited for; matrix products, arithmetic and copies ran while one was open for 11% of the time, Pallas kernels for 0%

profile of v5, /device:TPU:0, one launch (start us, length us, event | category | flops | bytes accessed | tf_op | source)
XLA Modules:
  0.0 181.8 jit_solution(13645695465702410153)
XLA Ops:
  2.3 0.9 convolution_convert_fusion.13
  3.3 1.3 convolution_convert_fusion.2
  4.6 3.0 %collective-permute-start.1 = (bf16[64,388]{0,1:T(8,128)(2,1)S(1)}, bf16[64,388]{0,1:T(8,128)(2,1)S(1)}, u32[]{:S(2)}, u32[]{:S(2)}) collective-permute-start(bf16[64,388]{0,1:T(8,128)(2,1)S(1)} %pad_maximum_fusion.1), channel_id=1, source_target_pairs={{0,16},{8,24},{16,0},{24,8},{1,17},{9,25},{17,1},{25,9},{2,18},{10... | collective-permute-start | bytes 149000 | tf_op jit(solution)/shard_map/ppermute | solution.py:23
  7.7 1.5 collective-permute-start
  12.6 14.9 %fusion.168 = (bf16[1,128,128,2,128]{4,3,2,1,0:T(2,128)(2,1)}, bf16[1,128,128,2,128]{4,3,2,1,0:T(2,128)(2,1)}) fusion(bf16[2,128,128,2,128]{4,3,2,1,0:T(2,128)(2,1)} %param.28), kind=kLoop, calls=%fused_computation.318 | loop fusion | bytes 33554432 | tf_op jit(solution)/shard_map/slice | solution.py:187
  29.6 5.9 %fusion.175 = (f32[128,2]{1,0:T(8,128)S(1)}, f32[128,2,128]{2,1,0:T(2,128)S(1)}) fusion(f32[128,2]{1,0:T(8,128)S(1)} %gather_fusion.1, f32[2,128,2,128]{3,2,1,0:T(2,128)S(1)} %copy-done.10, bf16[1,128,128,2,128]{4,3,2,1,0:T(2,128)(2,1)} %get-tuple-element.26, bf16[128,2,128]{2,1,0:T(2,128)(2,1)S(1)} %concatenate.33, ...), kind=kOutput, calls=%fused_computation.325 | convolution fusion | flops 17202944 | bytes 8734728 | tf_op jit(solution)/shard_map/pthc,pkhc->pkt/dot_general | solution.py:99
  36.4 4.7 %fusion = f32[128,2,2,128]{3,1,2,0:T(2,128)S(1)} fusion(bf16[1,128,128,2,128]{4,3,2,1,0:T(2,128)(2,1)} %get-tuple-element.26, f32[128,2,128]{2,1,0:T(2,128)S(1)} %get-tuple-element.59, pred[128,128]{1,0:T(8,128)(4,1)S(1)} %fusion.93, f32[128,2]{1,0:T(8,128)S(1)} %gather_fusion.2), kind=kOutput, calls=%fused_computation.8 | convolution fusion | flops 16875520 | bytes 8799232 | tf_op jit(solution)/shard_map/pkt,pthc->pkhc/dot_general | solution.py:109
  42.4 2.9 %collective-permute-start.5 = (f32[64,2,66]{0,1,2:T(2,128)S(1)}, f32[64,2,66]{0,1,2:T(2,128)S(1)}, u32[]{:S(2)}, u32[]{:S(2)}) collective-permute-start(f32[64,2,66]{0,1,2:T(2,128)S(1)} %pad_maximum_fusion.3), channel_id=1, source_target_pairs={{0,24},{8,16},{16,8},{24,0},{1,25},{9,17},{17,9},{25,1},{2,26},{10... | collective-permute-start | bytes 101384 | tf_op jit(solution)/shard_map/ppermute | solution.py:40
  46.3 1.4 collective-permute-done.5
  47.8 1.9 %collective-permute-done.4 = f32[64,2,66]{0,1,2:T(2,128)S(1)} collective-permute-done((f32[64,2,66]{0,1,2:T(2,128)S(1)}, f32[64,2,66]{0,1,2:T(2,128)S(1)}, u32[]{:S(2)}, u32[]{:S(2)}) %collective-permute-start.4) | collective-permute-done | bytes 33824 | tf_op jit(solution)/shard_map/ppermute | solution.py:40
  50.8 1.2 collective-permute-done.6
  52.0 3.7 %collective-permute-start.9 = (bf16[64,384]{1,0:T(8,128)(2,1)S(1)}, bf16[64,384]{1,0:T(8,128)(2,1)S(1)}, u32[]{:S(2)}, u32[]{:S(2)}) collective-permute-start(bf16[64,384]{1,0:T(8,128)(2,1)S(1)} %add_convert_fusion.3), channel_id=1, source_target_pairs={{0,6},{1,7},{2,4},{3,5},{4,2},{5,3},{6,0},{7,1},{8,14},{9,15},{10,... | collective-permute-start | bytes 147464 | tf_op jit(solution)/shard_map/ppermute | solution.py:40
  56.5 1.5 collective-permute-done.9
  58.0 2.6 %collective-permute-done.8 = bf16[64,384]{1,0:T(8,128)(2,1)S(1)} collective-permute-done((bf16[64,384]{1,0:T(8,128)(2,1)S(1)}, bf16[64,384]{1,0:T(8,128)(2,1)S(1)}, u32[]{:S(2)}, u32[]{:S(2)}) %collective-permute-start.8) | collective-permute-done | bytes 49184 | tf_op jit(solution)/shard_map/ppermute | solution.py:40
  61.6 11.0 %all-gather = bf16[256,1026]{1,0:T(8,128)(2,1)S(1)} all-gather(bf16[64,1026]{1,0:T(8,128)(2,1)S(1)} %concatenate.35), channel_id=2, replica_groups=mesh['gx'=4,'gy'=8] {'gx'}, dimensions={0}, use_global_device_ids=true | all-gather | bytes 656640 | tf_op jit(solution)/shard_map/all_gather | solution.py:17
  72.9 1.3 convolution_convert_fusion.10
  74.3 1.2 collective-permute-done.10
  75.5 2.5 %collective-permute-start.13 = (bf16[64,384]{1,0:T(8,128)(2,1)S(1)}, bf16[64,384]{1,0:T(8,128)(2,1)S(1)}, u32[]{:S(2)}, u32[]{:S(2)}) collective-permute-start(bf16[64,384]{1,0:T(8,128)(2,1)S(1)} %add_convert_fusion.2), channel_id=1, source_target_pairs={{0,6},{1,7},{2,4},{3,5},{4,2},{5,3},{6,0},{7,1},{8,14},{9,15},{10,... | collective-permute-start | bytes 147464 | tf_op jit(solution)/shard_map/ppermute | solution.py:40
  78.2 1.8 collective-permute-start.11
  80.0 1.7 collective-permute-done.13
  81.7 1.9 %collective-permute-done.12 = bf16[64,384]{1,0:T(8,128)(2,1)S(1)} collective-permute-done((bf16[64,384]{1,0:T(8,128)(2,1)S(1)}, bf16[64,384]{1,0:T(8,128)(2,1)S(1)}, u32[]{:S(2)}, u32[]{:S(2)}) %collective-permute-start.12) | collective-permute-done | bytes 49184 | tf_op jit(solution)/shard_map/ppermute | solution.py:40
  84.3 2.0 %collective-permute-start.14 = (bf16[64,388]{0,1:T(8,128)(2,1)S(1)}, bf16[64,388]{0,1:T(8,128)(2,1)S(1)}, u32[]{:S(2)}, u32[]{:S(2)}) collective-permute-start(bf16[64,388]{0,1:T(8,128)(2,1)S(1)} %pad_maximum_fusion.2), channel_id=1, source_target_pairs={{0,8},{8,0},{16,24},{24,16},{1,9},{9,1},{17,25},{25,17},{2,10},{10... | collective-permute-start | bytes 149000 | tf_op jit(solution)/shard_map/ppermute | solution.py:23
  86.3 1.5 collective-permute-start.16
  87.8 1.1 collective-permute-done.15
  88.9 1.1 collective-permute-done.14
  90.0 2.2 %collective-permute-done.16 = bf16[64,388]{0,1:T(8,128)(2,1)S(1)} collective-permute-done((bf16[64,388]{0,1:T(8,128)(2,1)S(1)}, bf16[64,388]{0,1:T(8,128)(2,1)S(1)}, u32[]{:S(2)}, u32[]{:S(2)}) %collective-permute-start.16) | collective-permute-done | bytes 49696 | tf_op jit(solution)/shard_map/ppermute | solution.py:23
  94.1 5.8 %fusion.176 = (f32[128,2]{1,0:T(8,128)S(1)}, f32[128,2,128]{2,1,0:T(2,128)S(1)}) fusion(f32[128,2]{1,0:T(8,128)S(1)} %gather_fusion.4, f32[2,128,2,128]{3,2,1,0:T(2,128)S(1)} %copy-done.10, bf16[1,128,128,2,128]{4,3,2,1,0:T(2,128)(2,1)} %get-tuple-element.25, bf16[128,2,128]{2,1,0:T(2,128)(2,1)S(1)} %concatenate.37, ...), kind=kOutput, calls=%fused_computation.326 | convolution fusion | flops 17202944 | bytes 8734728 | tf_op jit(solution)/shard_map/pthc,pkhc->pkt/dot_general | solution.py:99
  100.9 4.7 %fusion.2 = f32[128,2,2,128]{3,1,2,0:T(2,128)S(1)} fusion(bf16[1,128,128,2,128]{4,3,2,1,0:T(2,128)(2,1)} %get-tuple-element.25, f32[128,2,128]{2,1,0:T(2,128)S(1)} %get-tuple-element.61, pred[128,128]{1,0:T(8,128)(4,1)S(1)} %fusion.93, f32[128,2]{1,0:T(8,128)S(1)} %gather_fusion.5), kind=kOutput, calls=%fused_computation.10 | convolution fusion | flops 16875520 | bytes 8799232 | tf_op jit(solution)/shard_map/pkt,pthc->pkhc/dot_general | solution.py:109
  106.8 1.5 collective-permute-start.19
  108.7 1.7 collective-permute-start.17
  110.7 1.4 collective-permute-done.19
  113.6 1.2 collective-permute-done.20
  114.9 2.6 %collective-permute-start.23 = (bf16[64,384]{1,0:T(8,128)(2,1)S(1)}, bf16[64,384]{1,0:T(8,128)(2,1)S(1)}, u32[]{:S(2)}, u32[]{:S(2)}) collective-permute-start(bf16[64,384]{1,0:T(8,128)(2,1)S(1)} %add_convert_fusion.1), channel_id=1, source_target_pairs={{0,6},{1,7},{2,4},{3,5},{4,2},{5,3},{6,0},{7,1},{8,14},{9,15},{10,... | collective-permute-start | bytes 147464 | tf_op jit(solution)/shard_map/ppermute | solution.py:40
  117.5 1.9 %collective-permute-start.21 = (bf16[64,384]{1,0:T(8,128)(2,1)S(1)}, bf16[64,384]{1,0:T(8,128)(2,1)S(1)}, u32[]{:S(2)}, u32[]{:S(2)}) collective-permute-start(bf16[64,384]{1,0:T(8,128)(2,1)S(1)} %add_convert_fusion.1), channel_id=1, source_target_pairs={{0,2},{1,3},{2,0},{3,1},{4,6},{5,7},{6,4},{7,5},{8,10},{9,11},{10,... | collective-permute-start | bytes 147464 | tf_op jit(solution)/shard_map/ppermute | solution.py:40
  119.3 1.8 collective-permute-done.23
  121.1 1.6 collective-permute-done.22
  123.5 10.8 %all-gather.1 = bf16[256,1026]{1,0:T(8,128)(2,1)S(1)} all-gather(bf16[64,1026]{1,0:T(8,128)(2,1)S(1)} %concatenate.39), channel_id=3, replica_groups=mesh['gx'=4,'gy'=8] {'gx'}, dimensions={0}, use_global_device_ids=true | all-gather | bytes 656640 | tf_op jit(solution)/shard_map/all_gather | solution.py:17
  135.0 1.2 collective-permute-done.24
  136.2 2.4 %collective-permute-start.27 = (bf16[64,384]{1,0:T(8,128)(2,1)S(1)}, bf16[64,384]{1,0:T(8,128)(2,1)S(1)}, u32[]{:S(2)}, u32[]{:S(2)}) collective-permute-start(bf16[64,384]{1,0:T(8,128)(2,1)S(1)} %add_convert_fusion), channel_id=1, source_target_pairs={{0,6},{1,7},{2,4},{3,5},{4,2},{5,3},{6,0},{7,1},{8,14},{9,15},{10,... | collective-permute-start | bytes 147464 | tf_op jit(solution)/shard_map/ppermute | solution.py:40
  139.1 1.6 collective-permute-start.25
  140.7 1.7 collective-permute-done.27
  142.4 1.9 %collective-permute-done.26 = bf16[64,384]{1,0:T(8,128)(2,1)S(1)} collective-permute-done((bf16[64,384]{1,0:T(8,128)(2,1)S(1)}, bf16[64,384]{1,0:T(8,128)(2,1)S(1)}, u32[]{:S(2)}, u32[]{:S(2)}) %collective-permute-start.26) | collective-permute-done | bytes 49184 | tf_op jit(solution)/shard_map/ppermute | solution.py:40
  144.6 3.3 %convolution_convert_fusion = bf16[64,6144]{1,0:T(8,128)(2,1)S(1)} fusion(bf16[384,6144]{1,0:T(8,128)(2,1)} %param.27, f32[64,384]{1,0:T(8,128)S(1)} %get-tuple-element.10, f32[384]{0:T(512)S(1)} %copy-done.5), kind=kOutput, calls=%fused_computation.12 | convolution fusion | flops 302432256 | bytes 5604864 | tf_op jit(solution)/shard_map/dot_general | solution.py:231
  148.0 14.7 %all_to_all.5 = bf16[64,4,1538]{2,0,1:T(8,128)(2,1)S(1)} all-to-all(bf16[64,4,1538]{2,0,1:T(8,128)(2,1)S(1)} %pad_maximum_fusion), channel_id=1, replica_groups=mesh['gx'=4,'gy'=8] {'gx'}, dimensions={1} | all-to-all | bytes 1574912 | tf_op jit(solution)/shard_map/all_to_all | solution.py:242
  163.3 8.2 %pmax.7 = f32[64]{0:T(128)S(1)} all-reduce(f32[64]{0:T(128)S(1)} %get-tuple-element.7), channel_id=1, replica_groups=mesh['gx'=4,'gy'=8] {'gx'}, use_global_device_ids=true, to_apply=%region_19.20 | all-reduce | flops 64 | bytes 512 | tf_op jit(solution)/shard_map/pmax | solution.py:248
  171.5 2.7 %collective-permute-start.33 = (f32[64]{0:T(128)S(1)}, f32[64]{0:T(128)S(1)}, u32[]{:S(2)}, u32[]{:S(2)}) collective-permute-start(f32[64]{0:T(128)S(1)} %pmax.7), channel_id=1, source_target_pairs={{0,6},{1,7},{2,4},{3,5},{4,2},{5,3},{6,0},{7,1},{8,14},{9,15},{10,... | collective-permute-start | bytes 776 | tf_op jit(solution)/shard_map/ppermute | solution.py:61
  174.3 3.5 %collective-permute-start.31 = (f32[64]{0:T(128)S(1)}, f32[64]{0:T(128)S(1)}, u32[]{:S(2)}, u32[]{:S(2)}) collective-permute-start(f32[64]{0:T(128)S(1)} %pmax.7), channel_id=1, source_target_pairs={{0,4},{1,5},{2,6},{3,7},{4,0},{5,1},{6,2},{7,3},{8,12},{9,13},{10,... | collective-permute-start | bytes 776 | tf_op jit(solution)/shard_map/ppermute | solution.py:61
  178.7 0.9 collective-permute-start.28
  (197 shorter events, 26.6 us)
Async XLA Ops:
  4.6 23.0 %collective-permute-start.1 = (bf16[64,388]{0,1:T(8,128)(2,1)S(1)}, bf16[64,388]{0,1:T(8,128)(2,1)S(1)}, u32[]{:S(2)}, u32[]{:S(2)}) collective-permute-start(bf16[64,388]{0,1:T(8,128)(2,1)S(1)} %pad_maximum_fusion.1), channel_id=1, source_target_pairs={{0,16},{8,24},{16,0},{24,8},{1,17},{9,25},{17,1},{25,9},{2,18},{10... | collective-permute-start | bytes 149000 | tf_op jit(solution)/shard_map/ppermute | solution.py:23
  7.7 20.0 %collective-permute-start = (bf16[64,388]{0,1:T(8,128)(2,1)S(1)}, bf16[64,388]{0,1:T(8,128)(2,1)S(1)}, u32[]{:S(2)}, u32[]{:S(2)}) collective-permute-start(bf16[64,388]{0,1:T(8,128)(2,1)S(1)} %pad_maximum_fusion.1), channel_id=1, source_target_pairs={{0,8},{8,0},{16,24},{24,16},{1,9},{9,1},{17,25},{25,17},{2,10},{10... | collective-permute-start | bytes 149000 | tf_op jit(solution)/shard_map/ppermute | solution.py:23
  9.1 18.5 %collective-permute-start.2 = (bf16[64,388]{0,1:T(8,128)(2,1)S(1)}, bf16[64,388]{0,1:T(8,128)(2,1)S(1)}, u32[]{:S(2)}, u32[]{:S(2)}) collective-permute-start(bf16[64,388]{0,1:T(8,128)(2,1)S(1)} %pad_maximum_fusion.1), channel_id=1, source_target_pairs={{0,24},{8,16},{16,8},{24,0},{1,25},{9,17},{17,9},{25,1},{2,26},{10... | collective-permute-start | bytes 149000 | tf_op jit(solution)/shard_map/ppermute | solution.py:23
  12.5 17.0 %copy-start.10 = (f32[2,128,2,128]{3,2,1,0:T(2,128)S(1)}, f32[2,128,2,128]{3,2,1,0:T(2,128)}, u32[]{:S(2)}) copy-start(f32[2,128,2,128]{3,2,1,0:T(2,128)} %param.29) | copy-start | bytes 786436
  29.5 21.0 %copy-start.4 = (bf16[2,128,384]{2,1,0:T(8,128)(2,1)S(1)}, bf16[2,128,384]{2,1,0:T(8,128)(2,1)}, u32[]{:S(2)}) copy-start(bf16[2,128,384]{2,1,0:T(8,128)(2,1)} %param.23) | copy-start | bytes 589828
  29.5 27.0 %copy-start.6 = (f32[2,384]{1,0:T(2,128)S(1)}, f32[2,384]{1,0:T(2,128)}, u32[]{:S(2)}) copy-start(f32[2,384]{1,0:T(2,128)} %param.18) | copy-start | bytes 9220
  29.6 31.1 %copy-start.3 = (bf16[64,384]{1,0:T(8,128)(2,1)S(1)}, bf16[64,384]{1,0:T(8,128)(2,1)}, u32[]{:S(2)}) copy-start(bf16[64,384]{1,0:T(8,128)(2,1)} %param.16) | copy-start | bytes 147460
  35.4 25.6 %copy-start = (bf16[2,384,512]{2,1,0:T(8,128)(2,1)S(1)}, bf16[2,384,512]{2,1,0:T(8,128)(2,1)}, u32[]{:S(2)}) copy-start(bf16[2,384,512]{2,1,0:T(8,128)(2,1)} %param.25) | copy-start | bytes 2359300
  35.5 25.8 %copy-start.1 = (bf16[2,384,512]{2,1,0:T(8,128)(2,1)S(1)}, bf16[2,384,512]{2,1,0:T(8,128)(2,1)}, u32[]{:S(2)}) copy-start(bf16[2,384,512]{2,1,0:T(8,128)(2,1)} %param.24) | copy-start | bytes 2359300
  36.4 47.3 %copy-start.8 = (bf16[2,384,2]{1,2,0:T(2,128)(2,1)S(1)}, bf16[2,384,2]{1,2,0:T(2,128)(2,1)}, u32[]{:S(2)}) copy-start(bf16[2,384,2]{1,2,0:T(2,128)(2,1)} %param.21) | copy-start | bytes 9220
  36.4 47.5 %copy-start.2 = (bf16[2,384,384]{2,1,0:T(8,128)(2,1)S(1)}, bf16[2,384,384]{2,1,0:T(8,128)(2,1)}, u32[]{:S(2)}) copy-start(bf16[2,384,384]{2,1,0:T(8,128)(2,1)} %param.20) | copy-start | bytes 1769476
  42.4 5.4 %collective-permute-start.5 = (f32[64,2,66]{0,1,2:T(2,128)S(1)}, f32[64,2,66]{0,1,2:T(2,128)S(1)}, u32[]{:S(2)}, u32[]{:S(2)}) collective-permute-start(f32[64,2,66]{0,1,2:T(2,128)S(1)} %pad_maximum_fusion.3), channel_id=1, source_target_pairs={{0,24},{8,16},{16,8},{24,0},{1,25},{9,17},{17,9},{25,1},{2,26},{10... | collective-permute-start | bytes 101384 | tf_op jit(solution)/shard_map/ppermute | solution.py:40
  45.3 4.3 %collective-permute-start.4 = (f32[64,2,66]{0,1,2:T(2,128)S(1)}, f32[64,2,66]{0,1,2:T(2,128)S(1)}, u32[]{:S(2)}, u32[]{:S(2)}) collective-permute-start(f32[64,2,66]{0,1,2:T(2,128)S(1)} %pad_maximum_fusion.3), channel_id=1, source_target_pairs={{0,16},{8,24},{16,0},{24,8},{1,17},{9,25},{17,1},{25,9},{2,18},{10... | collective-permute-start | bytes 101384 | tf_op jit(solution)/shard_map/ppermute | solution.py:40
  45.9 4.3 %collective-permute-start.3 = (f32[64,2,66]{0,1,2:T(2,128)S(1)}, f32[64,2,66]{0,1,2:T(2,128)S(1)}, u32[]{:S(2)}, u32[]{:S(2)}) collective-permute-start(f32[64,2,66]{0,1,2:T(2,128)S(1)} %pad_maximum_fusion.3), channel_id=1, source_target_pairs={{0,8},{8,0},{16,24},{24,16},{1,9},{9,1},{17,25},{25,17},{2,10},{10... | collective-permute-start | bytes 101384 | tf_op jit(solution)/shard_map/ppermute | solution.py:40
  50.7 1.3 collective-permute-start.6
  52.0 6.0 %collective-permute-start.9 = (bf16[64,384]{1,0:T(8,128)(2,1)S(1)}, bf16[64,384]{1,0:T(8,128)(2,1)S(1)}, u32[]{:S(2)}, u32[]{:S(2)}) collective-permute-start(bf16[64,384]{1,0:T(8,128)(2,1)S(1)} %add_convert_fusion.3), channel_id=1, source_target_pairs={{0,6},{1,7},{2,4},{3,5},{4,2},{5,3},{6,0},{7,1},{8,14},{9,15},{10,... | collective-permute-start | bytes 147464 | tf_op jit(solution)/shard_map/ppermute | solution.py:40
  55.7 5.0 %collective-permute-start.8 = (bf16[64,384]{1,0:T(8,128)(2,1)S(1)}, bf16[64,384]{1,0:T(8,128)(2,1)S(1)}, u32[]{:S(2)}, u32[]{:S(2)}) collective-permute-start(bf16[64,384]{1,0:T(8,128)(2,1)S(1)} %add_convert_fusion.3), channel_id=1, source_target_pairs={{0,4},{1,5},{2,6},{3,7},{4,0},{5,1},{6,2},{7,3},{8,12},{9,13},{10,... | collective-permute-start | bytes 147464 | tf_op jit(solution)/shard_map/ppermute | solution.py:40
  55.7 5.0 %collective-permute-start.7 = (bf16[64,384]{1,0:T(8,128)(2,1)S(1)}, bf16[64,384]{1,0:T(8,128)(2,1)S(1)}, u32[]{:S(2)}, u32[]{:S(2)}) collective-permute-start(bf16[64,384]{1,0:T(8,128)(2,1)S(1)} %add_convert_fusion.3), channel_id=1, source_target_pairs={{0,2},{1,3},{2,0},{3,1},{4,6},{5,7},{6,4},{7,5},{8,10},{9,11},{10,... | collective-permute-start | bytes 147464 | tf_op jit(solution)/shard_map/ppermute | solution.py:40
  74.2 1.3 collective-permute-start.10
  75.5 6.2 %collective-permute-start.13 = (bf16[64,384]{1,0:T(8,128)(2,1)S(1)}, bf16[64,384]{1,0:T(8,128)(2,1)S(1)}, u32[]{:S(2)}, u32[]{:S(2)}) collective-permute-start(bf16[64,384]{1,0:T(8,128)(2,1)S(1)} %add_convert_fusion.2), channel_id=1, source_target_pairs={{0,6},{1,7},{2,4},{3,5},{4,2},{5,3},{6,0},{7,1},{8,14},{9,15},{10,... | collective-permute-start | bytes 147464 | tf_op jit(solution)/shard_map/ppermute | solution.py:40
  78.0 5.5 %collective-permute-start.12 = (bf16[64,384]{1,0:T(8,128)(2,1)S(1)}, bf16[64,384]{1,0:T(8,128)(2,1)S(1)}, u32[]{:S(2)}, u32[]{:S(2)}) collective-permute-start(bf16[64,384]{1,0:T(8,128)(2,1)S(1)} %add_convert_fusion.2), channel_id=1, source_target_pairs={{0,4},{1,5},{2,6},{3,7},{4,0},{5,1},{6,2},{7,3},{8,12},{9,13},{10,... | collective-permute-start | bytes 147464 | tf_op jit(solution)/shard_map/ppermute | solution.py:40
  78.2 5.4 %collective-permute-start.11 = (bf16[64,384]{1,0:T(8,128)(2,1)S(1)}, bf16[64,384]{1,0:T(8,128)(2,1)S(1)}, u32[]{:S(2)}, u32[]{:S(2)}) collective-permute-start(bf16[64,384]{1,0:T(8,128)(2,1)S(1)} %add_convert_fusion.2), channel_id=1, source_target_pairs={{0,2},{1,3},{2,0},{3,1},{4,6},{5,7},{6,4},{7,5},{8,10},{9,11},{10,... | collective-permute-start | bytes 147464 | tf_op jit(solution)/shard_map/ppermute | solution.py:40
  84.2 4.7 %collective-permute-start.15 = (bf16[64,388]{0,1:T(8,128)(2,1)S(1)}, bf16[64,388]{0,1:T(8,128)(2,1)S(1)}, u32[]{:S(2)}, u32[]{:S(2)}) collective-permute-start(bf16[64,388]{0,1:T(8,128)(2,1)S(1)} %pad_maximum_fusion.2), channel_id=1, source_target_pairs={{0,16},{8,24},{16,0},{24,8},{1,17},{9,25},{17,1},{25,9},{2,18},{10... | collective-permute-start | bytes 149000 | tf_op jit(solution)/shard_map/ppermute | solution.py:23
  84.3 5.7 %collective-permute-start.14 = (bf16[64,388]{0,1:T(8,128)(2,1)S(1)}, bf16[64,388]{0,1:T(8,128)(2,1)S(1)}, u32[]{:S(2)}, u32[]{:S(2)}) collective-permute-start(bf16[64,388]{0,1:T(8,128)(2,1)S(1)} %pad_maximum_fusion.2), channel_id=1, source_target_pairs={{0,8},{8,0},{16,24},{24,16},{1,9},{9,1},{17,25},{25,17},{2,10},{10... | collective-permute-start | bytes 149000 | tf_op jit(solution)/shard_map/ppermute | solution.py:23
  86.3 5.9 %collective-permute-start.16 = (bf16[64,388]{0,1:T(8,128)(2,1)S(1)}, bf16[64,388]{0,1:T(8,128)(2,1)S(1)}, u32[]{:S(2)}, u32[]{:S(2)}) collective-permute-start(bf16[64,388]{0,1:T(8,128)(2,1)S(1)} %pad_maximum_fusion.2), channel_id=1, source_target_pairs={{0,24},{8,16},{16,8},{24,0},{1,25},{9,17},{17,9},{25,1},{2,26},{10... | collective-permute-start | bytes 149000 | tf_op jit(solution)/shard_map/ppermute | solution.py:23
  99.9 34.7 %copy-start.9 = (bf16[2,512,384]{2,1,0:T(8,128)(2,1)S(1)}, bf16[2,512,384]{2,1,0:T(8,128)(2,1)}, u32[]{:S(2)}) copy-start(bf16[2,512,384]{2,1,0:T(8,128)(2,1)} %param.26) | copy-start | bytes 2359300
  100.8 43.7 %copy-start.5 = (f32[384]{0:T(512)S(1)}, f32[384]{0:T(512)}, u32[]{:S(2)}) copy-start(f32[384]{0:T(512)} %param.19) | copy-start | bytes 4612
  106.8 5.3 %collective-permute-start.19 = (f32[64,2,66]{0,1,2:T(2,128)S(1)}, f32[64,2,66]{0,1,2:T(2,128)S(1)}, u32[]{:S(2)}, u32[]{:S(2)}) collective-permute-start(f32[64,2,66]{0,1,2:T(2,128)S(1)} %pad_maximum_fusion.4), channel_id=1, source_target_pairs={{0,24},{8,16},{16,8},{24,0},{1,25},{9,17},{17,9},{25,1},{2,26},{10... | collective-permute-start | bytes 101384 | tf_op jit(solution)/shard_map/ppermute | solution.py:40
  108.3 4.4 %collective-permute-start.18 = (f32[64,2,66]{0,1,2:T(2,128)S(1)}, f32[64,2,66]{0,1,2:T(2,128)S(1)}, u32[]{:S(2)}, u32[]{:S(2)}) collective-permute-start(f32[64,2,66]{0,1,2:T(2,128)S(1)} %pad_maximum_fusion.4), channel_id=1, source_target_pairs={{0,16},{8,24},{16,0},{24,8},{1,17},{9,25},{17,1},{25,9},{2,18},{10... | collective-permute-start | bytes 101384 | tf_op jit(solution)/shard_map/ppermute | solution.py:40
  108.7 4.3 %collective-permute-start.17 = (f32[64,2,66]{0,1,2:T(2,128)S(1)}, f32[64,2,66]{0,1,2:T(2,128)S(1)}, u32[]{:S(2)}, u32[]{:S(2)}) collective-permute-start(f32[64,2,66]{0,1,2:T(2,128)S(1)} %pad_maximum_fusion.4), channel_id=1, source_target_pairs={{0,8},{8,0},{16,24},{24,16},{1,9},{9,1},{17,25},{25,17},{2,10},{10... | collective-permute-start | bytes 101384 | tf_op jit(solution)/shard_map/ppermute | solution.py:40
  113.5 1.3 collective-permute-start.20
  114.9 6.2 %collective-permute-start.23 = (bf16[64,384]{1,0:T(8,128)(2,1)S(1)}, bf16[64,384]{1,0:T(8,128)(2,1)S(1)}, u32[]{:S(2)}, u32[]{:S(2)}) collective-permute-start(bf16[64,384]{1,0:T(8,128)(2,1)S(1)} %add_convert_fusion.1), channel_id=1, source_target_pairs={{0,6},{1,7},{2,4},{3,5},{4,2},{5,3},{6,0},{7,1},{8,14},{9,15},{10,... | collective-permute-start | bytes 147464 | tf_op jit(solution)/shard_map/ppermute | solution.py:40
  117.5 5.2 %collective-permute-start.22 = (bf16[64,384]{1,0:T(8,128)(2,1)S(1)}, bf16[64,384]{1,0:T(8,128)(2,1)S(1)}, u32[]{:S(2)}, u32[]{:S(2)}) collective-permute-start(bf16[64,384]{1,0:T(8,128)(2,1)S(1)} %add_convert_fusion.1), channel_id=1, source_target_pairs={{0,4},{1,5},{2,6},{3,7},{4,0},{5,1},{6,2},{7,3},{8,12},{9,13},{10,... | collective-permute-start | bytes 147464 | tf_op jit(solution)/shard_map/ppermute | solution.py:40
  117.5 5.2 %collective-permute-start.21 = (bf16[64,384]{1,0:T(8,128)(2,1)S(1)}, bf16[64,384]{1,0:T(8,128)(2,1)S(1)}, u32[]{:S(2)}, u32[]{:S(2)}) collective-permute-start(bf16[64,384]{1,0:T(8,128)(2,1)S(1)} %add_convert_fusion.1), channel_id=1, source_target_pairs={{0,2},{1,3},{2,0},{3,1},{4,6},{5,7},{6,4},{7,5},{8,10},{9,11},{10,... | collective-permute-start | bytes 147464 | tf_op jit(solution)/shard_map/ppermute | solution.py:40
  134.9 1.3 collective-permute-start.24
  136.2 6.1 %collective-permute-start.27 = (bf16[64,384]{1,0:T(8,128)(2,1)S(1)}, bf16[64,384]{1,0:T(8,128)(2,1)S(1)}, u32[]{:S(2)}, u32[]{:S(2)}) collective-permute-start(bf16[64,384]{1,0:T(8,128)(2,1)S(1)} %add_convert_fusion), channel_id=1, source_target_pairs={{0,6},{1,7},{2,4},{3,5},{4,2},{5,3},{6,0},{7,1},{8,14},{9,15},{10,... | collective-permute-start | bytes 147464 | tf_op jit(solution)/shard_map/ppermute | solution.py:40
  138.7 5.7 %collective-permute-start.26 = (bf16[64,384]{1,0:T(8,128)(2,1)S(1)}, bf16[64,384]{1,0:T(8,128)(2,1)S(1)}, u32[]{:S(2)}, u32[]{:S(2)}) collective-permute-start(bf16[64,384]{1,0:T(8,128)(2,1)S(1)} %add_convert_fusion), channel_id=1, source_target_pairs={{0,4},{1,5},{2,6},{3,7},{4,0},{5,1},{6,2},{7,3},{8,12},{9,13},{10,... | collective-permute-start | bytes 147464 | tf_op jit(solution)/shard_map/ppermute | solution.py:40
  139.1 5.2 %collective-permute-start.25 = (bf16[64,384]{1,0:T(8,128)(2,1)S(1)}, bf16[64,384]{1,0:T(8,128)(2,1)S(1)}, u32[]{:S(2)}, u32[]{:S(2)}) collective-permute-start(bf16[64,384]{1,0:T(8,128)(2,1)S(1)} %add_convert_fusion), channel_id=1, source_target_pairs={{0,2},{1,3},{2,0},{3,1},{4,6},{5,7},{6,4},{7,5},{8,10},{9,11},{10,... | collective-permute-start | bytes 147464 | tf_op jit(solution)/shard_map/ppermute | solution.py:40
  163.3 18.6 %copy-start.7 = (f32[64]{0:T(128)}, f32[64]{0:T(128)S(1)}, u32[]{:S(2)}) copy-start(f32[64]{0:T(128)S(1)} %get-tuple-element.8) | copy-start | bytes 772
  171.5 6.3 %collective-permute-start.34 = (f32[64]{0:T(128)S(1)}, f32[64]{0:T(128)S(1)}, u32[]{:S(2)}, u32[]{:S(2)}) collective-permute-start(f32[64]{0:T(128)S(1)} %pmax.7), channel_id=1, source_target_pairs={{0,7},{1,6},{2,5},{3,4},{4,3},{5,2},{6,1},{7,0},{8,15},{9,14},{10,... | collective-permute-start | bytes 776 | tf_op jit(solution)/shard_map/ppermute | solution.py:61
  171.5 7.1 %collective-permute-start.33 = (f32[64]{0:T(128)S(1)}, f32[64]{0:T(128)S(1)}, u32[]{:S(2)}, u32[]{:S(2)}) collective-permute-start(f32[64]{0:T(128)S(1)} %pmax.7), channel_id=1, source_target_pairs={{0,6},{1,7},{2,4},{3,5},{4,2},{5,3},{6,0},{7,1},{8,14},{9,15},{10,... | collective-permute-start | bytes 776 | tf_op jit(solution)/shard_map/ppermute | solution.py:61
  174.3 6.0 %collective-permute-start.32 = (f32[64]{0:T(128)S(1)}, f32[64]{0:T(128)S(1)}, u32[]{:S(2)}, u32[]{:S(2)}) collective-permute-start(f32[64]{0:T(128)S(1)} %pmax.7), channel_id=1, source_target_pairs={{0,5},{1,4},{2,7},{3,6},{4,1},{5,0},{6,3},{7,2},{8,13},{9,12},{10,... | collective-permute-start | bytes 776 | tf_op jit(solution)/shard_map/ppermute | solution.py:61
  174.3 6.0 %collective-permute-start.31 = (f32[64]{0:T(128)S(1)}, f32[64]{0:T(128)S(1)}, u32[]{:S(2)}, u32[]{:S(2)}) collective-permute-start(f32[64]{0:T(128)S(1)} %pmax.7), channel_id=1, source_target_pairs={{0,4},{1,5},{2,6},{3,7},{4,0},{5,1},{6,2},{7,3},{8,12},{9,13},{10,... | collective-permute-start | bytes 776 | tf_op jit(solution)/shard_map/ppermute | solution.py:61
  177.7 3.0 %collective-permute-start.30 = (f32[64]{0:T(128)S(1)}, f32[64]{0:T(128)S(1)}, u32[]{:S(2)}, u32[]{:S(2)}) collective-permute-start(f32[64]{0:T(128)S(1)} %pmax.7), channel_id=1, source_target_pairs={{0,3},{1,2},{2,1},{3,0},{4,7},{5,6},{6,5},{7,4},{8,11},{9,10},{10,... | collective-permute-start | bytes 776 | tf_op jit(solution)/shard_map/ppermute | solution.py:61
  177.8 3.6 %collective-permute-start.29 = (f32[64]{0:T(128)S(1)}, f32[64]{0:T(128)S(1)}, u32[]{:S(2)}, u32[]{:S(2)}) collective-permute-start(f32[64]{0:T(128)S(1)} %pmax.7), channel_id=1, source_target_pairs={{0,2},{1,3},{2,0},{3,1},{4,6},{5,7},{6,4},{7,5},{8,10},{9,11},{10,... | collective-permute-start | bytes 776 | tf_op jit(solution)/shard_map/ppermute | solution.py:61
  178.7 2.7 %collective-permute-start.28 = (f32[64]{0:T(128)S(1)}, f32[64]{0:T(128)S(1)}, u32[]{:S(2)}, u32[]{:S(2)}) collective-permute-start(f32[64]{0:T(128)S(1)} %pmax.7), channel_id=1, source_target_pairs={{0,1},{1,0},{2,3},{3,2},{4,5},{5,4},{6,7},{7,6},{8,9},{9,8},{10,11... | collective-permute-start | bytes 776 | tf_op jit(solution)/shard_map/ppermute | solution.py:61

commit v6 on v5

--- a/solution.py
+++ b/solution.py
@@ -47,6 +47,13 @@
     count = lax.axis_size(axis)
     parts = [pair] + [exchange(pair, axis, k) for k in range(2, count, 2)]
     return butterfly([part.astype(jnp.float32) for part in parts], jnp.add)
+
+
+def core_first_max(value, axis):
+    pair = jnp.maximum(value, exchange(value, axis, 1))
+    count = lax.axis_size(axis)
+    parts = [pair] + [exchange(pair, axis, k) for k in range(2, count, 2)]
+    return butterfly(parts, jnp.maximum)
 
 
 def split_pair(value):
@@ -245,7 +252,7 @@
     rms_value = jnp.sqrt(total_squares / width + EPSILON)
     final_hidden = (stream / rms_value[:, None] * final_gain[None, :]).astype(jnp.bfloat16)
     local_top = jnp.max(top_part, axis=1) / rms_value
-    top_logits = xor_max(lax.pmax(local_top, "gx"), "gy")
+    top_logits = core_first_max(xor_max(local_top, "gx"), "gy")
     return (final_hidden, rms_value, top_logits)
 
 

time: 182 us -> 178 us (0.978)
  blocking collectives: 44.7 us -> 36.5 us
  waiting for transfers between devices: 31.2 us -> 35.5 us
    pmax x1 -> x0, blocking collectives: 8.21 us -> none  [local(): top_logits = xor_max(lax.pmax(local_top, 'gx'), 'gy')]
    ppermute x7 -> x3, starting transfers between devices: 8.09 us -> 3.55 us  [xor_max(): lax.ppermute(value, axis, [(i, i ^ k) for i in range(count)])]
    ppermute x22 -> x26, starting transfers between devices: 25.2 us -> 29.6 us  [exchange(): return lax.ppermute(value, axis, [(i, i ^ partner) for i in range(count)])]
    ppermute x22 -> x26, waiting for transfers between devices: 25.7 us -> 28.8 us  [exchange(): return lax.ppermute(value, axis, [(i, i ^ partner) for i in range(count)])]
  transfers between devices with their start and end apart: 35 -> 35, of which waited for: 23 -> 26; matrix products, arithmetic and copies ran while one was open for 11% -> 11% of each run, Pallas kernels for 0% -> 0%
where the time goes in v6:
time: 178 us
  starting transfers between devices  41.3 us (23%)
  blocking collectives  36.5 us (21%)
  waiting for transfers between devices  35.5 us (20%)
  matrix products  30.8 us (17%)
  local copies, waits for them, and re-layouts  24.7 us (14%)
  other arithmetic  7.7 us (4%)
    ppermute x26, starting transfers between devices, exchange(): return lax.ppermute(value, axis, [(i, i ^ partner) for i in range(count)])  29.6 us
    ppermute x26, waiting for transfers between devices, exchange(): return lax.ppermute(value, axis, [(i, i ^ partner) for i in range(count)])  28.8 us
    all_gather x2, blocking collectives, gather_sum(): return jnp.sum(lax.all_gather(value, axis).astype(jnp.float32), axis=0)  21.8 us
    slice x1, local copies, waits for them, and re-layouts, local(): kv_cache[layer_id]  14.9 us
    all_to_all x1, blocking collectives, local(): pieces = lax.all_to_all(pieces, 'gx', 1, 1, tiled=True).astype(jnp.float32)  14.7 us
    dot_general x2, matrix products, local_attention(): jnp.einsum('pthc,pkhc->pkt', kv_layer, query_block, preferred_element_typ...  11.7 us
    dot_general x2, matrix products, local_attention(): jnp.einsum('pkt,pthc->pkhc', weights.astype(jnp.bfloat16), kv_layer, pref...  9.37 us
    ppermute x6, starting transfers between devices, xor_sum(): lax.ppermute(value, axis, [(i, i ^ k) for i in range(count)])  8.13 us
  transfers between devices with their start and end apart: 35, of which 26 were waited for; matrix products, arithmetic and copies ran while one was open for 11% of the time, Pallas kernels for 0%

profile of v6, /device:TPU:0, one launch (start us, length us, event | category | flops | bytes accessed | tf_op | source)
XLA Modules:
  0.0 177.8 jit_solution(5061590026565691740)
XLA Ops:
  3.3 1.3 convolution_convert_fusion.2
  4.6 3.0 %collective-permute-start.1 = (bf16[64,388]{0,1:T(8,128)(2,1)S(1)}, bf16[64,388]{0,1:T(8,128)(2,1)S(1)}, u32[]{:S(2)}, u32[]{:S(2)}) collective-permute-start(bf16[64,388]{0,1:T(8,128)(2,1)S(1)} %pad_maximum_fusion.1), channel_id=1, source_target_pairs={{0,16},{8,24},{16,0},{24,8},{1,17},{9,25},{17,1},{25,9},{2,18},{10... | collective-permute-start | bytes 149000 | tf_op jit(solution)/shard_map/ppermute | solution.py:23
  7.7 1.5 collective-permute-start
  12.6 14.9 %fusion.168 = (bf16[1,128,128,2,128]{4,3,2,1,0:T(2,128)(2,1)}, bf16[1,128,128,2,128]{4,3,2,1,0:T(2,128)(2,1)}) fusion(bf16[2,128,128,2,128]{4,3,2,1,0:T(2,128)(2,1)} %param.28), kind=kLoop, calls=%fused_computation.319 | loop fusion | bytes 33554432 | tf_op jit(solution)/shard_map/slice | solution.py:194
  29.6 5.9 %fusion.175 = (f32[128,2]{1,0:T(8,128)S(1)}, f32[128,2,128]{2,1,0:T(2,128)S(1)}) fusion(f32[128,2]{1,0:T(8,128)S(1)} %gather_fusion.1, f32[2,128,2,128]{3,2,1,0:T(2,128)S(1)} %copy-done.10, bf16[1,128,128,2,128]{4,3,2,1,0:T(2,128)(2,1)} %get-tuple-element.26, bf16[128,2,128]{2,1,0:T(2,128)(2,1)S(1)} %concatenate.33, ...), kind=kOutput, calls=%fused_computation.326 | convolution fusion | flops 17202944 | bytes 8734728 | tf_op jit(solution)/shard_map/pthc,pkhc->pkt/dot_general | solution.py:106
  36.4 4.7 %fusion = f32[128,2,2,128]{3,1,2,0:T(2,128)S(1)} fusion(bf16[1,128,128,2,128]{4,3,2,1,0:T(2,128)(2,1)} %get-tuple-element.26, f32[128,2,128]{2,1,0:T(2,128)S(1)} %get-tuple-element.59, pred[128,128]{1,0:T(8,128)(4,1)S(1)} %fusion.93, f32[128,2]{1,0:T(8,128)S(1)} %gather_fusion.2), kind=kOutput, calls=%fused_computation.8 | convolution fusion | flops 16875520 | bytes 8799232 | tf_op jit(solution)/shard_map/pkt,pthc->pkhc/dot_general | solution.py:116
  42.4 2.9 %collective-permute-start.5 = (f32[64,2,66]{0,1,2:T(2,128)S(1)}, f32[64,2,66]{0,1,2:T(2,128)S(1)}, u32[]{:S(2)}, u32[]{:S(2)}) collective-permute-start(f32[64,2,66]{0,1,2:T(2,128)S(1)} %pad_maximum_fusion.3), channel_id=1, source_target_pairs={{0,24},{8,16},{16,8},{24,0},{1,25},{9,17},{17,9},{25,1},{2,26},{10... | collective-permute-start | bytes 101384 | tf_op jit(solution)/shard_map/ppermute | solution.py:40
  46.3 1.5 collective-permute-done.5
  47.8 1.9 %collective-permute-done.4 = f32[64,2,66]{0,1,2:T(2,128)S(1)} collective-permute-done((f32[64,2,66]{0,1,2:T(2,128)S(1)}, f32[64,2,66]{0,1,2:T(2,128)S(1)}, u32[]{:S(2)}, u32[]{:S(2)}) %collective-permute-start.4) | collective-permute-done | bytes 33824 | tf_op jit(solution)/shard_map/ppermute | solution.py:40
  50.8 1.2 collective-permute-done.6
  52.1 3.7 %collective-permute-start.9 = (bf16[64,384]{1,0:T(8,128)(2,1)S(1)}, bf16[64,384]{1,0:T(8,128)(2,1)S(1)}, u32[]{:S(2)}, u32[]{:S(2)}) collective-permute-start(bf16[64,384]{1,0:T(8,128)(2,1)S(1)} %add_convert_fusion.3), channel_id=1, source_target_pairs={{0,6},{1,7},{2,4},{3,5},{4,2},{5,3},{6,0},{7,1},{8,14},{9,15},{10,... | collective-permute-start | bytes 147464 | tf_op jit(solution)/shard_map/ppermute | solution.py:40
  56.5 1.5 collective-permute-done.9
  58.1 2.6 %collective-permute-done.8 = bf16[64,384]{1,0:T(8,128)(2,1)S(1)} collective-permute-done((bf16[64,384]{1,0:T(8,128)(2,1)S(1)}, bf16[64,384]{1,0:T(8,128)(2,1)S(1)}, u32[]{:S(2)}, u32[]{:S(2)}) %collective-permute-start.8) | collective-permute-done | bytes 49184 | tf_op jit(solution)/shard_map/ppermute | solution.py:40
  61.6 11.0 %all-gather = bf16[256,1026]{1,0:T(8,128)(2,1)S(1)} all-gather(bf16[64,1026]{1,0:T(8,128)(2,1)S(1)} %concatenate.35), channel_id=2, replica_groups=mesh['gx'=4,'gy'=8] {'gx'}, dimensions={0}, use_global_device_ids=true | all-gather | bytes 656640 | tf_op jit(solution)/shard_map/all_gather | solution.py:17
  72.9 1.3 convolution_convert_fusion.10
  74.3 1.2 collective-permute-done.10
  75.5 2.5 %collective-permute-start.13 = (bf16[64,384]{1,0:T(8,128)(2,1)S(1)}, bf16[64,384]{1,0:T(8,128)(2,1)S(1)}, u32[]{:S(2)}, u32[]{:S(2)}) collective-permute-start(bf16[64,384]{1,0:T(8,128)(2,1)S(1)} %add_convert_fusion.2), channel_id=1, source_target_pairs={{0,6},{1,7},{2,4},{3,5},{4,2},{5,3},{6,0},{7,1},{8,14},{9,15},{10,... | collective-permute-start | bytes 147464 | tf_op jit(solution)/shard_map/ppermute | solution.py:40
  78.2 1.8 collective-permute-start.11
  80.0 1.7 collective-permute-done.13
  81.7 1.9 %collective-permute-done.12 = bf16[64,384]{1,0:T(8,128)(2,1)S(1)} collective-permute-done((bf16[64,384]{1,0:T(8,128)(2,1)S(1)}, bf16[64,384]{1,0:T(8,128)(2,1)S(1)}, u32[]{:S(2)}, u32[]{:S(2)}) %collective-permute-start.12) | collective-permute-done | bytes 49184 | tf_op jit(solution)/shard_map/ppermute | solution.py:40
  84.3 2.0 %collective-permute-start.14 = (bf16[64,388]{0,1:T(8,128)(2,1)S(1)}, bf16[64,388]{0,1:T(8,128)(2,1)S(1)}, u32[]{:S(2)}, u32[]{:S(2)}) collective-permute-start(bf16[64,388]{0,1:T(8,128)(2,1)S(1)} %pad_maximum_fusion.2), channel_id=1, source_target_pairs={{0,8},{8,0},{16,24},{24,16},{1,9},{9,1},{17,25},{25,17},{2,10},{10... | collective-permute-start | bytes 149000 | tf_op jit(solution)/shard_map/ppermute | solution.py:23
  86.3 1.5 collective-permute-start.16
  87.8 1.1 collective-permute-done.15
  90.0 2.2 %collective-permute-done.16 = bf16[64,388]{0,1:T(8,128)(2,1)S(1)} collective-permute-done((bf16[64,388]{0,1:T(8,128)(2,1)S(1)}, bf16[64,388]{0,1:T(8,128)(2,1)S(1)}, u32[]{:S(2)}, u32[]{:S(2)}) %collective-permute-start.16) | collective-permute-done | bytes 49696 | tf_op jit(solution)/shard_map/ppermute | solution.py:23
  94.1 5.8 %fusion.176 = (f32[128,2]{1,0:T(8,128)S(1)}, f32[128,2,128]{2,1,0:T(2,128)S(1)}) fusion(f32[128,2]{1,0:T(8,128)S(1)} %gather_fusion.4, f32[2,128,2,128]{3,2,1,0:T(2,128)S(1)} %copy-done.10, bf16[1,128,128,2,128]{4,3,2,1,0:T(2,128)(2,1)} %get-tuple-element.25, bf16[128,2,128]{2,1,0:T(2,128)(2,1)S(1)} %concatenate.37, ...), kind=kOutput, calls=%fused_computation.327 | convolution fusion | flops 17202944 | bytes 8734728 | tf_op jit(solution)/shard_map/pthc,pkhc->pkt/dot_general | solution.py:106
  100.9 4.7 %fusion.2 = f32[128,2,2,128]{3,1,2,0:T(2,128)S(1)} fusion(bf16[1,128,128,2,128]{4,3,2,1,0:T(2,128)(2,1)} %get-tuple-element.25, f32[128,2,128]{2,1,0:T(2,128)S(1)} %get-tuple-element.61, pred[128,128]{1,0:T(8,128)(4,1)S(1)} %fusion.93, f32[128,2]{1,0:T(8,128)S(1)} %gather_fusion.5), kind=kOutput, calls=%fused_computation.10 | convolution fusion | flops 16875520 | bytes 8799232 | tf_op jit(solution)/shard_map/pkt,pthc->pkhc/dot_general | solution.py:116
  106.8 1.5 collective-permute-start.19
  108.7 1.7 collective-permute-start.17
  110.7 1.4 collective-permute-done.19
  113.6 1.2 collective-permute-done.20
  114.9 2.6 %collective-permute-start.23 = (bf16[64,384]{1,0:T(8,128)(2,1)S(1)}, bf16[64,384]{1,0:T(8,128)(2,1)S(1)}, u32[]{:S(2)}, u32[]{:S(2)}) collective-permute-start(bf16[64,384]{1,0:T(8,128)(2,1)S(1)} %add_convert_fusion.1), channel_id=1, source_target_pairs={{0,6},{1,7},{2,4},{3,5},{4,2},{5,3},{6,0},{7,1},{8,14},{9,15},{10,... | collective-permute-start | bytes 147464 | tf_op jit(solution)/shard_map/ppermute | solution.py:40
  117.5 1.8 %collective-permute-start.21 = (bf16[64,384]{1,0:T(8,128)(2,1)S(1)}, bf16[64,384]{1,0:T(8,128)(2,1)S(1)}, u32[]{:S(2)}, u32[]{:S(2)}) collective-permute-start(bf16[64,384]{1,0:T(8,128)(2,1)S(1)} %add_convert_fusion.1), channel_id=1, source_target_pairs={{0,2},{1,3},{2,0},{3,1},{4,6},{5,7},{6,4},{7,5},{8,10},{9,11},{10,... | collective-permute-start | bytes 147464 | tf_op jit(solution)/shard_map/ppermute | solution.py:40
  119.3 1.8 collective-permute-done.23
  121.1 1.6 collective-permute-done.22
  123.5 10.8 %all-gather.1 = bf16[256,1026]{1,0:T(8,128)(2,1)S(1)} all-gather(bf16[64,1026]{1,0:T(8,128)(2,1)S(1)} %concatenate.39), channel_id=3, replica_groups=mesh['gx'=4,'gy'=8] {'gx'}, dimensions={0}, use_global_device_ids=true | all-gather | bytes 656640 | tf_op jit(solution)/shard_map/all_gather | solution.py:17
  135.0 1.2 collective-permute-done.24
  136.3 2.4 %collective-permute-start.27 = (bf16[64,384]{1,0:T(8,128)(2,1)S(1)}, bf16[64,384]{1,0:T(8,128)(2,1)S(1)}, u32[]{:S(2)}, u32[]{:S(2)}) collective-permute-start(bf16[64,384]{1,0:T(8,128)(2,1)S(1)} %add_convert_fusion), channel_id=1, source_target_pairs={{0,6},{1,7},{2,4},{3,5},{4,2},{5,3},{6,0},{7,1},{8,14},{9,15},{10,... | collective-permute-start | bytes 147464 | tf_op jit(solution)/shard_map/ppermute | solution.py:40
  139.1 1.6 collective-permute-start.25
  140.7 1.7 collective-permute-done.27
  142.4 1.9 %collective-permute-done.26 = bf16[64,384]{1,0:T(8,128)(2,1)S(1)} collective-permute-done((bf16[64,384]{1,0:T(8,128)(2,1)S(1)}, bf16[64,384]{1,0:T(8,128)(2,1)S(1)}, u32[]{:S(2)}, u32[]{:S(2)}) %collective-permute-start.26) | collective-permute-done | bytes 49184 | tf_op jit(solution)/shard_map/ppermute | solution.py:40
  144.6 3.3 %convolution_convert_fusion = bf16[64,6144]{1,0:T(8,128)(2,1)S(1)} fusion(bf16[384,6144]{1,0:T(8,128)(2,1)} %param.27, f32[64,384]{1,0:T(8,128)S(1)} %get-tuple-element.10, f32[384]{0:T(512)S(1)} %copy-done.5), kind=kOutput, calls=%fused_computation.12 | convolution fusion | flops 302432256 | bytes 5604864 | tf_op jit(solution)/shard_map/dot_general | solution.py:238
  148.1 14.7 %all_to_all.5 = bf16[64,4,1538]{2,0,1:T(8,128)(2,1)S(1)} all-to-all(bf16[64,4,1538]{2,0,1:T(8,128)(2,1)S(1)} %pad_maximum_fusion), channel_id=1, replica_groups=mesh['gx'=4,'gy'=8] {'gx'}, dimensions={1} | all-to-all | bytes 1574912 | tf_op jit(solution)/shard_map/all_to_all | solution.py:249
  164.1 1.5 collective-permute-start.29
  165.5 1.3 collective-permute-start.28
  167.8 1.3 collective-permute-done.28
  170.2 2.7 %collective-permute-start.34 = (f32[64]{0:T(128)S(1)}, f32[64]{0:T(128)S(1)}, u32[]{:S(2)}, u32[]{:S(2)}) collective-permute-start(f32[64]{0:T(128)S(1)} %max.146), channel_id=1, source_target_pairs={{0,6},{1,7},{2,4},{3,5},{4,2},{5,3},{6,0},{7,1},{8,14},{9,15},{10,... | collective-permute-start | bytes 776 | tf_op jit(solution)/shard_map/ppermute | solution.py:40
  172.9 1.7 collective-permute-start.32
  175.6 1.8 collective-permute-done.33
  (198 shorter events, 29.8 us)
Async XLA Ops:
  4.6 23.0 %collective-permute-start.1 = (bf16[64,388]{0,1:T(8,128)(2,1)S(1)}, bf16[64,388]{0,1:T(8,128)(2,1)S(1)}, u32[]{:S(2)}, u32[]{:S(2)}) collective-permute-start(bf16[64,388]{0,1:T(8,128)(2,1)S(1)} %pad_maximum_fusion.1), channel_id=1, source_target_pairs={{0,16},{8,24},{16,0},{24,8},{1,17},{9,25},{17,1},{25,9},{2,18},{10... | collective-permute-start | bytes 149000 | tf_op jit(solution)/shard_map/ppermute | solution.py:23
  7.7 20.0 %collective-permute-start = (bf16[64,388]{0,1:T(8,128)(2,1)S(1)}, bf16[64,388]{0,1:T(8,128)(2,1)S(1)}, u32[]{:S(2)}, u32[]{:S(2)}) collective-permute-start(bf16[64,388]{0,1:T(8,128)(2,1)S(1)} %pad_maximum_fusion.1), channel_id=1, source_target_pairs={{0,8},{8,0},{16,24},{24,16},{1,9},{9,1},{17,25},{25,17},{2,10},{10... | collective-permute-start | bytes 149000 | tf_op jit(solution)/shard_map/ppermute | solution.py:23
  9.1 18.5 %collective-permute-start.2 = (bf16[64,388]{0,1:T(8,128)(2,1)S(1)}, bf16[64,388]{0,1:T(8,128)(2,1)S(1)}, u32[]{:S(2)}, u32[]{:S(2)}) collective-permute-start(bf16[64,388]{0,1:T(8,128)(2,1)S(1)} %pad_maximum_fusion.1), channel_id=1, source_target_pairs={{0,24},{8,16},{16,8},{24,0},{1,25},{9,17},{17,9},{25,1},{2,26},{10... | collective-permute-start | bytes 149000 | tf_op jit(solution)/shard_map/ppermute | solution.py:23
  12.5 17.0 %copy-start.10 = (f32[2,128,2,128]{3,2,1,0:T(2,128)S(1)}, f32[2,128,2,128]{3,2,1,0:T(2,128)}, u32[]{:S(2)}) copy-start(f32[2,128,2,128]{3,2,1,0:T(2,128)} %param.29) | copy-start | bytes 786436
  29.5 21.0 %copy-start.4 = (bf16[2,128,384]{2,1,0:T(8,128)(2,1)S(1)}, bf16[2,128,384]{2,1,0:T(8,128)(2,1)}, u32[]{:S(2)}) copy-start(bf16[2,128,384]{2,1,0:T(8,128)(2,1)} %param.23) | copy-start | bytes 589828
  29.6 27.0 %copy-start.6 = (f32[2,384]{1,0:T(2,128)S(1)}, f32[2,384]{1,0:T(2,128)}, u32[]{:S(2)}) copy-start(f32[2,384]{1,0:T(2,128)} %param.18) | copy-start | bytes 9220
  29.6 31.1 %copy-start.3 = (bf16[64,384]{1,0:T(8,128)(2,1)S(1)}, bf16[64,384]{1,0:T(8,128)(2,1)}, u32[]{:S(2)}) copy-start(bf16[64,384]{1,0:T(8,128)(2,1)} %param.16) | copy-start | bytes 147460
  35.5 25.6 %copy-start = (bf16[2,384,512]{2,1,0:T(8,128)(2,1)S(1)}, bf16[2,384,512]{2,1,0:T(8,128)(2,1)}, u32[]{:S(2)}) copy-start(bf16[2,384,512]{2,1,0:T(8,128)(2,1)} %param.25) | copy-start | bytes 2359300
  35.5 25.8 %copy-start.1 = (bf16[2,384,512]{2,1,0:T(8,128)(2,1)S(1)}, bf16[2,384,512]{2,1,0:T(8,128)(2,1)}, u32[]{:S(2)}) copy-start(bf16[2,384,512]{2,1,0:T(8,128)(2,1)} %param.24) | copy-start | bytes 2359300
  36.4 47.3 %copy-start.8 = (bf16[2,384,2]{1,2,0:T(2,128)(2,1)S(1)}, bf16[2,384,2]{1,2,0:T(2,128)(2,1)}, u32[]{:S(2)}) copy-start(bf16[2,384,2]{1,2,0:T(2,128)(2,1)} %param.21) | copy-start | bytes 9220
  36.4 47.5 %copy-start.2 = (bf16[2,384,384]{2,1,0:T(8,128)(2,1)S(1)}, bf16[2,384,384]{2,1,0:T(8,128)(2,1)}, u32[]{:S(2)}) copy-start(bf16[2,384,384]{2,1,0:T(8,128)(2,1)} %param.20) | copy-start | bytes 1769476
  42.4 5.4 %collective-permute-start.5 = (f32[64,2,66]{0,1,2:T(2,128)S(1)}, f32[64,2,66]{0,1,2:T(2,128)S(1)}, u32[]{:S(2)}, u32[]{:S(2)}) collective-permute-start(f32[64,2,66]{0,1,2:T(2,128)S(1)} %pad_maximum_fusion.3), channel_id=1, source_target_pairs={{0,24},{8,16},{16,8},{24,0},{1,25},{9,17},{17,9},{25,1},{2,26},{10... | collective-permute-start | bytes 101384 | tf_op jit(solution)/shard_map/ppermute | solution.py:40
  45.4 4.3 %collective-permute-start.4 = (f32[64,2,66]{0,1,2:T(2,128)S(1)}, f32[64,2,66]{0,1,2:T(2,128)S(1)}, u32[]{:S(2)}, u32[]{:S(2)}) collective-permute-start(f32[64,2,66]{0,1,2:T(2,128)S(1)} %pad_maximum_fusion.3), channel_id=1, source_target_pairs={{0,16},{8,24},{16,0},{24,8},{1,17},{9,25},{17,1},{25,9},{2,18},{10... | collective-permute-start | bytes 101384 | tf_op jit(solution)/shard_map/ppermute | solution.py:40
  45.9 4.3 %collective-permute-start.3 = (f32[64,2,66]{0,1,2:T(2,128)S(1)}, f32[64,2,66]{0,1,2:T(2,128)S(1)}, u32[]{:S(2)}, u32[]{:S(2)}) collective-permute-start(f32[64,2,66]{0,1,2:T(2,128)S(1)} %pad_maximum_fusion.3), channel_id=1, source_target_pairs={{0,8},{8,0},{16,24},{24,16},{1,9},{9,1},{17,25},{25,17},{2,10},{10... | collective-permute-start | bytes 101384 | tf_op jit(solution)/shard_map/ppermute | solution.py:40
  50.7 1.3 collective-permute-start.6
  52.1 6.0 %collective-permute-start.9 = (bf16[64,384]{1,0:T(8,128)(2,1)S(1)}, bf16[64,384]{1,0:T(8,128)(2,1)S(1)}, u32[]{:S(2)}, u32[]{:S(2)}) collective-permute-start(bf16[64,384]{1,0:T(8,128)(2,1)S(1)} %add_convert_fusion.3), channel_id=1, source_target_pairs={{0,6},{1,7},{2,4},{3,5},{4,2},{5,3},{6,0},{7,1},{8,14},{9,15},{10,... | collective-permute-start | bytes 147464 | tf_op jit(solution)/shard_map/ppermute | solution.py:40
  55.7 5.0 %collective-permute-start.8 = (bf16[64,384]{1,0:T(8,128)(2,1)S(1)}, bf16[64,384]{1,0:T(8,128)(2,1)S(1)}, u32[]{:S(2)}, u32[]{:S(2)}) collective-permute-start(bf16[64,384]{1,0:T(8,128)(2,1)S(1)} %add_convert_fusion.3), channel_id=1, source_target_pairs={{0,4},{1,5},{2,6},{3,7},{4,0},{5,1},{6,2},{7,3},{8,12},{9,13},{10,... | collective-permute-start | bytes 147464 | tf_op jit(solution)/shard_map/ppermute | solution.py:40
  55.7 5.0 %collective-permute-start.7 = (bf16[64,384]{1,0:T(8,128)(2,1)S(1)}, bf16[64,384]{1,0:T(8,128)(2,1)S(1)}, u32[]{:S(2)}, u32[]{:S(2)}) collective-permute-start(bf16[64,384]{1,0:T(8,128)(2,1)S(1)} %add_convert_fusion.3), channel_id=1, source_target_pairs={{0,2},{1,3},{2,0},{3,1},{4,6},{5,7},{6,4},{7,5},{8,10},{9,11},{10,... | collective-permute-start | bytes 147464 | tf_op jit(solution)/shard_map/ppermute | solution.py:40
  74.2 1.3 collective-permute-start.10
  75.5 6.2 %collective-permute-start.13 = (bf16[64,384]{1,0:T(8,128)(2,1)S(1)}, bf16[64,384]{1,0:T(8,128)(2,1)S(1)}, u32[]{:S(2)}, u32[]{:S(2)}) collective-permute-start(bf16[64,384]{1,0:T(8,128)(2,1)S(1)} %add_convert_fusion.2), channel_id=1, source_target_pairs={{0,6},{1,7},{2,4},{3,5},{4,2},{5,3},{6,0},{7,1},{8,14},{9,15},{10,... | collective-permute-start | bytes 147464 | tf_op jit(solution)/shard_map/ppermute | solution.py:40
  78.0 5.5 %collective-permute-start.12 = (bf16[64,384]{1,0:T(8,128)(2,1)S(1)}, bf16[64,384]{1,0:T(8,128)(2,1)S(1)}, u32[]{:S(2)}, u32[]{:S(2)}) collective-permute-start(bf16[64,384]{1,0:T(8,128)(2,1)S(1)} %add_convert_fusion.2), channel_id=1, source_target_pairs={{0,4},{1,5},{2,6},{3,7},{4,0},{5,1},{6,2},{7,3},{8,12},{9,13},{10,... | collective-permute-start | bytes 147464 | tf_op jit(solution)/shard_map/ppermute | solution.py:40
  78.2 5.4 %collective-permute-start.11 = (bf16[64,384]{1,0:T(8,128)(2,1)S(1)}, bf16[64,384]{1,0:T(8,128)(2,1)S(1)}, u32[]{:S(2)}, u32[]{:S(2)}) collective-permute-start(bf16[64,384]{1,0:T(8,128)(2,1)S(1)} %add_convert_fusion.2), channel_id=1, source_target_pairs={{0,2},{1,3},{2,0},{3,1},{4,6},{5,7},{6,4},{7,5},{8,10},{9,11},{10,... | collective-permute-start | bytes 147464 | tf_op jit(solution)/shard_map/ppermute | solution.py:40
  84.2 4.7 %collective-permute-start.15 = (bf16[64,388]{0,1:T(8,128)(2,1)S(1)}, bf16[64,388]{0,1:T(8,128)(2,1)S(1)}, u32[]{:S(2)}, u32[]{:S(2)}) collective-permute-start(bf16[64,388]{0,1:T(8,128)(2,1)S(1)} %pad_maximum_fusion.2), channel_id=1, source_target_pairs={{0,16},{8,24},{16,0},{24,8},{1,17},{9,25},{17,1},{25,9},{2,18},{10... | collective-permute-start | bytes 149000 | tf_op jit(solution)/shard_map/ppermute | solution.py:23
  84.3 5.7 %collective-permute-start.14 = (bf16[64,388]{0,1:T(8,128)(2,1)S(1)}, bf16[64,388]{0,1:T(8,128)(2,1)S(1)}, u32[]{:S(2)}, u32[]{:S(2)}) collective-permute-start(bf16[64,388]{0,1:T(8,128)(2,1)S(1)} %pad_maximum_fusion.2), channel_id=1, source_target_pairs={{0,8},{8,0},{16,24},{24,16},{1,9},{9,1},{17,25},{25,17},{2,10},{10... | collective-permute-start | bytes 149000 | tf_op jit(solution)/shard_map/ppermute | solution.py:23
  86.3 5.9 %collective-permute-start.16 = (bf16[64,388]{0,1:T(8,128)(2,1)S(1)}, bf16[64,388]{0,1:T(8,128)(2,1)S(1)}, u32[]{:S(2)}, u32[]{:S(2)}) collective-permute-start(bf16[64,388]{0,1:T(8,128)(2,1)S(1)} %pad_maximum_fusion.2), channel_id=1, source_target_pairs={{0,24},{8,16},{16,8},{24,0},{1,25},{9,17},{17,9},{25,1},{2,26},{10... | collective-permute-start | bytes 149000 | tf_op jit(solution)/shard_map/ppermute | solution.py:23
  99.9 34.7 %copy-start.9 = (bf16[2,512,384]{2,1,0:T(8,128)(2,1)S(1)}, bf16[2,512,384]{2,1,0:T(8,128)(2,1)}, u32[]{:S(2)}) copy-start(bf16[2,512,384]{2,1,0:T(8,128)(2,1)} %param.26) | copy-start | bytes 2359300
  100.9 43.7 %copy-start.5 = (f32[384]{0:T(512)S(1)}, f32[384]{0:T(512)}, u32[]{:S(2)}) copy-start(f32[384]{0:T(512)} %param.19) | copy-start | bytes 4612
  106.8 5.3 %collective-permute-start.19 = (f32[64,2,66]{0,1,2:T(2,128)S(1)}, f32[64,2,66]{0,1,2:T(2,128)S(1)}, u32[]{:S(2)}, u32[]{:S(2)}) collective-permute-start(f32[64,2,66]{0,1,2:T(2,128)S(1)} %pad_maximum_fusion.4), channel_id=1, source_target_pairs={{0,24},{8,16},{16,8},{24,0},{1,25},{9,17},{17,9},{25,1},{2,26},{10... | collective-permute-start | bytes 101384 | tf_op jit(solution)/shard_map/ppermute | solution.py:40
  108.3 4.5 %collective-permute-start.18 = (f32[64,2,66]{0,1,2:T(2,128)S(1)}, f32[64,2,66]{0,1,2:T(2,128)S(1)}, u32[]{:S(2)}, u32[]{:S(2)}) collective-permute-start(f32[64,2,66]{0,1,2:T(2,128)S(1)} %pad_maximum_fusion.4), channel_id=1, source_target_pairs={{0,16},{8,24},{16,0},{24,8},{1,17},{9,25},{17,1},{25,9},{2,18},{10... | collective-permute-start | bytes 101384 | tf_op jit(solution)/shard_map/ppermute | solution.py:40
  108.7 4.3 %collective-permute-start.17 = (f32[64,2,66]{0,1,2:T(2,128)S(1)}, f32[64,2,66]{0,1,2:T(2,128)S(1)}, u32[]{:S(2)}, u32[]{:S(2)}) collective-permute-start(f32[64,2,66]{0,1,2:T(2,128)S(1)} %pad_maximum_fusion.4), channel_id=1, source_target_pairs={{0,8},{8,0},{16,24},{24,16},{1,9},{9,1},{17,25},{25,17},{2,10},{10... | collective-permute-start | bytes 101384 | tf_op jit(solution)/shard_map/ppermute | solution.py:40
  113.6 1.3 collective-permute-start.20
  114.9 6.2 %collective-permute-start.23 = (bf16[64,384]{1,0:T(8,128)(2,1)S(1)}, bf16[64,384]{1,0:T(8,128)(2,1)S(1)}, u32[]{:S(2)}, u32[]{:S(2)}) collective-permute-start(bf16[64,384]{1,0:T(8,128)(2,1)S(1)} %add_convert_fusion.1), channel_id=1, source_target_pairs={{0,6},{1,7},{2,4},{3,5},{4,2},{5,3},{6,0},{7,1},{8,14},{9,15},{10,... | collective-permute-start | bytes 147464 | tf_op jit(solution)/shard_map/ppermute | solution.py:40
  117.5 5.2 %collective-permute-start.22 = (bf16[64,384]{1,0:T(8,128)(2,1)S(1)}, bf16[64,384]{1,0:T(8,128)(2,1)S(1)}, u32[]{:S(2)}, u32[]{:S(2)}) collective-permute-start(bf16[64,384]{1,0:T(8,128)(2,1)S(1)} %add_convert_fusion.1), channel_id=1, source_target_pairs={{0,4},{1,5},{2,6},{3,7},{4,0},{5,1},{6,2},{7,3},{8,12},{9,13},{10,... | collective-permute-start | bytes 147464 | tf_op jit(solution)/shard_map/ppermute | solution.py:40
  117.5 5.2 %collective-permute-start.21 = (bf16[64,384]{1,0:T(8,128)(2,1)S(1)}, bf16[64,384]{1,0:T(8,128)(2,1)S(1)}, u32[]{:S(2)}, u32[]{:S(2)}) collective-permute-start(bf16[64,384]{1,0:T(8,128)(2,1)S(1)} %add_convert_fusion.1), channel_id=1, source_target_pairs={{0,2},{1,3},{2,0},{3,1},{4,6},{5,7},{6,4},{7,5},{8,10},{9,11},{10,... | collective-permute-start | bytes 147464 | tf_op jit(solution)/shard_map/ppermute | solution.py:40
  135.0 1.3 collective-permute-start.24
  136.3 6.1 %collective-permute-start.27 = (bf16[64,384]{1,0:T(8,128)(2,1)S(1)}, bf16[64,384]{1,0:T(8,128)(2,1)S(1)}, u32[]{:S(2)}, u32[]{:S(2)}) collective-permute-start(bf16[64,384]{1,0:T(8,128)(2,1)S(1)} %add_convert_fusion), channel_id=1, source_target_pairs={{0,6},{1,7},{2,4},{3,5},{4,2},{5,3},{6,0},{7,1},{8,14},{9,15},{10,... | collective-permute-start | bytes 147464 | tf_op jit(solution)/shard_map/ppermute | solution.py:40
  138.7 5.7 %collective-permute-start.26 = (bf16[64,384]{1,0:T(8,128)(2,1)S(1)}, bf16[64,384]{1,0:T(8,128)(2,1)S(1)}, u32[]{:S(2)}, u32[]{:S(2)}) collective-permute-start(bf16[64,384]{1,0:T(8,128)(2,1)S(1)} %add_convert_fusion), channel_id=1, source_target_pairs={{0,4},{1,5},{2,6},{3,7},{4,0},{5,1},{6,2},{7,3},{8,12},{9,13},{10,... | collective-permute-start | bytes 147464 | tf_op jit(solution)/shard_map/ppermute | solution.py:40
  139.1 5.2 %collective-permute-start.25 = (bf16[64,384]{1,0:T(8,128)(2,1)S(1)}, bf16[64,384]{1,0:T(8,128)(2,1)S(1)}, u32[]{:S(2)}, u32[]{:S(2)}) collective-permute-start(bf16[64,384]{1,0:T(8,128)(2,1)S(1)} %add_convert_fusion), channel_id=1, source_target_pairs={{0,2},{1,3},{2,0},{3,1},{4,6},{5,7},{6,4},{7,5},{8,10},{9,11},{10,... | collective-permute-start | bytes 147464 | tf_op jit(solution)/shard_map/ppermute | solution.py:40
  163.3 14.6 %copy-start.7 = (f32[64]{0:T(128)}, f32[64]{0:T(128)S(1)}, u32[]{:S(2)}) copy-start(f32[64]{0:T(128)S(1)} %get-tuple-element.8) | copy-start | bytes 772
  163.3 4.5 %collective-permute-start.30 = (f32[64]{0:T(128)S(1)}, f32[64]{0:T(128)S(1)}, u32[]{:S(2)}, u32[]{:S(2)}) collective-permute-start(f32[64]{0:T(128)S(1)} %get-tuple-element.7), channel_id=1, source_target_pairs={{0,24},{8,16},{16,8},{24,0},{1,25},{9,17},{17,9},{25,1},{2,26},{10... | collective-permute-start | bytes 776 | tf_op jit(solution)/shard_map/ppermute | solution.py:68
  164.1 3.7 %collective-permute-start.29 = (f32[64]{0:T(128)S(1)}, f32[64]{0:T(128)S(1)}, u32[]{:S(2)}, u32[]{:S(2)}) collective-permute-start(f32[64]{0:T(128)S(1)} %get-tuple-element.7), channel_id=1, source_target_pairs={{0,16},{8,24},{16,0},{24,8},{1,17},{9,25},{17,1},{25,9},{2,18},{10... | collective-permute-start | bytes 776 | tf_op jit(solution)/shard_map/ppermute | solution.py:68
  165.5 3.5 %collective-permute-start.28 = (f32[64]{0:T(128)S(1)}, f32[64]{0:T(128)S(1)}, u32[]{:S(2)}, u32[]{:S(2)}) collective-permute-start(f32[64]{0:T(128)S(1)} %get-tuple-element.7), channel_id=1, source_target_pairs={{0,8},{8,0},{16,24},{24,16},{1,9},{9,1},{17,25},{25,17},{2,10},{10... | collective-permute-start | bytes 776 | tf_op jit(solution)/shard_map/ppermute | solution.py:68
  169.1 1.1 collective-permute-start.31
  170.2 5.3 %collective-permute-start.34 = (f32[64]{0:T(128)S(1)}, f32[64]{0:T(128)S(1)}, u32[]{:S(2)}, u32[]{:S(2)}) collective-permute-start(f32[64]{0:T(128)S(1)} %max.146), channel_id=1, source_target_pairs={{0,6},{1,7},{2,4},{3,5},{4,2},{5,3},{6,0},{7,1},{8,14},{9,15},{10,... | collective-permute-start | bytes 776 | tf_op jit(solution)/shard_map/ppermute | solution.py:40
  172.9 4.4 %collective-permute-start.33 = (f32[64]{0:T(128)S(1)}, f32[64]{0:T(128)S(1)}, u32[]{:S(2)}, u32[]{:S(2)}) collective-permute-start(f32[64]{0:T(128)S(1)} %max.146), channel_id=1, source_target_pairs={{0,4},{1,5},{2,6},{3,7},{4,0},{5,1},{6,2},{7,3},{8,12},{9,13},{10,... | collective-permute-start | bytes 776 | tf_op jit(solution)/shard_map/ppermute | solution.py:40
  172.9 4.4 %collective-permute-start.32 = (f32[64]{0:T(128)S(1)}, f32[64]{0:T(128)S(1)}, u32[]{:S(2)}, u32[]{:S(2)}) collective-permute-start(f32[64]{0:T(128)S(1)} %max.146), channel_id=1, source_target_pairs={{0,2},{1,3},{2,0},{3,1},{4,6},{5,7},{6,4},{7,5},{8,10},{9,11},{10,... | collective-permute-start | bytes 776 | tf_op jit(solution)/shard_map/ppermute | solution.py:40

commit v7 on v6

--- a/solution.py
+++ b/solution.py
@@ -236,22 +236,25 @@
     squares = jnp.sum(stream * stream, axis=1)
     scaled = (stream * final_gain[None, :]).astype(jnp.bfloat16)
     logits = jnp.dot(scaled, head_weight, preferred_element_type=jnp.float32)
-    parts = lax.axis_size("gx")
-    chunk = logits.shape[1] // parts
-    squares_pair = split_pair(squares)
-    pieces = jnp.concatenate(
-        [
-            logits.astype(jnp.bfloat16).reshape(request_count, parts, chunk),
-            jnp.broadcast_to(squares_pair[:, None, :], (request_count, parts, 2)),
-        ],
-        axis=2,
-    )
-    pieces = lax.all_to_all(pieces, "gx", 1, 1, tiled=True).astype(jnp.float32)
-    top_part = jnp.sum(pieces[:, :, :chunk], axis=1)
-    total_squares = jnp.sum(pieces[:, :, chunk] + pieces[:, :, chunk + 1], axis=1)
-    rms_value = jnp.sqrt(total_squares / width + EPSILON)
+    current = logits
+    current_squares = squares
+    position = lax.axis_index("gx")
+    step = 1
+    while step < lax.axis_size("gx"):
+        half = current.shape[1] // 2
+        side = (position // step) % 2
+        keep = lax.dynamic_slice_in_dim(current, side * half, half, axis=1)
+        send = lax.dynamic_slice_in_dim(current, (1 - side) * half, half, axis=1)
+        pair = split_pair(current_squares)
+        payload = jnp.concatenate([send.astype(jnp.bfloat16), pair], axis=1)
+        got = exchange(payload, "gx", step).astype(jnp.float32)
+        own_squares = pair[:, 0].astype(jnp.float32) + pair[:, 1].astype(jnp.float32)
+        current_squares = own_squares + (got[:, half] + got[:, half + 1])
+        current = keep + got[:, :half]
+        step *= 2
+    rms_value = jnp.sqrt(current_squares / width + EPSILON)
     final_hidden = (stream / rms_value[:, None] * final_gain[None, :]).astype(jnp.bfloat16)
-    local_top = jnp.max(top_part, axis=1) / rms_value
+    local_top = jnp.max(current, axis=1) / rms_value
     top_logits = core_first_max(xor_max(local_top, "gx"), "gy")
     return (final_hidden, rms_value, top_logits)
 

time: 178 us -> 193 us (1.084)
  waiting for transfers between devices: 35.5 us -> 53.8 us
  blocking collectives: 36.5 us -> 21.8 us
  local copies, waits for them, and re-layouts: 24.7 us -> 31.7 us
  other arithmetic: 7.7 us -> 10.5 us
    ppermute x26 -> x28, waiting for transfers between devices: 28.8 us -> 47.3 us  [exchange(): return lax.ppermute(value, axis, [(i, i ^ partner) for i in range(count)])]
    all_to_all x1 -> x0, blocking collectives: 14.7 us -> none  [local(): pieces = lax.all_to_all(pieces, 'gx', 1, 1, tiled=True).astype(jnp.float32)]
    unnamed x31 -> x30, local copies, waits for them, and re-layouts: 0.77 us -> 3.49 us
    ppermute x0 -> x1, local copies, waits for them, and re-layouts: none -> 2.17 us  [exchange(): return lax.ppermute(value, axis, [(i, i ^ partner) for i in range(count)])]
    ppermute x26 -> x28, starting transfers between devices: 29.6 us -> 30 us  [exchange(): return lax.ppermute(value, axis, [(i, i ^ partner) for i in range(count)])]
  transfers between devices with their start and end apart: 35 -> 37, of which waited for: 26 -> 29; matrix products, arithmetic and copies ran while one was open for 11% -> 12% of each run, Pallas kernels for 0% -> 0%
where the time goes in v7:
time: 193 us
  waiting for transfers between devices  53.8 us (28%)
  starting transfers between devices  41.6 us (22%)
  local copies, waits for them, and re-layouts  31.7 us (16%)
  matrix products  31.7 us (16%)
  blocking collectives  21.8 us (11%)
  other arithmetic  10.5 us (5%)
    ppermute x28, waiting for transfers between devices, exchange(): return lax.ppermute(value, axis, [(i, i ^ partner) for i in range(count)])  47.3 us
    ppermute x28, starting transfers between devices, exchange(): return lax.ppermute(value, axis, [(i, i ^ partner) for i in range(count)])  30 us
    all_gather x2, blocking collectives, gather_sum(): return jnp.sum(lax.all_gather(value, axis).astype(jnp.float32), axis=0)  21.8 us
    slice x1, local copies, waits for them, and re-layouts, local(): kv_cache[layer_id]  14.9 us
    dot_general x2, matrix products, local_attention(): jnp.einsum('pthc,pkhc->pkt', kv_layer, query_block, preferred_element_typ...  11.7 us
    dot_general x2, matrix products, local_attention(): jnp.einsum('pkt,pthc->pkhc', weights.astype(jnp.bfloat16), kv_layer, pref...  9.34 us
    ppermute x6, starting transfers between devices, xor_sum(): lax.ppermute(value, axis, [(i, i ^ k) for i in range(count)])  8.13 us
    ppermute x6, waiting for transfers between devices, xor_sum(): lax.ppermute(value, axis, [(i, i ^ k) for i in range(count)])  4.45 us
  transfers between devices with their start and end apart: 37, of which 29 were waited for; matrix products, arithmetic and copies ran while one was open for 12% of the time, Pallas kernels for 0%

profile of v7, /device:TPU:0, one launch (start us, length us, event | category | flops | bytes accessed | tf_op | source)
XLA Modules:
  0.0 192.5 jit_solution(7093075799579333520)
XLA Ops:
  3.3 1.3 convolution_convert_fusion.1
  4.6 3.0 %collective-permute-start.1 = (bf16[64,388]{0,1:T(8,128)(2,1)S(1)}, bf16[64,388]{0,1:T(8,128)(2,1)S(1)}, u32[]{:S(2)}, u32[]{:S(2)}) collective-permute-start(bf16[64,388]{0,1:T(8,128)(2,1)S(1)} %pad_maximum_fusion), channel_id=1, source_target_pairs={{0,16},{8,24},{16,0},{24,8},{1,17},{9,25},{17,1},{25,9},{2,18},{10... | collective-permute-start | bytes 149000 | tf_op jit(solution)/shard_map/ppermute | solution.py:23
  7.7 1.5 collective-permute-start
  12.6 14.9 %fusion.173 = (bf16[1,128,128,2,128]{4,3,2,1,0:T(2,128)(2,1)}, bf16[1,128,128,2,128]{4,3,2,1,0:T(2,128)(2,1)}) fusion(bf16[2,128,128,2,128]{4,3,2,1,0:T(2,128)(2,1)} %param.28), kind=kLoop, calls=%fused_computation.328 | loop fusion | bytes 33554432 | tf_op jit(solution)/shard_map/slice | solution.py:194
  29.6 5.9 %fusion.180 = (f32[128,2]{1,0:T(8,128)S(1)}, f32[128,2,128]{2,1,0:T(2,128)S(1)}) fusion(f32[128,2]{1,0:T(8,128)S(1)} %gather_fusion.1, f32[2,128,2,128]{3,2,1,0:T(2,128)S(1)} %copy-done.9, bf16[1,128,128,2,128]{4,3,2,1,0:T(2,128)(2,1)} %get-tuple-element.28, bf16[128,2,128]{2,1,0:T(2,128)(2,1)S(1)} %concatenate.36, ...), kind=kOutput, calls=%fused_computation.335 | convolution fusion | flops 17202944 | bytes 8734728 | tf_op jit(solution)/shard_map/pthc,pkhc->pkt/dot_general | solution.py:106
  36.4 4.7 %fusion = f32[128,2,2,128]{3,1,2,0:T(2,128)S(1)} fusion(bf16[1,128,128,2,128]{4,3,2,1,0:T(2,128)(2,1)} %get-tuple-element.28, f32[128,2,128]{2,1,0:T(2,128)S(1)} %get-tuple-element.61, pred[128,128]{1,0:T(8,128)(4,1)S(1)} %fusion.93, f32[128,2]{1,0:T(8,128)S(1)} %gather_fusion.2), kind=kOutput, calls=%fused_computation.8 | convolution fusion | flops 16875520 | bytes 8799232 | tf_op jit(solution)/shard_map/pkt,pthc->pkhc/dot_general | solution.py:116
  42.4 2.9 %collective-permute-start.5 = (f32[64,2,66]{0,1,2:T(2,128)S(1)}, f32[64,2,66]{0,1,2:T(2,128)S(1)}, u32[]{:S(2)}, u32[]{:S(2)}) collective-permute-start(f32[64,2,66]{0,1,2:T(2,128)S(1)} %pad_maximum_fusion.2), channel_id=1, source_target_pairs={{0,24},{8,16},{16,8},{24,0},{1,25},{9,17},{17,9},{25,1},{2,26},{10... | collective-permute-start | bytes 101384 | tf_op jit(solution)/shard_map/ppermute | solution.py:40
  46.3 1.5 collective-permute-done.5
  47.7 1.9 collective-permute-done.4
  52.0 3.7 %collective-permute-start.9 = (bf16[64,384]{1,0:T(8,128)(2,1)S(1)}, bf16[64,384]{1,0:T(8,128)(2,1)S(1)}, u32[]{:S(2)}, u32[]{:S(2)}) collective-permute-start(bf16[64,384]{1,0:T(8,128)(2,1)S(1)} %add_convert_fusion.3), channel_id=1, source_target_pairs={{0,6},{1,7},{2,4},{3,5},{4,2},{5,3},{6,0},{7,1},{8,14},{9,15},{10,... | collective-permute-start | bytes 147464 | tf_op jit(solution)/shard_map/ppermute | solution.py:40
  56.5 1.5 collective-permute-done.9
  58.0 2.6 %collective-permute-done.8 = bf16[64,384]{1,0:T(8,128)(2,1)S(1)} collective-permute-done((bf16[64,384]{1,0:T(8,128)(2,1)S(1)}, bf16[64,384]{1,0:T(8,128)(2,1)S(1)}, u32[]{:S(2)}, u32[]{:S(2)}) %collective-permute-start.8) | collective-permute-done | bytes 49184 | tf_op jit(solution)/shard_map/ppermute | solution.py:40
  61.6 11.0 %all-gather = bf16[256,1026]{1,0:T(8,128)(2,1)S(1)} all-gather(bf16[64,1026]{1,0:T(8,128)(2,1)S(1)} %concatenate.38), channel_id=2, replica_groups=mesh['gx'=4,'gy'=8] {'gx'}, dimensions={0}, use_global_device_ids=true | all-gather | bytes 656640 | tf_op jit(solution)/shard_map/all_gather | solution.py:17
  72.9 1.3 convolution_convert_fusion.9
  75.5 2.5 %collective-permute-start.13 = (bf16[64,384]{1,0:T(8,128)(2,1)S(1)}, bf16[64,384]{1,0:T(8,128)(2,1)S(1)}, u32[]{:S(2)}, u32[]{:S(2)}) collective-permute-start(bf16[64,384]{1,0:T(8,128)(2,1)S(1)} %add_convert_fusion.2), channel_id=1, source_target_pairs={{0,6},{1,7},{2,4},{3,5},{4,2},{5,3},{6,0},{7,1},{8,14},{9,15},{10,... | collective-permute-start | bytes 147464 | tf_op jit(solution)/shard_map/ppermute | solution.py:40
  78.2 1.8 collective-permute-start.11
  79.9 1.7 collective-permute-done.13
  81.6 1.9 collective-permute-done.12
  84.3 2.0 %collective-permute-start.14 = (bf16[64,388]{0,1:T(8,128)(2,1)S(1)}, bf16[64,388]{0,1:T(8,128)(2,1)S(1)}, u32[]{:S(2)}, u32[]{:S(2)}) collective-permute-start(bf16[64,388]{0,1:T(8,128)(2,1)S(1)} %pad_maximum_fusion.1), channel_id=1, source_target_pairs={{0,8},{8,0},{16,24},{24,16},{1,9},{9,1},{17,25},{25,17},{2,10},{10... | collective-permute-start | bytes 149000 | tf_op jit(solution)/shard_map/ppermute | solution.py:23
  86.3 1.5 collective-permute-start.16
  90.0 2.2 %collective-permute-done.16 = bf16[64,388]{0,1:T(8,128)(2,1)S(1)} collective-permute-done((bf16[64,388]{0,1:T(8,128)(2,1)S(1)}, bf16[64,388]{0,1:T(8,128)(2,1)S(1)}, u32[]{:S(2)}, u32[]{:S(2)}) %collective-permute-start.16) | collective-permute-done | bytes 49696 | tf_op jit(solution)/shard_map/ppermute | solution.py:23
  94.1 5.8 %fusion.181 = (f32[128,2]{1,0:T(8,128)S(1)}, f32[128,2,128]{2,1,0:T(2,128)S(1)}) fusion(f32[128,2]{1,0:T(8,128)S(1)} %gather_fusion.4, f32[2,128,2,128]{3,2,1,0:T(2,128)S(1)} %copy-done.9, bf16[1,128,128,2,128]{4,3,2,1,0:T(2,128)(2,1)} %get-tuple-element.27, bf16[128,2,128]{2,1,0:T(2,128)(2,1)S(1)} %concatenate.40, ...), kind=kOutput, calls=%fused_computation.336 | convolution fusion | flops 17202944 | bytes 8734728 | tf_op jit(solution)/shard_map/pthc,pkhc->pkt/dot_general | solution.py:106
  100.8 4.6 %fusion.2 = f32[128,2,2,128]{3,1,2,0:T(2,128)S(1)} fusion(bf16[1,128,128,2,128]{4,3,2,1,0:T(2,128)(2,1)} %get-tuple-element.27, f32[128,2,128]{2,1,0:T(2,128)S(1)} %get-tuple-element.63, pred[128,128]{1,0:T(8,128)(4,1)S(1)} %fusion.93, f32[128,2]{1,0:T(8,128)S(1)} %gather_fusion.5), kind=kOutput, calls=%fused_computation.10 | convolution fusion | flops 16875520 | bytes 8799232 | tf_op jit(solution)/shard_map/pkt,pthc->pkhc/dot_general | solution.py:116
  106.8 1.5 collective-permute-start.19
  108.6 1.7 collective-permute-start.17
  110.6 1.4 collective-permute-done.19
  114.8 2.6 %collective-permute-start.23 = (bf16[64,384]{1,0:T(8,128)(2,1)S(1)}, bf16[64,384]{1,0:T(8,128)(2,1)S(1)}, u32[]{:S(2)}, u32[]{:S(2)}) collective-permute-start(bf16[64,384]{1,0:T(8,128)(2,1)S(1)} %add_convert_fusion.1), channel_id=1, source_target_pairs={{0,6},{1,7},{2,4},{3,5},{4,2},{5,3},{6,0},{7,1},{8,14},{9,15},{10,... | collective-permute-start | bytes 147464 | tf_op jit(solution)/shard_map/ppermute | solution.py:40
  117.4 1.9 collective-permute-start.21
  119.3 1.8 collective-permute-done.23
  121.0 1.6 collective-permute-done.22
  123.5 10.8 %all-gather.1 = bf16[256,1026]{1,0:T(8,128)(2,1)S(1)} all-gather(bf16[64,1026]{1,0:T(8,128)(2,1)S(1)} %concatenate.42), channel_id=3, replica_groups=mesh['gx'=4,'gy'=8] {'gx'}, dimensions={0}, use_global_device_ids=true | all-gather | bytes 656640 | tf_op jit(solution)/shard_map/all_gather | solution.py:17
  134.6 1.3 convolution_convert_fusion.8
  137.2 2.4 %collective-permute-start.27 = (bf16[64,384]{1,0:T(8,128)(2,1)S(1)}, bf16[64,384]{1,0:T(8,128)(2,1)S(1)}, u32[]{:S(2)}, u32[]{:S(2)}) collective-permute-start(bf16[64,384]{1,0:T(8,128)(2,1)S(1)} %add_convert_fusion), channel_id=1, source_target_pairs={{0,6},{1,7},{2,4},{3,5},{4,2},{5,3},{6,0},{7,1},{8,14},{9,15},{10,... | collective-permute-start | bytes 147464 | tf_op jit(solution)/shard_map/ppermute | solution.py:40
  140.0 1.6 collective-permute-start.25
  141.6 1.8 collective-permute-done.27
  143.4 1.8 collective-permute-done.26
  145.6 3.3 %fusion.94 = f32[64,6144]{1,0:T(8,128)S(1)} fusion(bf16[384,6144]{1,0:T(8,128)(2,1)} %param.27, f32[64,384]{1,0:T(8,128)S(1)} %get-tuple-element.12, f32[384]{0:T(512)S(1)} %copy-done.6), kind=kOutput, calls=%fused_computation.180 | convolution fusion | flops 302039040 | bytes 6391296 | tf_op jit(solution)/shard_map/dot_general | solution.py:238
  150.8 1.6 copy.291
  152.4 8.7 %collective-permute-done.28 = bf16[64,3074]{1,0:T(8,128)(2,1)} collective-permute-done((bf16[64,3074]{1,0:T(8,128)(2,1)}, bf16[64,3074]{1,0:T(8,128)(2,1)}, u32[]{:S(2)}, u32[]{:S(2)}) %collective-permute-start.28) | collective-permute-done | bytes 393504 | tf_op jit(solution)/shard_map/ppermute | solution.py:40
  161.1 2.2 %copy.267 = bf16[64,3074]{0,1:T(8,128)(2,1)} copy(bf16[64,3074]{1,0:T(8,128)(2,1)} %collective-permute-done.28) | data formatting | bytes 786944 | tf_op jit(solution)/shard_map/ppermute | solution.py:40
  163.3 1.2 convert_element_type.609
  166.5 9.4 %collective-permute-done.29 = bf16[64,1538]{0,1:T(8,128)(2,1)S(1)} collective-permute-done((bf16[64,1538]{0,1:T(8,128)(2,1)S(1)}, bf16[64,1538]{0,1:T(8,128)(2,1)S(1)}, u32[]{:S(2)}, u32[]{:S(2)}) %collective-permute-start.29) | collective-permute-done | bytes 196896 | tf_op jit(solution)/shard_map/ppermute | solution.py:40
  175.9 1.4 fusion.14
  177.8 1.5 collective-permute-start.32
  179.9 1.4 collective-permute-start.30
  184.6 3.0 %collective-permute-start.36 = (f32[64]{0:T(128)S(1)}, f32[64]{0:T(128)S(1)}, u32[]{:S(2)}, u32[]{:S(2)}) collective-permute-start(f32[64]{0:T(128)S(1)} %max.146), channel_id=1, source_target_pairs={{0,6},{1,7},{2,4},{3,5},{4,2},{5,3},{6,0},{7,1},{8,14},{9,15},{10,... | collective-permute-start | bytes 776 | tf_op jit(solution)/shard_map/ppermute | solution.py:40
  187.6 1.4 collective-permute-start.34
  189.9 2.1 %collective-permute-done.35 = f32[64]{0:T(128)S(1)} collective-permute-done((f32[64]{0:T(128)S(1)}, f32[64]{0:T(128)S(1)}, u32[]{:S(2)}, u32[]{:S(2)}) %collective-permute-start.35) | collective-permute-done | bytes 288 | tf_op jit(solution)/shard_map/ppermute | solution.py:40
  (206 shorter events, 40.3 us)
Async XLA Ops:
  4.6 23.0 %collective-permute-start.1 = (bf16[64,388]{0,1:T(8,128)(2,1)S(1)}, bf16[64,388]{0,1:T(8,128)(2,1)S(1)}, u32[]{:S(2)}, u32[]{:S(2)}) collective-permute-start(bf16[64,388]{0,1:T(8,128)(2,1)S(1)} %pad_maximum_fusion), channel_id=1, source_target_pairs={{0,16},{8,24},{16,0},{24,8},{1,17},{9,25},{17,1},{25,9},{2,18},{10... | collective-permute-start | bytes 149000 | tf_op jit(solution)/shard_map/ppermute | solution.py:23
  7.7 20.0 %collective-permute-start = (bf16[64,388]{0,1:T(8,128)(2,1)S(1)}, bf16[64,388]{0,1:T(8,128)(2,1)S(1)}, u32[]{:S(2)}, u32[]{:S(2)}) collective-permute-start(bf16[64,388]{0,1:T(8,128)(2,1)S(1)} %pad_maximum_fusion), channel_id=1, source_target_pairs={{0,8},{8,0},{16,24},{24,16},{1,9},{9,1},{17,25},{25,17},{2,10},{10... | collective-permute-start | bytes 149000 | tf_op jit(solution)/shard_map/ppermute | solution.py:23
  9.1 18.5 %collective-permute-start.2 = (bf16[64,388]{0,1:T(8,128)(2,1)S(1)}, bf16[64,388]{0,1:T(8,128)(2,1)S(1)}, u32[]{:S(2)}, u32[]{:S(2)}) collective-permute-start(bf16[64,388]{0,1:T(8,128)(2,1)S(1)} %pad_maximum_fusion), channel_id=1, source_target_pairs={{0,24},{8,16},{16,8},{24,0},{1,25},{9,17},{17,9},{25,1},{2,26},{10... | collective-permute-start | bytes 149000 | tf_op jit(solution)/shard_map/ppermute | solution.py:23
  12.5 17.0 %copy-start.9 = (f32[2,128,2,128]{3,2,1,0:T(2,128)S(1)}, f32[2,128,2,128]{3,2,1,0:T(2,128)}, u32[]{:S(2)}) copy-start(f32[2,128,2,128]{3,2,1,0:T(2,128)} %param.29) | copy-start | bytes 786436
  29.5 21.0 %copy-start.5 = (bf16[2,128,384]{2,1,0:T(8,128)(2,1)S(1)}, bf16[2,128,384]{2,1,0:T(8,128)(2,1)}, u32[]{:S(2)}) copy-start(bf16[2,128,384]{2,1,0:T(8,128)(2,1)} %param.23) | copy-start | bytes 589828
  29.5 26.9 %copy-start.7 = (f32[2,384]{1,0:T(2,128)S(1)}, f32[2,384]{1,0:T(2,128)}, u32[]{:S(2)}) copy-start(f32[2,384]{1,0:T(2,128)} %param.18) | copy-start | bytes 9220
  29.6 31.1 %copy-start.4 = (bf16[64,384]{1,0:T(8,128)(2,1)S(1)}, bf16[64,384]{1,0:T(8,128)(2,1)}, u32[]{:S(2)}) copy-start(bf16[64,384]{1,0:T(8,128)(2,1)} %param.16) | copy-start | bytes 147460
  35.4 25.6 %copy-start.1 = (bf16[2,384,512]{2,1,0:T(8,128)(2,1)S(1)}, bf16[2,384,512]{2,1,0:T(8,128)(2,1)}, u32[]{:S(2)}) copy-start(bf16[2,384,512]{2,1,0:T(8,128)(2,1)} %param.25) | copy-start | bytes 2359300
  35.4 25.8 %copy-start.2 = (bf16[2,384,512]{2,1,0:T(8,128)(2,1)S(1)}, bf16[2,384,512]{2,1,0:T(8,128)(2,1)}, u32[]{:S(2)}) copy-start(bf16[2,384,512]{2,1,0:T(8,128)(2,1)} %param.24) | copy-start | bytes 2359300
  36.4 47.3 %copy-start.8 = (bf16[2,384,2]{1,2,0:T(2,128)(2,1)S(1)}, bf16[2,384,2]{1,2,0:T(2,128)(2,1)}, u32[]{:S(2)}) copy-start(bf16[2,384,2]{1,2,0:T(2,128)(2,1)} %param.21) | copy-start | bytes 9220
  36.4 47.4 %copy-start.3 = (bf16[2,384,384]{2,1,0:T(8,128)(2,1)S(1)}, bf16[2,384,384]{2,1,0:T(8,128)(2,1)}, u32[]{:S(2)}) copy-start(bf16[2,384,384]{2,1,0:T(8,128)(2,1)} %param.20) | copy-start | bytes 1769476
  42.4 5.4 %collective-permute-start.5 = (f32[64,2,66]{0,1,2:T(2,128)S(1)}, f32[64,2,66]{0,1,2:T(2,128)S(1)}, u32[]{:S(2)}, u32[]{:S(2)}) collective-permute-start(f32[64,2,66]{0,1,2:T(2,128)S(1)} %pad_maximum_fusion.2), channel_id=1, source_target_pairs={{0,24},{8,16},{16,8},{24,0},{1,25},{9,17},{17,9},{25,1},{2,26},{10... | collective-permute-start | bytes 101384 | tf_op jit(solution)/shard_map/ppermute | solution.py:40
  45.3 4.3 %collective-permute-start.4 = (f32[64,2,66]{0,1,2:T(2,128)S(1)}, f32[64,2,66]{0,1,2:T(2,128)S(1)}, u32[]{:S(2)}, u32[]{:S(2)}) collective-permute-start(f32[64,2,66]{0,1,2:T(2,128)S(1)} %pad_maximum_fusion.2), channel_id=1, source_target_pairs={{0,16},{8,24},{16,0},{24,8},{1,17},{9,25},{17,1},{25,9},{2,18},{10... | collective-permute-start | bytes 101384 | tf_op jit(solution)/shard_map/ppermute | solution.py:40
  45.8 4.3 %collective-permute-start.3 = (f32[64,2,66]{0,1,2:T(2,128)S(1)}, f32[64,2,66]{0,1,2:T(2,128)S(1)}, u32[]{:S(2)}, u32[]{:S(2)}) collective-permute-start(f32[64,2,66]{0,1,2:T(2,128)S(1)} %pad_maximum_fusion.2), channel_id=1, source_target_pairs={{0,8},{8,0},{16,24},{24,16},{1,9},{9,1},{17,25},{25,17},{2,10},{10... | collective-permute-start | bytes 101384 | tf_op jit(solution)/shard_map/ppermute | solution.py:40
  50.7 1.3 collective-permute-start.6
  52.0 6.0 %collective-permute-start.9 = (bf16[64,384]{1,0:T(8,128)(2,1)S(1)}, bf16[64,384]{1,0:T(8,128)(2,1)S(1)}, u32[]{:S(2)}, u32[]{:S(2)}) collective-permute-start(bf16[64,384]{1,0:T(8,128)(2,1)S(1)} %add_convert_fusion.3), channel_id=1, source_target_pairs={{0,6},{1,7},{2,4},{3,5},{4,2},{5,3},{6,0},{7,1},{8,14},{9,15},{10,... | collective-permute-start | bytes 147464 | tf_op jit(solution)/shard_map/ppermute | solution.py:40
  55.7 5.0 %collective-permute-start.8 = (bf16[64,384]{1,0:T(8,128)(2,1)S(1)}, bf16[64,384]{1,0:T(8,128)(2,1)S(1)}, u32[]{:S(2)}, u32[]{:S(2)}) collective-permute-start(bf16[64,384]{1,0:T(8,128)(2,1)S(1)} %add_convert_fusion.3), channel_id=1, source_target_pairs={{0,4},{1,5},{2,6},{3,7},{4,0},{5,1},{6,2},{7,3},{8,12},{9,13},{10,... | collective-permute-start | bytes 147464 | tf_op jit(solution)/shard_map/ppermute | solution.py:40
  55.7 5.0 %collective-permute-start.7 = (bf16[64,384]{1,0:T(8,128)(2,1)S(1)}, bf16[64,384]{1,0:T(8,128)(2,1)S(1)}, u32[]{:S(2)}, u32[]{:S(2)}) collective-permute-start(bf16[64,384]{1,0:T(8,128)(2,1)S(1)} %add_convert_fusion.3), channel_id=1, source_target_pairs={{0,2},{1,3},{2,0},{3,1},{4,6},{5,7},{6,4},{7,5},{8,10},{9,11},{10,... | collective-permute-start | bytes 147464 | tf_op jit(solution)/shard_map/ppermute | solution.py:40
  74.2 1.3 collective-permute-start.10
  75.5 6.2 %collective-permute-start.13 = (bf16[64,384]{1,0:T(8,128)(2,1)S(1)}, bf16[64,384]{1,0:T(8,128)(2,1)S(1)}, u32[]{:S(2)}, u32[]{:S(2)}) collective-permute-start(bf16[64,384]{1,0:T(8,128)(2,1)S(1)} %add_convert_fusion.2), channel_id=1, source_target_pairs={{0,6},{1,7},{2,4},{3,5},{4,2},{5,3},{6,0},{7,1},{8,14},{9,15},{10,... | collective-permute-start | bytes 147464 | tf_op jit(solution)/shard_map/ppermute | solution.py:40
  78.0 5.5 %collective-permute-start.12 = (bf16[64,384]{1,0:T(8,128)(2,1)S(1)}, bf16[64,384]{1,0:T(8,128)(2,1)S(1)}, u32[]{:S(2)}, u32[]{:S(2)}) collective-permute-start(bf16[64,384]{1,0:T(8,128)(2,1)S(1)} %add_convert_fusion.2), channel_id=1, source_target_pairs={{0,4},{1,5},{2,6},{3,7},{4,0},{5,1},{6,2},{7,3},{8,12},{9,13},{10,... | collective-permute-start | bytes 147464 | tf_op jit(solution)/shard_map/ppermute | solution.py:40
  78.2 5.4 %collective-permute-start.11 = (bf16[64,384]{1,0:T(8,128)(2,1)S(1)}, bf16[64,384]{1,0:T(8,128)(2,1)S(1)}, u32[]{:S(2)}, u32[]{:S(2)}) collective-permute-start(bf16[64,384]{1,0:T(8,128)(2,1)S(1)} %add_convert_fusion.2), channel_id=1, source_target_pairs={{0,2},{1,3},{2,0},{3,1},{4,6},{5,7},{6,4},{7,5},{8,10},{9,11},{10,... | collective-permute-start | bytes 147464 | tf_op jit(solution)/shard_map/ppermute | solution.py:40
  84.2 4.7 %collective-permute-start.15 = (bf16[64,388]{0,1:T(8,128)(2,1)S(1)}, bf16[64,388]{0,1:T(8,128)(2,1)S(1)}, u32[]{:S(2)}, u32[]{:S(2)}) collective-permute-start(bf16[64,388]{0,1:T(8,128)(2,1)S(1)} %pad_maximum_fusion.1), channel_id=1, source_target_pairs={{0,16},{8,24},{16,0},{24,8},{1,17},{9,25},{17,1},{25,9},{2,18},{10... | collective-permute-start | bytes 149000 | tf_op jit(solution)/shard_map/ppermute | solution.py:23
  84.3 5.7 %collective-permute-start.14 = (bf16[64,388]{0,1:T(8,128)(2,1)S(1)}, bf16[64,388]{0,1:T(8,128)(2,1)S(1)}, u32[]{:S(2)}, u32[]{:S(2)}) collective-permute-start(bf16[64,388]{0,1:T(8,128)(2,1)S(1)} %pad_maximum_fusion.1), channel_id=1, source_target_pairs={{0,8},{8,0},{16,24},{24,16},{1,9},{9,1},{17,25},{25,17},{2,10},{10... | collective-permute-start | bytes 149000 | tf_op jit(solution)/shard_map/ppermute | solution.py:23
  86.3 5.9 %collective-permute-start.16 = (bf16[64,388]{0,1:T(8,128)(2,1)S(1)}, bf16[64,388]{0,1:T(8,128)(2,1)S(1)}, u32[]{:S(2)}, u32[]{:S(2)}) collective-permute-start(bf16[64,388]{0,1:T(8,128)(2,1)S(1)} %pad_maximum_fusion.1), channel_id=1, source_target_pairs={{0,24},{8,16},{16,8},{24,0},{1,25},{9,17},{17,9},{25,1},{2,26},{10... | collective-permute-start | bytes 149000 | tf_op jit(solution)/shard_map/ppermute | solution.py:23
  100.8 44.8 %copy-start.6 = (f32[384]{0:T(512)S(1)}, f32[384]{0:T(512)}, u32[]{:S(2)}) copy-start(f32[384]{0:T(512)} %param.19) | copy-start | bytes 4612
  106.8 5.3 %collective-permute-start.19 = (f32[64,2,66]{0,1,2:T(2,128)S(1)}, f32[64,2,66]{0,1,2:T(2,128)S(1)}, u32[]{:S(2)}, u32[]{:S(2)}) collective-permute-start(f32[64,2,66]{0,1,2:T(2,128)S(1)} %pad_maximum_fusion.3), channel_id=1, source_target_pairs={{0,24},{8,16},{16,8},{24,0},{1,25},{9,17},{17,9},{25,1},{2,26},{10... | collective-permute-start | bytes 101384 | tf_op jit(solution)/shard_map/ppermute | solution.py:40
  108.3 4.5 %collective-permute-start.18 = (f32[64,2,66]{0,1,2:T(2,128)S(1)}, f32[64,2,66]{0,1,2:T(2,128)S(1)}, u32[]{:S(2)}, u32[]{:S(2)}) collective-permute-start(f32[64,2,66]{0,1,2:T(2,128)S(1)} %pad_maximum_fusion.3), channel_id=1, source_target_pairs={{0,16},{8,24},{16,0},{24,8},{1,17},{9,25},{17,1},{25,9},{2,18},{10... | collective-permute-start | bytes 101384 | tf_op jit(solution)/shard_map/ppermute | solution.py:40
  108.6 4.3 %collective-permute-start.17 = (f32[64,2,66]{0,1,2:T(2,128)S(1)}, f32[64,2,66]{0,1,2:T(2,128)S(1)}, u32[]{:S(2)}, u32[]{:S(2)}) collective-permute-start(f32[64,2,66]{0,1,2:T(2,128)S(1)} %pad_maximum_fusion.3), channel_id=1, source_target_pairs={{0,8},{8,0},{16,24},{24,16},{1,9},{9,1},{17,25},{25,17},{2,10},{10... | collective-permute-start | bytes 101384 | tf_op jit(solution)/shard_map/ppermute | solution.py:40
  113.5 1.3 collective-permute-start.20
  114.8 6.2 %collective-permute-start.23 = (bf16[64,384]{1,0:T(8,128)(2,1)S(1)}, bf16[64,384]{1,0:T(8,128)(2,1)S(1)}, u32[]{:S(2)}, u32[]{:S(2)}) collective-permute-start(bf16[64,384]{1,0:T(8,128)(2,1)S(1)} %add_convert_fusion.1), channel_id=1, source_target_pairs={{0,6},{1,7},{2,4},{3,5},{4,2},{5,3},{6,0},{7,1},{8,14},{9,15},{10,... | collective-permute-start | bytes 147464 | tf_op jit(solution)/shard_map/ppermute | solution.py:40
  117.4 5.2 %collective-permute-start.22 = (bf16[64,384]{1,0:T(8,128)(2,1)S(1)}, bf16[64,384]{1,0:T(8,128)(2,1)S(1)}, u32[]{:S(2)}, u32[]{:S(2)}) collective-permute-start(bf16[64,384]{1,0:T(8,128)(2,1)S(1)} %add_convert_fusion.1), channel_id=1, source_target_pairs={{0,4},{1,5},{2,6},{3,7},{4,0},{5,1},{6,2},{7,3},{8,12},{9,13},{10,... | collective-permute-start | bytes 147464 | tf_op jit(solution)/shard_map/ppermute | solution.py:40
  117.4 5.2 %collective-permute-start.21 = (bf16[64,384]{1,0:T(8,128)(2,1)S(1)}, bf16[64,384]{1,0:T(8,128)(2,1)S(1)}, u32[]{:S(2)}, u32[]{:S(2)}) collective-permute-start(bf16[64,384]{1,0:T(8,128)(2,1)S(1)} %add_convert_fusion.1), channel_id=1, source_target_pairs={{0,2},{1,3},{2,0},{3,1},{4,6},{5,7},{6,4},{7,5},{8,10},{9,11},{10,... | collective-permute-start | bytes 147464 | tf_op jit(solution)/shard_map/ppermute | solution.py:40
  135.9 1.3 collective-permute-start.24
  137.2 6.2 %collective-permute-start.27 = (bf16[64,384]{1,0:T(8,128)(2,1)S(1)}, bf16[64,384]{1,0:T(8,128)(2,1)S(1)}, u32[]{:S(2)}, u32[]{:S(2)}) collective-permute-start(bf16[64,384]{1,0:T(8,128)(2,1)S(1)} %add_convert_fusion), channel_id=1, source_target_pairs={{0,6},{1,7},{2,4},{3,5},{4,2},{5,3},{6,0},{7,1},{8,14},{9,15},{10,... | collective-permute-start | bytes 147464 | tf_op jit(solution)/shard_map/ppermute | solution.py:40
  139.6 5.6 %collective-permute-start.26 = (bf16[64,384]{1,0:T(8,128)(2,1)S(1)}, bf16[64,384]{1,0:T(8,128)(2,1)S(1)}, u32[]{:S(2)}, u32[]{:S(2)}) collective-permute-start(bf16[64,384]{1,0:T(8,128)(2,1)S(1)} %add_convert_fusion), channel_id=1, source_target_pairs={{0,4},{1,5},{2,6},{3,7},{4,0},{5,1},{6,2},{7,3},{8,12},{9,13},{10,... | collective-permute-start | bytes 147464 | tf_op jit(solution)/shard_map/ppermute | solution.py:40
  140.0 5.2 %collective-permute-start.25 = (bf16[64,384]{1,0:T(8,128)(2,1)S(1)}, bf16[64,384]{1,0:T(8,128)(2,1)S(1)}, u32[]{:S(2)}, u32[]{:S(2)}) collective-permute-start(bf16[64,384]{1,0:T(8,128)(2,1)S(1)} %add_convert_fusion), channel_id=1, source_target_pairs={{0,2},{1,3},{2,0},{3,1},{4,6},{5,7},{6,4},{7,5},{8,10},{9,11},{10,... | collective-permute-start | bytes 147464 | tf_op jit(solution)/shard_map/ppermute | solution.py:40
  149.8 11.2 %collective-permute-start.28 = (bf16[64,3074]{1,0:T(8,128)(2,1)}, bf16[64,3074]{1,0:T(8,128)(2,1)}, u32[]{:S(2)}, u32[]{:S(2)}) collective-permute-start(bf16[64,3074]{1,0:T(8,128)(2,1)} %concatenate.43), channel_id=1, source_target_pairs={{0,8},{8,0},{16,24},{24,16},{1,9},{9,1},{17,25},{25,17},{2,10},{10... | collective-permute-start | bytes 1180424 | tf_op jit(solution)/shard_map/ppermute | solution.py:40
  164.7 1.2 copy-start
  166.1 9.8 %collective-permute-start.29 = (bf16[64,1538]{0,1:T(8,128)(2,1)S(1)}, bf16[64,1538]{0,1:T(8,128)(2,1)S(1)}, u32[]{:S(2)}, u32[]{:S(2)}) collective-permute-start(bf16[64,1538]{0,1:T(8,128)(2,1)S(1)} %concatenate.44), channel_id=1, source_target_pairs={{0,16},{8,24},{16,0},{24,8},{1,17},{9,25},{17,1},{25,9},{2,18},{10... | collective-permute-start | bytes 590600 | tf_op jit(solution)/shard_map/ppermute | solution.py:40
  177.8 4.4 %collective-permute-start.32 = (f32[64]{0:T(128)S(1)}, f32[64]{0:T(128)S(1)}, u32[]{:S(2)}, u32[]{:S(2)}) collective-permute-start(f32[64]{0:T(128)S(1)} %get-tuple-element.7), channel_id=1, source_target_pairs={{0,24},{8,16},{16,8},{24,0},{1,25},{9,17},{17,9},{25,1},{2,26},{10... | collective-permute-start | bytes 776 | tf_op jit(solution)/shard_map/ppermute | solution.py:68
  179.3 3.5 %collective-permute-start.31 = (f32[64]{0:T(128)S(1)}, f32[64]{0:T(128)S(1)}, u32[]{:S(2)}, u32[]{:S(2)}) collective-permute-start(f32[64]{0:T(128)S(1)} %get-tuple-element.7), channel_id=1, source_target_pairs={{0,16},{8,24},{16,0},{24,8},{1,17},{9,25},{17,1},{25,9},{2,18},{10... | collective-permute-start | bytes 776 | tf_op jit(solution)/shard_map/ppermute | solution.py:68
  179.9 3.5 %collective-permute-start.30 = (f32[64]{0:T(128)S(1)}, f32[64]{0:T(128)S(1)}, u32[]{:S(2)}, u32[]{:S(2)}) collective-permute-start(f32[64]{0:T(128)S(1)} %get-tuple-element.7), channel_id=1, source_target_pairs={{0,8},{8,0},{16,24},{24,16},{1,9},{9,1},{17,25},{25,17},{2,10},{10... | collective-permute-start | bytes 776 | tf_op jit(solution)/shard_map/ppermute | solution.py:68
  183.4 1.1 collective-permute-start.33
  184.6 5.3 %collective-permute-start.36 = (f32[64]{0:T(128)S(1)}, f32[64]{0:T(128)S(1)}, u32[]{:S(2)}, u32[]{:S(2)}) collective-permute-start(f32[64]{0:T(128)S(1)} %max.146), channel_id=1, source_target_pairs={{0,6},{1,7},{2,4},{3,5},{4,2},{5,3},{6,0},{7,1},{8,14},{9,15},{10,... | collective-permute-start | bytes 776 | tf_op jit(solution)/shard_map/ppermute | solution.py:40
  187.6 4.4 %collective-permute-start.35 = (f32[64]{0:T(128)S(1)}, f32[64]{0:T(128)S(1)}, u32[]{:S(2)}, u32[]{:S(2)}) collective-permute-start(f32[64]{0:T(128)S(1)} %max.146), channel_id=1, source_target_pairs={{0,4},{1,5},{2,6},{3,7},{4,0},{5,1},{6,2},{7,3},{8,12},{9,13},{10,... | collective-permute-start | bytes 776 | tf_op jit(solution)/shard_map/ppermute | solution.py:40
  187.6 4.4 %collective-permute-start.34 = (f32[64]{0:T(128)S(1)}, f32[64]{0:T(128)S(1)}, u32[]{:S(2)}, u32[]{:S(2)}) collective-permute-start(f32[64]{0:T(128)S(1)} %max.146), channel_id=1, source_target_pairs={{0,2},{1,3},{2,0},{3,1},{4,6},{5,7},{6,4},{7,5},{8,10},{9,11},{10,... | collective-permute-start | bytes 776 | tf_op jit(solution)/shard_map/ppermute | solution.py:40

commit v8 on v6

--- a/solution.py
+++ b/solution.py
@@ -27,6 +27,13 @@
     while len(parts) > 1:
         parts = [parts[i] + parts[i + 1] for i in range(0, len(parts), 2)]
     return parts[0]
+
+
+def gather_all(value, axis):
+    count = lax.axis_size(axis)
+    copies = jnp.broadcast_to(value[None], (count,) + value.shape)
+    received = lax.all_to_all(copies, axis, 0, 0, tiled=True)
+    return [received[k] for k in range(count)]
 
 
 def butterfly(parts, join):
@@ -126,7 +133,7 @@
 def merge_pages(row_peak, row_sum, row_out):
     packed = jnp.concatenate([row_peak[:, :, None], row_sum[:, :, None], row_out], axis=2)
     count = lax.axis_size("gx")
-    every = [packed] + [exchange(packed, "gx", k) for k in range(1, count)]
+    every = gather_all(packed, "gx")
     top = butterfly([part[:, :, 0] for part in every], jnp.maximum)
     scales = [jnp.exp(part[:, :, 0] - top) for part in every]
     total = butterfly([scale * part[:, :, 1] for scale, part in zip(scales, every)], jnp.add)
@@ -252,7 +259,7 @@
     rms_value = jnp.sqrt(total_squares / width + EPSILON)
     final_hidden = (stream / rms_value[:, None] * final_gain[None, :]).astype(jnp.bfloat16)
     local_top = jnp.max(top_part, axis=1) / rms_value
-    top_logits = core_first_max(xor_max(local_top, "gx"), "gy")
+    top_logits = core_first_max(butterfly(gather_all(local_top, "gx"), jnp.maximum), "gy")
     return (final_hidden, rms_value, top_logits)
 
 

time: 178 us -> 186 us (1.045)
  blocking collectives: 36.5 us -> 43.1 us
  starting transfers between devices: 41.3 us -> 38.2 us
  local copies, waits for them, and re-layouts: 24.7 us -> 27.3 us
    all_to_all x0 -> x2, waiting for transfers between devices: none -> 10.3 us  [gather_all(): received = lax.all_to_all(copies, axis, 0, 0, tiled=True)]
    all_to_all x0 -> x2, starting transfers between devices: none -> 7.55 us  [gather_all(): received = lax.all_to_all(copies, axis, 0, 0, tiled=True)]
    ppermute x26 -> x20, starting transfers between devices: 29.6 us -> 22.5 us  [exchange(): return lax.ppermute(value, axis, [(i, i ^ partner) for i in range(count)])]
    all_to_all x0 -> x1, blocking collectives: none -> 6.99 us  [gather_all(): received = lax.all_to_all(copies, axis, 0, 0, tiled=True)]
    ppermute x26 -> x20, waiting for transfers between devices: 28.8 us -> 22.2 us  [exchange(): return lax.ppermute(value, axis, [(i, i ^ partner) for i in range(count)])]
    ppermute x3 -> x0, starting transfers between devices: 3.55 us -> none  [xor_max(): lax.ppermute(value, axis, [(i, i ^ k) for i in range(count)])]
    ppermute x3 -> x0, waiting for transfers between devices: 2.25 us -> none  [xor_max(): lax.ppermute(value, axis, [(i, i ^ k) for i in range(count)])]
    broadcast_in_dim x0 -> x7, local copies, waits for them, and re-layouts: none -> 1.9 us  [the longest x3 1.44 us: gather_all(): copies = jnp.broadcast_to(value[None], (count,) + value.shape)]
  transfers between devices with their start and end apart: 35 -> 28, of which waited for: 26 -> 20; matrix products, arithmetic and copies ran while one was open for 11% -> 11% of each run, Pallas kernels for 0% -> 0%
where the time goes in v8:
time: 186 us; the launch traced here: 185 us
  blocking collectives  43.1 us (23%)
  starting transfers between devices  38.2 us (21%)
  waiting for transfers between devices  36.5 us (20%)
  matrix products  30.7 us (17%)
  local copies, waits for them, and re-layouts  27.3 us (15%)
  other arithmetic  7.78 us (4%)
    ppermute x20, starting transfers between devices, exchange(): return lax.ppermute(value, axis, [(i, i ^ partner) for i in range(count)])  22.5 us
    ppermute x20, waiting for transfers between devices, exchange(): return lax.ppermute(value, axis, [(i, i ^ partner) for i in range(count)])  22.2 us
    all_gather x2, blocking collectives, gather_sum(): return jnp.sum(lax.all_gather(value, axis).astype(jnp.float32), axis=0)  21.1 us
    all_to_all x1, blocking collectives, local(): pieces = lax.all_to_all(pieces, 'gx', 1, 1, tiled=True).astype(jnp.float32)  15.1 us
    slice x1, local copies, waits for them, and re-layouts, local(): kv_cache[layer_id]  14.9 us
    dot_general x2, matrix products, local_attention(): jnp.einsum('pthc,pkhc->pkt', kv_layer, query_block, preferred_element_typ...  11.6 us
    all_to_all x2, waiting for transfers between devices, gather_all(): received = lax.all_to_all(copies, axis, 0, 0, tiled=True)  10.3 us
    dot_general x2, matrix products, local_attention(): jnp.einsum('pkt,pthc->pkhc', weights.astype(jnp.bfloat16), kv_layer, pref...  9.43 us
  transfers between devices with their start and end apart: 28, of which 20 were waited for; matrix products, arithmetic and copies ran while one was open for 11% of the time, Pallas kernels for 0%

profile of v8, /device:TPU:0, one launch (start us, length us, event | category | flops | bytes accessed | tf_op | source)
XLA Modules:
  0.0 185.1 jit_solution(9326910407428461605)
XLA Ops:
  0.6 0.9 fusion.56
  2.3 0.9 convolution_convert_fusion.13
  3.3 1.3 convolution_convert_fusion.2
  4.6 3.0 %collective-permute-start.1 = (bf16[64,388]{0,1:T(8,128)(2,1)S(1)}, bf16[64,388]{0,1:T(8,128)(2,1)S(1)}, u32[]{:S(2)}, u32[]{:S(2)}) collective-permute-start(bf16[64,388]{0,1:T(8,128)(2,1)S(1)} %pad_maximum_fusion.1), channel_id=1, source_target_pairs={{0,16},{8,24},{16,0},{24,8},{1,17},{9,25},{17,1},{25,9},{2,18},{10... | collective-permute-start | bytes 149000 | tf_op jit(solution)/shard_map/ppermute | solution.py:23
  7.7 1.5 collective-permute-start
  9.2 0.8 subtract_bitcast_fusion
  12.6 14.9 %fusion.162 = (bf16[1,128,128,2,128]{4,3,2,1,0:T(2,128)(2,1)}, bf16[1,128,128,2,128]{4,3,2,1,0:T(2,128)(2,1)}) fusion(bf16[2,128,128,2,128]{4,3,2,1,0:T(2,128)(2,1)} %param.28), kind=kLoop, calls=%fused_computation.313 | loop fusion | bytes 33554432 | tf_op jit(solution)/shard_map/slice | solution.py:201
  29.5 5.8 %fusion.171 = (f32[128,2]{1,0:T(8,128)S(1)}, f32[128,2,128]{2,1,0:T(2,128)S(1)}) fusion(f32[128,2]{1,0:T(8,128)S(1)} %gather_fusion.1, f32[2,128,2,128]{3,2,1,0:T(2,128)S(1)} %copy-done.10, bf16[1,128,128,2,128]{4,3,2,1,0:T(2,128)(2,1)} %get-tuple-element.20, bf16[128,2,128]{2,1,0:T(2,128)(2,1)S(1)} %concatenate.33, ...), kind=kOutput, calls=%fused_computation.322 | convolution fusion | flops 17202944 | bytes 8734728 | tf_op jit(solution)/shard_map/pthc,pkhc->pkt/dot_general | solution.py:113
  36.3 4.7 %fusion = f32[128,2,2,128]{3,1,2,0:T(2,128)S(1)} fusion(bf16[1,128,128,2,128]{4,3,2,1,0:T(2,128)(2,1)} %get-tuple-element.20, f32[128,2,128]{2,1,0:T(2,128)S(1)} %get-tuple-element.65, pred[128,128]{1,0:T(8,128)(4,1)S(1)} %fusion.93, f32[128,2]{1,0:T(8,128)S(1)} %gather_fusion.2), kind=kOutput, calls=%fused_computation.8 | convolution fusion | flops 16875520 | bytes 8799232 | tf_op jit(solution)/shard_map/pkt,pthc->pkhc/dot_general | solution.py:123
  43.4 4.1 %all-to-all-start = ((f32[4,64,2,66]{3,1,2,0:T(8,128)}), f32[4,64,2,66]{3,1,2,0:T(8,128)S(1)}, u32[]{:S(2)}, u32[]{:S(2)}) async-start(f32[4,64,2,66]{3,1,2,0:T(8,128)} %broadcast_in_dim.95), calls=%async_computation | async-start | bytes 524288 | tf_op jit(solution)/shard_map/all_to_all | solution.py:35
  47.7 5.2 %all-to-all-done = f32[4,64,2,66]{3,1,2,0:T(8,128)S(1)} async-done(((f32[4,64,2,66]{3,1,2,0:T(8,128)}), f32[4,64,2,66]{3,1,2,0:T(8,128)S(1)}, u32[]{:S(2)}, u32[]{:S(2)}) %all-to-all-start) | async-done | bytes 135200 | tf_op jit(solution)/shard_map/all_to_all | solution.py:35
  54.0 1.2 collective-permute-done.3
  55.2 3.7 %collective-permute-start.6 = (bf16[64,384]{1,0:T(8,128)(2,1)S(1)}, bf16[64,384]{1,0:T(8,128)(2,1)S(1)}, u32[]{:S(2)}, u32[]{:S(2)}) collective-permute-start(bf16[64,384]{1,0:T(8,128)(2,1)S(1)} %add_convert_fusion.3), channel_id=1, source_target_pairs={{0,6},{1,7},{2,4},{3,5},{4,2},{5,3},{6,0},{7,1},{8,14},{9,15},{10,... | collective-permute-start | bytes 147464 | tf_op jit(solution)/shard_map/ppermute | solution.py:47
  59.7 1.5 collective-permute-done.6
  61.2 2.6 %collective-permute-done.5 = bf16[64,384]{1,0:T(8,128)(2,1)S(1)} collective-permute-done((bf16[64,384]{1,0:T(8,128)(2,1)S(1)}, bf16[64,384]{1,0:T(8,128)(2,1)S(1)}, u32[]{:S(2)}, u32[]{:S(2)}) %collective-permute-start.5) | collective-permute-done | bytes 49184 | tf_op jit(solution)/shard_map/ppermute | solution.py:47
  64.7 10.6 %all-gather = bf16[256,1026]{1,0:T(8,128)(2,1)S(1)} all-gather(bf16[64,1026]{1,0:T(8,128)(2,1)S(1)} %concatenate.35), channel_id=2, replica_groups=mesh['gx'=4,'gy'=8] {'gx'}, dimensions={0}, use_global_device_ids=true | all-gather | bytes 656640 | tf_op jit(solution)/shard_map/all_gather | solution.py:17
  75.7 1.3 convolution_convert_fusion.10
  77.0 1.2 collective-permute-done.7
  78.3 2.4 %collective-permute-start.10 = (bf16[64,384]{1,0:T(8,128)(2,1)S(1)}, bf16[64,384]{1,0:T(8,128)(2,1)S(1)}, u32[]{:S(2)}, u32[]{:S(2)}) collective-permute-start(bf16[64,384]{1,0:T(8,128)(2,1)S(1)} %add_convert_fusion.2), channel_id=1, source_target_pairs={{0,6},{1,7},{2,4},{3,5},{4,2},{5,3},{6,0},{7,1},{8,14},{9,15},{10,... | collective-permute-start | bytes 147464 | tf_op jit(solution)/shard_map/ppermute | solution.py:47
  80.9 1.8 collective-permute-start.8
  82.7 1.6 collective-permute-done.10
  84.3 2.0 %collective-permute-done.9 = bf16[64,384]{1,0:T(8,128)(2,1)S(1)} collective-permute-done((bf16[64,384]{1,0:T(8,128)(2,1)S(1)}, bf16[64,384]{1,0:T(8,128)(2,1)S(1)}, u32[]{:S(2)}, u32[]{:S(2)}) %collective-permute-start.9) | collective-permute-done | bytes 49184 | tf_op jit(solution)/shard_map/ppermute | solution.py:47
  87.5 1.6 collective-permute-start.11
  89.1 1.5 collective-permute-start.13
  90.5 2.2 %collective-permute-done.12 = bf16[64,388]{0,1:T(8,128)(2,1)S(1)} collective-permute-done((bf16[64,388]{0,1:T(8,128)(2,1)S(1)}, bf16[64,388]{0,1:T(8,128)(2,1)S(1)}, u32[]{:S(2)}, u32[]{:S(2)}) %collective-permute-start.12) | collective-permute-done | bytes 49696 | tf_op jit(solution)/shard_map/ppermute | solution.py:23
  92.8 1.8 collective-permute-done.13
  96.5 5.8 %fusion.172 = (f32[128,2]{1,0:T(8,128)S(1)}, f32[128,2,128]{2,1,0:T(2,128)S(1)}) fusion(f32[128,2]{1,0:T(8,128)S(1)} %gather_fusion.4, f32[2,128,2,128]{3,2,1,0:T(2,128)S(1)} %copy-done.10, bf16[1,128,128,2,128]{4,3,2,1,0:T(2,128)(2,1)} %get-tuple-element.19, bf16[128,2,128]{2,1,0:T(2,128)(2,1)S(1)} %concatenate.37, ...), kind=kOutput, calls=%fused_computation.323 | convolution fusion | flops 17202944 | bytes 8734728 | tf_op jit(solution)/shard_map/pthc,pkhc->pkt/dot_general | solution.py:113
  103.3 4.7 %fusion.2 = f32[128,2,2,128]{3,1,2,0:T(2,128)S(1)} fusion(bf16[1,128,128,2,128]{4,3,2,1,0:T(2,128)(2,1)} %get-tuple-element.19, f32[128,2,128]{2,1,0:T(2,128)S(1)} %get-tuple-element.67, pred[128,128]{1,0:T(8,128)(4,1)S(1)} %fusion.93, f32[128,2]{1,0:T(8,128)S(1)} %gather_fusion.5), kind=kOutput, calls=%fused_computation.10 | convolution fusion | flops 16875520 | bytes 8799232 | tf_op jit(solution)/shard_map/pkt,pthc->pkhc/dot_general | solution.py:123
  110.3 3.4 %all-to-all-start.1 = ((f32[4,64,2,66]{3,1,2,0:T(8,128)}), f32[4,64,2,66]{3,1,2,0:T(8,128)S(1)}, u32[]{:S(2)}, u32[]{:S(2)}) async-start(f32[4,64,2,66]{3,1,2,0:T(8,128)} %broadcast_in_dim.99), calls=%async_computation.1 | async-start | bytes 524288 | tf_op jit(solution)/shard_map/all_to_all | solution.py:35
  113.9 5.1 %all-to-all-done.1 = f32[4,64,2,66]{3,1,2,0:T(8,128)S(1)} async-done(((f32[4,64,2,66]{3,1,2,0:T(8,128)}), f32[4,64,2,66]{3,1,2,0:T(8,128)S(1)}, u32[]{:S(2)}, u32[]{:S(2)}) %all-to-all-start.1) | async-done | bytes 135200 | tf_op jit(solution)/shard_map/all_to_all | solution.py:35
  120.1 1.2 collective-permute-done.14
  121.3 2.9 %collective-permute-start.17 = (bf16[64,384]{1,0:T(8,128)(2,1)S(1)}, bf16[64,384]{1,0:T(8,128)(2,1)S(1)}, u32[]{:S(2)}, u32[]{:S(2)}) collective-permute-start(bf16[64,384]{1,0:T(8,128)(2,1)S(1)} %add_convert_fusion.1), channel_id=1, source_target_pairs={{0,6},{1,7},{2,4},{3,5},{4,2},{5,3},{6,0},{7,1},{8,14},{9,15},{10,... | collective-permute-start | bytes 147464 | tf_op jit(solution)/shard_map/ppermute | solution.py:47
  124.3 1.5 collective-permute-start.15
  125.8 1.8 collective-permute-done.17
  127.6 1.7 collective-permute-done.16
  130.3 10.5 %all-gather.1 = bf16[256,1026]{1,0:T(8,128)(2,1)S(1)} all-gather(bf16[64,1026]{1,0:T(8,128)(2,1)S(1)} %concatenate.39), channel_id=3, replica_groups=mesh['gx'=4,'gy'=8] {'gx'}, dimensions={0}, use_global_device_ids=true | all-gather | bytes 656640 | tf_op jit(solution)/shard_map/all_gather | solution.py:17
  141.5 1.2 collective-permute-done.18
  142.7 2.0 %collective-permute-start.21 = (bf16[64,384]{1,0:T(8,128)(2,1)S(1)}, bf16[64,384]{1,0:T(8,128)(2,1)S(1)}, u32[]{:S(2)}, u32[]{:S(2)}) collective-permute-start(bf16[64,384]{1,0:T(8,128)(2,1)S(1)} %add_convert_fusion), channel_id=1, source_target_pairs={{0,6},{1,7},{2,4},{3,5},{4,2},{5,3},{6,0},{7,1},{8,14},{9,15},{10,... | collective-permute-start | bytes 147464 | tf_op jit(solution)/shard_map/ppermute | solution.py:47
  145.1 2.1 %collective-permute-start.19 = (bf16[64,384]{1,0:T(8,128)(2,1)S(1)}, bf16[64,384]{1,0:T(8,128)(2,1)S(1)}, u32[]{:S(2)}, u32[]{:S(2)}) collective-permute-start(bf16[64,384]{1,0:T(8,128)(2,1)S(1)} %add_convert_fusion), channel_id=1, source_target_pairs={{0,2},{1,3},{2,0},{3,1},{4,6},{5,7},{6,4},{7,5},{8,10},{9,11},{10,... | collective-permute-start | bytes 147464 | tf_op jit(solution)/shard_map/ppermute | solution.py:47
  147.2 1.9 %collective-permute-done.21 = bf16[64,384]{1,0:T(8,128)(2,1)S(1)} collective-permute-done((bf16[64,384]{1,0:T(8,128)(2,1)S(1)}, bf16[64,384]{1,0:T(8,128)(2,1)S(1)}, u32[]{:S(2)}, u32[]{:S(2)}) %collective-permute-start.21) | collective-permute-done | bytes 49184 | tf_op jit(solution)/shard_map/ppermute | solution.py:47
  149.1 1.7 collective-permute-done.20
  151.1 3.3 %convolution_convert_fusion = bf16[64,6144]{1,0:T(8,128)(2,1)S(1)} fusion(bf16[384,6144]{1,0:T(8,128)(2,1)} %param.27, f32[64,384]{1,0:T(8,128)S(1)} %get-tuple-element.8, f32[384]{0:T(512)S(1)} %copy-done.5), kind=kOutput, calls=%fused_computation.12 | convolution fusion | flops 302432256 | bytes 5604864 | tf_op jit(solution)/shard_map/dot_general | solution.py:245
  154.5 15.1 %all_to_all.21 = bf16[64,4,1538]{2,0,1:T(8,128)(2,1)S(1)} all-to-all(bf16[64,4,1538]{2,0,1:T(8,128)(2,1)S(1)} %pad_maximum_fusion), channel_id=1, replica_groups=mesh['gx'=4,'gy'=8] {'gx'}, dimensions={1} | all-to-all | bytes 1574912 | tf_op jit(solution)/shard_map/all_to_all | solution.py:256
  170.1 7.0 %all_to_all.22 = f32[4,1,64]{2,1,0:T(1,128)S(1)} all-to-all(f32[4,1,64]{2,1,0:T(1,128)S(1)} %broadcast_in_dim.101), channel_id=1, replica_groups=mesh['gx'=4,'gy'=8] {'gx'}, dimensions={0} | all-to-all | bytes 2048 | tf_op jit(solution)/shard_map/all_to_all | solution.py:35
  177.1 1.1 collective-permute-done.22
  178.2 1.9 %collective-permute-start.25 = (f32[64]{0:T(128)S(1)}, f32[64]{0:T(128)S(1)}, u32[]{:S(2)}, u32[]{:S(2)}) collective-permute-start(f32[64]{0:T(128)S(1)} %fusion.178), channel_id=1, source_target_pairs={{0,6},{1,7},{2,4},{3,5},{4,2},{5,3},{6,0},{7,1},{8,14},{9,15},{10,... | collective-permute-start | bytes 776 | tf_op jit(solution)/shard_map/ppermute | solution.py:47
  180.1 2.5 %collective-permute-start.23 = (f32[64]{0:T(128)S(1)}, f32[64]{0:T(128)S(1)}, u32[]{:S(2)}, u32[]{:S(2)}) collective-permute-start(f32[64]{0:T(128)S(1)} %fusion.178), channel_id=1, source_target_pairs={{0,2},{1,3},{2,0},{3,1},{4,6},{5,7},{6,4},{7,5},{8,10},{9,11},{10,... | collective-permute-start | bytes 776 | tf_op jit(solution)/shard_map/ppermute | solution.py:47
  183.6 1.0 collective-permute-done.24
  (198 shorter events, 23.8 us)
Async XLA Ops:
  4.6 23.0 %collective-permute-start.1 = (bf16[64,388]{0,1:T(8,128)(2,1)S(1)}, bf16[64,388]{0,1:T(8,128)(2,1)S(1)}, u32[]{:S(2)}, u32[]{:S(2)}) collective-permute-start(bf16[64,388]{0,1:T(8,128)(2,1)S(1)} %pad_maximum_fusion.1), channel_id=1, source_target_pairs={{0,16},{8,24},{16,0},{24,8},{1,17},{9,25},{17,1},{25,9},{2,18},{10... | collective-permute-start | bytes 149000 | tf_op jit(solution)/shard_map/ppermute | solution.py:23
  7.7 20.0 %collective-permute-start = (bf16[64,388]{0,1:T(8,128)(2,1)S(1)}, bf16[64,388]{0,1:T(8,128)(2,1)S(1)}, u32[]{:S(2)}, u32[]{:S(2)}) collective-permute-start(bf16[64,388]{0,1:T(8,128)(2,1)S(1)} %pad_maximum_fusion.1), channel_id=1, source_target_pairs={{0,8},{8,0},{16,24},{24,16},{1,9},{9,1},{17,25},{25,17},{2,10},{10... | collective-permute-start | bytes 149000 | tf_op jit(solution)/shard_map/ppermute | solution.py:23
  9.1 18.5 %collective-permute-start.2 = (bf16[64,388]{0,1:T(8,128)(2,1)S(1)}, bf16[64,388]{0,1:T(8,128)(2,1)S(1)}, u32[]{:S(2)}, u32[]{:S(2)}) collective-permute-start(bf16[64,388]{0,1:T(8,128)(2,1)S(1)} %pad_maximum_fusion.1), channel_id=1, source_target_pairs={{0,24},{8,16},{16,8},{24,0},{1,25},{9,17},{17,9},{25,1},{2,26},{10... | collective-permute-start | bytes 149000 | tf_op jit(solution)/shard_map/ppermute | solution.py:23
  12.5 17.0 %copy-start.10 = (f32[2,128,2,128]{3,2,1,0:T(2,128)S(1)}, f32[2,128,2,128]{3,2,1,0:T(2,128)}, u32[]{:S(2)}) copy-start(f32[2,128,2,128]{3,2,1,0:T(2,128)} %param.29) | copy-start | bytes 786436
  35.3 18.4 %copy-start.4 = (bf16[2,128,384]{2,1,0:T(8,128)(2,1)S(1)}, bf16[2,128,384]{2,1,0:T(8,128)(2,1)}, u32[]{:S(2)}) copy-start(bf16[2,128,384]{2,1,0:T(8,128)(2,1)} %param.23) | copy-start | bytes 589828
  35.3 24.3 %copy-start.6 = (f32[2,384]{1,0:T(2,128)S(1)}, f32[2,384]{1,0:T(2,128)}, u32[]{:S(2)}) copy-start(f32[2,384]{1,0:T(2,128)} %param.18) | copy-start | bytes 9220
  35.4 28.5 %copy-start.3 = (bf16[64,384]{1,0:T(8,128)(2,1)S(1)}, bf16[64,384]{1,0:T(8,128)(2,1)}, u32[]{:S(2)}) copy-start(bf16[64,384]{1,0:T(8,128)(2,1)} %param.16) | copy-start | bytes 147460
  35.4 28.9 %copy-start = (bf16[2,384,512]{2,1,0:T(8,128)(2,1)S(1)}, bf16[2,384,512]{2,1,0:T(8,128)(2,1)}, u32[]{:S(2)}) copy-start(bf16[2,384,512]{2,1,0:T(8,128)(2,1)} %param.25) | copy-start | bytes 2359300
  35.4 29.1 %copy-start.1 = (bf16[2,384,512]{2,1,0:T(8,128)(2,1)S(1)}, bf16[2,384,512]{2,1,0:T(8,128)(2,1)}, u32[]{:S(2)}) copy-start(bf16[2,384,512]{2,1,0:T(8,128)(2,1)} %param.24) | copy-start | bytes 2359300
  36.3 50.2 %copy-start.8 = (bf16[2,384,2]{1,2,0:T(2,128)(2,1)S(1)}, bf16[2,384,2]{1,2,0:T(2,128)(2,1)}, u32[]{:S(2)}) copy-start(bf16[2,384,2]{1,2,0:T(2,128)(2,1)} %param.21) | copy-start | bytes 9220
  36.3 50.3 %copy-start.2 = (bf16[2,384,384]{2,1,0:T(8,128)(2,1)S(1)}, bf16[2,384,384]{2,1,0:T(8,128)(2,1)}, u32[]{:S(2)}) copy-start(bf16[2,384,384]{2,1,0:T(8,128)(2,1)} %param.20) | copy-start | bytes 1769476
  43.4 9.5 %all-to-all-start = ((f32[4,64,2,66]{3,1,2,0:T(8,128)}), f32[4,64,2,66]{3,1,2,0:T(8,128)S(1)}, u32[]{:S(2)}, u32[]{:S(2)}) async-start(f32[4,64,2,66]{3,1,2,0:T(8,128)} %broadcast_in_dim.95), calls=%async_computation | async-start | bytes 524288 | tf_op jit(solution)/shard_map/all_to_all | solution.py:35
  53.9 1.3 collective-permute-start.3
  55.2 6.0 %collective-permute-start.6 = (bf16[64,384]{1,0:T(8,128)(2,1)S(1)}, bf16[64,384]{1,0:T(8,128)(2,1)S(1)}, u32[]{:S(2)}, u32[]{:S(2)}) collective-permute-start(bf16[64,384]{1,0:T(8,128)(2,1)S(1)} %add_convert_fusion.3), channel_id=1, source_target_pairs={{0,6},{1,7},{2,4},{3,5},{4,2},{5,3},{6,0},{7,1},{8,14},{9,15},{10,... | collective-permute-start | bytes 147464 | tf_op jit(solution)/shard_map/ppermute | solution.py:47
  58.9 5.0 %collective-permute-start.5 = (bf16[64,384]{1,0:T(8,128)(2,1)S(1)}, bf16[64,384]{1,0:T(8,128)(2,1)S(1)}, u32[]{:S(2)}, u32[]{:S(2)}) collective-permute-start(bf16[64,384]{1,0:T(8,128)(2,1)S(1)} %add_convert_fusion.3), channel_id=1, source_target_pairs={{0,4},{1,5},{2,6},{3,7},{4,0},{5,1},{6,2},{7,3},{8,12},{9,13},{10,... | collective-permute-start | bytes 147464 | tf_op jit(solution)/shard_map/ppermute | solution.py:47
  58.9 5.0 %collective-permute-start.4 = (bf16[64,384]{1,0:T(8,128)(2,1)S(1)}, bf16[64,384]{1,0:T(8,128)(2,1)S(1)}, u32[]{:S(2)}, u32[]{:S(2)}) collective-permute-start(bf16[64,384]{1,0:T(8,128)(2,1)S(1)} %add_convert_fusion.3), channel_id=1, source_target_pairs={{0,2},{1,3},{2,0},{3,1},{4,6},{5,7},{6,4},{7,5},{8,10},{9,11},{10,... | collective-permute-start | bytes 147464 | tf_op jit(solution)/shard_map/ppermute | solution.py:47
  76.9 1.3 collective-permute-start.7
  78.3 6.1 %collective-permute-start.10 = (bf16[64,384]{1,0:T(8,128)(2,1)S(1)}, bf16[64,384]{1,0:T(8,128)(2,1)S(1)}, u32[]{:S(2)}, u32[]{:S(2)}) collective-permute-start(bf16[64,384]{1,0:T(8,128)(2,1)S(1)} %add_convert_fusion.2), channel_id=1, source_target_pairs={{0,6},{1,7},{2,4},{3,5},{4,2},{5,3},{6,0},{7,1},{8,14},{9,15},{10,... | collective-permute-start | bytes 147464 | tf_op jit(solution)/shard_map/ppermute | solution.py:47
  80.7 5.6 %collective-permute-start.9 = (bf16[64,384]{1,0:T(8,128)(2,1)S(1)}, bf16[64,384]{1,0:T(8,128)(2,1)S(1)}, u32[]{:S(2)}, u32[]{:S(2)}) collective-permute-start(bf16[64,384]{1,0:T(8,128)(2,1)S(1)} %add_convert_fusion.2), channel_id=1, source_target_pairs={{0,4},{1,5},{2,6},{3,7},{4,0},{5,1},{6,2},{7,3},{8,12},{9,13},{10,... | collective-permute-start | bytes 147464 | tf_op jit(solution)/shard_map/ppermute | solution.py:47
  80.9 5.4 %collective-permute-start.8 = (bf16[64,384]{1,0:T(8,128)(2,1)S(1)}, bf16[64,384]{1,0:T(8,128)(2,1)S(1)}, u32[]{:S(2)}, u32[]{:S(2)}) collective-permute-start(bf16[64,384]{1,0:T(8,128)(2,1)S(1)} %add_convert_fusion.2), channel_id=1, source_target_pairs={{0,2},{1,3},{2,0},{3,1},{4,6},{5,7},{6,4},{7,5},{8,10},{9,11},{10,... | collective-permute-start | bytes 147464 | tf_op jit(solution)/shard_map/ppermute | solution.py:47
  87.0 5.8 %collective-permute-start.12 = (bf16[64,388]{0,1:T(8,128)(2,1)S(1)}, bf16[64,388]{0,1:T(8,128)(2,1)S(1)}, u32[]{:S(2)}, u32[]{:S(2)}) collective-permute-start(bf16[64,388]{0,1:T(8,128)(2,1)S(1)} %pad_maximum_fusion.2), channel_id=1, source_target_pairs={{0,16},{8,24},{16,0},{24,8},{1,17},{9,25},{17,1},{25,9},{2,18},{10... | collective-permute-start | bytes 149000 | tf_op jit(solution)/shard_map/ppermute | solution.py:23
  87.5 5.3 %collective-permute-start.11 = (bf16[64,388]{0,1:T(8,128)(2,1)S(1)}, bf16[64,388]{0,1:T(8,128)(2,1)S(1)}, u32[]{:S(2)}, u32[]{:S(2)}) collective-permute-start(bf16[64,388]{0,1:T(8,128)(2,1)S(1)} %pad_maximum_fusion.2), channel_id=1, source_target_pairs={{0,8},{8,0},{16,24},{24,16},{1,9},{9,1},{17,25},{25,17},{2,10},{10... | collective-permute-start | bytes 149000 | tf_op jit(solution)/shard_map/ppermute | solution.py:23
  89.1 5.5 %collective-permute-start.13 = (bf16[64,388]{0,1:T(8,128)(2,1)S(1)}, bf16[64,388]{0,1:T(8,128)(2,1)S(1)}, u32[]{:S(2)}, u32[]{:S(2)}) collective-permute-start(bf16[64,388]{0,1:T(8,128)(2,1)S(1)} %pad_maximum_fusion.2), channel_id=1, source_target_pairs={{0,24},{8,16},{16,8},{24,0},{1,25},{9,17},{17,9},{25,1},{2,26},{10... | collective-permute-start | bytes 149000 | tf_op jit(solution)/shard_map/ppermute | solution.py:23
  103.2 37.9 %copy-start.9 = (bf16[2,512,384]{2,1,0:T(8,128)(2,1)S(1)}, bf16[2,512,384]{2,1,0:T(8,128)(2,1)}, u32[]{:S(2)}) copy-start(bf16[2,512,384]{2,1,0:T(8,128)(2,1)} %param.26) | copy-start | bytes 2359300
  103.2 47.8 %copy-start.5 = (f32[384]{0:T(512)S(1)}, f32[384]{0:T(512)}, u32[]{:S(2)}) copy-start(f32[384]{0:T(512)} %param.19) | copy-start | bytes 4612
  110.3 8.8 %all-to-all-start.1 = ((f32[4,64,2,66]{3,1,2,0:T(8,128)}), f32[4,64,2,66]{3,1,2,0:T(8,128)S(1)}, u32[]{:S(2)}, u32[]{:S(2)}) async-start(f32[4,64,2,66]{3,1,2,0:T(8,128)} %broadcast_in_dim.99), calls=%async_computation.1 | async-start | bytes 524288 | tf_op jit(solution)/shard_map/all_to_all | solution.py:35
  120.0 1.3 collective-permute-start.14
  121.3 6.2 %collective-permute-start.17 = (bf16[64,384]{1,0:T(8,128)(2,1)S(1)}, bf16[64,384]{1,0:T(8,128)(2,1)S(1)}, u32[]{:S(2)}, u32[]{:S(2)}) collective-permute-start(bf16[64,384]{1,0:T(8,128)(2,1)S(1)} %add_convert_fusion.1), channel_id=1, source_target_pairs={{0,6},{1,7},{2,4},{3,5},{4,2},{5,3},{6,0},{7,1},{8,14},{9,15},{10,... | collective-permute-start | bytes 147464 | tf_op jit(solution)/shard_map/ppermute | solution.py:47
  124.3 5.0 %collective-permute-start.16 = (bf16[64,384]{1,0:T(8,128)(2,1)S(1)}, bf16[64,384]{1,0:T(8,128)(2,1)S(1)}, u32[]{:S(2)}, u32[]{:S(2)}) collective-permute-start(bf16[64,384]{1,0:T(8,128)(2,1)S(1)} %add_convert_fusion.1), channel_id=1, source_target_pairs={{0,4},{1,5},{2,6},{3,7},{4,0},{5,1},{6,2},{7,3},{8,12},{9,13},{10,... | collective-permute-start | bytes 147464 | tf_op jit(solution)/shard_map/ppermute | solution.py:47
  124.3 5.1 %collective-permute-start.15 = (bf16[64,384]{1,0:T(8,128)(2,1)S(1)}, bf16[64,384]{1,0:T(8,128)(2,1)S(1)}, u32[]{:S(2)}, u32[]{:S(2)}) collective-permute-start(bf16[64,384]{1,0:T(8,128)(2,1)S(1)} %add_convert_fusion.1), channel_id=1, source_target_pairs={{0,2},{1,3},{2,0},{3,1},{4,6},{5,7},{6,4},{7,5},{8,10},{9,11},{10,... | collective-permute-start | bytes 147464 | tf_op jit(solution)/shard_map/ppermute | solution.py:47
  141.4 1.3 collective-permute-start.18
  142.7 6.4 %collective-permute-start.21 = (bf16[64,384]{1,0:T(8,128)(2,1)S(1)}, bf16[64,384]{1,0:T(8,128)(2,1)S(1)}, u32[]{:S(2)}, u32[]{:S(2)}) collective-permute-start(bf16[64,384]{1,0:T(8,128)(2,1)S(1)} %add_convert_fusion), channel_id=1, source_target_pairs={{0,6},{1,7},{2,4},{3,5},{4,2},{5,3},{6,0},{7,1},{8,14},{9,15},{10,... | collective-permute-start | bytes 147464 | tf_op jit(solution)/shard_map/ppermute | solution.py:47
  144.8 6.0 %collective-permute-start.20 = (bf16[64,384]{1,0:T(8,128)(2,1)S(1)}, bf16[64,384]{1,0:T(8,128)(2,1)S(1)}, u32[]{:S(2)}, u32[]{:S(2)}) collective-permute-start(bf16[64,384]{1,0:T(8,128)(2,1)S(1)} %add_convert_fusion), channel_id=1, source_target_pairs={{0,4},{1,5},{2,6},{3,7},{4,0},{5,1},{6,2},{7,3},{8,12},{9,13},{10,... | collective-permute-start | bytes 147464 | tf_op jit(solution)/shard_map/ppermute | solution.py:47
  145.1 5.6 %collective-permute-start.19 = (bf16[64,384]{1,0:T(8,128)(2,1)S(1)}, bf16[64,384]{1,0:T(8,128)(2,1)S(1)}, u32[]{:S(2)}, u32[]{:S(2)}) collective-permute-start(bf16[64,384]{1,0:T(8,128)(2,1)S(1)} %add_convert_fusion), channel_id=1, source_target_pairs={{0,2},{1,3},{2,0},{3,1},{4,6},{5,7},{6,4},{7,5},{8,10},{9,11},{10,... | collective-permute-start | bytes 147464 | tf_op jit(solution)/shard_map/ppermute | solution.py:47
  170.1 15.0 %copy-start.7 = (f32[64]{0:T(128)}, f32[64]{0:T(128)S(1)}, u32[]{:S(2)}) copy-start(f32[64]{0:T(128)S(1)} %get-tuple-element.63) | copy-start | bytes 772
  177.1 1.1 collective-permute-start.22
  178.2 5.3 %collective-permute-start.25 = (f32[64]{0:T(128)S(1)}, f32[64]{0:T(128)S(1)}, u32[]{:S(2)}, u32[]{:S(2)}) collective-permute-start(f32[64]{0:T(128)S(1)} %fusion.178), channel_id=1, source_target_pairs={{0,6},{1,7},{2,4},{3,5},{4,2},{5,3},{6,0},{7,1},{8,14},{9,15},{10,... | collective-permute-start | bytes 776 | tf_op jit(solution)/shard_map/ppermute | solution.py:47
  180.1 4.4 %collective-permute-start.24 = (f32[64]{0:T(128)S(1)}, f32[64]{0:T(128)S(1)}, u32[]{:S(2)}, u32[]{:S(2)}) collective-permute-start(f32[64]{0:T(128)S(1)} %fusion.178), channel_id=1, source_target_pairs={{0,4},{1,5},{2,6},{3,7},{4,0},{5,1},{6,2},{7,3},{8,12},{9,13},{10,... | collective-permute-start | bytes 776 | tf_op jit(solution)/shard_map/ppermute | solution.py:47
  180.1 4.4 %collective-permute-start.23 = (f32[64]{0:T(128)S(1)}, f32[64]{0:T(128)S(1)}, u32[]{:S(2)}, u32[]{:S(2)}) collective-permute-start(f32[64]{0:T(128)S(1)} %fusion.178), channel_id=1, source_target_pairs={{0,2},{1,3},{2,0},{3,1},{4,6},{5,7},{6,4},{7,5},{8,10},{9,11},{10,... | collective-permute-start | bytes 776 | tf_op jit(solution)/shard_map/ppermute | solution.py:47

commit v9 on v6

--- a/solution.py
+++ b/solution.py
@@ -2,6 +2,8 @@
 import jax.numpy as jnp
 from jax import lax
 from jax.sharding import PartitionSpec as P
+from jax.experimental import pallas as pl
+from jax.experimental.pallas import tpu as pltpu
 
 HEAD = 64
 DEPTH_NUMBER = 2
@@ -70,6 +72,25 @@
     while len(parts) > 1:
         parts = [jnp.maximum(parts[i], parts[i + 1]) for i in range(0, len(parts), 2)]
     return parts[0]
+
+
+def copy_block(source, target):
+    target[...] = source[...]
+
+
+def layer_slice(cache, layer_id):
+    layers, slots, tokens, heads, width = cache.shape
+    block = 16
+    return pl.pallas_call(
+        copy_block,
+        grid=(slots // block,),
+        in_specs=[pl.BlockSpec((None, block, tokens, heads, width), lambda i: (layer_id, i, 0, 0, 0))],
+        out_specs=pl.BlockSpec((block, tokens, heads, width), lambda i: (i, 0, 0, 0)),
+        out_shape=jax.ShapeDtypeStruct((slots, tokens, heads, width), cache.dtype),
+        cost_estimate=pl.CostEstimate(
+            flops=0, transcendentals=0, bytes_accessed=2 * slots * tokens * heads * width * 2
+        ),
+    )(cache)
 
 
 def local_slots(page_table, base, slot_count):
@@ -191,7 +212,7 @@
         new_values = projected[:, :, 2 * HEAD :].astype(jnp.bfloat16)
         forget_log = jax.nn.log_sigmoid(forget_logit + forget_bias[layer_id][None, :])
         local_peak, local_sum, local_out = local_attention(
-            queries, forget_log, kv_cache[layer_id], decay_cache[layer_id], owner, live, member
+            queries, forget_log, layer_slice(kv_cache, layer_id), decay_cache[layer_id], owner, live, member
         )
         row_peak, row_sum, row_out = merge_pages(local_peak, local_sum, local_out)
         own_score = (

time: 178 us -> 181 us (1.017)
  Pallas kernels: 0 us -> 18 us
  local copies, waits for them, and re-layouts: 24.7 us -> 9.83 us
    pallas_call x0 -> x2, Pallas kernels: none -> 18 us  [layer_slice(): pl.pallas_call(copy_block, grid=(slots // block,), in_specs=[pl.BlockSpec...]
    slice x1 -> x0, local copies, waits for them, and re-layouts: 14.9 us -> none  [local(): kv_cache[layer_id]]
    ppermute x26, waiting for transfers between devices: 28.8 us -> 34.3 us  [exchange(): return lax.ppermute(value, axis, [(i, i ^ partner) for i in range(count)])]
    ppermute x6, waiting for transfers between devices: 4.44 us -> 0.02 us  [xor_sum(): lax.ppermute(value, axis, [(i, i ^ k) for i in range(count)])]
  transfers between devices with their start and end apart: 35 -> 35, of which waited for: 26 -> 25; matrix products, arithmetic and copies ran while one was open for 11% -> 3% of each run, Pallas kernels for 0% -> 10%
where the time goes in v9:
time: 181 us
  starting transfers between devices  41.2 us (23%)
  waiting for transfers between devices  36.6 us (20%)
  blocking collectives  35 us (19%)
  matrix products  30.7 us (17%)
  Pallas kernels  18 us (10%)
  local copies, waits for them, and re-layouts  9.83 us (5%)
  other arithmetic  7.7 us (4%)
    ppermute x26, waiting for transfers between devices, exchange(): return lax.ppermute(value, axis, [(i, i ^ partner) for i in range(count)])  34.3 us
    ppermute x26, starting transfers between devices, exchange(): return lax.ppermute(value, axis, [(i, i ^ partner) for i in range(count)])  29.6 us
    all_gather x2, blocking collectives, gather_sum(): return jnp.sum(lax.all_gather(value, axis).astype(jnp.float32), axis=0)  21.3 us
    pallas_call x2, Pallas kernels, layer_slice(): pl.pallas_call(copy_block, grid=(slots // block,), in_specs=[pl.BlockSpec...  18 us
    all_to_all x1, blocking collectives, local(): pieces = lax.all_to_all(pieces, 'gx', 1, 1, tiled=True).astype(jnp.float32)  13.8 us
    dot_general x2, matrix products, local_attention(): jnp.einsum('pthc,pkhc->pkt', kv_layer, query_block, preferred_element_typ...  11.7 us
    dot_general x2, matrix products, local_attention(): jnp.einsum('pkt,pthc->pkhc', weights.astype(jnp.bfloat16), kv_layer, pref...  9.35 us
    ppermute x6, starting transfers between devices, xor_sum(): lax.ppermute(value, axis, [(i, i ^ k) for i in range(count)])  8.1 us
  transfers between devices with their start and end apart: 35, of which 25 were waited for; matrix products, arithmetic and copies ran while one was open for 3% of the time, Pallas kernels for 10%

profile of v9, /device:TPU:0, one launch (start us, length us, event | category | flops | bytes accessed | tf_op | source)
XLA Modules:
  0.0 180.5 jit_solution(7182569528696389211)
XLA Ops:
  2.3 1.3 convolution_convert_fusion.2
  4.6 3.0 %collective-permute-start = (bf16[64,388]{0,1:T(8,128)(2,1)S(1)}, bf16[64,388]{0,1:T(8,128)(2,1)S(1)}, u32[]{:S(2)}, u32[]{:S(2)}) collective-permute-start(bf16[64,388]{0,1:T(8,128)(2,1)S(1)} %pad_maximum_fusion.1), channel_id=1, source_target_pairs={{0,8},{8,0},{16,24},{24,16},{1,9},{9,1},{17,25},{25,17},{2,10},{10... | collective-permute-start | bytes 149000 | tf_op jit(solution)/shard_map/ppermute | solution.py:25
  7.6 1.5 collective-permute-start.1
  12.7 9.0 %shard_map.175 = bf16[128,128,2,128]{3,2,1,0:T(2,128)(2,1)} custom-call(bf16[2,128,128,2,128]{4,3,2,1,0:T(2,128)(2,1)} %source.3), custom_call_target="tpu_custom_call" | custom-call | bytes 16777216 | tf_op jit(solution)/shard_map/pallas_call | solution.py:84
  23.6 5.9 %fusion.198 = (f32[128,2]{1,0:T(8,128)S(1)}, f32[128,2,128]{2,1,0:T(2,128)S(1)}) fusion(f32[128,2]{1,0:T(8,128)S(1)} %gather_fusion.1, f32[2,128,2,128]{3,2,1,0:T(2,128)S(1)} %copy-done.10, bf16[128,128,2,128]{3,2,1,0:T(2,128)(2,1)} %shard_map.175, bf16[128,2,128]{2,1,0:T(2,128)(2,1)S(1)} %concatenate.33, bf16[2,2]{0,1:T(2,128)(2,1)S(1)} %compare_convert_fusion, ...), kind=kOutput, calls=%fused_computation.327 | convolution fusion | flops 17202944 | bytes 8734728 | tf_op jit(solution)/shard_map/pthc,pkhc->pkt/dot_general | solution.py:127
  30.9 4.7 %fusion.4 = f32[128,2,2,128]{3,1,2,0:T(2,128)S(1)} fusion(bf16[128,128,2,128]{3,2,1,0:T(2,128)(2,1)} %shard_map.175, f32[128,2,128]{2,1,0:T(2,128)S(1)} %get-tuple-element.57, pred[128,128]{1,0:T(8,128)(4,1)S(1)} %fusion.117, f32[128,2]{1,0:T(8,128)S(1)} %gather_fusion.2), kind=kOutput, calls=%fused_computation.10 | convolution fusion | flops 16875520 | bytes 8799232 | tf_op jit(solution)/shard_map/pkt,pthc->pkhc/dot_general | solution.py:137
  36.5 2.0 %collective-permute-start.3 = (f32[64,2,66]{0,1,2:T(2,128)S(1)}, f32[64,2,66]{0,1,2:T(2,128)S(1)}, u32[]{:S(2)}, u32[]{:S(2)}) collective-permute-start(f32[64,2,66]{0,1,2:T(2,128)S(1)} %pad_maximum_fusion.3), channel_id=1, source_target_pairs={{0,8},{8,0},{16,24},{24,16},{1,9},{9,1},{17,25},{25,17},{2,10},{10... | collective-permute-start | bytes 101384 | tf_op jit(solution)/shard_map/ppermute | solution.py:42
  38.5 1.5 collective-permute-start.4
  40.8 2.6 %collective-permute-done.4 = f32[64,2,66]{0,1,2:T(2,128)S(1)} collective-permute-done((f32[64,2,66]{0,1,2:T(2,128)S(1)}, f32[64,2,66]{0,1,2:T(2,128)S(1)}, u32[]{:S(2)}, u32[]{:S(2)}) %collective-permute-start.4) | collective-permute-done | bytes 33824 | tf_op jit(solution)/shard_map/ppermute | solution.py:42
  43.4 1.8 collective-permute-done.5
  45.8 1.2 collective-permute-done.6
  47.1 1.6 collective-permute-start.7
  48.7 2.6 %collective-permute-start.8 = (bf16[64,384]{1,0:T(8,128)(2,1)S(1)}, bf16[64,384]{1,0:T(8,128)(2,1)S(1)}, u32[]{:S(2)}, u32[]{:S(2)}) collective-permute-start(bf16[64,384]{1,0:T(8,128)(2,1)S(1)} %add_convert_fusion.3), channel_id=1, source_target_pairs={{0,4},{1,5},{2,6},{3,7},{4,0},{5,1},{6,2},{7,3},{8,12},{9,13},{10,... | collective-permute-start | bytes 147464 | tf_op jit(solution)/shard_map/ppermute | solution.py:42
  51.6 3.1 %collective-permute-done.8 = bf16[64,384]{1,0:T(8,128)(2,1)S(1)} collective-permute-done((bf16[64,384]{1,0:T(8,128)(2,1)S(1)}, bf16[64,384]{1,0:T(8,128)(2,1)S(1)}, u32[]{:S(2)}, u32[]{:S(2)}) %collective-permute-start.8) | collective-permute-done | bytes 49184 | tf_op jit(solution)/shard_map/ppermute | solution.py:42
  54.6 2.6 %collective-permute-done.9 = bf16[64,384]{1,0:T(8,128)(2,1)S(1)} collective-permute-done((bf16[64,384]{1,0:T(8,128)(2,1)S(1)}, bf16[64,384]{1,0:T(8,128)(2,1)S(1)}, u32[]{:S(2)}, u32[]{:S(2)}) %collective-permute-start.9) | collective-permute-done | bytes 49184 | tf_op jit(solution)/shard_map/ppermute | solution.py:42
  58.1 9.9 %all-gather = bf16[256,1026]{1,0:T(8,128)(2,1)S(1)} all-gather(bf16[64,1026]{1,0:T(8,128)(2,1)S(1)} %concatenate.35), channel_id=2, replica_groups=mesh['gx'=4,'gy'=8] {'gx'}, dimensions={0}, use_global_device_ids=true | all-gather | bytes 656640 | tf_op jit(solution)/shard_map/all_gather | solution.py:19
  68.4 1.3 convolution_convert_fusion.10
  69.7 1.2 collective-permute-done.10
  71.0 1.7 collective-permute-start.12
  72.7 2.7 %collective-permute-start.13 = (bf16[64,384]{1,0:T(8,128)(2,1)S(1)}, bf16[64,384]{1,0:T(8,128)(2,1)S(1)}, u32[]{:S(2)}, u32[]{:S(2)}) collective-permute-start(bf16[64,384]{1,0:T(8,128)(2,1)S(1)} %add_convert_fusion.2), channel_id=1, source_target_pairs={{0,6},{1,7},{2,4},{3,5},{4,2},{5,3},{6,0},{7,1},{8,14},{9,15},{10,... | collective-permute-start | bytes 147464 | tf_op jit(solution)/shard_map/ppermute | solution.py:42
  75.8 2.2 %collective-permute-done.12 = bf16[64,384]{1,0:T(8,128)(2,1)S(1)} collective-permute-done((bf16[64,384]{1,0:T(8,128)(2,1)S(1)}, bf16[64,384]{1,0:T(8,128)(2,1)S(1)}, u32[]{:S(2)}, u32[]{:S(2)}) %collective-permute-start.12) | collective-permute-done | bytes 49184 | tf_op jit(solution)/shard_map/ppermute | solution.py:42
  79.3 1.8 collective-permute-start.14
  81.4 1.5 collective-permute-start.16
  82.9 9.0 %shard_map.176 = bf16[128,128,2,128]{3,2,1,0:T(2,128)(2,1)} custom-call(bf16[2,128,128,2,128]{4,3,2,1,0:T(2,128)(2,1)} %source.3), custom_call_target="tpu_custom_call" | custom-call | bytes 16777216 | tf_op jit(solution)/shard_map/pallas_call | solution.py:84
  93.8 5.8 %fusion.199 = (f32[128,2]{1,0:T(8,128)S(1)}, f32[128,2,128]{2,1,0:T(2,128)S(1)}) fusion(f32[128,2]{1,0:T(8,128)S(1)} %gather_fusion.4, f32[2,128,2,128]{3,2,1,0:T(2,128)S(1)} %copy-done.10, bf16[128,128,2,128]{3,2,1,0:T(2,128)(2,1)} %shard_map.176, bf16[128,2,128]{2,1,0:T(2,128)(2,1)S(1)} %concatenate.37, bf16[2,2]{0,1:T(2,128)(2,1)S(1)} %compare_convert_fusion, ...), kind=kOutput, calls=%fused_computation.328 | convolution fusion | flops 17202944 | bytes 8734728 | tf_op jit(solution)/shard_map/pthc,pkhc->pkt/dot_general | solution.py:127
  100.9 4.7 %fusion = f32[128,2,2,128]{3,1,2,0:T(2,128)S(1)} fusion(bf16[128,128,2,128]{3,2,1,0:T(2,128)(2,1)} %shard_map.176, f32[128,2,128]{2,1,0:T(2,128)S(1)} %get-tuple-element.59, pred[128,128]{1,0:T(8,128)(4,1)S(1)} %fusion.117, f32[128,2]{1,0:T(8,128)S(1)} %gather_fusion.5), kind=kOutput, calls=%fused_computation.6 | convolution fusion | flops 16875520 | bytes 8799232 | tf_op jit(solution)/shard_map/pkt,pthc->pkhc/dot_general | solution.py:137
  106.5 1.8 collective-permute-start.17
  108.6 1.5 collective-permute-start.19
  111.0 1.5 collective-permute-done.18
  112.6 1.2 collective-permute-done.19
  114.4 1.2 collective-permute-done.20
  115.6 1.2 collective-permute-start.21
  116.8 2.0 %collective-permute-start.22 = (bf16[64,384]{1,0:T(8,128)(2,1)S(1)}, bf16[64,384]{1,0:T(8,128)(2,1)S(1)}, u32[]{:S(2)}, u32[]{:S(2)}) collective-permute-start(bf16[64,384]{1,0:T(8,128)(2,1)S(1)} %add_convert_fusion.1), channel_id=1, source_target_pairs={{0,4},{1,5},{2,6},{3,7},{4,0},{5,1},{6,2},{7,3},{8,12},{9,13},{10,... | collective-permute-start | bytes 147464 | tf_op jit(solution)/shard_map/ppermute | solution.py:42
  118.9 1.2 collective-permute-start.23
  120.1 2.7 %collective-permute-done.22 = bf16[64,384]{1,0:T(8,128)(2,1)S(1)} collective-permute-done((bf16[64,384]{1,0:T(8,128)(2,1)S(1)}, bf16[64,384]{1,0:T(8,128)(2,1)S(1)}, u32[]{:S(2)}, u32[]{:S(2)}) %collective-permute-start.22) | collective-permute-done | bytes 49184 | tf_op jit(solution)/shard_map/ppermute | solution.py:42
  122.8 1.9 %collective-permute-done.23 = bf16[64,384]{1,0:T(8,128)(2,1)S(1)} collective-permute-done((bf16[64,384]{1,0:T(8,128)(2,1)S(1)}, bf16[64,384]{1,0:T(8,128)(2,1)S(1)}, u32[]{:S(2)}, u32[]{:S(2)}) %collective-permute-start.23) | collective-permute-done | bytes 49184 | tf_op jit(solution)/shard_map/ppermute | solution.py:42
  125.6 11.3 %all-gather.1 = bf16[256,1026]{1,0:T(8,128)(2,1)S(1)} all-gather(bf16[64,1026]{1,0:T(8,128)(2,1)S(1)} %concatenate.39), channel_id=3, replica_groups=mesh['gx'=4,'gy'=8] {'gx'}, dimensions={0}, use_global_device_ids=true | all-gather | bytes 656640 | tf_op jit(solution)/shard_map/all_gather | solution.py:19
  137.7 1.2 collective-permute-done.24
  139.0 1.7 collective-permute-start.26
  140.7 2.7 %collective-permute-start.27 = (bf16[64,384]{1,0:T(8,128)(2,1)S(1)}, bf16[64,384]{1,0:T(8,128)(2,1)S(1)}, u32[]{:S(2)}, u32[]{:S(2)}) collective-permute-start(bf16[64,384]{1,0:T(8,128)(2,1)S(1)} %add_convert_fusion), channel_id=1, source_target_pairs={{0,6},{1,7},{2,4},{3,5},{4,2},{5,3},{6,0},{7,1},{8,14},{9,15},{10,... | collective-permute-start | bytes 147464 | tf_op jit(solution)/shard_map/ppermute | solution.py:42
  143.7 2.2 %collective-permute-done.26 = bf16[64,384]{1,0:T(8,128)(2,1)S(1)} collective-permute-done((bf16[64,384]{1,0:T(8,128)(2,1)S(1)}, bf16[64,384]{1,0:T(8,128)(2,1)S(1)}, u32[]{:S(2)}, u32[]{:S(2)}) %collective-permute-start.26) | collective-permute-done | bytes 49184 | tf_op jit(solution)/shard_map/ppermute | solution.py:42
  146.8 3.3 %convolution_convert_fusion = bf16[64,6144]{1,0:T(8,128)(2,1)S(1)} fusion(bf16[384,6144]{1,0:T(8,128)(2,1)} %param.27, f32[64,384]{1,0:T(8,128)S(1)} %get-tuple-element.10, f32[384]{0:T(512)S(1)} %copy-done.5), kind=kOutput, calls=%fused_computation.14 | convolution fusion | flops 302432256 | bytes 5604864 | tf_op jit(solution)/shard_map/dot_general | solution.py:259
  150.4 13.8 %all_to_all.5 = bf16[64,4,1538]{2,0,1:T(8,128)(2,1)S(1)} all-to-all(bf16[64,4,1538]{2,0,1:T(8,128)(2,1)S(1)} %pad_maximum_fusion), channel_id=1, replica_groups=mesh['gx'=4,'gy'=8] {'gx'}, dimensions={1} | all-to-all | bytes 1574912 | tf_op jit(solution)/shard_map/all_to_all | solution.py:270
  166.1 2.2 %collective-permute-start.30 = (f32[64]{0:T(128)S(1)}, f32[64]{0:T(128)S(1)}, u32[]{:S(2)}, u32[]{:S(2)}) collective-permute-start(f32[64]{0:T(128)S(1)} %get-tuple-element.7), channel_id=1, source_target_pairs={{0,24},{8,16},{16,8},{24,0},{1,25},{9,17},{17,9},{25,1},{2,26},{10... | collective-permute-start | bytes 776 | tf_op jit(solution)/shard_map/ppermute | solution.py:70
  169.1 1.5 collective-permute-done.30
  171.7 2.9 %collective-permute-start.33 = (f32[64]{0:T(128)S(1)}, f32[64]{0:T(128)S(1)}, u32[]{:S(2)}, u32[]{:S(2)}) collective-permute-start(f32[64]{0:T(128)S(1)} %max.146), channel_id=1, source_target_pairs={{0,4},{1,5},{2,6},{3,7},{4,0},{5,1},{6,2},{7,3},{8,12},{9,13},{10,... | collective-permute-start | bytes 776 | tf_op jit(solution)/shard_map/ppermute | solution.py:42
  174.7 1.4 collective-permute-start.34
  176.8 3.2 %collective-permute-done.34 = f32[64]{0:T(128)S(1)} collective-permute-done((f32[64]{0:T(128)S(1)}, f32[64]{0:T(128)S(1)}, u32[]{:S(2)}, u32[]{:S(2)}) %collective-permute-start.34) | collective-permute-done | bytes 288 | tf_op jit(solution)/shard_map/ppermute | solution.py:42
  (199 shorter events, 29.3 us)
Async XLA Ops:
  4.6 17.1 %collective-permute-start = (bf16[64,388]{0,1:T(8,128)(2,1)S(1)}, bf16[64,388]{0,1:T(8,128)(2,1)S(1)}, u32[]{:S(2)}, u32[]{:S(2)}) collective-permute-start(bf16[64,388]{0,1:T(8,128)(2,1)S(1)} %pad_maximum_fusion.1), channel_id=1, source_target_pairs={{0,8},{8,0},{16,24},{24,16},{1,9},{9,1},{17,25},{25,17},{2,10},{10... | collective-permute-start | bytes 149000 | tf_op jit(solution)/shard_map/ppermute | solution.py:25
  7.6 14.1 %collective-permute-start.1 = (bf16[64,388]{0,1:T(8,128)(2,1)S(1)}, bf16[64,388]{0,1:T(8,128)(2,1)S(1)}, u32[]{:S(2)}, u32[]{:S(2)}) collective-permute-start(bf16[64,388]{0,1:T(8,128)(2,1)S(1)} %pad_maximum_fusion.1), channel_id=1, source_target_pairs={{0,16},{8,24},{16,0},{24,8},{1,17},{9,25},{17,1},{25,9},{2,18},{10... | collective-permute-start | bytes 149000 | tf_op jit(solution)/shard_map/ppermute | solution.py:25
  9.1 12.6 %collective-permute-start.2 = (bf16[64,388]{0,1:T(8,128)(2,1)S(1)}, bf16[64,388]{0,1:T(8,128)(2,1)S(1)}, u32[]{:S(2)}, u32[]{:S(2)}) collective-permute-start(bf16[64,388]{0,1:T(8,128)(2,1)S(1)} %pad_maximum_fusion.1), channel_id=1, source_target_pairs={{0,24},{8,16},{16,8},{24,0},{1,25},{9,17},{17,9},{25,1},{2,26},{10... | collective-permute-start | bytes 149000 | tf_op jit(solution)/shard_map/ppermute | solution.py:25
  12.7 11.0 %copy-start.10 = (f32[2,128,2,128]{3,2,1,0:T(2,128)S(1)}, f32[2,128,2,128]{3,2,1,0:T(2,128)}, u32[]{:S(2)}) copy-start(f32[2,128,2,128]{3,2,1,0:T(2,128)} %param.29) | copy-start | bytes 786436
  23.6 22.0 %copy-start.4 = (bf16[2,128,384]{2,1,0:T(8,128)(2,1)S(1)}, bf16[2,128,384]{2,1,0:T(8,128)(2,1)}, u32[]{:S(2)}) copy-start(bf16[2,128,384]{2,1,0:T(8,128)(2,1)} %param.23) | copy-start | bytes 589828
  23.6 27.9 %copy-start.6 = (f32[2,384]{1,0:T(2,128)S(1)}, f32[2,384]{1,0:T(2,128)}, u32[]{:S(2)}) copy-start(f32[2,384]{1,0:T(2,128)} %param.18) | copy-start | bytes 9220
  23.6 33.6 %copy-start.3 = (bf16[64,384]{1,0:T(8,128)(2,1)S(1)}, bf16[64,384]{1,0:T(8,128)(2,1)}, u32[]{:S(2)}) copy-start(bf16[64,384]{1,0:T(8,128)(2,1)} %param.16) | copy-start | bytes 147460
  29.5 27.8 %copy-start = (bf16[2,384,512]{2,1,0:T(8,128)(2,1)S(1)}, bf16[2,384,512]{2,1,0:T(8,128)(2,1)}, u32[]{:S(2)}) copy-start(bf16[2,384,512]{2,1,0:T(8,128)(2,1)} %param.25) | copy-start | bytes 2359300
  29.5 28.0 %copy-start.1 = (bf16[2,384,512]{2,1,0:T(8,128)(2,1)S(1)}, bf16[2,384,512]{2,1,0:T(8,128)(2,1)}, u32[]{:S(2)}) copy-start(bf16[2,384,512]{2,1,0:T(8,128)(2,1)} %param.24) | copy-start | bytes 2359300
  30.9 48.0 %copy-start.2 = (bf16[2,384,384]{2,1,0:T(8,128)(2,1)S(1)}, bf16[2,384,384]{2,1,0:T(8,128)(2,1)}, u32[]{:S(2)}) copy-start(bf16[2,384,384]{2,1,0:T(8,128)(2,1)} %param.20) | copy-start | bytes 1769476
  30.9 48.3 %copy-start.8 = (bf16[2,384,2]{1,2,0:T(2,128)(2,1)S(1)}, bf16[2,384,2]{1,2,0:T(2,128)(2,1)}, u32[]{:S(2)}) copy-start(bf16[2,384,2]{1,2,0:T(2,128)(2,1)} %param.21) | copy-start | bytes 9220
  36.5 4.4 %collective-permute-start.3 = (f32[64,2,66]{0,1,2:T(2,128)S(1)}, f32[64,2,66]{0,1,2:T(2,128)S(1)}, u32[]{:S(2)}, u32[]{:S(2)}) collective-permute-start(f32[64,2,66]{0,1,2:T(2,128)S(1)} %pad_maximum_fusion.3), channel_id=1, source_target_pairs={{0,8},{8,0},{16,24},{24,16},{1,9},{9,1},{17,25},{25,17},{2,10},{10... | collective-permute-start | bytes 101384 | tf_op jit(solution)/shard_map/ppermute | solution.py:42
  38.5 4.9 %collective-permute-start.4 = (f32[64,2,66]{0,1,2:T(2,128)S(1)}, f32[64,2,66]{0,1,2:T(2,128)S(1)}, u32[]{:S(2)}, u32[]{:S(2)}) collective-permute-start(f32[64,2,66]{0,1,2:T(2,128)S(1)} %pad_maximum_fusion.3), channel_id=1, source_target_pairs={{0,16},{8,24},{16,0},{24,8},{1,17},{9,25},{17,1},{25,9},{2,18},{10... | collective-permute-start | bytes 101384 | tf_op jit(solution)/shard_map/ppermute | solution.py:42
  40.0 5.2 %collective-permute-start.5 = (f32[64,2,66]{0,1,2:T(2,128)S(1)}, f32[64,2,66]{0,1,2:T(2,128)S(1)}, u32[]{:S(2)}, u32[]{:S(2)}) collective-permute-start(f32[64,2,66]{0,1,2:T(2,128)S(1)} %pad_maximum_fusion.3), channel_id=1, source_target_pairs={{0,24},{8,16},{16,8},{24,0},{1,25},{9,17},{17,9},{25,1},{2,26},{10... | collective-permute-start | bytes 101384 | tf_op jit(solution)/shard_map/ppermute | solution.py:42
  45.8 1.3 collective-permute-start.6
  47.1 4.5 %collective-permute-start.7 = (bf16[64,384]{1,0:T(8,128)(2,1)S(1)}, bf16[64,384]{1,0:T(8,128)(2,1)S(1)}, u32[]{:S(2)}, u32[]{:S(2)}) collective-permute-start(bf16[64,384]{1,0:T(8,128)(2,1)S(1)} %add_convert_fusion.3), channel_id=1, source_target_pairs={{0,2},{1,3},{2,0},{3,1},{4,6},{5,7},{6,4},{7,5},{8,10},{9,11},{10,... | collective-permute-start | bytes 147464 | tf_op jit(solution)/shard_map/ppermute | solution.py:42
  48.7 5.9 %collective-permute-start.8 = (bf16[64,384]{1,0:T(8,128)(2,1)S(1)}, bf16[64,384]{1,0:T(8,128)(2,1)S(1)}, u32[]{:S(2)}, u32[]{:S(2)}) collective-permute-start(bf16[64,384]{1,0:T(8,128)(2,1)S(1)} %add_convert_fusion.3), channel_id=1, source_target_pairs={{0,4},{1,5},{2,6},{3,7},{4,0},{5,1},{6,2},{7,3},{8,12},{9,13},{10,... | collective-permute-start | bytes 147464 | tf_op jit(solution)/shard_map/ppermute | solution.py:42
  51.3 5.9 %collective-permute-start.9 = (bf16[64,384]{1,0:T(8,128)(2,1)S(1)}, bf16[64,384]{1,0:T(8,128)(2,1)S(1)}, u32[]{:S(2)}, u32[]{:S(2)}) collective-permute-start(bf16[64,384]{1,0:T(8,128)(2,1)S(1)} %add_convert_fusion.3), channel_id=1, source_target_pairs={{0,6},{1,7},{2,4},{3,5},{4,2},{5,3},{6,0},{7,1},{8,14},{9,15},{10,... | collective-permute-start | bytes 147464 | tf_op jit(solution)/shard_map/ppermute | solution.py:42
  69.6 1.3 collective-permute-start.10
  70.9 4.9 %collective-permute-start.11 = (bf16[64,384]{1,0:T(8,128)(2,1)S(1)}, bf16[64,384]{1,0:T(8,128)(2,1)S(1)}, u32[]{:S(2)}, u32[]{:S(2)}) collective-permute-start(bf16[64,384]{1,0:T(8,128)(2,1)S(1)} %add_convert_fusion.2), channel_id=1, source_target_pairs={{0,2},{1,3},{2,0},{3,1},{4,6},{5,7},{6,4},{7,5},{8,10},{9,11},{10,... | collective-permute-start | bytes 147464 | tf_op jit(solution)/shard_map/ppermute | solution.py:42
  71.0 7.0 %collective-permute-start.12 = (bf16[64,384]{1,0:T(8,128)(2,1)S(1)}, bf16[64,384]{1,0:T(8,128)(2,1)S(1)}, u32[]{:S(2)}, u32[]{:S(2)}) collective-permute-start(bf16[64,384]{1,0:T(8,128)(2,1)S(1)} %add_convert_fusion.2), channel_id=1, source_target_pairs={{0,4},{1,5},{2,6},{3,7},{4,0},{5,1},{6,2},{7,3},{8,12},{9,13},{10,... | collective-permute-start | bytes 147464 | tf_op jit(solution)/shard_map/ppermute | solution.py:42
  72.7 5.9 %collective-permute-start.13 = (bf16[64,384]{1,0:T(8,128)(2,1)S(1)}, bf16[64,384]{1,0:T(8,128)(2,1)S(1)}, u32[]{:S(2)}, u32[]{:S(2)}) collective-permute-start(bf16[64,384]{1,0:T(8,128)(2,1)S(1)} %add_convert_fusion.2), channel_id=1, source_target_pairs={{0,6},{1,7},{2,4},{3,5},{4,2},{5,3},{6,0},{7,1},{8,14},{9,15},{10,... | collective-permute-start | bytes 147464 | tf_op jit(solution)/shard_map/ppermute | solution.py:42
  79.3 12.5 %collective-permute-start.14 = (bf16[64,388]{0,1:T(8,128)(2,1)S(1)}, bf16[64,388]{0,1:T(8,128)(2,1)S(1)}, u32[]{:S(2)}, u32[]{:S(2)}) collective-permute-start(bf16[64,388]{0,1:T(8,128)(2,1)S(1)} %pad_maximum_fusion.2), channel_id=1, source_target_pairs={{0,8},{8,0},{16,24},{24,16},{1,9},{9,1},{17,25},{25,17},{2,10},{10... | collective-permute-start | bytes 149000 | tf_op jit(solution)/shard_map/ppermute | solution.py:25
  81.1 10.8 %collective-permute-start.15 = (bf16[64,388]{0,1:T(8,128)(2,1)S(1)}, bf16[64,388]{0,1:T(8,128)(2,1)S(1)}, u32[]{:S(2)}, u32[]{:S(2)}) collective-permute-start(bf16[64,388]{0,1:T(8,128)(2,1)S(1)} %pad_maximum_fusion.2), channel_id=1, source_target_pairs={{0,16},{8,24},{16,0},{24,8},{1,17},{9,25},{17,1},{25,9},{2,18},{10... | collective-permute-start | bytes 149000 | tf_op jit(solution)/shard_map/ppermute | solution.py:25
  81.4 10.5 %collective-permute-start.16 = (bf16[64,388]{0,1:T(8,128)(2,1)S(1)}, bf16[64,388]{0,1:T(8,128)(2,1)S(1)}, u32[]{:S(2)}, u32[]{:S(2)}) collective-permute-start(bf16[64,388]{0,1:T(8,128)(2,1)S(1)} %pad_maximum_fusion.2), channel_id=1, source_target_pairs={{0,24},{8,16},{16,8},{24,0},{1,25},{9,17},{17,9},{25,1},{2,26},{10... | collective-permute-start | bytes 149000 | tf_op jit(solution)/shard_map/ppermute | solution.py:25
  99.6 37.7 %copy-start.9 = (bf16[2,512,384]{2,1,0:T(8,128)(2,1)S(1)}, bf16[2,512,384]{2,1,0:T(8,128)(2,1)}, u32[]{:S(2)}) copy-start(bf16[2,512,384]{2,1,0:T(8,128)(2,1)} %param.26) | copy-start | bytes 2359300
  100.9 45.9 %copy-start.5 = (f32[384]{0:T(512)S(1)}, f32[384]{0:T(512)}, u32[]{:S(2)}) copy-start(f32[384]{0:T(512)} %param.19) | copy-start | bytes 4612
  106.5 4.5 %collective-permute-start.17 = (f32[64,2,66]{0,1,2:T(2,128)S(1)}, f32[64,2,66]{0,1,2:T(2,128)S(1)}, u32[]{:S(2)}, u32[]{:S(2)}) collective-permute-start(f32[64,2,66]{0,1,2:T(2,128)S(1)} %pad_maximum_fusion.4), channel_id=1, source_target_pairs={{0,8},{8,0},{16,24},{24,16},{1,9},{9,1},{17,25},{25,17},{2,10},{10... | collective-permute-start | bytes 101384 | tf_op jit(solution)/shard_map/ppermute | solution.py:42
  108.3 4.3 %collective-permute-start.18 = (f32[64,2,66]{0,1,2:T(2,128)S(1)}, f32[64,2,66]{0,1,2:T(2,128)S(1)}, u32[]{:S(2)}, u32[]{:S(2)}) collective-permute-start(f32[64,2,66]{0,1,2:T(2,128)S(1)} %pad_maximum_fusion.4), channel_id=1, source_target_pairs={{0,16},{8,24},{16,0},{24,8},{1,17},{9,25},{17,1},{25,9},{2,18},{10... | collective-permute-start | bytes 101384 | tf_op jit(solution)/shard_map/ppermute | solution.py:42
  108.6 5.2 %collective-permute-start.19 = (f32[64,2,66]{0,1,2:T(2,128)S(1)}, f32[64,2,66]{0,1,2:T(2,128)S(1)}, u32[]{:S(2)}, u32[]{:S(2)}) collective-permute-start(f32[64,2,66]{0,1,2:T(2,128)S(1)} %pad_maximum_fusion.4), channel_id=1, source_target_pairs={{0,24},{8,16},{16,8},{24,0},{1,25},{9,17},{17,9},{25,1},{2,26},{10... | collective-permute-start | bytes 101384 | tf_op jit(solution)/shard_map/ppermute | solution.py:42
  114.3 1.3 collective-permute-start.20
  115.6 4.5 %collective-permute-start.21 = (bf16[64,384]{1,0:T(8,128)(2,1)S(1)}, bf16[64,384]{1,0:T(8,128)(2,1)S(1)}, u32[]{:S(2)}, u32[]{:S(2)}) collective-permute-start(bf16[64,384]{1,0:T(8,128)(2,1)S(1)} %add_convert_fusion.1), channel_id=1, source_target_pairs={{0,2},{1,3},{2,0},{3,1},{4,6},{5,7},{6,4},{7,5},{8,10},{9,11},{10,... | collective-permute-start | bytes 147464 | tf_op jit(solution)/shard_map/ppermute | solution.py:42
  116.8 6.0 %collective-permute-start.22 = (bf16[64,384]{1,0:T(8,128)(2,1)S(1)}, bf16[64,384]{1,0:T(8,128)(2,1)S(1)}, u32[]{:S(2)}, u32[]{:S(2)}) collective-permute-start(bf16[64,384]{1,0:T(8,128)(2,1)S(1)} %add_convert_fusion.1), channel_id=1, source_target_pairs={{0,4},{1,5},{2,6},{3,7},{4,0},{5,1},{6,2},{7,3},{8,12},{9,13},{10,... | collective-permute-start | bytes 147464 | tf_op jit(solution)/shard_map/ppermute | solution.py:42
  118.9 5.9 %collective-permute-start.23 = (bf16[64,384]{1,0:T(8,128)(2,1)S(1)}, bf16[64,384]{1,0:T(8,128)(2,1)S(1)}, u32[]{:S(2)}, u32[]{:S(2)}) collective-permute-start(bf16[64,384]{1,0:T(8,128)(2,1)S(1)} %add_convert_fusion.1), channel_id=1, source_target_pairs={{0,6},{1,7},{2,4},{3,5},{4,2},{5,3},{6,0},{7,1},{8,14},{9,15},{10,... | collective-permute-start | bytes 147464 | tf_op jit(solution)/shard_map/ppermute | solution.py:42
  137.6 1.3 collective-permute-start.24
  138.9 4.8 %collective-permute-start.25 = (bf16[64,384]{1,0:T(8,128)(2,1)S(1)}, bf16[64,384]{1,0:T(8,128)(2,1)S(1)}, u32[]{:S(2)}, u32[]{:S(2)}) collective-permute-start(bf16[64,384]{1,0:T(8,128)(2,1)S(1)} %add_convert_fusion), channel_id=1, source_target_pairs={{0,2},{1,3},{2,0},{3,1},{4,6},{5,7},{6,4},{7,5},{8,10},{9,11},{10,... | collective-permute-start | bytes 147464 | tf_op jit(solution)/shard_map/ppermute | solution.py:42
  139.0 6.9 %collective-permute-start.26 = (bf16[64,384]{1,0:T(8,128)(2,1)S(1)}, bf16[64,384]{1,0:T(8,128)(2,1)S(1)}, u32[]{:S(2)}, u32[]{:S(2)}) collective-permute-start(bf16[64,384]{1,0:T(8,128)(2,1)S(1)} %add_convert_fusion), channel_id=1, source_target_pairs={{0,4},{1,5},{2,6},{3,7},{4,0},{5,1},{6,2},{7,3},{8,12},{9,13},{10,... | collective-permute-start | bytes 147464 | tf_op jit(solution)/shard_map/ppermute | solution.py:42
  140.7 5.9 %collective-permute-start.27 = (bf16[64,384]{1,0:T(8,128)(2,1)S(1)}, bf16[64,384]{1,0:T(8,128)(2,1)S(1)}, u32[]{:S(2)}, u32[]{:S(2)}) collective-permute-start(bf16[64,384]{1,0:T(8,128)(2,1)S(1)} %add_convert_fusion), channel_id=1, source_target_pairs={{0,6},{1,7},{2,4},{3,5},{4,2},{5,3},{6,0},{7,1},{8,14},{9,15},{10,... | collective-permute-start | bytes 147464 | tf_op jit(solution)/shard_map/ppermute | solution.py:42
  164.7 15.8 %copy-start.7 = (f32[64]{0:T(128)}, f32[64]{0:T(128)S(1)}, u32[]{:S(2)}) copy-start(f32[64]{0:T(128)S(1)} %get-tuple-element.8) | copy-start | bytes 772
  164.7 3.6 %collective-permute-start.28 = (f32[64]{0:T(128)S(1)}, f32[64]{0:T(128)S(1)}, u32[]{:S(2)}, u32[]{:S(2)}) collective-permute-start(f32[64]{0:T(128)S(1)} %get-tuple-element.7), channel_id=1, source_target_pairs={{0,8},{8,0},{16,24},{24,16},{1,9},{9,1},{17,25},{25,17},{2,10},{10... | collective-permute-start | bytes 776 | tf_op jit(solution)/shard_map/ppermute | solution.py:70
  165.5 3.5 %collective-permute-start.29 = (f32[64]{0:T(128)S(1)}, f32[64]{0:T(128)S(1)}, u32[]{:S(2)}, u32[]{:S(2)}) collective-permute-start(f32[64]{0:T(128)S(1)} %get-tuple-element.7), channel_id=1, source_target_pairs={{0,16},{8,24},{16,0},{24,8},{1,17},{9,25},{17,1},{25,9},{2,18},{10... | collective-permute-start | bytes 776 | tf_op jit(solution)/shard_map/ppermute | solution.py:70
  166.1 4.4 %collective-permute-start.30 = (f32[64]{0:T(128)S(1)}, f32[64]{0:T(128)S(1)}, u32[]{:S(2)}, u32[]{:S(2)}) collective-permute-start(f32[64]{0:T(128)S(1)} %get-tuple-element.7), channel_id=1, source_target_pairs={{0,24},{8,16},{16,8},{24,0},{1,25},{9,17},{17,9},{25,1},{2,26},{10... | collective-permute-start | bytes 776 | tf_op jit(solution)/shard_map/ppermute | solution.py:70
  170.5 1.1 collective-permute-start.31
  171.7 5.1 %collective-permute-start.32 = (f32[64]{0:T(128)S(1)}, f32[64]{0:T(128)S(1)}, u32[]{:S(2)}, u32[]{:S(2)}) collective-permute-start(f32[64]{0:T(128)S(1)} %max.146), channel_id=1, source_target_pairs={{0,2},{1,3},{2,0},{3,1},{4,6},{5,7},{6,4},{7,5},{8,10},{9,11},{10,... | collective-permute-start | bytes 776 | tf_op jit(solution)/shard_map/ppermute | solution.py:42
  171.7 5.1 %collective-permute-start.33 = (f32[64]{0:T(128)S(1)}, f32[64]{0:T(128)S(1)}, u32[]{:S(2)}, u32[]{:S(2)}) collective-permute-start(f32[64]{0:T(128)S(1)} %max.146), channel_id=1, source_target_pairs={{0,4},{1,5},{2,6},{3,7},{4,0},{5,1},{6,2},{7,3},{8,12},{9,13},{10,... | collective-permute-start | bytes 776 | tf_op jit(solution)/shard_map/ppermute | solution.py:42
  174.7 5.3 %collective-permute-start.34 = (f32[64]{0:T(128)S(1)}, f32[64]{0:T(128)S(1)}, u32[]{:S(2)}, u32[]{:S(2)}) collective-permute-start(f32[64]{0:T(128)S(1)} %max.146), channel_id=1, source_target_pairs={{0,6},{1,7},{2,4},{3,5},{4,2},{5,3},{6,0},{7,1},{8,14},{9,15},{10,... | collective-permute-start | bytes 776 | tf_op jit(solution)/shard_map/ppermute | solution.py:42

commit v10 on v9

--- a/solution.py
+++ b/solution.py
@@ -80,7 +80,7 @@
 
 def layer_slice(cache, layer_id):
     layers, slots, tokens, heads, width = cache.shape
-    block = 16
+    block = 32
     return pl.pallas_call(
         copy_block,
         grid=(slots // block,),

time: 181 us -> 177 us (0.978)
  Pallas kernels: 18 us -> 14.2 us
    pallas_call x2, Pallas kernels: 18 us -> 14.2 us  [layer_slice(): pl.pallas_call(copy_block, grid=(slots // block,), in_specs=[pl.BlockSpec...]
  transfers between devices with their start and end apart: 35 -> 35, of which waited for: 25 -> 25; matrix products, arithmetic and copies ran while one was open for 3% -> 3% of each run, Pallas kernels for 10% -> 8%
where the time goes in v10:
time: 177 us
  starting transfers between devices  41.2 us (23%)
  waiting for transfers between devices  36.6 us (21%)
  blocking collectives  35 us (20%)
  matrix products  30.7 us (17%)
  Pallas kernels  14.2 us (8%)
  local copies, waits for them, and re-layouts  9.83 us (6%)
  other arithmetic  7.7 us (4%)
    ppermute x26, waiting for transfers between devices, exchange(): return lax.ppermute(value, axis, [(i, i ^ partner) for i in range(count)])  34.3 us
    ppermute x26, starting transfers between devices, exchange(): return lax.ppermute(value, axis, [(i, i ^ partner) for i in range(count)])  29.6 us
    all_gather x2, blocking collectives, gather_sum(): return jnp.sum(lax.all_gather(value, axis).astype(jnp.float32), axis=0)  21.3 us
    pallas_call x2, Pallas kernels, layer_slice(): pl.pallas_call(copy_block, grid=(slots // block,), in_specs=[pl.BlockSpec...  14.2 us
    all_to_all x1, blocking collectives, local(): pieces = lax.all_to_all(pieces, 'gx', 1, 1, tiled=True).astype(jnp.float32)  13.8 us
    dot_general x2, matrix products, local_attention(): jnp.einsum('pthc,pkhc->pkt', kv_layer, query_block, preferred_element_typ...  11.7 us
    dot_general x2, matrix products, local_attention(): jnp.einsum('pkt,pthc->pkhc', weights.astype(jnp.bfloat16), kv_layer, pref...  9.35 us
    ppermute x6, starting transfers between devices, xor_sum(): lax.ppermute(value, axis, [(i, i ^ k) for i in range(count)])  8.1 us
  transfers between devices with their start and end apart: 35, of which 25 were waited for; matrix products, arithmetic and copies ran while one was open for 3% of the time, Pallas kernels for 8%

profile of v10, /device:TPU:0, one launch (start us, length us, event | category | flops | bytes accessed | tf_op | source)
XLA Modules:
  0.0 176.7 jit_solution(4631141753327702122)
XLA Ops:
  2.3 1.3 convolution_convert_fusion.2
  4.6 3.0 %collective-permute-start = (bf16[64,388]{0,1:T(8,128)(2,1)S(1)}, bf16[64,388]{0,1:T(8,128)(2,1)S(1)}, u32[]{:S(2)}, u32[]{:S(2)}) collective-permute-start(bf16[64,388]{0,1:T(8,128)(2,1)S(1)} %pad_maximum_fusion.1), channel_id=1, source_target_pairs={{0,8},{8,0},{16,24},{24,16},{1,9},{9,1},{17,25},{25,17},{2,10},{10... | collective-permute-start | bytes 149000 | tf_op jit(solution)/shard_map/ppermute | solution.py:25
  7.6 1.5 collective-permute-start.1
  12.7 7.1 %shard_map.175 = bf16[128,128,2,128]{3,2,1,0:T(2,128)(2,1)} custom-call(bf16[2,128,128,2,128]{4,3,2,1,0:T(2,128)(2,1)} %source.3), custom_call_target="tpu_custom_call" | custom-call | bytes 16777216 | tf_op jit(solution)/shard_map/pallas_call | solution.py:84
  21.7 5.9 %fusion.198 = (f32[128,2]{1,0:T(8,128)S(1)}, f32[128,2,128]{2,1,0:T(2,128)S(1)}) fusion(f32[128,2]{1,0:T(8,128)S(1)} %gather_fusion.1, f32[2,128,2,128]{3,2,1,0:T(2,128)S(1)} %copy-done.10, bf16[128,128,2,128]{3,2,1,0:T(2,128)(2,1)} %shard_map.175, bf16[128,2,128]{2,1,0:T(2,128)(2,1)S(1)} %concatenate.33, bf16[2,2]{0,1:T(2,128)(2,1)S(1)} %compare_convert_fusion, ...), kind=kOutput, calls=%fused_computation.327 | convolution fusion | flops 17202944 | bytes 8734728 | tf_op jit(solution)/shard_map/pthc,pkhc->pkt/dot_general | solution.py:127
  29.0 4.7 %fusion.4 = f32[128,2,2,128]{3,1,2,0:T(2,128)S(1)} fusion(bf16[128,128,2,128]{3,2,1,0:T(2,128)(2,1)} %shard_map.175, f32[128,2,128]{2,1,0:T(2,128)S(1)} %get-tuple-element.57, pred[128,128]{1,0:T(8,128)(4,1)S(1)} %fusion.117, f32[128,2]{1,0:T(8,128)S(1)} %gather_fusion.2), kind=kOutput, calls=%fused_computation.10 | convolution fusion | flops 16875520 | bytes 8799232 | tf_op jit(solution)/shard_map/pkt,pthc->pkhc/dot_general | solution.py:137
  34.6 2.0 %collective-permute-start.3 = (f32[64,2,66]{0,1,2:T(2,128)S(1)}, f32[64,2,66]{0,1,2:T(2,128)S(1)}, u32[]{:S(2)}, u32[]{:S(2)}) collective-permute-start(f32[64,2,66]{0,1,2:T(2,128)S(1)} %pad_maximum_fusion.3), channel_id=1, source_target_pairs={{0,8},{8,0},{16,24},{24,16},{1,9},{9,1},{17,25},{25,17},{2,10},{10... | collective-permute-start | bytes 101384 | tf_op jit(solution)/shard_map/ppermute | solution.py:42
  36.6 1.5 collective-permute-start.4
  38.9 2.6 %collective-permute-done.4 = f32[64,2,66]{0,1,2:T(2,128)S(1)} collective-permute-done((f32[64,2,66]{0,1,2:T(2,128)S(1)}, f32[64,2,66]{0,1,2:T(2,128)S(1)}, u32[]{:S(2)}, u32[]{:S(2)}) %collective-permute-start.4) | collective-permute-done | bytes 33824 | tf_op jit(solution)/shard_map/ppermute | solution.py:42
  41.5 1.8 %collective-permute-done.5 = f32[64,2,66]{0,1,2:T(2,128)S(1)} collective-permute-done((f32[64,2,66]{0,1,2:T(2,128)S(1)}, f32[64,2,66]{0,1,2:T(2,128)S(1)}, u32[]{:S(2)}, u32[]{:S(2)}) %collective-permute-start.5) | collective-permute-done | bytes 33824 | tf_op jit(solution)/shard_map/ppermute | solution.py:42
  43.9 1.2 collective-permute-done.6
  45.2 1.6 collective-permute-start.7
  46.8 2.6 %collective-permute-start.8 = (bf16[64,384]{1,0:T(8,128)(2,1)S(1)}, bf16[64,384]{1,0:T(8,128)(2,1)S(1)}, u32[]{:S(2)}, u32[]{:S(2)}) collective-permute-start(bf16[64,384]{1,0:T(8,128)(2,1)S(1)} %add_convert_fusion.3), channel_id=1, source_target_pairs={{0,4},{1,5},{2,6},{3,7},{4,0},{5,1},{6,2},{7,3},{8,12},{9,13},{10,... | collective-permute-start | bytes 147464 | tf_op jit(solution)/shard_map/ppermute | solution.py:42
  49.7 3.1 %collective-permute-done.8 = bf16[64,384]{1,0:T(8,128)(2,1)S(1)} collective-permute-done((bf16[64,384]{1,0:T(8,128)(2,1)S(1)}, bf16[64,384]{1,0:T(8,128)(2,1)S(1)}, u32[]{:S(2)}, u32[]{:S(2)}) %collective-permute-start.8) | collective-permute-done | bytes 49184 | tf_op jit(solution)/shard_map/ppermute | solution.py:42
  52.7 2.6 %collective-permute-done.9 = bf16[64,384]{1,0:T(8,128)(2,1)S(1)} collective-permute-done((bf16[64,384]{1,0:T(8,128)(2,1)S(1)}, bf16[64,384]{1,0:T(8,128)(2,1)S(1)}, u32[]{:S(2)}, u32[]{:S(2)}) %collective-permute-start.9) | collective-permute-done | bytes 49184 | tf_op jit(solution)/shard_map/ppermute | solution.py:42
  56.2 9.9 %all-gather = bf16[256,1026]{1,0:T(8,128)(2,1)S(1)} all-gather(bf16[64,1026]{1,0:T(8,128)(2,1)S(1)} %concatenate.35), channel_id=2, replica_groups=mesh['gx'=4,'gy'=8] {'gx'}, dimensions={0}, use_global_device_ids=true | all-gather | bytes 656640 | tf_op jit(solution)/shard_map/all_gather | solution.py:19
  66.4 1.3 convolution_convert_fusion.10
  67.8 1.2 collective-permute-done.10
  69.1 1.7 collective-permute-start.12
  70.8 2.7 %collective-permute-start.13 = (bf16[64,384]{1,0:T(8,128)(2,1)S(1)}, bf16[64,384]{1,0:T(8,128)(2,1)S(1)}, u32[]{:S(2)}, u32[]{:S(2)}) collective-permute-start(bf16[64,384]{1,0:T(8,128)(2,1)S(1)} %add_convert_fusion.2), channel_id=1, source_target_pairs={{0,6},{1,7},{2,4},{3,5},{4,2},{5,3},{6,0},{7,1},{8,14},{9,15},{10,... | collective-permute-start | bytes 147464 | tf_op jit(solution)/shard_map/ppermute | solution.py:42
  73.9 2.2 %collective-permute-done.12 = bf16[64,384]{1,0:T(8,128)(2,1)S(1)} collective-permute-done((bf16[64,384]{1,0:T(8,128)(2,1)S(1)}, bf16[64,384]{1,0:T(8,128)(2,1)S(1)}, u32[]{:S(2)}, u32[]{:S(2)}) %collective-permute-start.12) | collective-permute-done | bytes 49184 | tf_op jit(solution)/shard_map/ppermute | solution.py:42
  77.4 1.8 %collective-permute-start.14 = (bf16[64,388]{0,1:T(8,128)(2,1)S(1)}, bf16[64,388]{0,1:T(8,128)(2,1)S(1)}, u32[]{:S(2)}, u32[]{:S(2)}) collective-permute-start(bf16[64,388]{0,1:T(8,128)(2,1)S(1)} %pad_maximum_fusion.2), channel_id=1, source_target_pairs={{0,8},{8,0},{16,24},{24,16},{1,9},{9,1},{17,25},{25,17},{2,10},{10... | collective-permute-start | bytes 149000 | tf_op jit(solution)/shard_map/ppermute | solution.py:25
  79.5 1.5 collective-permute-start.16
  81.0 7.1 %shard_map.176 = bf16[128,128,2,128]{3,2,1,0:T(2,128)(2,1)} custom-call(bf16[2,128,128,2,128]{4,3,2,1,0:T(2,128)(2,1)} %source.3), custom_call_target="tpu_custom_call" | custom-call | bytes 16777216 | tf_op jit(solution)/shard_map/pallas_call | solution.py:84
  89.9 5.8 %fusion.199 = (f32[128,2]{1,0:T(8,128)S(1)}, f32[128,2,128]{2,1,0:T(2,128)S(1)}) fusion(f32[128,2]{1,0:T(8,128)S(1)} %gather_fusion.4, f32[2,128,2,128]{3,2,1,0:T(2,128)S(1)} %copy-done.10, bf16[128,128,2,128]{3,2,1,0:T(2,128)(2,1)} %shard_map.176, bf16[128,2,128]{2,1,0:T(2,128)(2,1)S(1)} %concatenate.37, bf16[2,2]{0,1:T(2,128)(2,1)S(1)} %compare_convert_fusion, ...), kind=kOutput, calls=%fused_computation.328 | convolution fusion | flops 17202944 | bytes 8734728 | tf_op jit(solution)/shard_map/pthc,pkhc->pkt/dot_general | solution.py:127
  97.1 4.7 %fusion = f32[128,2,2,128]{3,1,2,0:T(2,128)S(1)} fusion(bf16[128,128,2,128]{3,2,1,0:T(2,128)(2,1)} %shard_map.176, f32[128,2,128]{2,1,0:T(2,128)S(1)} %get-tuple-element.59, pred[128,128]{1,0:T(8,128)(4,1)S(1)} %fusion.117, f32[128,2]{1,0:T(8,128)S(1)} %gather_fusion.5), kind=kOutput, calls=%fused_computation.6 | convolution fusion | flops 16875520 | bytes 8799232 | tf_op jit(solution)/shard_map/pkt,pthc->pkhc/dot_general | solution.py:137
  102.6 1.8 %collective-permute-start.17 = (f32[64,2,66]{0,1,2:T(2,128)S(1)}, f32[64,2,66]{0,1,2:T(2,128)S(1)}, u32[]{:S(2)}, u32[]{:S(2)}) collective-permute-start(f32[64,2,66]{0,1,2:T(2,128)S(1)} %pad_maximum_fusion.4), channel_id=1, source_target_pairs={{0,8},{8,0},{16,24},{24,16},{1,9},{9,1},{17,25},{25,17},{2,10},{10... | collective-permute-start | bytes 101384 | tf_op jit(solution)/shard_map/ppermute | solution.py:42
  104.7 1.5 collective-permute-start.19
  107.2 1.6 collective-permute-done.18
  108.7 1.2 collective-permute-done.19
  110.6 1.2 collective-permute-done.20
  111.8 1.2 collective-permute-start.21
  113.0 2.0 %collective-permute-start.22 = (bf16[64,384]{1,0:T(8,128)(2,1)S(1)}, bf16[64,384]{1,0:T(8,128)(2,1)S(1)}, u32[]{:S(2)}, u32[]{:S(2)}) collective-permute-start(bf16[64,384]{1,0:T(8,128)(2,1)S(1)} %add_convert_fusion.1), channel_id=1, source_target_pairs={{0,4},{1,5},{2,6},{3,7},{4,0},{5,1},{6,2},{7,3},{8,12},{9,13},{10,... | collective-permute-start | bytes 147464 | tf_op jit(solution)/shard_map/ppermute | solution.py:42
  115.0 1.2 collective-permute-start.23
  116.3 2.7 %collective-permute-done.22 = bf16[64,384]{1,0:T(8,128)(2,1)S(1)} collective-permute-done((bf16[64,384]{1,0:T(8,128)(2,1)S(1)}, bf16[64,384]{1,0:T(8,128)(2,1)S(1)}, u32[]{:S(2)}, u32[]{:S(2)}) %collective-permute-start.22) | collective-permute-done | bytes 49184 | tf_op jit(solution)/shard_map/ppermute | solution.py:42
  119.0 1.9 %collective-permute-done.23 = bf16[64,384]{1,0:T(8,128)(2,1)S(1)} collective-permute-done((bf16[64,384]{1,0:T(8,128)(2,1)S(1)}, bf16[64,384]{1,0:T(8,128)(2,1)S(1)}, u32[]{:S(2)}, u32[]{:S(2)}) %collective-permute-start.23) | collective-permute-done | bytes 49184 | tf_op jit(solution)/shard_map/ppermute | solution.py:42
  121.8 11.3 %all-gather.1 = bf16[256,1026]{1,0:T(8,128)(2,1)S(1)} all-gather(bf16[64,1026]{1,0:T(8,128)(2,1)S(1)} %concatenate.39), channel_id=3, replica_groups=mesh['gx'=4,'gy'=8] {'gx'}, dimensions={0}, use_global_device_ids=true | all-gather | bytes 656640 | tf_op jit(solution)/shard_map/all_gather | solution.py:19
  133.8 1.2 collective-permute-done.24
  135.2 1.7 collective-permute-start.26
  136.9 2.7 %collective-permute-start.27 = (bf16[64,384]{1,0:T(8,128)(2,1)S(1)}, bf16[64,384]{1,0:T(8,128)(2,1)S(1)}, u32[]{:S(2)}, u32[]{:S(2)}) collective-permute-start(bf16[64,384]{1,0:T(8,128)(2,1)S(1)} %add_convert_fusion), channel_id=1, source_target_pairs={{0,6},{1,7},{2,4},{3,5},{4,2},{5,3},{6,0},{7,1},{8,14},{9,15},{10,... | collective-permute-start | bytes 147464 | tf_op jit(solution)/shard_map/ppermute | solution.py:42
  139.9 2.2 %collective-permute-done.26 = bf16[64,384]{1,0:T(8,128)(2,1)S(1)} collective-permute-done((bf16[64,384]{1,0:T(8,128)(2,1)S(1)}, bf16[64,384]{1,0:T(8,128)(2,1)S(1)}, u32[]{:S(2)}, u32[]{:S(2)}) %collective-permute-start.26) | collective-permute-done | bytes 49184 | tf_op jit(solution)/shard_map/ppermute | solution.py:42
  143.0 3.3 %convolution_convert_fusion = bf16[64,6144]{1,0:T(8,128)(2,1)S(1)} fusion(bf16[384,6144]{1,0:T(8,128)(2,1)} %param.27, f32[64,384]{1,0:T(8,128)S(1)} %get-tuple-element.10, f32[384]{0:T(512)S(1)} %copy-done.5), kind=kOutput, calls=%fused_computation.14 | convolution fusion | flops 302432256 | bytes 5604864 | tf_op jit(solution)/shard_map/dot_general | solution.py:259
  146.6 13.8 %all_to_all.5 = bf16[64,4,1538]{2,0,1:T(8,128)(2,1)S(1)} all-to-all(bf16[64,4,1538]{2,0,1:T(8,128)(2,1)S(1)} %pad_maximum_fusion), channel_id=1, replica_groups=mesh['gx'=4,'gy'=8] {'gx'}, dimensions={1} | all-to-all | bytes 1574912 | tf_op jit(solution)/shard_map/all_to_all | solution.py:270
  162.2 2.2 %collective-permute-start.30 = (f32[64]{0:T(128)S(1)}, f32[64]{0:T(128)S(1)}, u32[]{:S(2)}, u32[]{:S(2)}) collective-permute-start(f32[64]{0:T(128)S(1)} %get-tuple-element.7), channel_id=1, source_target_pairs={{0,24},{8,16},{16,8},{24,0},{1,25},{9,17},{17,9},{25,1},{2,26},{10... | collective-permute-start | bytes 776 | tf_op jit(solution)/shard_map/ppermute | solution.py:70
  165.2 1.5 collective-permute-done.30
  167.9 2.9 %collective-permute-start.33 = (f32[64]{0:T(128)S(1)}, f32[64]{0:T(128)S(1)}, u32[]{:S(2)}, u32[]{:S(2)}) collective-permute-start(f32[64]{0:T(128)S(1)} %max.146), channel_id=1, source_target_pairs={{0,4},{1,5},{2,6},{3,7},{4,0},{5,1},{6,2},{7,3},{8,12},{9,13},{10,... | collective-permute-start | bytes 776 | tf_op jit(solution)/shard_map/ppermute | solution.py:42
  170.8 1.4 collective-permute-start.34
  172.9 3.2 %collective-permute-done.34 = f32[64]{0:T(128)S(1)} collective-permute-done((f32[64]{0:T(128)S(1)}, f32[64]{0:T(128)S(1)}, u32[]{:S(2)}, u32[]{:S(2)}) %collective-permute-start.34) | collective-permute-done | bytes 288 | tf_op jit(solution)/shard_map/ppermute | solution.py:42
  (199 shorter events, 29.3 us)
Async XLA Ops:
  4.6 15.2 %collective-permute-start = (bf16[64,388]{0,1:T(8,128)(2,1)S(1)}, bf16[64,388]{0,1:T(8,128)(2,1)S(1)}, u32[]{:S(2)}, u32[]{:S(2)}) collective-permute-start(bf16[64,388]{0,1:T(8,128)(2,1)S(1)} %pad_maximum_fusion.1), channel_id=1, source_target_pairs={{0,8},{8,0},{16,24},{24,16},{1,9},{9,1},{17,25},{25,17},{2,10},{10... | collective-permute-start | bytes 149000 | tf_op jit(solution)/shard_map/ppermute | solution.py:25
  7.6 12.2 %collective-permute-start.1 = (bf16[64,388]{0,1:T(8,128)(2,1)S(1)}, bf16[64,388]{0,1:T(8,128)(2,1)S(1)}, u32[]{:S(2)}, u32[]{:S(2)}) collective-permute-start(bf16[64,388]{0,1:T(8,128)(2,1)S(1)} %pad_maximum_fusion.1), channel_id=1, source_target_pairs={{0,16},{8,24},{16,0},{24,8},{1,17},{9,25},{17,1},{25,9},{2,18},{10... | collective-permute-start | bytes 149000 | tf_op jit(solution)/shard_map/ppermute | solution.py:25
  9.1 10.6 %collective-permute-start.2 = (bf16[64,388]{0,1:T(8,128)(2,1)S(1)}, bf16[64,388]{0,1:T(8,128)(2,1)S(1)}, u32[]{:S(2)}, u32[]{:S(2)}) collective-permute-start(bf16[64,388]{0,1:T(8,128)(2,1)S(1)} %pad_maximum_fusion.1), channel_id=1, source_target_pairs={{0,24},{8,16},{16,8},{24,0},{1,25},{9,17},{17,9},{25,1},{2,26},{10... | collective-permute-start | bytes 149000 | tf_op jit(solution)/shard_map/ppermute | solution.py:25
  12.7 9.0 %copy-start.10 = (f32[2,128,2,128]{3,2,1,0:T(2,128)S(1)}, f32[2,128,2,128]{3,2,1,0:T(2,128)}, u32[]{:S(2)}) copy-start(f32[2,128,2,128]{3,2,1,0:T(2,128)} %param.29) | copy-start | bytes 786436
  21.7 22.0 %copy-start.4 = (bf16[2,128,384]{2,1,0:T(8,128)(2,1)S(1)}, bf16[2,128,384]{2,1,0:T(8,128)(2,1)}, u32[]{:S(2)}) copy-start(bf16[2,128,384]{2,1,0:T(8,128)(2,1)} %param.23) | copy-start | bytes 589828
  21.7 27.9 %copy-start.6 = (f32[2,384]{1,0:T(2,128)S(1)}, f32[2,384]{1,0:T(2,128)}, u32[]{:S(2)}) copy-start(f32[2,384]{1,0:T(2,128)} %param.18) | copy-start | bytes 9220
  21.7 33.6 %copy-start.3 = (bf16[64,384]{1,0:T(8,128)(2,1)S(1)}, bf16[64,384]{1,0:T(8,128)(2,1)}, u32[]{:S(2)}) copy-start(bf16[64,384]{1,0:T(8,128)(2,1)} %param.16) | copy-start | bytes 147460
  27.6 27.8 %copy-start = (bf16[2,384,512]{2,1,0:T(8,128)(2,1)S(1)}, bf16[2,384,512]{2,1,0:T(8,128)(2,1)}, u32[]{:S(2)}) copy-start(bf16[2,384,512]{2,1,0:T(8,128)(2,1)} %param.25) | copy-start | bytes 2359300
  27.6 28.0 %copy-start.1 = (bf16[2,384,512]{2,1,0:T(8,128)(2,1)S(1)}, bf16[2,384,512]{2,1,0:T(8,128)(2,1)}, u32[]{:S(2)}) copy-start(bf16[2,384,512]{2,1,0:T(8,128)(2,1)} %param.24) | copy-start | bytes 2359300
  28.9 48.0 %copy-start.2 = (bf16[2,384,384]{2,1,0:T(8,128)(2,1)S(1)}, bf16[2,384,384]{2,1,0:T(8,128)(2,1)}, u32[]{:S(2)}) copy-start(bf16[2,384,384]{2,1,0:T(8,128)(2,1)} %param.20) | copy-start | bytes 1769476
  29.0 48.3 %copy-start.8 = (bf16[2,384,2]{1,2,0:T(2,128)(2,1)S(1)}, bf16[2,384,2]{1,2,0:T(2,128)(2,1)}, u32[]{:S(2)}) copy-start(bf16[2,384,2]{1,2,0:T(2,128)(2,1)} %param.21) | copy-start | bytes 9220
  34.6 4.4 %collective-permute-start.3 = (f32[64,2,66]{0,1,2:T(2,128)S(1)}, f32[64,2,66]{0,1,2:T(2,128)S(1)}, u32[]{:S(2)}, u32[]{:S(2)}) collective-permute-start(f32[64,2,66]{0,1,2:T(2,128)S(1)} %pad_maximum_fusion.3), channel_id=1, source_target_pairs={{0,8},{8,0},{16,24},{24,16},{1,9},{9,1},{17,25},{25,17},{2,10},{10... | collective-permute-start | bytes 101384 | tf_op jit(solution)/shard_map/ppermute | solution.py:42
  36.6 4.9 %collective-permute-start.4 = (f32[64,2,66]{0,1,2:T(2,128)S(1)}, f32[64,2,66]{0,1,2:T(2,128)S(1)}, u32[]{:S(2)}, u32[]{:S(2)}) collective-permute-start(f32[64,2,66]{0,1,2:T(2,128)S(1)} %pad_maximum_fusion.3), channel_id=1, source_target_pairs={{0,16},{8,24},{16,0},{24,8},{1,17},{9,25},{17,1},{25,9},{2,18},{10... | collective-permute-start | bytes 101384 | tf_op jit(solution)/shard_map/ppermute | solution.py:42
  38.1 5.2 %collective-permute-start.5 = (f32[64,2,66]{0,1,2:T(2,128)S(1)}, f32[64,2,66]{0,1,2:T(2,128)S(1)}, u32[]{:S(2)}, u32[]{:S(2)}) collective-permute-start(f32[64,2,66]{0,1,2:T(2,128)S(1)} %pad_maximum_fusion.3), channel_id=1, source_target_pairs={{0,24},{8,16},{16,8},{24,0},{1,25},{9,17},{17,9},{25,1},{2,26},{10... | collective-permute-start | bytes 101384 | tf_op jit(solution)/shard_map/ppermute | solution.py:42
  43.9 1.3 collective-permute-start.6
  45.2 4.5 %collective-permute-start.7 = (bf16[64,384]{1,0:T(8,128)(2,1)S(1)}, bf16[64,384]{1,0:T(8,128)(2,1)S(1)}, u32[]{:S(2)}, u32[]{:S(2)}) collective-permute-start(bf16[64,384]{1,0:T(8,128)(2,1)S(1)} %add_convert_fusion.3), channel_id=1, source_target_pairs={{0,2},{1,3},{2,0},{3,1},{4,6},{5,7},{6,4},{7,5},{8,10},{9,11},{10,... | collective-permute-start | bytes 147464 | tf_op jit(solution)/shard_map/ppermute | solution.py:42
  46.8 5.9 %collective-permute-start.8 = (bf16[64,384]{1,0:T(8,128)(2,1)S(1)}, bf16[64,384]{1,0:T(8,128)(2,1)S(1)}, u32[]{:S(2)}, u32[]{:S(2)}) collective-permute-start(bf16[64,384]{1,0:T(8,128)(2,1)S(1)} %add_convert_fusion.3), channel_id=1, source_target_pairs={{0,4},{1,5},{2,6},{3,7},{4,0},{5,1},{6,2},{7,3},{8,12},{9,13},{10,... | collective-permute-start | bytes 147464 | tf_op jit(solution)/shard_map/ppermute | solution.py:42
  49.4 5.9 %collective-permute-start.9 = (bf16[64,384]{1,0:T(8,128)(2,1)S(1)}, bf16[64,384]{1,0:T(8,128)(2,1)S(1)}, u32[]{:S(2)}, u32[]{:S(2)}) collective-permute-start(bf16[64,384]{1,0:T(8,128)(2,1)S(1)} %add_convert_fusion.3), channel_id=1, source_target_pairs={{0,6},{1,7},{2,4},{3,5},{4,2},{5,3},{6,0},{7,1},{8,14},{9,15},{10,... | collective-permute-start | bytes 147464 | tf_op jit(solution)/shard_map/ppermute | solution.py:42
  67.7 1.3 collective-permute-start.10
  69.0 4.9 %collective-permute-start.11 = (bf16[64,384]{1,0:T(8,128)(2,1)S(1)}, bf16[64,384]{1,0:T(8,128)(2,1)S(1)}, u32[]{:S(2)}, u32[]{:S(2)}) collective-permute-start(bf16[64,384]{1,0:T(8,128)(2,1)S(1)} %add_convert_fusion.2), channel_id=1, source_target_pairs={{0,2},{1,3},{2,0},{3,1},{4,6},{5,7},{6,4},{7,5},{8,10},{9,11},{10,... | collective-permute-start | bytes 147464 | tf_op jit(solution)/shard_map/ppermute | solution.py:42
  69.1 7.0 %collective-permute-start.12 = (bf16[64,384]{1,0:T(8,128)(2,1)S(1)}, bf16[64,384]{1,0:T(8,128)(2,1)S(1)}, u32[]{:S(2)}, u32[]{:S(2)}) collective-permute-start(bf16[64,384]{1,0:T(8,128)(2,1)S(1)} %add_convert_fusion.2), channel_id=1, source_target_pairs={{0,4},{1,5},{2,6},{3,7},{4,0},{5,1},{6,2},{7,3},{8,12},{9,13},{10,... | collective-permute-start | bytes 147464 | tf_op jit(solution)/shard_map/ppermute | solution.py:42
  70.8 5.9 %collective-permute-start.13 = (bf16[64,384]{1,0:T(8,128)(2,1)S(1)}, bf16[64,384]{1,0:T(8,128)(2,1)S(1)}, u32[]{:S(2)}, u32[]{:S(2)}) collective-permute-start(bf16[64,384]{1,0:T(8,128)(2,1)S(1)} %add_convert_fusion.2), channel_id=1, source_target_pairs={{0,6},{1,7},{2,4},{3,5},{4,2},{5,3},{6,0},{7,1},{8,14},{9,15},{10,... | collective-permute-start | bytes 147464 | tf_op jit(solution)/shard_map/ppermute | solution.py:42
  77.4 10.6 %collective-permute-start.14 = (bf16[64,388]{0,1:T(8,128)(2,1)S(1)}, bf16[64,388]{0,1:T(8,128)(2,1)S(1)}, u32[]{:S(2)}, u32[]{:S(2)}) collective-permute-start(bf16[64,388]{0,1:T(8,128)(2,1)S(1)} %pad_maximum_fusion.2), channel_id=1, source_target_pairs={{0,8},{8,0},{16,24},{24,16},{1,9},{9,1},{17,25},{25,17},{2,10},{10... | collective-permute-start | bytes 149000 | tf_op jit(solution)/shard_map/ppermute | solution.py:25
  79.2 8.8 %collective-permute-start.15 = (bf16[64,388]{0,1:T(8,128)(2,1)S(1)}, bf16[64,388]{0,1:T(8,128)(2,1)S(1)}, u32[]{:S(2)}, u32[]{:S(2)}) collective-permute-start(bf16[64,388]{0,1:T(8,128)(2,1)S(1)} %pad_maximum_fusion.2), channel_id=1, source_target_pairs={{0,16},{8,24},{16,0},{24,8},{1,17},{9,25},{17,1},{25,9},{2,18},{10... | collective-permute-start | bytes 149000 | tf_op jit(solution)/shard_map/ppermute | solution.py:25
  79.5 8.5 %collective-permute-start.16 = (bf16[64,388]{0,1:T(8,128)(2,1)S(1)}, bf16[64,388]{0,1:T(8,128)(2,1)S(1)}, u32[]{:S(2)}, u32[]{:S(2)}) collective-permute-start(bf16[64,388]{0,1:T(8,128)(2,1)S(1)} %pad_maximum_fusion.2), channel_id=1, source_target_pairs={{0,24},{8,16},{16,8},{24,0},{1,25},{9,17},{17,9},{25,1},{2,26},{10... | collective-permute-start | bytes 149000 | tf_op jit(solution)/shard_map/ppermute | solution.py:25
  95.8 37.7 %copy-start.9 = (bf16[2,512,384]{2,1,0:T(8,128)(2,1)S(1)}, bf16[2,512,384]{2,1,0:T(8,128)(2,1)}, u32[]{:S(2)}) copy-start(bf16[2,512,384]{2,1,0:T(8,128)(2,1)} %param.26) | copy-start | bytes 2359300
  97.1 45.9 %copy-start.5 = (f32[384]{0:T(512)S(1)}, f32[384]{0:T(512)}, u32[]{:S(2)}) copy-start(f32[384]{0:T(512)} %param.19) | copy-start | bytes 4612
  102.6 4.5 %collective-permute-start.17 = (f32[64,2,66]{0,1,2:T(2,128)S(1)}, f32[64,2,66]{0,1,2:T(2,128)S(1)}, u32[]{:S(2)}, u32[]{:S(2)}) collective-permute-start(f32[64,2,66]{0,1,2:T(2,128)S(1)} %pad_maximum_fusion.4), channel_id=1, source_target_pairs={{0,8},{8,0},{16,24},{24,16},{1,9},{9,1},{17,25},{25,17},{2,10},{10... | collective-permute-start | bytes 101384 | tf_op jit(solution)/shard_map/ppermute | solution.py:42
  104.4 4.3 %collective-permute-start.18 = (f32[64,2,66]{0,1,2:T(2,128)S(1)}, f32[64,2,66]{0,1,2:T(2,128)S(1)}, u32[]{:S(2)}, u32[]{:S(2)}) collective-permute-start(f32[64,2,66]{0,1,2:T(2,128)S(1)} %pad_maximum_fusion.4), channel_id=1, source_target_pairs={{0,16},{8,24},{16,0},{24,8},{1,17},{9,25},{17,1},{25,9},{2,18},{10... | collective-permute-start | bytes 101384 | tf_op jit(solution)/shard_map/ppermute | solution.py:42
  104.7 5.2 %collective-permute-start.19 = (f32[64,2,66]{0,1,2:T(2,128)S(1)}, f32[64,2,66]{0,1,2:T(2,128)S(1)}, u32[]{:S(2)}, u32[]{:S(2)}) collective-permute-start(f32[64,2,66]{0,1,2:T(2,128)S(1)} %pad_maximum_fusion.4), channel_id=1, source_target_pairs={{0,24},{8,16},{16,8},{24,0},{1,25},{9,17},{17,9},{25,1},{2,26},{10... | collective-permute-start | bytes 101384 | tf_op jit(solution)/shard_map/ppermute | solution.py:42
  110.5 1.3 collective-permute-start.20
  111.8 4.5 %collective-permute-start.21 = (bf16[64,384]{1,0:T(8,128)(2,1)S(1)}, bf16[64,384]{1,0:T(8,128)(2,1)S(1)}, u32[]{:S(2)}, u32[]{:S(2)}) collective-permute-start(bf16[64,384]{1,0:T(8,128)(2,1)S(1)} %add_convert_fusion.1), channel_id=1, source_target_pairs={{0,2},{1,3},{2,0},{3,1},{4,6},{5,7},{6,4},{7,5},{8,10},{9,11},{10,... | collective-permute-start | bytes 147464 | tf_op jit(solution)/shard_map/ppermute | solution.py:42
  113.0 6.0 %collective-permute-start.22 = (bf16[64,384]{1,0:T(8,128)(2,1)S(1)}, bf16[64,384]{1,0:T(8,128)(2,1)S(1)}, u32[]{:S(2)}, u32[]{:S(2)}) collective-permute-start(bf16[64,384]{1,0:T(8,128)(2,1)S(1)} %add_convert_fusion.1), channel_id=1, source_target_pairs={{0,4},{1,5},{2,6},{3,7},{4,0},{5,1},{6,2},{7,3},{8,12},{9,13},{10,... | collective-permute-start | bytes 147464 | tf_op jit(solution)/shard_map/ppermute | solution.py:42
  115.0 5.9 %collective-permute-start.23 = (bf16[64,384]{1,0:T(8,128)(2,1)S(1)}, bf16[64,384]{1,0:T(8,128)(2,1)S(1)}, u32[]{:S(2)}, u32[]{:S(2)}) collective-permute-start(bf16[64,384]{1,0:T(8,128)(2,1)S(1)} %add_convert_fusion.1), channel_id=1, source_target_pairs={{0,6},{1,7},{2,4},{3,5},{4,2},{5,3},{6,0},{7,1},{8,14},{9,15},{10,... | collective-permute-start | bytes 147464 | tf_op jit(solution)/shard_map/ppermute | solution.py:42
  133.8 1.3 collective-permute-start.24
  135.1 4.8 %collective-permute-start.25 = (bf16[64,384]{1,0:T(8,128)(2,1)S(1)}, bf16[64,384]{1,0:T(8,128)(2,1)S(1)}, u32[]{:S(2)}, u32[]{:S(2)}) collective-permute-start(bf16[64,384]{1,0:T(8,128)(2,1)S(1)} %add_convert_fusion), channel_id=1, source_target_pairs={{0,2},{1,3},{2,0},{3,1},{4,6},{5,7},{6,4},{7,5},{8,10},{9,11},{10,... | collective-permute-start | bytes 147464 | tf_op jit(solution)/shard_map/ppermute | solution.py:42
  135.2 6.9 %collective-permute-start.26 = (bf16[64,384]{1,0:T(8,128)(2,1)S(1)}, bf16[64,384]{1,0:T(8,128)(2,1)S(1)}, u32[]{:S(2)}, u32[]{:S(2)}) collective-permute-start(bf16[64,384]{1,0:T(8,128)(2,1)S(1)} %add_convert_fusion), channel_id=1, source_target_pairs={{0,4},{1,5},{2,6},{3,7},{4,0},{5,1},{6,2},{7,3},{8,12},{9,13},{10,... | collective-permute-start | bytes 147464 | tf_op jit(solution)/shard_map/ppermute | solution.py:42
  136.9 5.9 %collective-permute-start.27 = (bf16[64,384]{1,0:T(8,128)(2,1)S(1)}, bf16[64,384]{1,0:T(8,128)(2,1)S(1)}, u32[]{:S(2)}, u32[]{:S(2)}) collective-permute-start(bf16[64,384]{1,0:T(8,128)(2,1)S(1)} %add_convert_fusion), channel_id=1, source_target_pairs={{0,6},{1,7},{2,4},{3,5},{4,2},{5,3},{6,0},{7,1},{8,14},{9,15},{10,... | collective-permute-start | bytes 147464 | tf_op jit(solution)/shard_map/ppermute | solution.py:42
  160.9 15.8 %copy-start.7 = (f32[64]{0:T(128)}, f32[64]{0:T(128)S(1)}, u32[]{:S(2)}) copy-start(f32[64]{0:T(128)S(1)} %get-tuple-element.8) | copy-start | bytes 772
  160.9 3.6 %collective-permute-start.28 = (f32[64]{0:T(128)S(1)}, f32[64]{0:T(128)S(1)}, u32[]{:S(2)}, u32[]{:S(2)}) collective-permute-start(f32[64]{0:T(128)S(1)} %get-tuple-element.7), channel_id=1, source_target_pairs={{0,8},{8,0},{16,24},{24,16},{1,9},{9,1},{17,25},{25,17},{2,10},{10... | collective-permute-start | bytes 776 | tf_op jit(solution)/shard_map/ppermute | solution.py:70
  161.7 3.5 %collective-permute-start.29 = (f32[64]{0:T(128)S(1)}, f32[64]{0:T(128)S(1)}, u32[]{:S(2)}, u32[]{:S(2)}) collective-permute-start(f32[64]{0:T(128)S(1)} %get-tuple-element.7), channel_id=1, source_target_pairs={{0,16},{8,24},{16,0},{24,8},{1,17},{9,25},{17,1},{25,9},{2,18},{10... | collective-permute-start | bytes 776 | tf_op jit(solution)/shard_map/ppermute | solution.py:70
  162.2 4.4 %collective-permute-start.30 = (f32[64]{0:T(128)S(1)}, f32[64]{0:T(128)S(1)}, u32[]{:S(2)}, u32[]{:S(2)}) collective-permute-start(f32[64]{0:T(128)S(1)} %get-tuple-element.7), channel_id=1, source_target_pairs={{0,24},{8,16},{16,8},{24,0},{1,25},{9,17},{17,9},{25,1},{2,26},{10... | collective-permute-start | bytes 776 | tf_op jit(solution)/shard_map/ppermute | solution.py:70
  166.7 1.1 collective-permute-start.31
  167.8 5.1 %collective-permute-start.32 = (f32[64]{0:T(128)S(1)}, f32[64]{0:T(128)S(1)}, u32[]{:S(2)}, u32[]{:S(2)}) collective-permute-start(f32[64]{0:T(128)S(1)} %max.146), channel_id=1, source_target_pairs={{0,2},{1,3},{2,0},{3,1},{4,6},{5,7},{6,4},{7,5},{8,10},{9,11},{10,... | collective-permute-start | bytes 776 | tf_op jit(solution)/shard_map/ppermute | solution.py:42
  167.9 5.0 %collective-permute-start.33 = (f32[64]{0:T(128)S(1)}, f32[64]{0:T(128)S(1)}, u32[]{:S(2)}, u32[]{:S(2)}) collective-permute-start(f32[64]{0:T(128)S(1)} %max.146), channel_id=1, source_target_pairs={{0,4},{1,5},{2,6},{3,7},{4,0},{5,1},{6,2},{7,3},{8,12},{9,13},{10,... | collective-permute-start | bytes 776 | tf_op jit(solution)/shard_map/ppermute | solution.py:42
  170.8 5.3 %collective-permute-start.34 = (f32[64]{0:T(128)S(1)}, f32[64]{0:T(128)S(1)}, u32[]{:S(2)}, u32[]{:S(2)}) collective-permute-start(f32[64]{0:T(128)S(1)} %max.146), channel_id=1, source_target_pairs={{0,6},{1,7},{2,4},{3,5},{4,2},{5,3},{6,0},{7,1},{8,14},{9,15},{10,... | collective-permute-start | bytes 776 | tf_op jit(solution)/shard_map/ppermute | solution.py:42

commit v11 on v10

--- a/solution.py
+++ b/solution.py
@@ -80,7 +80,7 @@
 
 def layer_slice(cache, layer_id):
     layers, slots, tokens, heads, width = cache.shape
-    block = 32
+    block = 64
     return pl.pallas_call(
         copy_block,
         grid=(slots // block,),

time: 177 us -> 175 us (0.989)
  Pallas kernels: 14.2 us -> 11.5 us
    pallas_call x2, Pallas kernels: 14.2 us -> 11.5 us  [layer_slice(): pl.pallas_call(copy_block, grid=(slots // block,), in_specs=[pl.BlockSpec...]
  transfers between devices with their start and end apart: 35 -> 35, of which waited for: 25 -> 25; matrix products, arithmetic and copies ran while one was open for 3% -> 3% of each run, Pallas kernels for 8% -> 7%
where the time goes in v11:
time: 175 us; the launch traced here: 174 us
  starting transfers between devices  41.2 us (24%)
  waiting for transfers between devices  36.6 us (21%)
  blocking collectives  35 us (20%)
  matrix products  30.7 us (18%)
  Pallas kernels  11.5 us (7%)
  local copies, waits for them, and re-layouts  9.83 us (6%)
  other arithmetic  7.7 us (4%)
    ppermute x26, waiting for transfers between devices, exchange(): return lax.ppermute(value, axis, [(i, i ^ partner) for i in range(count)])  34.3 us
    ppermute x26, starting transfers between devices, exchange(): return lax.ppermute(value, axis, [(i, i ^ partner) for i in range(count)])  29.6 us
    all_gather x2, blocking collectives, gather_sum(): return jnp.sum(lax.all_gather(value, axis).astype(jnp.float32), axis=0)  21.3 us
    all_to_all x1, blocking collectives, local(): pieces = lax.all_to_all(pieces, 'gx', 1, 1, tiled=True).astype(jnp.float32)  13.8 us
    dot_general x2, matrix products, local_attention(): jnp.einsum('pthc,pkhc->pkt', kv_layer, query_block, preferred_element_typ...  11.7 us
    pallas_call x2, Pallas kernels, layer_slice(): pl.pallas_call(copy_block, grid=(slots // block,), in_specs=[pl.BlockSpec...  11.5 us
    dot_general x2, matrix products, local_attention(): jnp.einsum('pkt,pthc->pkhc', weights.astype(jnp.bfloat16), kv_layer, pref...  9.35 us
    ppermute x6, starting transfers between devices, xor_sum(): lax.ppermute(value, axis, [(i, i ^ k) for i in range(count)])  8.1 us
  transfers between devices with their start and end apart: 35, of which 25 were waited for; matrix products, arithmetic and copies ran while one was open for 3% of the time, Pallas kernels for 7%

profile of v11, /device:TPU:0, one launch (start us, length us, event | category | flops | bytes accessed | tf_op | source)
XLA Modules:
  0.0 174.0 jit_solution(9022373516221960549)
XLA Ops:
  2.3 1.3 convolution_convert_fusion.2
  4.6 3.0 %collective-permute-start = (bf16[64,388]{0,1:T(8,128)(2,1)S(1)}, bf16[64,388]{0,1:T(8,128)(2,1)S(1)}, u32[]{:S(2)}, u32[]{:S(2)}) collective-permute-start(bf16[64,388]{0,1:T(8,128)(2,1)S(1)} %pad_maximum_fusion.1), channel_id=1, source_target_pairs={{0,8},{8,0},{16,24},{24,16},{1,9},{9,1},{17,25},{25,17},{2,10},{10... | collective-permute-start | bytes 149000 | tf_op jit(solution)/shard_map/ppermute | solution.py:25
  7.6 1.5 collective-permute-start.1
  12.7 5.8 %shard_map.175 = bf16[128,128,2,128]{3,2,1,0:T(2,128)(2,1)} custom-call(bf16[2,128,128,2,128]{4,3,2,1,0:T(2,128)(2,1)} %source.3), custom_call_target="tpu_custom_call" | custom-call | bytes 16777216 | tf_op jit(solution)/shard_map/pallas_call | solution.py:84
  20.4 5.9 %fusion.198 = (f32[128,2]{1,0:T(8,128)S(1)}, f32[128,2,128]{2,1,0:T(2,128)S(1)}) fusion(f32[128,2]{1,0:T(8,128)S(1)} %gather_fusion.1, f32[2,128,2,128]{3,2,1,0:T(2,128)S(1)} %copy-done.10, bf16[128,128,2,128]{3,2,1,0:T(2,128)(2,1)} %shard_map.175, bf16[128,2,128]{2,1,0:T(2,128)(2,1)S(1)} %concatenate.33, bf16[2,2]{0,1:T(2,128)(2,1)S(1)} %compare_convert_fusion, ...), kind=kOutput, calls=%fused_computation.327 | convolution fusion | flops 17202944 | bytes 8734728 | tf_op jit(solution)/shard_map/pthc,pkhc->pkt/dot_general | solution.py:127
  27.6 4.7 %fusion.4 = f32[128,2,2,128]{3,1,2,0:T(2,128)S(1)} fusion(bf16[128,128,2,128]{3,2,1,0:T(2,128)(2,1)} %shard_map.175, f32[128,2,128]{2,1,0:T(2,128)S(1)} %get-tuple-element.57, pred[128,128]{1,0:T(8,128)(4,1)S(1)} %fusion.117, f32[128,2]{1,0:T(8,128)S(1)} %gather_fusion.2), kind=kOutput, calls=%fused_computation.10 | convolution fusion | flops 16875520 | bytes 8799232 | tf_op jit(solution)/shard_map/pkt,pthc->pkhc/dot_general | solution.py:137
  33.2 2.0 %collective-permute-start.3 = (f32[64,2,66]{0,1,2:T(2,128)S(1)}, f32[64,2,66]{0,1,2:T(2,128)S(1)}, u32[]{:S(2)}, u32[]{:S(2)}) collective-permute-start(f32[64,2,66]{0,1,2:T(2,128)S(1)} %pad_maximum_fusion.3), channel_id=1, source_target_pairs={{0,8},{8,0},{16,24},{24,16},{1,9},{9,1},{17,25},{25,17},{2,10},{10... | collective-permute-start | bytes 101384 | tf_op jit(solution)/shard_map/ppermute | solution.py:42
  35.2 1.5 collective-permute-start.4
  37.5 2.6 %collective-permute-done.4 = f32[64,2,66]{0,1,2:T(2,128)S(1)} collective-permute-done((f32[64,2,66]{0,1,2:T(2,128)S(1)}, f32[64,2,66]{0,1,2:T(2,128)S(1)}, u32[]{:S(2)}, u32[]{:S(2)}) %collective-permute-start.4) | collective-permute-done | bytes 33824 | tf_op jit(solution)/shard_map/ppermute | solution.py:42
  40.1 1.8 %collective-permute-done.5 = f32[64,2,66]{0,1,2:T(2,128)S(1)} collective-permute-done((f32[64,2,66]{0,1,2:T(2,128)S(1)}, f32[64,2,66]{0,1,2:T(2,128)S(1)}, u32[]{:S(2)}, u32[]{:S(2)}) %collective-permute-start.5) | collective-permute-done | bytes 33824 | tf_op jit(solution)/shard_map/ppermute | solution.py:42
  42.6 1.2 collective-permute-done.6
  43.8 1.6 collective-permute-start.7
  45.4 2.6 %collective-permute-start.8 = (bf16[64,384]{1,0:T(8,128)(2,1)S(1)}, bf16[64,384]{1,0:T(8,128)(2,1)S(1)}, u32[]{:S(2)}, u32[]{:S(2)}) collective-permute-start(bf16[64,384]{1,0:T(8,128)(2,1)S(1)} %add_convert_fusion.3), channel_id=1, source_target_pairs={{0,4},{1,5},{2,6},{3,7},{4,0},{5,1},{6,2},{7,3},{8,12},{9,13},{10,... | collective-permute-start | bytes 147464 | tf_op jit(solution)/shard_map/ppermute | solution.py:42
  48.3 3.1 %collective-permute-done.8 = bf16[64,384]{1,0:T(8,128)(2,1)S(1)} collective-permute-done((bf16[64,384]{1,0:T(8,128)(2,1)S(1)}, bf16[64,384]{1,0:T(8,128)(2,1)S(1)}, u32[]{:S(2)}, u32[]{:S(2)}) %collective-permute-start.8) | collective-permute-done | bytes 49184 | tf_op jit(solution)/shard_map/ppermute | solution.py:42
  51.3 2.6 %collective-permute-done.9 = bf16[64,384]{1,0:T(8,128)(2,1)S(1)} collective-permute-done((bf16[64,384]{1,0:T(8,128)(2,1)S(1)}, bf16[64,384]{1,0:T(8,128)(2,1)S(1)}, u32[]{:S(2)}, u32[]{:S(2)}) %collective-permute-start.9) | collective-permute-done | bytes 49184 | tf_op jit(solution)/shard_map/ppermute | solution.py:42
  54.8 9.9 %all-gather = bf16[256,1026]{1,0:T(8,128)(2,1)S(1)} all-gather(bf16[64,1026]{1,0:T(8,128)(2,1)S(1)} %concatenate.35), channel_id=2, replica_groups=mesh['gx'=4,'gy'=8] {'gx'}, dimensions={0}, use_global_device_ids=true | all-gather | bytes 656640 | tf_op jit(solution)/shard_map/all_gather | solution.py:19
  65.1 1.3 convolution_convert_fusion.10
  66.4 1.2 collective-permute-done.10
  67.8 1.7 collective-permute-start.12
  69.5 2.7 %collective-permute-start.13 = (bf16[64,384]{1,0:T(8,128)(2,1)S(1)}, bf16[64,384]{1,0:T(8,128)(2,1)S(1)}, u32[]{:S(2)}, u32[]{:S(2)}) collective-permute-start(bf16[64,384]{1,0:T(8,128)(2,1)S(1)} %add_convert_fusion.2), channel_id=1, source_target_pairs={{0,6},{1,7},{2,4},{3,5},{4,2},{5,3},{6,0},{7,1},{8,14},{9,15},{10,... | collective-permute-start | bytes 147464 | tf_op jit(solution)/shard_map/ppermute | solution.py:42
  72.6 2.2 %collective-permute-done.12 = bf16[64,384]{1,0:T(8,128)(2,1)S(1)} collective-permute-done((bf16[64,384]{1,0:T(8,128)(2,1)S(1)}, bf16[64,384]{1,0:T(8,128)(2,1)S(1)}, u32[]{:S(2)}, u32[]{:S(2)}) %collective-permute-start.12) | collective-permute-done | bytes 49184 | tf_op jit(solution)/shard_map/ppermute | solution.py:42
  76.0 1.8 %collective-permute-start.14 = (bf16[64,388]{0,1:T(8,128)(2,1)S(1)}, bf16[64,388]{0,1:T(8,128)(2,1)S(1)}, u32[]{:S(2)}, u32[]{:S(2)}) collective-permute-start(bf16[64,388]{0,1:T(8,128)(2,1)S(1)} %pad_maximum_fusion.2), channel_id=1, source_target_pairs={{0,8},{8,0},{16,24},{24,16},{1,9},{9,1},{17,25},{25,17},{2,10},{10... | collective-permute-start | bytes 149000 | tf_op jit(solution)/shard_map/ppermute | solution.py:25
  78.1 1.5 collective-permute-start.16
  79.6 5.7 %shard_map.176 = bf16[128,128,2,128]{3,2,1,0:T(2,128)(2,1)} custom-call(bf16[2,128,128,2,128]{4,3,2,1,0:T(2,128)(2,1)} %source.3), custom_call_target="tpu_custom_call" | custom-call | bytes 16777216 | tf_op jit(solution)/shard_map/pallas_call | solution.py:84
  87.2 5.8 %fusion.199 = (f32[128,2]{1,0:T(8,128)S(1)}, f32[128,2,128]{2,1,0:T(2,128)S(1)}) fusion(f32[128,2]{1,0:T(8,128)S(1)} %gather_fusion.4, f32[2,128,2,128]{3,2,1,0:T(2,128)S(1)} %copy-done.10, bf16[128,128,2,128]{3,2,1,0:T(2,128)(2,1)} %shard_map.176, bf16[128,2,128]{2,1,0:T(2,128)(2,1)S(1)} %concatenate.37, bf16[2,2]{0,1:T(2,128)(2,1)S(1)} %compare_convert_fusion, ...), kind=kOutput, calls=%fused_computation.328 | convolution fusion | flops 17202944 | bytes 8734728 | tf_op jit(solution)/shard_map/pthc,pkhc->pkt/dot_general | solution.py:127
  94.4 4.7 %fusion = f32[128,2,2,128]{3,1,2,0:T(2,128)S(1)} fusion(bf16[128,128,2,128]{3,2,1,0:T(2,128)(2,1)} %shard_map.176, f32[128,2,128]{2,1,0:T(2,128)S(1)} %get-tuple-element.59, pred[128,128]{1,0:T(8,128)(4,1)S(1)} %fusion.117, f32[128,2]{1,0:T(8,128)S(1)} %gather_fusion.5), kind=kOutput, calls=%fused_computation.6 | convolution fusion | flops 16875520 | bytes 8799232 | tf_op jit(solution)/shard_map/pkt,pthc->pkhc/dot_general | solution.py:137
  99.9 1.8 %collective-permute-start.17 = (f32[64,2,66]{0,1,2:T(2,128)S(1)}, f32[64,2,66]{0,1,2:T(2,128)S(1)}, u32[]{:S(2)}, u32[]{:S(2)}) collective-permute-start(f32[64,2,66]{0,1,2:T(2,128)S(1)} %pad_maximum_fusion.4), channel_id=1, source_target_pairs={{0,8},{8,0},{16,24},{24,16},{1,9},{9,1},{17,25},{25,17},{2,10},{10... | collective-permute-start | bytes 101384 | tf_op jit(solution)/shard_map/ppermute | solution.py:42
  102.0 1.5 collective-permute-start.19
  104.4 1.5 collective-permute-done.18
  106.0 1.2 collective-permute-done.19
  107.8 1.2 collective-permute-done.20
  109.1 1.2 collective-permute-start.21
  110.3 2.0 %collective-permute-start.22 = (bf16[64,384]{1,0:T(8,128)(2,1)S(1)}, bf16[64,384]{1,0:T(8,128)(2,1)S(1)}, u32[]{:S(2)}, u32[]{:S(2)}) collective-permute-start(bf16[64,384]{1,0:T(8,128)(2,1)S(1)} %add_convert_fusion.1), channel_id=1, source_target_pairs={{0,4},{1,5},{2,6},{3,7},{4,0},{5,1},{6,2},{7,3},{8,12},{9,13},{10,... | collective-permute-start | bytes 147464 | tf_op jit(solution)/shard_map/ppermute | solution.py:42
  112.3 1.2 collective-permute-start.23
  113.5 2.7 %collective-permute-done.22 = bf16[64,384]{1,0:T(8,128)(2,1)S(1)} collective-permute-done((bf16[64,384]{1,0:T(8,128)(2,1)S(1)}, bf16[64,384]{1,0:T(8,128)(2,1)S(1)}, u32[]{:S(2)}, u32[]{:S(2)}) %collective-permute-start.22) | collective-permute-done | bytes 49184 | tf_op jit(solution)/shard_map/ppermute | solution.py:42
  116.3 1.9 %collective-permute-done.23 = bf16[64,384]{1,0:T(8,128)(2,1)S(1)} collective-permute-done((bf16[64,384]{1,0:T(8,128)(2,1)S(1)}, bf16[64,384]{1,0:T(8,128)(2,1)S(1)}, u32[]{:S(2)}, u32[]{:S(2)}) %collective-permute-start.23) | collective-permute-done | bytes 49184 | tf_op jit(solution)/shard_map/ppermute | solution.py:42
  119.1 11.3 %all-gather.1 = bf16[256,1026]{1,0:T(8,128)(2,1)S(1)} all-gather(bf16[64,1026]{1,0:T(8,128)(2,1)S(1)} %concatenate.39), channel_id=3, replica_groups=mesh['gx'=4,'gy'=8] {'gx'}, dimensions={0}, use_global_device_ids=true | all-gather | bytes 656640 | tf_op jit(solution)/shard_map/all_gather | solution.py:19
  131.1 1.2 collective-permute-done.24
  132.4 1.7 collective-permute-start.26
  134.2 2.7 %collective-permute-start.27 = (bf16[64,384]{1,0:T(8,128)(2,1)S(1)}, bf16[64,384]{1,0:T(8,128)(2,1)S(1)}, u32[]{:S(2)}, u32[]{:S(2)}) collective-permute-start(bf16[64,384]{1,0:T(8,128)(2,1)S(1)} %add_convert_fusion), channel_id=1, source_target_pairs={{0,6},{1,7},{2,4},{3,5},{4,2},{5,3},{6,0},{7,1},{8,14},{9,15},{10,... | collective-permute-start | bytes 147464 | tf_op jit(solution)/shard_map/ppermute | solution.py:42
  137.1 2.2 %collective-permute-done.26 = bf16[64,384]{1,0:T(8,128)(2,1)S(1)} collective-permute-done((bf16[64,384]{1,0:T(8,128)(2,1)S(1)}, bf16[64,384]{1,0:T(8,128)(2,1)S(1)}, u32[]{:S(2)}, u32[]{:S(2)}) %collective-permute-start.26) | collective-permute-done | bytes 49184 | tf_op jit(solution)/shard_map/ppermute | solution.py:42
  140.3 3.3 %convolution_convert_fusion = bf16[64,6144]{1,0:T(8,128)(2,1)S(1)} fusion(bf16[384,6144]{1,0:T(8,128)(2,1)} %param.27, f32[64,384]{1,0:T(8,128)S(1)} %get-tuple-element.10, f32[384]{0:T(512)S(1)} %copy-done.5), kind=kOutput, calls=%fused_computation.14 | convolution fusion | flops 302432256 | bytes 5604864 | tf_op jit(solution)/shard_map/dot_general | solution.py:259
  143.8 13.8 %all_to_all.5 = bf16[64,4,1538]{2,0,1:T(8,128)(2,1)S(1)} all-to-all(bf16[64,4,1538]{2,0,1:T(8,128)(2,1)S(1)} %pad_maximum_fusion), channel_id=1, replica_groups=mesh['gx'=4,'gy'=8] {'gx'}, dimensions={1} | all-to-all | bytes 1574912 | tf_op jit(solution)/shard_map/all_to_all | solution.py:270
  159.5 2.2 %collective-permute-start.30 = (f32[64]{0:T(128)S(1)}, f32[64]{0:T(128)S(1)}, u32[]{:S(2)}, u32[]{:S(2)}) collective-permute-start(f32[64]{0:T(128)S(1)} %get-tuple-element.7), channel_id=1, source_target_pairs={{0,24},{8,16},{16,8},{24,0},{1,25},{9,17},{17,9},{25,1},{2,26},{10... | collective-permute-start | bytes 776 | tf_op jit(solution)/shard_map/ppermute | solution.py:70
  162.5 1.5 collective-permute-done.30
  165.2 2.9 %collective-permute-start.33 = (f32[64]{0:T(128)S(1)}, f32[64]{0:T(128)S(1)}, u32[]{:S(2)}, u32[]{:S(2)}) collective-permute-start(f32[64]{0:T(128)S(1)} %max.146), channel_id=1, source_target_pairs={{0,4},{1,5},{2,6},{3,7},{4,0},{5,1},{6,2},{7,3},{8,12},{9,13},{10,... | collective-permute-start | bytes 776 | tf_op jit(solution)/shard_map/ppermute | solution.py:42
  168.1 1.4 collective-permute-start.34
  170.2 3.2 %collective-permute-done.34 = f32[64]{0:T(128)S(1)} collective-permute-done((f32[64]{0:T(128)S(1)}, f32[64]{0:T(128)S(1)}, u32[]{:S(2)}, u32[]{:S(2)}) %collective-permute-start.34) | collective-permute-done | bytes 288 | tf_op jit(solution)/shard_map/ppermute | solution.py:42
  (199 shorter events, 29.3 us)
Async XLA Ops:
  4.6 13.8 %collective-permute-start = (bf16[64,388]{0,1:T(8,128)(2,1)S(1)}, bf16[64,388]{0,1:T(8,128)(2,1)S(1)}, u32[]{:S(2)}, u32[]{:S(2)}) collective-permute-start(bf16[64,388]{0,1:T(8,128)(2,1)S(1)} %pad_maximum_fusion.1), channel_id=1, source_target_pairs={{0,8},{8,0},{16,24},{24,16},{1,9},{9,1},{17,25},{25,17},{2,10},{10... | collective-permute-start | bytes 149000 | tf_op jit(solution)/shard_map/ppermute | solution.py:25
  7.6 10.8 %collective-permute-start.1 = (bf16[64,388]{0,1:T(8,128)(2,1)S(1)}, bf16[64,388]{0,1:T(8,128)(2,1)S(1)}, u32[]{:S(2)}, u32[]{:S(2)}) collective-permute-start(bf16[64,388]{0,1:T(8,128)(2,1)S(1)} %pad_maximum_fusion.1), channel_id=1, source_target_pairs={{0,16},{8,24},{16,0},{24,8},{1,17},{9,25},{17,1},{25,9},{2,18},{10... | collective-permute-start | bytes 149000 | tf_op jit(solution)/shard_map/ppermute | solution.py:25
  9.1 9.3 %collective-permute-start.2 = (bf16[64,388]{0,1:T(8,128)(2,1)S(1)}, bf16[64,388]{0,1:T(8,128)(2,1)S(1)}, u32[]{:S(2)}, u32[]{:S(2)}) collective-permute-start(bf16[64,388]{0,1:T(8,128)(2,1)S(1)} %pad_maximum_fusion.1), channel_id=1, source_target_pairs={{0,24},{8,16},{16,8},{24,0},{1,25},{9,17},{17,9},{25,1},{2,26},{10... | collective-permute-start | bytes 149000 | tf_op jit(solution)/shard_map/ppermute | solution.py:25
  12.7 7.7 %copy-start.10 = (f32[2,128,2,128]{3,2,1,0:T(2,128)S(1)}, f32[2,128,2,128]{3,2,1,0:T(2,128)}, u32[]{:S(2)}) copy-start(f32[2,128,2,128]{3,2,1,0:T(2,128)} %param.29) | copy-start | bytes 786436
  20.3 22.0 %copy-start.4 = (bf16[2,128,384]{2,1,0:T(8,128)(2,1)S(1)}, bf16[2,128,384]{2,1,0:T(8,128)(2,1)}, u32[]{:S(2)}) copy-start(bf16[2,128,384]{2,1,0:T(8,128)(2,1)} %param.23) | copy-start | bytes 589828
  20.3 27.9 %copy-start.6 = (f32[2,384]{1,0:T(2,128)S(1)}, f32[2,384]{1,0:T(2,128)}, u32[]{:S(2)}) copy-start(f32[2,384]{1,0:T(2,128)} %param.18) | copy-start | bytes 9220
  20.4 33.6 %copy-start.3 = (bf16[64,384]{1,0:T(8,128)(2,1)S(1)}, bf16[64,384]{1,0:T(8,128)(2,1)}, u32[]{:S(2)}) copy-start(bf16[64,384]{1,0:T(8,128)(2,1)} %param.16) | copy-start | bytes 147460
  26.2 27.8 %copy-start = (bf16[2,384,512]{2,1,0:T(8,128)(2,1)S(1)}, bf16[2,384,512]{2,1,0:T(8,128)(2,1)}, u32[]{:S(2)}) copy-start(bf16[2,384,512]{2,1,0:T(8,128)(2,1)} %param.25) | copy-start | bytes 2359300
  26.2 28.0 %copy-start.1 = (bf16[2,384,512]{2,1,0:T(8,128)(2,1)S(1)}, bf16[2,384,512]{2,1,0:T(8,128)(2,1)}, u32[]{:S(2)}) copy-start(bf16[2,384,512]{2,1,0:T(8,128)(2,1)} %param.24) | copy-start | bytes 2359300
  27.6 48.0 %copy-start.2 = (bf16[2,384,384]{2,1,0:T(8,128)(2,1)S(1)}, bf16[2,384,384]{2,1,0:T(8,128)(2,1)}, u32[]{:S(2)}) copy-start(bf16[2,384,384]{2,1,0:T(8,128)(2,1)} %param.20) | copy-start | bytes 1769476
  27.6 48.3 %copy-start.8 = (bf16[2,384,2]{1,2,0:T(2,128)(2,1)S(1)}, bf16[2,384,2]{1,2,0:T(2,128)(2,1)}, u32[]{:S(2)}) copy-start(bf16[2,384,2]{1,2,0:T(2,128)(2,1)} %param.21) | copy-start | bytes 9220
  33.2 4.4 %collective-permute-start.3 = (f32[64,2,66]{0,1,2:T(2,128)S(1)}, f32[64,2,66]{0,1,2:T(2,128)S(1)}, u32[]{:S(2)}, u32[]{:S(2)}) collective-permute-start(f32[64,2,66]{0,1,2:T(2,128)S(1)} %pad_maximum_fusion.3), channel_id=1, source_target_pairs={{0,8},{8,0},{16,24},{24,16},{1,9},{9,1},{17,25},{25,17},{2,10},{10... | collective-permute-start | bytes 101384 | tf_op jit(solution)/shard_map/ppermute | solution.py:42
  35.2 4.9 %collective-permute-start.4 = (f32[64,2,66]{0,1,2:T(2,128)S(1)}, f32[64,2,66]{0,1,2:T(2,128)S(1)}, u32[]{:S(2)}, u32[]{:S(2)}) collective-permute-start(f32[64,2,66]{0,1,2:T(2,128)S(1)} %pad_maximum_fusion.3), channel_id=1, source_target_pairs={{0,16},{8,24},{16,0},{24,8},{1,17},{9,25},{17,1},{25,9},{2,18},{10... | collective-permute-start | bytes 101384 | tf_op jit(solution)/shard_map/ppermute | solution.py:42
  36.7 5.2 %collective-permute-start.5 = (f32[64,2,66]{0,1,2:T(2,128)S(1)}, f32[64,2,66]{0,1,2:T(2,128)S(1)}, u32[]{:S(2)}, u32[]{:S(2)}) collective-permute-start(f32[64,2,66]{0,1,2:T(2,128)S(1)} %pad_maximum_fusion.3), channel_id=1, source_target_pairs={{0,24},{8,16},{16,8},{24,0},{1,25},{9,17},{17,9},{25,1},{2,26},{10... | collective-permute-start | bytes 101384 | tf_op jit(solution)/shard_map/ppermute | solution.py:42
  42.5 1.3 collective-permute-start.6
  43.8 4.5 %collective-permute-start.7 = (bf16[64,384]{1,0:T(8,128)(2,1)S(1)}, bf16[64,384]{1,0:T(8,128)(2,1)S(1)}, u32[]{:S(2)}, u32[]{:S(2)}) collective-permute-start(bf16[64,384]{1,0:T(8,128)(2,1)S(1)} %add_convert_fusion.3), channel_id=1, source_target_pairs={{0,2},{1,3},{2,0},{3,1},{4,6},{5,7},{6,4},{7,5},{8,10},{9,11},{10,... | collective-permute-start | bytes 147464 | tf_op jit(solution)/shard_map/ppermute | solution.py:42
  45.4 5.9 %collective-permute-start.8 = (bf16[64,384]{1,0:T(8,128)(2,1)S(1)}, bf16[64,384]{1,0:T(8,128)(2,1)S(1)}, u32[]{:S(2)}, u32[]{:S(2)}) collective-permute-start(bf16[64,384]{1,0:T(8,128)(2,1)S(1)} %add_convert_fusion.3), channel_id=1, source_target_pairs={{0,4},{1,5},{2,6},{3,7},{4,0},{5,1},{6,2},{7,3},{8,12},{9,13},{10,... | collective-permute-start | bytes 147464 | tf_op jit(solution)/shard_map/ppermute | solution.py:42
  48.0 5.9 %collective-permute-start.9 = (bf16[64,384]{1,0:T(8,128)(2,1)S(1)}, bf16[64,384]{1,0:T(8,128)(2,1)S(1)}, u32[]{:S(2)}, u32[]{:S(2)}) collective-permute-start(bf16[64,384]{1,0:T(8,128)(2,1)S(1)} %add_convert_fusion.3), channel_id=1, source_target_pairs={{0,6},{1,7},{2,4},{3,5},{4,2},{5,3},{6,0},{7,1},{8,14},{9,15},{10,... | collective-permute-start | bytes 147464 | tf_op jit(solution)/shard_map/ppermute | solution.py:42
  66.4 1.3 collective-permute-start.10
  67.7 4.9 %collective-permute-start.11 = (bf16[64,384]{1,0:T(8,128)(2,1)S(1)}, bf16[64,384]{1,0:T(8,128)(2,1)S(1)}, u32[]{:S(2)}, u32[]{:S(2)}) collective-permute-start(bf16[64,384]{1,0:T(8,128)(2,1)S(1)} %add_convert_fusion.2), channel_id=1, source_target_pairs={{0,2},{1,3},{2,0},{3,1},{4,6},{5,7},{6,4},{7,5},{8,10},{9,11},{10,... | collective-permute-start | bytes 147464 | tf_op jit(solution)/shard_map/ppermute | solution.py:42
  67.8 7.0 %collective-permute-start.12 = (bf16[64,384]{1,0:T(8,128)(2,1)S(1)}, bf16[64,384]{1,0:T(8,128)(2,1)S(1)}, u32[]{:S(2)}, u32[]{:S(2)}) collective-permute-start(bf16[64,384]{1,0:T(8,128)(2,1)S(1)} %add_convert_fusion.2), channel_id=1, source_target_pairs={{0,4},{1,5},{2,6},{3,7},{4,0},{5,1},{6,2},{7,3},{8,12},{9,13},{10,... | collective-permute-start | bytes 147464 | tf_op jit(solution)/shard_map/ppermute | solution.py:42
  69.5 5.9 %collective-permute-start.13 = (bf16[64,384]{1,0:T(8,128)(2,1)S(1)}, bf16[64,384]{1,0:T(8,128)(2,1)S(1)}, u32[]{:S(2)}, u32[]{:S(2)}) collective-permute-start(bf16[64,384]{1,0:T(8,128)(2,1)S(1)} %add_convert_fusion.2), channel_id=1, source_target_pairs={{0,6},{1,7},{2,4},{3,5},{4,2},{5,3},{6,0},{7,1},{8,14},{9,15},{10,... | collective-permute-start | bytes 147464 | tf_op jit(solution)/shard_map/ppermute | solution.py:42
  76.0 9.3 %collective-permute-start.14 = (bf16[64,388]{0,1:T(8,128)(2,1)S(1)}, bf16[64,388]{0,1:T(8,128)(2,1)S(1)}, u32[]{:S(2)}, u32[]{:S(2)}) collective-permute-start(bf16[64,388]{0,1:T(8,128)(2,1)S(1)} %pad_maximum_fusion.2), channel_id=1, source_target_pairs={{0,8},{8,0},{16,24},{24,16},{1,9},{9,1},{17,25},{25,17},{2,10},{10... | collective-permute-start | bytes 149000 | tf_op jit(solution)/shard_map/ppermute | solution.py:25
  77.8 7.5 %collective-permute-start.15 = (bf16[64,388]{0,1:T(8,128)(2,1)S(1)}, bf16[64,388]{0,1:T(8,128)(2,1)S(1)}, u32[]{:S(2)}, u32[]{:S(2)}) collective-permute-start(bf16[64,388]{0,1:T(8,128)(2,1)S(1)} %pad_maximum_fusion.2), channel_id=1, source_target_pairs={{0,16},{8,24},{16,0},{24,8},{1,17},{9,25},{17,1},{25,9},{2,18},{10... | collective-permute-start | bytes 149000 | tf_op jit(solution)/shard_map/ppermute | solution.py:25
  78.1 7.2 %collective-permute-start.16 = (bf16[64,388]{0,1:T(8,128)(2,1)S(1)}, bf16[64,388]{0,1:T(8,128)(2,1)S(1)}, u32[]{:S(2)}, u32[]{:S(2)}) collective-permute-start(bf16[64,388]{0,1:T(8,128)(2,1)S(1)} %pad_maximum_fusion.2), channel_id=1, source_target_pairs={{0,24},{8,16},{16,8},{24,0},{1,25},{9,17},{17,9},{25,1},{2,26},{10... | collective-permute-start | bytes 149000 | tf_op jit(solution)/shard_map/ppermute | solution.py:25
  93.0 37.7 %copy-start.9 = (bf16[2,512,384]{2,1,0:T(8,128)(2,1)S(1)}, bf16[2,512,384]{2,1,0:T(8,128)(2,1)}, u32[]{:S(2)}) copy-start(bf16[2,512,384]{2,1,0:T(8,128)(2,1)} %param.26) | copy-start | bytes 2359300
  94.4 45.9 %copy-start.5 = (f32[384]{0:T(512)S(1)}, f32[384]{0:T(512)}, u32[]{:S(2)}) copy-start(f32[384]{0:T(512)} %param.19) | copy-start | bytes 4612
  99.9 4.5 %collective-permute-start.17 = (f32[64,2,66]{0,1,2:T(2,128)S(1)}, f32[64,2,66]{0,1,2:T(2,128)S(1)}, u32[]{:S(2)}, u32[]{:S(2)}) collective-permute-start(f32[64,2,66]{0,1,2:T(2,128)S(1)} %pad_maximum_fusion.4), channel_id=1, source_target_pairs={{0,8},{8,0},{16,24},{24,16},{1,9},{9,1},{17,25},{25,17},{2,10},{10... | collective-permute-start | bytes 101384 | tf_op jit(solution)/shard_map/ppermute | solution.py:42
  101.7 4.3 %collective-permute-start.18 = (f32[64,2,66]{0,1,2:T(2,128)S(1)}, f32[64,2,66]{0,1,2:T(2,128)S(1)}, u32[]{:S(2)}, u32[]{:S(2)}) collective-permute-start(f32[64,2,66]{0,1,2:T(2,128)S(1)} %pad_maximum_fusion.4), channel_id=1, source_target_pairs={{0,16},{8,24},{16,0},{24,8},{1,17},{9,25},{17,1},{25,9},{2,18},{10... | collective-permute-start | bytes 101384 | tf_op jit(solution)/shard_map/ppermute | solution.py:42
  102.0 5.2 %collective-permute-start.19 = (f32[64,2,66]{0,1,2:T(2,128)S(1)}, f32[64,2,66]{0,1,2:T(2,128)S(1)}, u32[]{:S(2)}, u32[]{:S(2)}) collective-permute-start(f32[64,2,66]{0,1,2:T(2,128)S(1)} %pad_maximum_fusion.4), channel_id=1, source_target_pairs={{0,24},{8,16},{16,8},{24,0},{1,25},{9,17},{17,9},{25,1},{2,26},{10... | collective-permute-start | bytes 101384 | tf_op jit(solution)/shard_map/ppermute | solution.py:42
  107.8 1.3 collective-permute-start.20
  109.1 4.5 %collective-permute-start.21 = (bf16[64,384]{1,0:T(8,128)(2,1)S(1)}, bf16[64,384]{1,0:T(8,128)(2,1)S(1)}, u32[]{:S(2)}, u32[]{:S(2)}) collective-permute-start(bf16[64,384]{1,0:T(8,128)(2,1)S(1)} %add_convert_fusion.1), channel_id=1, source_target_pairs={{0,2},{1,3},{2,0},{3,1},{4,6},{5,7},{6,4},{7,5},{8,10},{9,11},{10,... | collective-permute-start | bytes 147464 | tf_op jit(solution)/shard_map/ppermute | solution.py:42
  110.3 6.0 %collective-permute-start.22 = (bf16[64,384]{1,0:T(8,128)(2,1)S(1)}, bf16[64,384]{1,0:T(8,128)(2,1)S(1)}, u32[]{:S(2)}, u32[]{:S(2)}) collective-permute-start(bf16[64,384]{1,0:T(8,128)(2,1)S(1)} %add_convert_fusion.1), channel_id=1, source_target_pairs={{0,4},{1,5},{2,6},{3,7},{4,0},{5,1},{6,2},{7,3},{8,12},{9,13},{10,... | collective-permute-start | bytes 147464 | tf_op jit(solution)/shard_map/ppermute | solution.py:42
  112.3 5.9 %collective-permute-start.23 = (bf16[64,384]{1,0:T(8,128)(2,1)S(1)}, bf16[64,384]{1,0:T(8,128)(2,1)S(1)}, u32[]{:S(2)}, u32[]{:S(2)}) collective-permute-start(bf16[64,384]{1,0:T(8,128)(2,1)S(1)} %add_convert_fusion.1), channel_id=1, source_target_pairs={{0,6},{1,7},{2,4},{3,5},{4,2},{5,3},{6,0},{7,1},{8,14},{9,15},{10,... | collective-permute-start | bytes 147464 | tf_op jit(solution)/shard_map/ppermute | solution.py:42
  131.0 1.3 collective-permute-start.24
  132.4 4.8 %collective-permute-start.25 = (bf16[64,384]{1,0:T(8,128)(2,1)S(1)}, bf16[64,384]{1,0:T(8,128)(2,1)S(1)}, u32[]{:S(2)}, u32[]{:S(2)}) collective-permute-start(bf16[64,384]{1,0:T(8,128)(2,1)S(1)} %add_convert_fusion), channel_id=1, source_target_pairs={{0,2},{1,3},{2,0},{3,1},{4,6},{5,7},{6,4},{7,5},{8,10},{9,11},{10,... | collective-permute-start | bytes 147464 | tf_op jit(solution)/shard_map/ppermute | solution.py:42
  132.4 6.9 %collective-permute-start.26 = (bf16[64,384]{1,0:T(8,128)(2,1)S(1)}, bf16[64,384]{1,0:T(8,128)(2,1)S(1)}, u32[]{:S(2)}, u32[]{:S(2)}) collective-permute-start(bf16[64,384]{1,0:T(8,128)(2,1)S(1)} %add_convert_fusion), channel_id=1, source_target_pairs={{0,4},{1,5},{2,6},{3,7},{4,0},{5,1},{6,2},{7,3},{8,12},{9,13},{10,... | collective-permute-start | bytes 147464 | tf_op jit(solution)/shard_map/ppermute | solution.py:42
  134.2 5.9 %collective-permute-start.27 = (bf16[64,384]{1,0:T(8,128)(2,1)S(1)}, bf16[64,384]{1,0:T(8,128)(2,1)S(1)}, u32[]{:S(2)}, u32[]{:S(2)}) collective-permute-start(bf16[64,384]{1,0:T(8,128)(2,1)S(1)} %add_convert_fusion), channel_id=1, source_target_pairs={{0,6},{1,7},{2,4},{3,5},{4,2},{5,3},{6,0},{7,1},{8,14},{9,15},{10,... | collective-permute-start | bytes 147464 | tf_op jit(solution)/shard_map/ppermute | solution.py:42
  158.2 15.8 %copy-start.7 = (f32[64]{0:T(128)}, f32[64]{0:T(128)S(1)}, u32[]{:S(2)}) copy-start(f32[64]{0:T(128)S(1)} %get-tuple-element.8) | copy-start | bytes 772
  158.2 3.6 %collective-permute-start.28 = (f32[64]{0:T(128)S(1)}, f32[64]{0:T(128)S(1)}, u32[]{:S(2)}, u32[]{:S(2)}) collective-permute-start(f32[64]{0:T(128)S(1)} %get-tuple-element.7), channel_id=1, source_target_pairs={{0,8},{8,0},{16,24},{24,16},{1,9},{9,1},{17,25},{25,17},{2,10},{10... | collective-permute-start | bytes 776 | tf_op jit(solution)/shard_map/ppermute | solution.py:70
  159.0 3.5 %collective-permute-start.29 = (f32[64]{0:T(128)S(1)}, f32[64]{0:T(128)S(1)}, u32[]{:S(2)}, u32[]{:S(2)}) collective-permute-start(f32[64]{0:T(128)S(1)} %get-tuple-element.7), channel_id=1, source_target_pairs={{0,16},{8,24},{16,0},{24,8},{1,17},{9,25},{17,1},{25,9},{2,18},{10... | collective-permute-start | bytes 776 | tf_op jit(solution)/shard_map/ppermute | solution.py:70
  159.5 4.4 %collective-permute-start.30 = (f32[64]{0:T(128)S(1)}, f32[64]{0:T(128)S(1)}, u32[]{:S(2)}, u32[]{:S(2)}) collective-permute-start(f32[64]{0:T(128)S(1)} %get-tuple-element.7), channel_id=1, source_target_pairs={{0,24},{8,16},{16,8},{24,0},{1,25},{9,17},{17,9},{25,1},{2,26},{10... | collective-permute-start | bytes 776 | tf_op jit(solution)/shard_map/ppermute | solution.py:70
  164.0 1.1 collective-permute-start.31
  165.1 5.1 %collective-permute-start.32 = (f32[64]{0:T(128)S(1)}, f32[64]{0:T(128)S(1)}, u32[]{:S(2)}, u32[]{:S(2)}) collective-permute-start(f32[64]{0:T(128)S(1)} %max.146), channel_id=1, source_target_pairs={{0,2},{1,3},{2,0},{3,1},{4,6},{5,7},{6,4},{7,5},{8,10},{9,11},{10,... | collective-permute-start | bytes 776 | tf_op jit(solution)/shard_map/ppermute | solution.py:42
  165.2 5.0 %collective-permute-start.33 = (f32[64]{0:T(128)S(1)}, f32[64]{0:T(128)S(1)}, u32[]{:S(2)}, u32[]{:S(2)}) collective-permute-start(f32[64]{0:T(128)S(1)} %max.146), channel_id=1, source_target_pairs={{0,4},{1,5},{2,6},{3,7},{4,0},{5,1},{6,2},{7,3},{8,12},{9,13},{10,... | collective-permute-start | bytes 776 | tf_op jit(solution)/shard_map/ppermute | solution.py:42
  168.1 5.3 %collective-permute-start.34 = (f32[64]{0:T(128)S(1)}, f32[64]{0:T(128)S(1)}, u32[]{:S(2)}, u32[]{:S(2)}) collective-permute-start(f32[64]{0:T(128)S(1)} %max.146), channel_id=1, source_target_pairs={{0,6},{1,7},{2,4},{3,5},{4,2},{5,3},{6,0},{7,1},{8,14},{9,15},{10,... | collective-permute-start | bytes 776 | tf_op jit(solution)/shard_map/ppermute | solution.py:42

commit v12 on v11

--- a/solution.py
+++ b/solution.py
@@ -120,18 +120,24 @@
 def local_attention(queries, forget_log, kv_layer, decay_layer, owner, live, member):
     slots, tokens, heads, width = kv_layer.shape
     safe_owner = jnp.maximum(owner, 0)
-    slot_queries = queries[safe_owner]
+    hot = member.T
+    hot_half = hot.astype(jnp.bfloat16)
+    hot_full = hot.astype(jnp.float32)
+    slot_queries = jnp.einsum(
+        "pr,rhd->phd", hot_half, queries, preferred_element_type=jnp.float32
+    ).astype(jnp.bfloat16)
     padded = jnp.concatenate([slot_queries, jnp.zeros_like(slot_queries)], axis=2)
     diagonal = jnp.eye(heads, dtype=jnp.bfloat16)
     query_block = diagonal[None, :, :, None] * padded[:, :, None, :]
     scores = jnp.einsum(
         "pthc,pkhc->pkt", kv_layer, query_block, preferred_element_type=jnp.float32
     ) * SCORE_SCALE
-    scores = scores + decay_layer + forget_log[safe_owner][:, :, None]
+    slot_forget = jnp.einsum("pr,rh->ph", hot_full, forget_log, precision=lax.Precision.HIGHEST)
+    scores = scores + decay_layer + slot_forget[:, :, None]
     scores = jnp.where(live[:, None, :], scores, NEGATIVE)
     page_peak = jnp.max(scores, axis=2)
     row_peak = jnp.max(jnp.where(member[:, :, None], page_peak[None], NEGATIVE), axis=1)
-    slot_peak = row_peak[safe_owner]
+    slot_peak = jnp.einsum("pr,rh->ph", hot_full, row_peak, precision=lax.Precision.HIGHEST)
     weights = jnp.where(live[:, None, :], jnp.exp(scores - slot_peak[:, :, None]), 0.0)
     page_sum = jnp.sum(weights, axis=2)
     mixed = jnp.einsum(

time: 175 us -> 171 us (0.977)
  local copies, waits for them, and re-layouts: 9.83 us -> 4.98 us
    gather x6 -> x0, local copies, waits for them, and re-layouts: 4.1 us -> none  [the longest x2 1.48 us: local_attention(): slot_queries = queries[safe_owner]]
  transfers between devices with their start and end apart: 35 -> 35, of which waited for: 25 -> 25; matrix products, arithmetic and copies ran while one was open for 3% -> 2% of each run, Pallas kernels for 7% -> 7%
where the time goes in v12:
time: 171 us
  starting transfers between devices  41.2 us (24%)
  waiting for transfers between devices  37.2 us (22%)
  blocking collectives  35 us (20%)
  matrix products  32 us (19%)
  Pallas kernels  11.5 us (7%)
  other arithmetic  7.34 us (4%)
  local copies, waits for them, and re-layouts  4.98 us (3%)
    ppermute x26, waiting for transfers between devices, exchange(): return lax.ppermute(value, axis, [(i, i ^ partner) for i in range(count)])  34.9 us
    ppermute x26, starting transfers between devices, exchange(): return lax.ppermute(value, axis, [(i, i ^ partner) for i in range(count)])  29.6 us
    all_gather x2, blocking collectives, gather_sum(): return jnp.sum(lax.all_gather(value, axis).astype(jnp.float32), axis=0)  21.3 us
    all_to_all x1, blocking collectives, local(): pieces = lax.all_to_all(pieces, 'gx', 1, 1, tiled=True).astype(jnp.float32)  13.8 us
    dot_general x2, matrix products, local_attention(): jnp.einsum('pthc,pkhc->pkt', kv_layer, query_block, preferred_element_typ...  11.7 us
    pallas_call x2, Pallas kernels, layer_slice(): pl.pallas_call(copy_block, grid=(slots // block,), in_specs=[pl.BlockSpec...  11.5 us
    dot_general x2, matrix products, local_attention(): jnp.einsum('pkt,pthc->pkhc', weights.astype(jnp.bfloat16), kv_layer, pref...  9.36 us
    ppermute x6, starting transfers between devices, xor_sum(): lax.ppermute(value, axis, [(i, i ^ k) for i in range(count)])  8.1 us
  transfers between devices with their start and end apart: 35, of which 25 were waited for; matrix products, arithmetic and copies ran while one was open for 2% of the time, Pallas kernels for 7%

profile of v12, /device:TPU:0, one launch (start us, length us, event | category | flops | bytes accessed | tf_op | source)
XLA Modules:
  0.0 170.7 jit_solution(8873436748068645183)
XLA Ops:
  2.3 1.3 convolution_convert_fusion.2
  4.6 3.0 %collective-permute-start = (bf16[64,388]{0,1:T(8,128)(2,1)S(1)}, bf16[64,388]{0,1:T(8,128)(2,1)S(1)}, u32[]{:S(2)}, u32[]{:S(2)}) collective-permute-start(bf16[64,388]{0,1:T(8,128)(2,1)S(1)} %pad_maximum_fusion.1), channel_id=1, source_target_pairs={{0,8},{8,0},{16,24},{24,16},{1,9},{9,1},{17,25},{25,17},{2,10},{10... | collective-permute-start | bytes 149000 | tf_op jit(solution)/shard_map/ppermute | solution.py:25
  7.6 1.5 collective-permute-start.1
  12.6 5.8 %shard_map.175 = bf16[128,128,2,128]{3,2,1,0:T(2,128)(2,1)} custom-call(bf16[2,128,128,2,128]{4,3,2,1,0:T(2,128)(2,1)} %source.3), custom_call_target="tpu_custom_call" | custom-call | bytes 16777216 | tf_op jit(solution)/shard_map/pallas_call | solution.py:84
  19.1 5.9 %fusion.239 = (f32[128,2]{1,0:T(8,128)S(1)}, f32[128,2,128]{2,1,0:T(2,128)S(1)}) fusion(f32[128,2]{1,0:T(8,128)S(1)} %fusion.134, f32[2,128,2,128]{3,2,1,0:T(2,128)S(1)} %copy-done.10, bf16[128,128,2,128]{3,2,1,0:T(2,128)(2,1)} %shard_map.175, bf16[128,2,128]{2,1,0:T(2,128)(2,1)S(1)} %concatenate.33.clone, bf16[2,2]{0,1:T(2,128)(2,1)S(1)} %compare_convert_fusion, ...), kind=kOutput, calls=%fused_computation.352 | convolution fusion | flops 17202944 | bytes 8734728 | tf_op jit(solution)/shard_map/pthc,pkhc->pkt/dot_general | solution.py:132
  25.9 4.7 %fusion.4 = f32[128,2,2,128]{3,1,2,0:T(2,128)S(1)} fusion(bf16[128,128,2,128]{3,2,1,0:T(2,128)(2,1)} %shard_map.175, f32[128,2,128]{2,1,0:T(2,128)S(1)} %get-tuple-element.54, pred[128,128]{1,0:T(8,128)(4,1)S(1)} %fusion.117, f32[128,2]{1,0:T(8,128)S(1)} %fusion.132), kind=kOutput, calls=%fused_computation.4 | convolution fusion | flops 16875520 | bytes 8799232 | tf_op jit(solution)/shard_map/pkt,pthc->pkhc/dot_general | solution.py:143
  31.5 2.0 %collective-permute-start.3 = (f32[64,2,66]{0,1,2:T(2,128)S(1)}, f32[64,2,66]{0,1,2:T(2,128)S(1)}, u32[]{:S(2)}, u32[]{:S(2)}) collective-permute-start(f32[64,2,66]{0,1,2:T(2,128)S(1)} %pad_maximum_fusion.3), channel_id=1, source_target_pairs={{0,8},{8,0},{16,24},{24,16},{1,9},{9,1},{17,25},{25,17},{2,10},{10... | collective-permute-start | bytes 101384 | tf_op jit(solution)/shard_map/ppermute | solution.py:42
  33.5 1.5 collective-permute-start.4
  35.9 2.6 %collective-permute-done.4 = f32[64,2,66]{0,1,2:T(2,128)S(1)} collective-permute-done((f32[64,2,66]{0,1,2:T(2,128)S(1)}, f32[64,2,66]{0,1,2:T(2,128)S(1)}, u32[]{:S(2)}, u32[]{:S(2)}) %collective-permute-start.4) | collective-permute-done | bytes 33824 | tf_op jit(solution)/shard_map/ppermute | solution.py:42
  38.4 1.8 %collective-permute-done.5 = f32[64,2,66]{0,1,2:T(2,128)S(1)} collective-permute-done((f32[64,2,66]{0,1,2:T(2,128)S(1)}, f32[64,2,66]{0,1,2:T(2,128)S(1)}, u32[]{:S(2)}, u32[]{:S(2)}) %collective-permute-start.5) | collective-permute-done | bytes 33824 | tf_op jit(solution)/shard_map/ppermute | solution.py:42
  40.9 1.2 collective-permute-done.6
  42.1 1.6 collective-permute-start.7
  43.8 2.6 %collective-permute-start.8 = (bf16[64,384]{1,0:T(8,128)(2,1)S(1)}, bf16[64,384]{1,0:T(8,128)(2,1)S(1)}, u32[]{:S(2)}, u32[]{:S(2)}) collective-permute-start(bf16[64,384]{1,0:T(8,128)(2,1)S(1)} %add_convert_fusion.3), channel_id=1, source_target_pairs={{0,4},{1,5},{2,6},{3,7},{4,0},{5,1},{6,2},{7,3},{8,12},{9,13},{10,... | collective-permute-start | bytes 147464 | tf_op jit(solution)/shard_map/ppermute | solution.py:42
  46.6 3.1 %collective-permute-done.8 = bf16[64,384]{1,0:T(8,128)(2,1)S(1)} collective-permute-done((bf16[64,384]{1,0:T(8,128)(2,1)S(1)}, bf16[64,384]{1,0:T(8,128)(2,1)S(1)}, u32[]{:S(2)}, u32[]{:S(2)}) %collective-permute-start.8) | collective-permute-done | bytes 49184 | tf_op jit(solution)/shard_map/ppermute | solution.py:42
  49.7 2.6 %collective-permute-done.9 = bf16[64,384]{1,0:T(8,128)(2,1)S(1)} collective-permute-done((bf16[64,384]{1,0:T(8,128)(2,1)S(1)}, bf16[64,384]{1,0:T(8,128)(2,1)S(1)}, u32[]{:S(2)}, u32[]{:S(2)}) %collective-permute-start.9) | collective-permute-done | bytes 49184 | tf_op jit(solution)/shard_map/ppermute | solution.py:42
  53.1 9.9 %all-gather = bf16[256,1026]{1,0:T(8,128)(2,1)S(1)} all-gather(bf16[64,1026]{1,0:T(8,128)(2,1)S(1)} %concatenate.35), channel_id=2, replica_groups=mesh['gx'=4,'gy'=8] {'gx'}, dimensions={0}, use_global_device_ids=true | all-gather | bytes 656640 | tf_op jit(solution)/shard_map/all_gather | solution.py:19
  63.4 1.3 convolution_convert_fusion.10
  64.8 1.2 collective-permute-done.10
  66.1 1.7 %collective-permute-start.12 = (bf16[64,384]{1,0:T(8,128)(2,1)S(1)}, bf16[64,384]{1,0:T(8,128)(2,1)S(1)}, u32[]{:S(2)}, u32[]{:S(2)}) collective-permute-start(bf16[64,384]{1,0:T(8,128)(2,1)S(1)} %add_convert_fusion.2), channel_id=1, source_target_pairs={{0,4},{1,5},{2,6},{3,7},{4,0},{5,1},{6,2},{7,3},{8,12},{9,13},{10,... | collective-permute-start | bytes 147464 | tf_op jit(solution)/shard_map/ppermute | solution.py:42
  67.8 2.7 %collective-permute-start.13 = (bf16[64,384]{1,0:T(8,128)(2,1)S(1)}, bf16[64,384]{1,0:T(8,128)(2,1)S(1)}, u32[]{:S(2)}, u32[]{:S(2)}) collective-permute-start(bf16[64,384]{1,0:T(8,128)(2,1)S(1)} %add_convert_fusion.2), channel_id=1, source_target_pairs={{0,6},{1,7},{2,4},{3,5},{4,2},{5,3},{6,0},{7,1},{8,14},{9,15},{10,... | collective-permute-start | bytes 147464 | tf_op jit(solution)/shard_map/ppermute | solution.py:42
  70.9 2.2 %collective-permute-done.12 = bf16[64,384]{1,0:T(8,128)(2,1)S(1)} collective-permute-done((bf16[64,384]{1,0:T(8,128)(2,1)S(1)}, bf16[64,384]{1,0:T(8,128)(2,1)S(1)}, u32[]{:S(2)}, u32[]{:S(2)}) %collective-permute-start.12) | collective-permute-done | bytes 49184 | tf_op jit(solution)/shard_map/ppermute | solution.py:42
  74.4 1.8 %collective-permute-start.14 = (bf16[64,388]{0,1:T(8,128)(2,1)S(1)}, bf16[64,388]{0,1:T(8,128)(2,1)S(1)}, u32[]{:S(2)}, u32[]{:S(2)}) collective-permute-start(bf16[64,388]{0,1:T(8,128)(2,1)S(1)} %pad_maximum_fusion.2), channel_id=1, source_target_pairs={{0,8},{8,0},{16,24},{24,16},{1,9},{9,1},{17,25},{25,17},{2,10},{10... | collective-permute-start | bytes 149000 | tf_op jit(solution)/shard_map/ppermute | solution.py:25
  76.5 1.5 collective-permute-start.16
  77.9 5.7 %shard_map.176 = bf16[128,128,2,128]{3,2,1,0:T(2,128)(2,1)} custom-call(bf16[2,128,128,2,128]{4,3,2,1,0:T(2,128)(2,1)} %source.3), custom_call_target="tpu_custom_call" | custom-call | bytes 16777216 | tf_op jit(solution)/shard_map/pallas_call | solution.py:84
  84.4 5.8 %fusion.240 = (f32[128,2]{1,0:T(8,128)S(1)}, f32[128,2,128]{2,1,0:T(2,128)S(1)}) fusion(f32[128,2]{1,0:T(8,128)S(1)} %fusion.130, f32[2,128,2,128]{3,2,1,0:T(2,128)S(1)} %copy-done.10, bf16[128,128,2,128]{3,2,1,0:T(2,128)(2,1)} %shard_map.176, bf16[128,2,128]{2,1,0:T(2,128)(2,1)S(1)} %concatenate.37.clone, bf16[2,2]{0,1:T(2,128)(2,1)S(1)} %compare_convert_fusion, ...), kind=kOutput, calls=%fused_computation.353 | convolution fusion | flops 17202944 | bytes 8734728 | tf_op jit(solution)/shard_map/pthc,pkhc->pkt/dot_general | solution.py:132
  91.1 4.7 %fusion = f32[128,2,2,128]{3,1,2,0:T(2,128)S(1)} fusion(bf16[128,128,2,128]{3,2,1,0:T(2,128)(2,1)} %shard_map.176, f32[128,2,128]{2,1,0:T(2,128)S(1)} %get-tuple-element.56, pred[128,128]{1,0:T(8,128)(4,1)S(1)} %fusion.117, f32[128,2]{1,0:T(8,128)S(1)} %fusion.128), kind=kOutput, calls=%fused_computation | convolution fusion | flops 16875520 | bytes 8799232 | tf_op jit(solution)/shard_map/pkt,pthc->pkhc/dot_general | solution.py:143
  96.6 1.8 %collective-permute-start.17 = (f32[64,2,66]{0,1,2:T(2,128)S(1)}, f32[64,2,66]{0,1,2:T(2,128)S(1)}, u32[]{:S(2)}, u32[]{:S(2)}) collective-permute-start(f32[64,2,66]{0,1,2:T(2,128)S(1)} %pad_maximum_fusion.4), channel_id=1, source_target_pairs={{0,8},{8,0},{16,24},{24,16},{1,9},{9,1},{17,25},{25,17},{2,10},{10... | collective-permute-start | bytes 101384 | tf_op jit(solution)/shard_map/ppermute | solution.py:42
  98.7 1.5 collective-permute-start.19
  101.1 1.5 collective-permute-done.18
  102.7 1.2 collective-permute-done.19
  104.5 1.2 collective-permute-done.20
  105.8 1.2 collective-permute-start.21
  107.0 2.0 %collective-permute-start.22 = (bf16[64,384]{1,0:T(8,128)(2,1)S(1)}, bf16[64,384]{1,0:T(8,128)(2,1)S(1)}, u32[]{:S(2)}, u32[]{:S(2)}) collective-permute-start(bf16[64,384]{1,0:T(8,128)(2,1)S(1)} %add_convert_fusion.1), channel_id=1, source_target_pairs={{0,4},{1,5},{2,6},{3,7},{4,0},{5,1},{6,2},{7,3},{8,12},{9,13},{10,... | collective-permute-start | bytes 147464 | tf_op jit(solution)/shard_map/ppermute | solution.py:42
  109.0 1.2 collective-permute-start.23
  110.2 2.7 %collective-permute-done.22 = bf16[64,384]{1,0:T(8,128)(2,1)S(1)} collective-permute-done((bf16[64,384]{1,0:T(8,128)(2,1)S(1)}, bf16[64,384]{1,0:T(8,128)(2,1)S(1)}, u32[]{:S(2)}, u32[]{:S(2)}) %collective-permute-start.22) | collective-permute-done | bytes 49184 | tf_op jit(solution)/shard_map/ppermute | solution.py:42
  113.0 1.9 %collective-permute-done.23 = bf16[64,384]{1,0:T(8,128)(2,1)S(1)} collective-permute-done((bf16[64,384]{1,0:T(8,128)(2,1)S(1)}, bf16[64,384]{1,0:T(8,128)(2,1)S(1)}, u32[]{:S(2)}, u32[]{:S(2)}) %collective-permute-start.23) | collective-permute-done | bytes 49184 | tf_op jit(solution)/shard_map/ppermute | solution.py:42
  115.8 11.3 %all-gather.1 = bf16[256,1026]{1,0:T(8,128)(2,1)S(1)} all-gather(bf16[64,1026]{1,0:T(8,128)(2,1)S(1)} %concatenate.39), channel_id=3, replica_groups=mesh['gx'=4,'gy'=8] {'gx'}, dimensions={0}, use_global_device_ids=true | all-gather | bytes 656640 | tf_op jit(solution)/shard_map/all_gather | solution.py:19
  127.8 1.2 collective-permute-done.24
  129.1 1.7 %collective-permute-start.26 = (bf16[64,384]{1,0:T(8,128)(2,1)S(1)}, bf16[64,384]{1,0:T(8,128)(2,1)S(1)}, u32[]{:S(2)}, u32[]{:S(2)}) collective-permute-start(bf16[64,384]{1,0:T(8,128)(2,1)S(1)} %add_convert_fusion), channel_id=1, source_target_pairs={{0,4},{1,5},{2,6},{3,7},{4,0},{5,1},{6,2},{7,3},{8,12},{9,13},{10,... | collective-permute-start | bytes 147464 | tf_op jit(solution)/shard_map/ppermute | solution.py:42
  130.8 2.7 %collective-permute-start.27 = (bf16[64,384]{1,0:T(8,128)(2,1)S(1)}, bf16[64,384]{1,0:T(8,128)(2,1)S(1)}, u32[]{:S(2)}, u32[]{:S(2)}) collective-permute-start(bf16[64,384]{1,0:T(8,128)(2,1)S(1)} %add_convert_fusion), channel_id=1, source_target_pairs={{0,6},{1,7},{2,4},{3,5},{4,2},{5,3},{6,0},{7,1},{8,14},{9,15},{10,... | collective-permute-start | bytes 147464 | tf_op jit(solution)/shard_map/ppermute | solution.py:42
  133.8 2.2 %collective-permute-done.26 = bf16[64,384]{1,0:T(8,128)(2,1)S(1)} collective-permute-done((bf16[64,384]{1,0:T(8,128)(2,1)S(1)}, bf16[64,384]{1,0:T(8,128)(2,1)S(1)}, u32[]{:S(2)}, u32[]{:S(2)}) %collective-permute-start.26) | collective-permute-done | bytes 49184 | tf_op jit(solution)/shard_map/ppermute | solution.py:42
  137.0 3.3 %convolution_convert_fusion = bf16[64,6144]{1,0:T(8,128)(2,1)S(1)} fusion(bf16[384,6144]{1,0:T(8,128)(2,1)} %param.27, f32[64,384]{1,0:T(8,128)S(1)} %get-tuple-element.10, f32[384]{0:T(512)S(1)} %copy-done.5), kind=kOutput, calls=%fused_computation.8 | convolution fusion | flops 302432256 | bytes 5604864 | tf_op jit(solution)/shard_map/dot_general | solution.py:265
  140.5 13.8 %all_to_all.5 = bf16[64,4,1538]{2,0,1:T(8,128)(2,1)S(1)} all-to-all(bf16[64,4,1538]{2,0,1:T(8,128)(2,1)S(1)} %pad_maximum_fusion), channel_id=1, replica_groups=mesh['gx'=4,'gy'=8] {'gx'}, dimensions={1} | all-to-all | bytes 1574912 | tf_op jit(solution)/shard_map/all_to_all | solution.py:276
  156.2 2.2 %collective-permute-start.30 = (f32[64]{0:T(128)S(1)}, f32[64]{0:T(128)S(1)}, u32[]{:S(2)}, u32[]{:S(2)}) collective-permute-start(f32[64]{0:T(128)S(1)} %get-tuple-element.7), channel_id=1, source_target_pairs={{0,24},{8,16},{16,8},{24,0},{1,25},{9,17},{17,9},{25,1},{2,26},{10... | collective-permute-start | bytes 776 | tf_op jit(solution)/shard_map/ppermute | solution.py:70
  159.2 1.5 collective-permute-done.30
  161.8 2.9 %collective-permute-start.33 = (f32[64]{0:T(128)S(1)}, f32[64]{0:T(128)S(1)}, u32[]{:S(2)}, u32[]{:S(2)}) collective-permute-start(f32[64]{0:T(128)S(1)} %max.129), channel_id=1, source_target_pairs={{0,4},{1,5},{2,6},{3,7},{4,0},{5,1},{6,2},{7,3},{8,12},{9,13},{10,... | collective-permute-start | bytes 776 | tf_op jit(solution)/shard_map/ppermute | solution.py:42
  164.8 1.4 collective-permute-start.34
  166.9 3.2 %collective-permute-done.34 = f32[64]{0:T(128)S(1)} collective-permute-done((f32[64]{0:T(128)S(1)}, f32[64]{0:T(128)S(1)}, u32[]{:S(2)}, u32[]{:S(2)}) %collective-permute-start.34) | collective-permute-done | bytes 288 | tf_op jit(solution)/shard_map/ppermute | solution.py:42
  (189 shorter events, 25.9 us)
Async XLA Ops:
  4.6 13.7 %collective-permute-start = (bf16[64,388]{0,1:T(8,128)(2,1)S(1)}, bf16[64,388]{0,1:T(8,128)(2,1)S(1)}, u32[]{:S(2)}, u32[]{:S(2)}) collective-permute-start(bf16[64,388]{0,1:T(8,128)(2,1)S(1)} %pad_maximum_fusion.1), channel_id=1, source_target_pairs={{0,8},{8,0},{16,24},{24,16},{1,9},{9,1},{17,25},{25,17},{2,10},{10... | collective-permute-start | bytes 149000 | tf_op jit(solution)/shard_map/ppermute | solution.py:25
  7.6 10.7 %collective-permute-start.1 = (bf16[64,388]{0,1:T(8,128)(2,1)S(1)}, bf16[64,388]{0,1:T(8,128)(2,1)S(1)}, u32[]{:S(2)}, u32[]{:S(2)}) collective-permute-start(bf16[64,388]{0,1:T(8,128)(2,1)S(1)} %pad_maximum_fusion.1), channel_id=1, source_target_pairs={{0,16},{8,24},{16,0},{24,8},{1,17},{9,25},{17,1},{25,9},{2,18},{10... | collective-permute-start | bytes 149000 | tf_op jit(solution)/shard_map/ppermute | solution.py:25
  9.1 9.2 %collective-permute-start.2 = (bf16[64,388]{0,1:T(8,128)(2,1)S(1)}, bf16[64,388]{0,1:T(8,128)(2,1)S(1)}, u32[]{:S(2)}, u32[]{:S(2)}) collective-permute-start(bf16[64,388]{0,1:T(8,128)(2,1)S(1)} %pad_maximum_fusion.1), channel_id=1, source_target_pairs={{0,24},{8,16},{16,8},{24,0},{1,25},{9,17},{17,9},{25,1},{2,26},{10... | collective-permute-start | bytes 149000 | tf_op jit(solution)/shard_map/ppermute | solution.py:25
  12.6 6.5 %copy-start.10 = (f32[2,128,2,128]{3,2,1,0:T(2,128)S(1)}, f32[2,128,2,128]{3,2,1,0:T(2,128)}, u32[]{:S(2)}) copy-start(f32[2,128,2,128]{3,2,1,0:T(2,128)} %param.29) | copy-start | bytes 786436
  19.1 21.5 %copy-start.4 = (bf16[2,128,384]{2,1,0:T(8,128)(2,1)S(1)}, bf16[2,128,384]{2,1,0:T(8,128)(2,1)}, u32[]{:S(2)}) copy-start(bf16[2,128,384]{2,1,0:T(8,128)(2,1)} %param.23) | copy-start | bytes 589828
  19.1 27.5 %copy-start.6 = (f32[2,384]{1,0:T(2,128)S(1)}, f32[2,384]{1,0:T(2,128)}, u32[]{:S(2)}) copy-start(f32[2,384]{1,0:T(2,128)} %param.18) | copy-start | bytes 9220
  19.1 33.1 %copy-start.3 = (bf16[64,384]{1,0:T(8,128)(2,1)S(1)}, bf16[64,384]{1,0:T(8,128)(2,1)}, u32[]{:S(2)}) copy-start(bf16[64,384]{1,0:T(8,128)(2,1)} %param.16) | copy-start | bytes 147460
  19.1 33.3 %copy-start = (bf16[2,384,512]{2,1,0:T(8,128)(2,1)S(1)}, bf16[2,384,512]{2,1,0:T(8,128)(2,1)}, u32[]{:S(2)}) copy-start(bf16[2,384,512]{2,1,0:T(8,128)(2,1)} %param.25) | copy-start | bytes 2359300
  25.1 27.6 %copy-start.1 = (bf16[2,384,512]{2,1,0:T(8,128)(2,1)S(1)}, bf16[2,384,512]{2,1,0:T(8,128)(2,1)}, u32[]{:S(2)}) copy-start(bf16[2,384,512]{2,1,0:T(8,128)(2,1)} %param.24) | copy-start | bytes 2359300
  25.9 48.0 %copy-start.2 = (bf16[2,384,384]{2,1,0:T(8,128)(2,1)S(1)}, bf16[2,384,384]{2,1,0:T(8,128)(2,1)}, u32[]{:S(2)}) copy-start(bf16[2,384,384]{2,1,0:T(8,128)(2,1)} %param.20) | copy-start | bytes 1769476
  25.9 48.3 %copy-start.8 = (bf16[2,384,2]{1,2,0:T(2,128)(2,1)S(1)}, bf16[2,384,2]{1,2,0:T(2,128)(2,1)}, u32[]{:S(2)}) copy-start(bf16[2,384,2]{1,2,0:T(2,128)(2,1)} %param.21) | copy-start | bytes 9220
  31.5 4.4 %collective-permute-start.3 = (f32[64,2,66]{0,1,2:T(2,128)S(1)}, f32[64,2,66]{0,1,2:T(2,128)S(1)}, u32[]{:S(2)}, u32[]{:S(2)}) collective-permute-start(f32[64,2,66]{0,1,2:T(2,128)S(1)} %pad_maximum_fusion.3), channel_id=1, source_target_pairs={{0,8},{8,0},{16,24},{24,16},{1,9},{9,1},{17,25},{25,17},{2,10},{10... | collective-permute-start | bytes 101384 | tf_op jit(solution)/shard_map/ppermute | solution.py:42
  33.5 4.9 %collective-permute-start.4 = (f32[64,2,66]{0,1,2:T(2,128)S(1)}, f32[64,2,66]{0,1,2:T(2,128)S(1)}, u32[]{:S(2)}, u32[]{:S(2)}) collective-permute-start(f32[64,2,66]{0,1,2:T(2,128)S(1)} %pad_maximum_fusion.3), channel_id=1, source_target_pairs={{0,16},{8,24},{16,0},{24,8},{1,17},{9,25},{17,1},{25,9},{2,18},{10... | collective-permute-start | bytes 101384 | tf_op jit(solution)/shard_map/ppermute | solution.py:42
  35.0 5.2 %collective-permute-start.5 = (f32[64,2,66]{0,1,2:T(2,128)S(1)}, f32[64,2,66]{0,1,2:T(2,128)S(1)}, u32[]{:S(2)}, u32[]{:S(2)}) collective-permute-start(f32[64,2,66]{0,1,2:T(2,128)S(1)} %pad_maximum_fusion.3), channel_id=1, source_target_pairs={{0,24},{8,16},{16,8},{24,0},{1,25},{9,17},{17,9},{25,1},{2,26},{10... | collective-permute-start | bytes 101384 | tf_op jit(solution)/shard_map/ppermute | solution.py:42
  40.8 1.3 collective-permute-start.6
  42.1 4.5 %collective-permute-start.7 = (bf16[64,384]{1,0:T(8,128)(2,1)S(1)}, bf16[64,384]{1,0:T(8,128)(2,1)S(1)}, u32[]{:S(2)}, u32[]{:S(2)}) collective-permute-start(bf16[64,384]{1,0:T(8,128)(2,1)S(1)} %add_convert_fusion.3), channel_id=1, source_target_pairs={{0,2},{1,3},{2,0},{3,1},{4,6},{5,7},{6,4},{7,5},{8,10},{9,11},{10,... | collective-permute-start | bytes 147464 | tf_op jit(solution)/shard_map/ppermute | solution.py:42
  43.8 5.9 %collective-permute-start.8 = (bf16[64,384]{1,0:T(8,128)(2,1)S(1)}, bf16[64,384]{1,0:T(8,128)(2,1)S(1)}, u32[]{:S(2)}, u32[]{:S(2)}) collective-permute-start(bf16[64,384]{1,0:T(8,128)(2,1)S(1)} %add_convert_fusion.3), channel_id=1, source_target_pairs={{0,4},{1,5},{2,6},{3,7},{4,0},{5,1},{6,2},{7,3},{8,12},{9,13},{10,... | collective-permute-start | bytes 147464 | tf_op jit(solution)/shard_map/ppermute | solution.py:42
  46.4 5.9 %collective-permute-start.9 = (bf16[64,384]{1,0:T(8,128)(2,1)S(1)}, bf16[64,384]{1,0:T(8,128)(2,1)S(1)}, u32[]{:S(2)}, u32[]{:S(2)}) collective-permute-start(bf16[64,384]{1,0:T(8,128)(2,1)S(1)} %add_convert_fusion.3), channel_id=1, source_target_pairs={{0,6},{1,7},{2,4},{3,5},{4,2},{5,3},{6,0},{7,1},{8,14},{9,15},{10,... | collective-permute-start | bytes 147464 | tf_op jit(solution)/shard_map/ppermute | solution.py:42
  64.7 1.3 collective-permute-start.10
  66.0 4.9 %collective-permute-start.11 = (bf16[64,384]{1,0:T(8,128)(2,1)S(1)}, bf16[64,384]{1,0:T(8,128)(2,1)S(1)}, u32[]{:S(2)}, u32[]{:S(2)}) collective-permute-start(bf16[64,384]{1,0:T(8,128)(2,1)S(1)} %add_convert_fusion.2), channel_id=1, source_target_pairs={{0,2},{1,3},{2,0},{3,1},{4,6},{5,7},{6,4},{7,5},{8,10},{9,11},{10,... | collective-permute-start | bytes 147464 | tf_op jit(solution)/shard_map/ppermute | solution.py:42
  66.1 7.0 %collective-permute-start.12 = (bf16[64,384]{1,0:T(8,128)(2,1)S(1)}, bf16[64,384]{1,0:T(8,128)(2,1)S(1)}, u32[]{:S(2)}, u32[]{:S(2)}) collective-permute-start(bf16[64,384]{1,0:T(8,128)(2,1)S(1)} %add_convert_fusion.2), channel_id=1, source_target_pairs={{0,4},{1,5},{2,6},{3,7},{4,0},{5,1},{6,2},{7,3},{8,12},{9,13},{10,... | collective-permute-start | bytes 147464 | tf_op jit(solution)/shard_map/ppermute | solution.py:42
  67.8 5.9 %collective-permute-start.13 = (bf16[64,384]{1,0:T(8,128)(2,1)S(1)}, bf16[64,384]{1,0:T(8,128)(2,1)S(1)}, u32[]{:S(2)}, u32[]{:S(2)}) collective-permute-start(bf16[64,384]{1,0:T(8,128)(2,1)S(1)} %add_convert_fusion.2), channel_id=1, source_target_pairs={{0,6},{1,7},{2,4},{3,5},{4,2},{5,3},{6,0},{7,1},{8,14},{9,15},{10,... | collective-permute-start | bytes 147464 | tf_op jit(solution)/shard_map/ppermute | solution.py:42
  74.4 9.3 %collective-permute-start.14 = (bf16[64,388]{0,1:T(8,128)(2,1)S(1)}, bf16[64,388]{0,1:T(8,128)(2,1)S(1)}, u32[]{:S(2)}, u32[]{:S(2)}) collective-permute-start(bf16[64,388]{0,1:T(8,128)(2,1)S(1)} %pad_maximum_fusion.2), channel_id=1, source_target_pairs={{0,8},{8,0},{16,24},{24,16},{1,9},{9,1},{17,25},{25,17},{2,10},{10... | collective-permute-start | bytes 149000 | tf_op jit(solution)/shard_map/ppermute | solution.py:25
  76.2 7.5 %collective-permute-start.15 = (bf16[64,388]{0,1:T(8,128)(2,1)S(1)}, bf16[64,388]{0,1:T(8,128)(2,1)S(1)}, u32[]{:S(2)}, u32[]{:S(2)}) collective-permute-start(bf16[64,388]{0,1:T(8,128)(2,1)S(1)} %pad_maximum_fusion.2), channel_id=1, source_target_pairs={{0,16},{8,24},{16,0},{24,8},{1,17},{9,25},{17,1},{25,9},{2,18},{10... | collective-permute-start | bytes 149000 | tf_op jit(solution)/shard_map/ppermute | solution.py:25
  76.5 7.2 %collective-permute-start.16 = (bf16[64,388]{0,1:T(8,128)(2,1)S(1)}, bf16[64,388]{0,1:T(8,128)(2,1)S(1)}, u32[]{:S(2)}, u32[]{:S(2)}) collective-permute-start(bf16[64,388]{0,1:T(8,128)(2,1)S(1)} %pad_maximum_fusion.2), channel_id=1, source_target_pairs={{0,24},{8,16},{16,8},{24,0},{1,25},{9,17},{17,9},{25,1},{2,26},{10... | collective-permute-start | bytes 149000 | tf_op jit(solution)/shard_map/ppermute | solution.py:25
  90.2 37.2 %copy-start.9 = (bf16[2,512,384]{2,1,0:T(8,128)(2,1)S(1)}, bf16[2,512,384]{2,1,0:T(8,128)(2,1)}, u32[]{:S(2)}) copy-start(bf16[2,512,384]{2,1,0:T(8,128)(2,1)} %param.26) | copy-start | bytes 2359300
  91.1 45.9 %copy-start.5 = (f32[384]{0:T(512)S(1)}, f32[384]{0:T(512)}, u32[]{:S(2)}) copy-start(f32[384]{0:T(512)} %param.19) | copy-start | bytes 4612
  96.6 4.5 %collective-permute-start.17 = (f32[64,2,66]{0,1,2:T(2,128)S(1)}, f32[64,2,66]{0,1,2:T(2,128)S(1)}, u32[]{:S(2)}, u32[]{:S(2)}) collective-permute-start(f32[64,2,66]{0,1,2:T(2,128)S(1)} %pad_maximum_fusion.4), channel_id=1, source_target_pairs={{0,8},{8,0},{16,24},{24,16},{1,9},{9,1},{17,25},{25,17},{2,10},{10... | collective-permute-start | bytes 101384 | tf_op jit(solution)/shard_map/ppermute | solution.py:42
  98.4 4.3 %collective-permute-start.18 = (f32[64,2,66]{0,1,2:T(2,128)S(1)}, f32[64,2,66]{0,1,2:T(2,128)S(1)}, u32[]{:S(2)}, u32[]{:S(2)}) collective-permute-start(f32[64,2,66]{0,1,2:T(2,128)S(1)} %pad_maximum_fusion.4), channel_id=1, source_target_pairs={{0,16},{8,24},{16,0},{24,8},{1,17},{9,25},{17,1},{25,9},{2,18},{10... | collective-permute-start | bytes 101384 | tf_op jit(solution)/shard_map/ppermute | solution.py:42
  98.7 5.2 %collective-permute-start.19 = (f32[64,2,66]{0,1,2:T(2,128)S(1)}, f32[64,2,66]{0,1,2:T(2,128)S(1)}, u32[]{:S(2)}, u32[]{:S(2)}) collective-permute-start(f32[64,2,66]{0,1,2:T(2,128)S(1)} %pad_maximum_fusion.4), channel_id=1, source_target_pairs={{0,24},{8,16},{16,8},{24,0},{1,25},{9,17},{17,9},{25,1},{2,26},{10... | collective-permute-start | bytes 101384 | tf_op jit(solution)/shard_map/ppermute | solution.py:42
  104.5 1.3 collective-permute-start.20
  105.8 4.5 %collective-permute-start.21 = (bf16[64,384]{1,0:T(8,128)(2,1)S(1)}, bf16[64,384]{1,0:T(8,128)(2,1)S(1)}, u32[]{:S(2)}, u32[]{:S(2)}) collective-permute-start(bf16[64,384]{1,0:T(8,128)(2,1)S(1)} %add_convert_fusion.1), channel_id=1, source_target_pairs={{0,2},{1,3},{2,0},{3,1},{4,6},{5,7},{6,4},{7,5},{8,10},{9,11},{10,... | collective-permute-start | bytes 147464 | tf_op jit(solution)/shard_map/ppermute | solution.py:42
  107.0 6.0 %collective-permute-start.22 = (bf16[64,384]{1,0:T(8,128)(2,1)S(1)}, bf16[64,384]{1,0:T(8,128)(2,1)S(1)}, u32[]{:S(2)}, u32[]{:S(2)}) collective-permute-start(bf16[64,384]{1,0:T(8,128)(2,1)S(1)} %add_convert_fusion.1), channel_id=1, source_target_pairs={{0,4},{1,5},{2,6},{3,7},{4,0},{5,1},{6,2},{7,3},{8,12},{9,13},{10,... | collective-permute-start | bytes 147464 | tf_op jit(solution)/shard_map/ppermute | solution.py:42
  109.0 5.9 %collective-permute-start.23 = (bf16[64,384]{1,0:T(8,128)(2,1)S(1)}, bf16[64,384]{1,0:T(8,128)(2,1)S(1)}, u32[]{:S(2)}, u32[]{:S(2)}) collective-permute-start(bf16[64,384]{1,0:T(8,128)(2,1)S(1)} %add_convert_fusion.1), channel_id=1, source_target_pairs={{0,6},{1,7},{2,4},{3,5},{4,2},{5,3},{6,0},{7,1},{8,14},{9,15},{10,... | collective-permute-start | bytes 147464 | tf_op jit(solution)/shard_map/ppermute | solution.py:42
  127.7 1.3 collective-permute-start.24
  129.0 4.8 %collective-permute-start.25 = (bf16[64,384]{1,0:T(8,128)(2,1)S(1)}, bf16[64,384]{1,0:T(8,128)(2,1)S(1)}, u32[]{:S(2)}, u32[]{:S(2)}) collective-permute-start(bf16[64,384]{1,0:T(8,128)(2,1)S(1)} %add_convert_fusion), channel_id=1, source_target_pairs={{0,2},{1,3},{2,0},{3,1},{4,6},{5,7},{6,4},{7,5},{8,10},{9,11},{10,... | collective-permute-start | bytes 147464 | tf_op jit(solution)/shard_map/ppermute | solution.py:42
  129.1 6.9 %collective-permute-start.26 = (bf16[64,384]{1,0:T(8,128)(2,1)S(1)}, bf16[64,384]{1,0:T(8,128)(2,1)S(1)}, u32[]{:S(2)}, u32[]{:S(2)}) collective-permute-start(bf16[64,384]{1,0:T(8,128)(2,1)S(1)} %add_convert_fusion), channel_id=1, source_target_pairs={{0,4},{1,5},{2,6},{3,7},{4,0},{5,1},{6,2},{7,3},{8,12},{9,13},{10,... | collective-permute-start | bytes 147464 | tf_op jit(solution)/shard_map/ppermute | solution.py:42
  130.8 5.9 %collective-permute-start.27 = (bf16[64,384]{1,0:T(8,128)(2,1)S(1)}, bf16[64,384]{1,0:T(8,128)(2,1)S(1)}, u32[]{:S(2)}, u32[]{:S(2)}) collective-permute-start(bf16[64,384]{1,0:T(8,128)(2,1)S(1)} %add_convert_fusion), channel_id=1, source_target_pairs={{0,6},{1,7},{2,4},{3,5},{4,2},{5,3},{6,0},{7,1},{8,14},{9,15},{10,... | collective-permute-start | bytes 147464 | tf_op jit(solution)/shard_map/ppermute | solution.py:42
  154.8 15.8 %copy-start.7 = (f32[64]{0:T(128)}, f32[64]{0:T(128)S(1)}, u32[]{:S(2)}) copy-start(f32[64]{0:T(128)S(1)} %get-tuple-element.8) | copy-start | bytes 772
  154.9 3.6 %collective-permute-start.28 = (f32[64]{0:T(128)S(1)}, f32[64]{0:T(128)S(1)}, u32[]{:S(2)}, u32[]{:S(2)}) collective-permute-start(f32[64]{0:T(128)S(1)} %get-tuple-element.7), channel_id=1, source_target_pairs={{0,8},{8,0},{16,24},{24,16},{1,9},{9,1},{17,25},{25,17},{2,10},{10... | collective-permute-start | bytes 776 | tf_op jit(solution)/shard_map/ppermute | solution.py:70
  155.7 3.5 %collective-permute-start.29 = (f32[64]{0:T(128)S(1)}, f32[64]{0:T(128)S(1)}, u32[]{:S(2)}, u32[]{:S(2)}) collective-permute-start(f32[64]{0:T(128)S(1)} %get-tuple-element.7), channel_id=1, source_target_pairs={{0,16},{8,24},{16,0},{24,8},{1,17},{9,25},{17,1},{25,9},{2,18},{10... | collective-permute-start | bytes 776 | tf_op jit(solution)/shard_map/ppermute | solution.py:70
  156.2 4.4 %collective-permute-start.30 = (f32[64]{0:T(128)S(1)}, f32[64]{0:T(128)S(1)}, u32[]{:S(2)}, u32[]{:S(2)}) collective-permute-start(f32[64]{0:T(128)S(1)} %get-tuple-element.7), channel_id=1, source_target_pairs={{0,24},{8,16},{16,8},{24,0},{1,25},{9,17},{17,9},{25,1},{2,26},{10... | collective-permute-start | bytes 776 | tf_op jit(solution)/shard_map/ppermute | solution.py:70
  160.7 1.1 collective-permute-start.31
  161.8 5.1 %collective-permute-start.32 = (f32[64]{0:T(128)S(1)}, f32[64]{0:T(128)S(1)}, u32[]{:S(2)}, u32[]{:S(2)}) collective-permute-start(f32[64]{0:T(128)S(1)} %max.129), channel_id=1, source_target_pairs={{0,2},{1,3},{2,0},{3,1},{4,6},{5,7},{6,4},{7,5},{8,10},{9,11},{10,... | collective-permute-start | bytes 776 | tf_op jit(solution)/shard_map/ppermute | solution.py:42
  161.8 5.0 %collective-permute-start.33 = (f32[64]{0:T(128)S(1)}, f32[64]{0:T(128)S(1)}, u32[]{:S(2)}, u32[]{:S(2)}) collective-permute-start(f32[64]{0:T(128)S(1)} %max.129), channel_id=1, source_target_pairs={{0,4},{1,5},{2,6},{3,7},{4,0},{5,1},{6,2},{7,3},{8,12},{9,13},{10,... | collective-permute-start | bytes 776 | tf_op jit(solution)/shard_map/ppermute | solution.py:42
  164.8 5.3 %collective-permute-start.34 = (f32[64]{0:T(128)S(1)}, f32[64]{0:T(128)S(1)}, u32[]{:S(2)}, u32[]{:S(2)}) collective-permute-start(f32[64]{0:T(128)S(1)} %max.129), channel_id=1, source_target_pairs={{0,6},{1,7},{2,4},{3,5},{4,2},{5,3},{6,0},{7,1},{8,14},{9,15},{10,... | collective-permute-start | bytes 776 | tf_op jit(solution)/shard_map/ppermute | solution.py:42

commit v13 on v12

--- a/solution.py
+++ b/solution.py
@@ -140,10 +140,11 @@
     slot_peak = jnp.einsum("pr,rh->ph", hot_full, row_peak, precision=lax.Precision.HIGHEST)
     weights = jnp.where(live[:, None, :], jnp.exp(scores - slot_peak[:, :, None]), 0.0)
     page_sum = jnp.sum(weights, axis=2)
+    weight_block = diagonal[None, :, None, :] * weights.astype(jnp.bfloat16)[:, :, :, None]
     mixed = jnp.einsum(
-        "pkt,pthc->pkhc", weights.astype(jnp.bfloat16), kv_layer, preferred_element_type=jnp.float32
-    )
-    page_out = jnp.stack([mixed[:, h, h, HEAD:] for h in range(heads)], axis=1)
+        "pkth,pthc->pkc", weight_block, kv_layer, preferred_element_type=jnp.float32
+    )
+    page_out = mixed[:, :, HEAD:]
     member_f = member.astype(jnp.float32)
     row_sum = jnp.einsum("rp,ph->rh", member_f, page_sum, precision=lax.Precision.HIGHEST)
     row_out = jnp.einsum("rp,phd->rhd", member_f, page_out, precision=lax.Precision.HIGHEST)

time: 171 us -> 171 us (level)
  no operation moved by 1% of the time
where the time goes in v13:
time: 171 us; the launch traced here: 170 us
  starting transfers between devices  41.2 us (24%)
  waiting for transfers between devices  37.2 us (22%)
  blocking collectives  35 us (20%)
  matrix products  31.9 us (19%)
  Pallas kernels  11.5 us (7%)
  other arithmetic  7.32 us (4%)
  local copies, waits for them, and re-layouts  4.67 us (3%)
    ppermute x26, waiting for transfers between devices, exchange(): return lax.ppermute(value, axis, [(i, i ^ partner) for i in range(count)])  34.9 us
    ppermute x26, starting transfers between devices, exchange(): return lax.ppermute(value, axis, [(i, i ^ partner) for i in range(count)])  29.6 us
    all_gather x2, blocking collectives, gather_sum(): return jnp.sum(lax.all_gather(value, axis).astype(jnp.float32), axis=0)  21.3 us
    all_to_all x1, blocking collectives, local(): pieces = lax.all_to_all(pieces, 'gx', 1, 1, tiled=True).astype(jnp.float32)  13.8 us
    dot_general x2, matrix products, local_attention(): jnp.einsum('pthc,pkhc->pkt', kv_layer, query_block, preferred_element_typ...  11.7 us
    pallas_call x2, Pallas kernels, layer_slice(): pl.pallas_call(copy_block, grid=(slots // block,), in_specs=[pl.BlockSpec...  11.5 us
    dot_general x2, matrix products, local_attention(): jnp.einsum('pkth,pthc->pkc', weight_block, kv_layer, preferred_element_ty...  9.34 us
    ppermute x6, starting transfers between devices, xor_sum(): lax.ppermute(value, axis, [(i, i ^ k) for i in range(count)])  8.1 us
  transfers between devices with their start and end apart: 35, of which 25 were waited for; matrix products, arithmetic and copies ran while one was open for 2% of the time, Pallas kernels for 7%

profile of v13, /device:TPU:0, one launch (start us, length us, event | category | flops | bytes accessed | tf_op | source)
XLA Modules:
  0.0 170.3 jit_solution(3712533164937590498)
XLA Ops:
  2.3 1.3 convolution_convert_fusion.2
  4.6 3.0 %collective-permute-start = (bf16[64,388]{0,1:T(8,128)(2,1)S(1)}, bf16[64,388]{0,1:T(8,128)(2,1)S(1)}, u32[]{:S(2)}, u32[]{:S(2)}) collective-permute-start(bf16[64,388]{0,1:T(8,128)(2,1)S(1)} %pad_maximum_fusion.1), channel_id=1, source_target_pairs={{0,8},{8,0},{16,24},{24,16},{1,9},{9,1},{17,25},{25,17},{2,10},{10... | collective-permute-start | bytes 149000 | tf_op jit(solution)/shard_map/ppermute | solution.py:25
  7.6 1.5 collective-permute-start.1
  12.6 5.8 %shard_map.175 = bf16[128,128,2,128]{3,2,1,0:T(2,128)(2,1)} custom-call(bf16[2,128,128,2,128]{4,3,2,1,0:T(2,128)(2,1)} %source.3), custom_call_target="tpu_custom_call" | custom-call | bytes 16777216 | tf_op jit(solution)/shard_map/pallas_call | solution.py:84
  19.2 5.9 %fusion.241 = (f32[128,2]{1,0:T(8,128)S(1)}, f32[128,2,128]{2,1,0:T(2,128)S(1)}) fusion(f32[128,2]{1,0:T(8,128)S(1)} %fusion.138, f32[2,128,2,128]{3,2,1,0:T(2,128)S(1)} %copy-done.10, bf16[128,128,2,128]{3,2,1,0:T(2,128)(2,1)} %shard_map.175, bf16[128,2,128]{2,1,0:T(2,128)(2,1)S(1)} %concatenate.33.clone, bf16[2,2]{0,1:T(2,128)(2,1)S(1)} %compare_convert_fusion, ...), kind=kOutput, calls=%fused_computation.350 | convolution fusion | flops 17202944 | bytes 8734728 | tf_op jit(solution)/shard_map/pthc,pkhc->pkt/dot_general | solution.py:132
  26.1 4.7 %fusion.11 = f32[128,2,128]{2,1,0:T(2,128)S(1)} fusion(bf16[128,128,2,128]{3,2,1,0:T(2,128)(2,1)} %shard_map.175, bf16[128,2,128]{2,1,0:T(2,128)(2,1)S(1)} %get-tuple-element.32, bf16[2,2]{0,1:T(2,128)(2,1)S(1)} %compare_convert_fusion), kind=kOutput, calls=%fused_computation.15 | convolution fusion | flops 17039360 | bytes 8585224 | tf_op jit(solution)/shard_map/pkth,pthc->pkc/dot_general | solution.py:144
  31.3 2.0 %collective-permute-start.3 = (f32[64,2,66]{0,1,2:T(2,128)S(1)}, f32[64,2,66]{0,1,2:T(2,128)S(1)}, u32[]{:S(2)}, u32[]{:S(2)}) collective-permute-start(f32[64,2,66]{0,1,2:T(2,128)S(1)} %pad_maximum_fusion.3), channel_id=1, source_target_pairs={{0,8},{8,0},{16,24},{24,16},{1,9},{9,1},{17,25},{25,17},{2,10},{10... | collective-permute-start | bytes 101384 | tf_op jit(solution)/shard_map/ppermute | solution.py:42
  33.3 1.5 collective-permute-start.4
  35.6 2.6 %collective-permute-done.4 = f32[64,2,66]{0,1,2:T(2,128)S(1)} collective-permute-done((f32[64,2,66]{0,1,2:T(2,128)S(1)}, f32[64,2,66]{0,1,2:T(2,128)S(1)}, u32[]{:S(2)}, u32[]{:S(2)}) %collective-permute-start.4) | collective-permute-done | bytes 33824 | tf_op jit(solution)/shard_map/ppermute | solution.py:42
  38.2 1.8 %collective-permute-done.5 = f32[64,2,66]{0,1,2:T(2,128)S(1)} collective-permute-done((f32[64,2,66]{0,1,2:T(2,128)S(1)}, f32[64,2,66]{0,1,2:T(2,128)S(1)}, u32[]{:S(2)}, u32[]{:S(2)}) %collective-permute-start.5) | collective-permute-done | bytes 33824 | tf_op jit(solution)/shard_map/ppermute | solution.py:42
  40.7 1.2 collective-permute-done.6
  41.9 1.6 collective-permute-start.7
  43.6 2.6 %collective-permute-start.8 = (bf16[64,384]{1,0:T(8,128)(2,1)S(1)}, bf16[64,384]{1,0:T(8,128)(2,1)S(1)}, u32[]{:S(2)}, u32[]{:S(2)}) collective-permute-start(bf16[64,384]{1,0:T(8,128)(2,1)S(1)} %add_convert_fusion.3), channel_id=1, source_target_pairs={{0,4},{1,5},{2,6},{3,7},{4,0},{5,1},{6,2},{7,3},{8,12},{9,13},{10,... | collective-permute-start | bytes 147464 | tf_op jit(solution)/shard_map/ppermute | solution.py:42
  46.4 3.1 %collective-permute-done.8 = bf16[64,384]{1,0:T(8,128)(2,1)S(1)} collective-permute-done((bf16[64,384]{1,0:T(8,128)(2,1)S(1)}, bf16[64,384]{1,0:T(8,128)(2,1)S(1)}, u32[]{:S(2)}, u32[]{:S(2)}) %collective-permute-start.8) | collective-permute-done | bytes 49184 | tf_op jit(solution)/shard_map/ppermute | solution.py:42
  49.5 2.6 %collective-permute-done.9 = bf16[64,384]{1,0:T(8,128)(2,1)S(1)} collective-permute-done((bf16[64,384]{1,0:T(8,128)(2,1)S(1)}, bf16[64,384]{1,0:T(8,128)(2,1)S(1)}, u32[]{:S(2)}, u32[]{:S(2)}) %collective-permute-start.9) | collective-permute-done | bytes 49184 | tf_op jit(solution)/shard_map/ppermute | solution.py:42
  52.9 9.9 %all-gather = bf16[256,1026]{1,0:T(8,128)(2,1)S(1)} all-gather(bf16[64,1026]{1,0:T(8,128)(2,1)S(1)} %concatenate.35), channel_id=2, replica_groups=mesh['gx'=4,'gy'=8] {'gx'}, dimensions={0}, use_global_device_ids=true | all-gather | bytes 656640 | tf_op jit(solution)/shard_map/all_gather | solution.py:19
  63.2 1.3 convolution_convert_fusion.10
  64.6 1.2 collective-permute-done.10
  65.9 1.7 %collective-permute-start.12 = (bf16[64,384]{1,0:T(8,128)(2,1)S(1)}, bf16[64,384]{1,0:T(8,128)(2,1)S(1)}, u32[]{:S(2)}, u32[]{:S(2)}) collective-permute-start(bf16[64,384]{1,0:T(8,128)(2,1)S(1)} %add_convert_fusion.2), channel_id=1, source_target_pairs={{0,4},{1,5},{2,6},{3,7},{4,0},{5,1},{6,2},{7,3},{8,12},{9,13},{10,... | collective-permute-start | bytes 147464 | tf_op jit(solution)/shard_map/ppermute | solution.py:42
  67.6 2.7 %collective-permute-start.13 = (bf16[64,384]{1,0:T(8,128)(2,1)S(1)}, bf16[64,384]{1,0:T(8,128)(2,1)S(1)}, u32[]{:S(2)}, u32[]{:S(2)}) collective-permute-start(bf16[64,384]{1,0:T(8,128)(2,1)S(1)} %add_convert_fusion.2), channel_id=1, source_target_pairs={{0,6},{1,7},{2,4},{3,5},{4,2},{5,3},{6,0},{7,1},{8,14},{9,15},{10,... | collective-permute-start | bytes 147464 | tf_op jit(solution)/shard_map/ppermute | solution.py:42
  70.7 2.2 %collective-permute-done.12 = bf16[64,384]{1,0:T(8,128)(2,1)S(1)} collective-permute-done((bf16[64,384]{1,0:T(8,128)(2,1)S(1)}, bf16[64,384]{1,0:T(8,128)(2,1)S(1)}, u32[]{:S(2)}, u32[]{:S(2)}) %collective-permute-start.12) | collective-permute-done | bytes 49184 | tf_op jit(solution)/shard_map/ppermute | solution.py:42
  74.2 1.8 %collective-permute-start.14 = (bf16[64,388]{0,1:T(8,128)(2,1)S(1)}, bf16[64,388]{0,1:T(8,128)(2,1)S(1)}, u32[]{:S(2)}, u32[]{:S(2)}) collective-permute-start(bf16[64,388]{0,1:T(8,128)(2,1)S(1)} %pad_maximum_fusion.2), channel_id=1, source_target_pairs={{0,8},{8,0},{16,24},{24,16},{1,9},{9,1},{17,25},{25,17},{2,10},{10... | collective-permute-start | bytes 149000 | tf_op jit(solution)/shard_map/ppermute | solution.py:25
  76.3 1.5 collective-permute-start.16
  77.7 5.7 %shard_map.176 = bf16[128,128,2,128]{3,2,1,0:T(2,128)(2,1)} custom-call(bf16[2,128,128,2,128]{4,3,2,1,0:T(2,128)(2,1)} %source.3), custom_call_target="tpu_custom_call" | custom-call | bytes 16777216 | tf_op jit(solution)/shard_map/pallas_call | solution.py:84
  84.2 5.8 %fusion.242 = (f32[128,2]{1,0:T(8,128)S(1)}, f32[128,2,128]{2,1,0:T(2,128)S(1)}) fusion(f32[128,2]{1,0:T(8,128)S(1)} %fusion.134, f32[2,128,2,128]{3,2,1,0:T(2,128)S(1)} %copy-done.10, bf16[128,128,2,128]{3,2,1,0:T(2,128)(2,1)} %shard_map.176, bf16[128,2,128]{2,1,0:T(2,128)(2,1)S(1)} %concatenate.37.clone, bf16[2,2]{0,1:T(2,128)(2,1)S(1)} %compare_convert_fusion, ...), kind=kOutput, calls=%fused_computation.351 | convolution fusion | flops 17202944 | bytes 8734728 | tf_op jit(solution)/shard_map/pthc,pkhc->pkt/dot_general | solution.py:132
  91.0 4.7 %fusion.17 = f32[128,2,128]{2,1,0:T(2,128)S(1)} fusion(bf16[128,128,2,128]{3,2,1,0:T(2,128)(2,1)} %shard_map.176, bf16[128,2,128]{2,1,0:T(2,128)(2,1)S(1)} %get-tuple-element.30, bf16[2,2]{0,1:T(2,128)(2,1)S(1)} %compare_convert_fusion), kind=kOutput, calls=%fused_computation.17 | convolution fusion | flops 17039360 | bytes 8585224 | tf_op jit(solution)/shard_map/pkth,pthc->pkc/dot_general | solution.py:144
  96.2 1.8 %collective-permute-start.17 = (f32[64,2,66]{0,1,2:T(2,128)S(1)}, f32[64,2,66]{0,1,2:T(2,128)S(1)}, u32[]{:S(2)}, u32[]{:S(2)}) collective-permute-start(f32[64,2,66]{0,1,2:T(2,128)S(1)} %pad_maximum_fusion.4), channel_id=1, source_target_pairs={{0,8},{8,0},{16,24},{24,16},{1,9},{9,1},{17,25},{25,17},{2,10},{10... | collective-permute-start | bytes 101384 | tf_op jit(solution)/shard_map/ppermute | solution.py:42
  98.3 1.5 collective-permute-start.19
  100.8 1.6 collective-permute-done.18
  102.3 1.2 collective-permute-done.19
  104.2 1.2 collective-permute-done.20
  105.4 1.2 collective-permute-start.21
  106.6 2.0 %collective-permute-start.22 = (bf16[64,384]{1,0:T(8,128)(2,1)S(1)}, bf16[64,384]{1,0:T(8,128)(2,1)S(1)}, u32[]{:S(2)}, u32[]{:S(2)}) collective-permute-start(bf16[64,384]{1,0:T(8,128)(2,1)S(1)} %add_convert_fusion.1), channel_id=1, source_target_pairs={{0,4},{1,5},{2,6},{3,7},{4,0},{5,1},{6,2},{7,3},{8,12},{9,13},{10,... | collective-permute-start | bytes 147464 | tf_op jit(solution)/shard_map/ppermute | solution.py:42
  108.6 1.2 collective-permute-start.23
  109.9 2.7 %collective-permute-done.22 = bf16[64,384]{1,0:T(8,128)(2,1)S(1)} collective-permute-done((bf16[64,384]{1,0:T(8,128)(2,1)S(1)}, bf16[64,384]{1,0:T(8,128)(2,1)S(1)}, u32[]{:S(2)}, u32[]{:S(2)}) %collective-permute-start.22) | collective-permute-done | bytes 49184 | tf_op jit(solution)/shard_map/ppermute | solution.py:42
  112.6 1.9 %collective-permute-done.23 = bf16[64,384]{1,0:T(8,128)(2,1)S(1)} collective-permute-done((bf16[64,384]{1,0:T(8,128)(2,1)S(1)}, bf16[64,384]{1,0:T(8,128)(2,1)S(1)}, u32[]{:S(2)}, u32[]{:S(2)}) %collective-permute-start.23) | collective-permute-done | bytes 49184 | tf_op jit(solution)/shard_map/ppermute | solution.py:42
  115.4 11.3 %all-gather.1 = bf16[256,1026]{1,0:T(8,128)(2,1)S(1)} all-gather(bf16[64,1026]{1,0:T(8,128)(2,1)S(1)} %concatenate.39), channel_id=3, replica_groups=mesh['gx'=4,'gy'=8] {'gx'}, dimensions={0}, use_global_device_ids=true | all-gather | bytes 656640 | tf_op jit(solution)/shard_map/all_gather | solution.py:19
  127.4 1.2 collective-permute-done.24
  128.7 1.7 %collective-permute-start.26 = (bf16[64,384]{1,0:T(8,128)(2,1)S(1)}, bf16[64,384]{1,0:T(8,128)(2,1)S(1)}, u32[]{:S(2)}, u32[]{:S(2)}) collective-permute-start(bf16[64,384]{1,0:T(8,128)(2,1)S(1)} %add_convert_fusion), channel_id=1, source_target_pairs={{0,4},{1,5},{2,6},{3,7},{4,0},{5,1},{6,2},{7,3},{8,12},{9,13},{10,... | collective-permute-start | bytes 147464 | tf_op jit(solution)/shard_map/ppermute | solution.py:42
  130.5 2.7 %collective-permute-start.27 = (bf16[64,384]{1,0:T(8,128)(2,1)S(1)}, bf16[64,384]{1,0:T(8,128)(2,1)S(1)}, u32[]{:S(2)}, u32[]{:S(2)}) collective-permute-start(bf16[64,384]{1,0:T(8,128)(2,1)S(1)} %add_convert_fusion), channel_id=1, source_target_pairs={{0,6},{1,7},{2,4},{3,5},{4,2},{5,3},{6,0},{7,1},{8,14},{9,15},{10,... | collective-permute-start | bytes 147464 | tf_op jit(solution)/shard_map/ppermute | solution.py:42
  133.5 2.2 %collective-permute-done.26 = bf16[64,384]{1,0:T(8,128)(2,1)S(1)} collective-permute-done((bf16[64,384]{1,0:T(8,128)(2,1)S(1)}, bf16[64,384]{1,0:T(8,128)(2,1)S(1)}, u32[]{:S(2)}, u32[]{:S(2)}) %collective-permute-start.26) | collective-permute-done | bytes 49184 | tf_op jit(solution)/shard_map/ppermute | solution.py:42
  136.6 3.3 %convolution_convert_fusion = bf16[64,6144]{1,0:T(8,128)(2,1)S(1)} fusion(bf16[384,6144]{1,0:T(8,128)(2,1)} %param.27, f32[64,384]{1,0:T(8,128)S(1)} %get-tuple-element.10, f32[384]{0:T(512)S(1)} %copy-done.5), kind=kOutput, calls=%fused_computation.8 | convolution fusion | flops 302432256 | bytes 5604864 | tf_op jit(solution)/shard_map/dot_general | solution.py:266
  140.2 13.8 %all_to_all.5 = bf16[64,4,1538]{2,0,1:T(8,128)(2,1)S(1)} all-to-all(bf16[64,4,1538]{2,0,1:T(8,128)(2,1)S(1)} %pad_maximum_fusion), channel_id=1, replica_groups=mesh['gx'=4,'gy'=8] {'gx'}, dimensions={1} | all-to-all | bytes 1574912 | tf_op jit(solution)/shard_map/all_to_all | solution.py:277
  155.8 2.2 %collective-permute-start.30 = (f32[64]{0:T(128)S(1)}, f32[64]{0:T(128)S(1)}, u32[]{:S(2)}, u32[]{:S(2)}) collective-permute-start(f32[64]{0:T(128)S(1)} %get-tuple-element.7), channel_id=1, source_target_pairs={{0,24},{8,16},{16,8},{24,0},{1,25},{9,17},{17,9},{25,1},{2,26},{10... | collective-permute-start | bytes 776 | tf_op jit(solution)/shard_map/ppermute | solution.py:70
  158.8 1.5 collective-permute-done.30
  161.5 2.9 %collective-permute-start.33 = (f32[64]{0:T(128)S(1)}, f32[64]{0:T(128)S(1)}, u32[]{:S(2)}, u32[]{:S(2)}) collective-permute-start(f32[64]{0:T(128)S(1)} %max.129), channel_id=1, source_target_pairs={{0,4},{1,5},{2,6},{3,7},{4,0},{5,1},{6,2},{7,3},{8,12},{9,13},{10,... | collective-permute-start | bytes 776 | tf_op jit(solution)/shard_map/ppermute | solution.py:42
  164.4 1.4 collective-permute-start.34
  166.5 3.2 %collective-permute-done.34 = f32[64]{0:T(128)S(1)} collective-permute-done((f32[64]{0:T(128)S(1)}, f32[64]{0:T(128)S(1)}, u32[]{:S(2)}, u32[]{:S(2)}) %collective-permute-start.34) | collective-permute-done | bytes 288 | tf_op jit(solution)/shard_map/ppermute | solution.py:42
  (189 shorter events, 25.6 us)
Async XLA Ops:
  4.6 13.7 %collective-permute-start = (bf16[64,388]{0,1:T(8,128)(2,1)S(1)}, bf16[64,388]{0,1:T(8,128)(2,1)S(1)}, u32[]{:S(2)}, u32[]{:S(2)}) collective-permute-start(bf16[64,388]{0,1:T(8,128)(2,1)S(1)} %pad_maximum_fusion.1), channel_id=1, source_target_pairs={{0,8},{8,0},{16,24},{24,16},{1,9},{9,1},{17,25},{25,17},{2,10},{10... | collective-permute-start | bytes 149000 | tf_op jit(solution)/shard_map/ppermute | solution.py:25
  7.6 10.7 %collective-permute-start.1 = (bf16[64,388]{0,1:T(8,128)(2,1)S(1)}, bf16[64,388]{0,1:T(8,128)(2,1)S(1)}, u32[]{:S(2)}, u32[]{:S(2)}) collective-permute-start(bf16[64,388]{0,1:T(8,128)(2,1)S(1)} %pad_maximum_fusion.1), channel_id=1, source_target_pairs={{0,16},{8,24},{16,0},{24,8},{1,17},{9,25},{17,1},{25,9},{2,18},{10... | collective-permute-start | bytes 149000 | tf_op jit(solution)/shard_map/ppermute | solution.py:25
  9.1 9.2 %collective-permute-start.2 = (bf16[64,388]{0,1:T(8,128)(2,1)S(1)}, bf16[64,388]{0,1:T(8,128)(2,1)S(1)}, u32[]{:S(2)}, u32[]{:S(2)}) collective-permute-start(bf16[64,388]{0,1:T(8,128)(2,1)S(1)} %pad_maximum_fusion.1), channel_id=1, source_target_pairs={{0,24},{8,16},{16,8},{24,0},{1,25},{9,17},{17,9},{25,1},{2,26},{10... | collective-permute-start | bytes 149000 | tf_op jit(solution)/shard_map/ppermute | solution.py:25
  12.6 6.5 %copy-start.10 = (f32[2,128,2,128]{3,2,1,0:T(2,128)S(1)}, f32[2,128,2,128]{3,2,1,0:T(2,128)}, u32[]{:S(2)}) copy-start(f32[2,128,2,128]{3,2,1,0:T(2,128)} %param.29) | copy-start | bytes 786436
  19.1 21.3 %copy-start.4 = (bf16[2,128,384]{2,1,0:T(8,128)(2,1)S(1)}, bf16[2,128,384]{2,1,0:T(8,128)(2,1)}, u32[]{:S(2)}) copy-start(bf16[2,128,384]{2,1,0:T(8,128)(2,1)} %param.23) | copy-start | bytes 589828
  19.1 27.2 %copy-start.6 = (f32[2,384]{1,0:T(2,128)S(1)}, f32[2,384]{1,0:T(2,128)}, u32[]{:S(2)}) copy-start(f32[2,384]{1,0:T(2,128)} %param.18) | copy-start | bytes 9220
  19.1 32.9 %copy-start.3 = (bf16[64,384]{1,0:T(8,128)(2,1)S(1)}, bf16[64,384]{1,0:T(8,128)(2,1)}, u32[]{:S(2)}) copy-start(bf16[64,384]{1,0:T(8,128)(2,1)} %param.16) | copy-start | bytes 147460
  19.1 33.0 %copy-start = (bf16[2,384,512]{2,1,0:T(8,128)(2,1)S(1)}, bf16[2,384,512]{2,1,0:T(8,128)(2,1)}, u32[]{:S(2)}) copy-start(bf16[2,384,512]{2,1,0:T(8,128)(2,1)} %param.25) | copy-start | bytes 2359300
  25.1 27.3 %copy-start.1 = (bf16[2,384,512]{2,1,0:T(8,128)(2,1)S(1)}, bf16[2,384,512]{2,1,0:T(8,128)(2,1)}, u32[]{:S(2)}) copy-start(bf16[2,384,512]{2,1,0:T(8,128)(2,1)} %param.24) | copy-start | bytes 2359300
  25.9 47.8 %copy-start.2 = (bf16[2,384,384]{2,1,0:T(8,128)(2,1)S(1)}, bf16[2,384,384]{2,1,0:T(8,128)(2,1)}, u32[]{:S(2)}) copy-start(bf16[2,384,384]{2,1,0:T(8,128)(2,1)} %param.20) | copy-start | bytes 1769476
  26.1 47.9 %copy-start.8 = (bf16[2,384,2]{1,2,0:T(2,128)(2,1)S(1)}, bf16[2,384,2]{1,2,0:T(2,128)(2,1)}, u32[]{:S(2)}) copy-start(bf16[2,384,2]{1,2,0:T(2,128)(2,1)} %param.21) | copy-start | bytes 9220
  31.3 4.4 %collective-permute-start.3 = (f32[64,2,66]{0,1,2:T(2,128)S(1)}, f32[64,2,66]{0,1,2:T(2,128)S(1)}, u32[]{:S(2)}, u32[]{:S(2)}) collective-permute-start(f32[64,2,66]{0,1,2:T(2,128)S(1)} %pad_maximum_fusion.3), channel_id=1, source_target_pairs={{0,8},{8,0},{16,24},{24,16},{1,9},{9,1},{17,25},{25,17},{2,10},{10... | collective-permute-start | bytes 101384 | tf_op jit(solution)/shard_map/ppermute | solution.py:42
  33.3 4.9 %collective-permute-start.4 = (f32[64,2,66]{0,1,2:T(2,128)S(1)}, f32[64,2,66]{0,1,2:T(2,128)S(1)}, u32[]{:S(2)}, u32[]{:S(2)}) collective-permute-start(f32[64,2,66]{0,1,2:T(2,128)S(1)} %pad_maximum_fusion.3), channel_id=1, source_target_pairs={{0,16},{8,24},{16,0},{24,8},{1,17},{9,25},{17,1},{25,9},{2,18},{10... | collective-permute-start | bytes 101384 | tf_op jit(solution)/shard_map/ppermute | solution.py:42
  34.8 5.2 %collective-permute-start.5 = (f32[64,2,66]{0,1,2:T(2,128)S(1)}, f32[64,2,66]{0,1,2:T(2,128)S(1)}, u32[]{:S(2)}, u32[]{:S(2)}) collective-permute-start(f32[64,2,66]{0,1,2:T(2,128)S(1)} %pad_maximum_fusion.3), channel_id=1, source_target_pairs={{0,24},{8,16},{16,8},{24,0},{1,25},{9,17},{17,9},{25,1},{2,26},{10... | collective-permute-start | bytes 101384 | tf_op jit(solution)/shard_map/ppermute | solution.py:42
  40.6 1.3 collective-permute-start.6
  41.9 4.5 %collective-permute-start.7 = (bf16[64,384]{1,0:T(8,128)(2,1)S(1)}, bf16[64,384]{1,0:T(8,128)(2,1)S(1)}, u32[]{:S(2)}, u32[]{:S(2)}) collective-permute-start(bf16[64,384]{1,0:T(8,128)(2,1)S(1)} %add_convert_fusion.3), channel_id=1, source_target_pairs={{0,2},{1,3},{2,0},{3,1},{4,6},{5,7},{6,4},{7,5},{8,10},{9,11},{10,... | collective-permute-start | bytes 147464 | tf_op jit(solution)/shard_map/ppermute | solution.py:42
  43.6 5.9 %collective-permute-start.8 = (bf16[64,384]{1,0:T(8,128)(2,1)S(1)}, bf16[64,384]{1,0:T(8,128)(2,1)S(1)}, u32[]{:S(2)}, u32[]{:S(2)}) collective-permute-start(bf16[64,384]{1,0:T(8,128)(2,1)S(1)} %add_convert_fusion.3), channel_id=1, source_target_pairs={{0,4},{1,5},{2,6},{3,7},{4,0},{5,1},{6,2},{7,3},{8,12},{9,13},{10,... | collective-permute-start | bytes 147464 | tf_op jit(solution)/shard_map/ppermute | solution.py:42
  46.1 5.9 %collective-permute-start.9 = (bf16[64,384]{1,0:T(8,128)(2,1)S(1)}, bf16[64,384]{1,0:T(8,128)(2,1)S(1)}, u32[]{:S(2)}, u32[]{:S(2)}) collective-permute-start(bf16[64,384]{1,0:T(8,128)(2,1)S(1)} %add_convert_fusion.3), channel_id=1, source_target_pairs={{0,6},{1,7},{2,4},{3,5},{4,2},{5,3},{6,0},{7,1},{8,14},{9,15},{10,... | collective-permute-start | bytes 147464 | tf_op jit(solution)/shard_map/ppermute | solution.py:42
  64.5 1.3 collective-permute-start.10
  65.8 4.9 %collective-permute-start.11 = (bf16[64,384]{1,0:T(8,128)(2,1)S(1)}, bf16[64,384]{1,0:T(8,128)(2,1)S(1)}, u32[]{:S(2)}, u32[]{:S(2)}) collective-permute-start(bf16[64,384]{1,0:T(8,128)(2,1)S(1)} %add_convert_fusion.2), channel_id=1, source_target_pairs={{0,2},{1,3},{2,0},{3,1},{4,6},{5,7},{6,4},{7,5},{8,10},{9,11},{10,... | collective-permute-start | bytes 147464 | tf_op jit(solution)/shard_map/ppermute | solution.py:42
  65.9 7.0 %collective-permute-start.12 = (bf16[64,384]{1,0:T(8,128)(2,1)S(1)}, bf16[64,384]{1,0:T(8,128)(2,1)S(1)}, u32[]{:S(2)}, u32[]{:S(2)}) collective-permute-start(bf16[64,384]{1,0:T(8,128)(2,1)S(1)} %add_convert_fusion.2), channel_id=1, source_target_pairs={{0,4},{1,5},{2,6},{3,7},{4,0},{5,1},{6,2},{7,3},{8,12},{9,13},{10,... | collective-permute-start | bytes 147464 | tf_op jit(solution)/shard_map/ppermute | solution.py:42
  67.6 5.9 %collective-permute-start.13 = (bf16[64,384]{1,0:T(8,128)(2,1)S(1)}, bf16[64,384]{1,0:T(8,128)(2,1)S(1)}, u32[]{:S(2)}, u32[]{:S(2)}) collective-permute-start(bf16[64,384]{1,0:T(8,128)(2,1)S(1)} %add_convert_fusion.2), channel_id=1, source_target_pairs={{0,6},{1,7},{2,4},{3,5},{4,2},{5,3},{6,0},{7,1},{8,14},{9,15},{10,... | collective-permute-start | bytes 147464 | tf_op jit(solution)/shard_map/ppermute | solution.py:42
  74.2 9.3 %collective-permute-start.14 = (bf16[64,388]{0,1:T(8,128)(2,1)S(1)}, bf16[64,388]{0,1:T(8,128)(2,1)S(1)}, u32[]{:S(2)}, u32[]{:S(2)}) collective-permute-start(bf16[64,388]{0,1:T(8,128)(2,1)S(1)} %pad_maximum_fusion.2), channel_id=1, source_target_pairs={{0,8},{8,0},{16,24},{24,16},{1,9},{9,1},{17,25},{25,17},{2,10},{10... | collective-permute-start | bytes 149000 | tf_op jit(solution)/shard_map/ppermute | solution.py:25
  76.0 7.5 %collective-permute-start.15 = (bf16[64,388]{0,1:T(8,128)(2,1)S(1)}, bf16[64,388]{0,1:T(8,128)(2,1)S(1)}, u32[]{:S(2)}, u32[]{:S(2)}) collective-permute-start(bf16[64,388]{0,1:T(8,128)(2,1)S(1)} %pad_maximum_fusion.2), channel_id=1, source_target_pairs={{0,16},{8,24},{16,0},{24,8},{1,17},{9,25},{17,1},{25,9},{2,18},{10... | collective-permute-start | bytes 149000 | tf_op jit(solution)/shard_map/ppermute | solution.py:25
  76.3 7.2 %collective-permute-start.16 = (bf16[64,388]{0,1:T(8,128)(2,1)S(1)}, bf16[64,388]{0,1:T(8,128)(2,1)S(1)}, u32[]{:S(2)}, u32[]{:S(2)}) collective-permute-start(bf16[64,388]{0,1:T(8,128)(2,1)S(1)} %pad_maximum_fusion.2), channel_id=1, source_target_pairs={{0,24},{8,16},{16,8},{24,0},{1,25},{9,17},{17,9},{25,1},{2,26},{10... | collective-permute-start | bytes 149000 | tf_op jit(solution)/shard_map/ppermute | solution.py:25
  90.0 37.1 %copy-start.9 = (bf16[2,512,384]{2,1,0:T(8,128)(2,1)S(1)}, bf16[2,512,384]{2,1,0:T(8,128)(2,1)}, u32[]{:S(2)}) copy-start(bf16[2,512,384]{2,1,0:T(8,128)(2,1)} %param.26) | copy-start | bytes 2359300
  90.8 45.7 %copy-start.5 = (f32[384]{0:T(512)S(1)}, f32[384]{0:T(512)}, u32[]{:S(2)}) copy-start(f32[384]{0:T(512)} %param.19) | copy-start | bytes 4612
  96.2 4.5 %collective-permute-start.17 = (f32[64,2,66]{0,1,2:T(2,128)S(1)}, f32[64,2,66]{0,1,2:T(2,128)S(1)}, u32[]{:S(2)}, u32[]{:S(2)}) collective-permute-start(f32[64,2,66]{0,1,2:T(2,128)S(1)} %pad_maximum_fusion.4), channel_id=1, source_target_pairs={{0,8},{8,0},{16,24},{24,16},{1,9},{9,1},{17,25},{25,17},{2,10},{10... | collective-permute-start | bytes 101384 | tf_op jit(solution)/shard_map/ppermute | solution.py:42
  98.0 4.3 %collective-permute-start.18 = (f32[64,2,66]{0,1,2:T(2,128)S(1)}, f32[64,2,66]{0,1,2:T(2,128)S(1)}, u32[]{:S(2)}, u32[]{:S(2)}) collective-permute-start(f32[64,2,66]{0,1,2:T(2,128)S(1)} %pad_maximum_fusion.4), channel_id=1, source_target_pairs={{0,16},{8,24},{16,0},{24,8},{1,17},{9,25},{17,1},{25,9},{2,18},{10... | collective-permute-start | bytes 101384 | tf_op jit(solution)/shard_map/ppermute | solution.py:42
  98.3 5.2 %collective-permute-start.19 = (f32[64,2,66]{0,1,2:T(2,128)S(1)}, f32[64,2,66]{0,1,2:T(2,128)S(1)}, u32[]{:S(2)}, u32[]{:S(2)}) collective-permute-start(f32[64,2,66]{0,1,2:T(2,128)S(1)} %pad_maximum_fusion.4), channel_id=1, source_target_pairs={{0,24},{8,16},{16,8},{24,0},{1,25},{9,17},{17,9},{25,1},{2,26},{10... | collective-permute-start | bytes 101384 | tf_op jit(solution)/shard_map/ppermute | solution.py:42
  104.1 1.3 collective-permute-start.20
  105.4 4.5 %collective-permute-start.21 = (bf16[64,384]{1,0:T(8,128)(2,1)S(1)}, bf16[64,384]{1,0:T(8,128)(2,1)S(1)}, u32[]{:S(2)}, u32[]{:S(2)}) collective-permute-start(bf16[64,384]{1,0:T(8,128)(2,1)S(1)} %add_convert_fusion.1), channel_id=1, source_target_pairs={{0,2},{1,3},{2,0},{3,1},{4,6},{5,7},{6,4},{7,5},{8,10},{9,11},{10,... | collective-permute-start | bytes 147464 | tf_op jit(solution)/shard_map/ppermute | solution.py:42
  106.6 6.0 %collective-permute-start.22 = (bf16[64,384]{1,0:T(8,128)(2,1)S(1)}, bf16[64,384]{1,0:T(8,128)(2,1)S(1)}, u32[]{:S(2)}, u32[]{:S(2)}) collective-permute-start(bf16[64,384]{1,0:T(8,128)(2,1)S(1)} %add_convert_fusion.1), channel_id=1, source_target_pairs={{0,4},{1,5},{2,6},{3,7},{4,0},{5,1},{6,2},{7,3},{8,12},{9,13},{10,... | collective-permute-start | bytes 147464 | tf_op jit(solution)/shard_map/ppermute | solution.py:42
  108.6 5.9 %collective-permute-start.23 = (bf16[64,384]{1,0:T(8,128)(2,1)S(1)}, bf16[64,384]{1,0:T(8,128)(2,1)S(1)}, u32[]{:S(2)}, u32[]{:S(2)}) collective-permute-start(bf16[64,384]{1,0:T(8,128)(2,1)S(1)} %add_convert_fusion.1), channel_id=1, source_target_pairs={{0,6},{1,7},{2,4},{3,5},{4,2},{5,3},{6,0},{7,1},{8,14},{9,15},{10,... | collective-permute-start | bytes 147464 | tf_op jit(solution)/shard_map/ppermute | solution.py:42
  127.4 1.3 collective-permute-start.24
  128.7 4.8 %collective-permute-start.25 = (bf16[64,384]{1,0:T(8,128)(2,1)S(1)}, bf16[64,384]{1,0:T(8,128)(2,1)S(1)}, u32[]{:S(2)}, u32[]{:S(2)}) collective-permute-start(bf16[64,384]{1,0:T(8,128)(2,1)S(1)} %add_convert_fusion), channel_id=1, source_target_pairs={{0,2},{1,3},{2,0},{3,1},{4,6},{5,7},{6,4},{7,5},{8,10},{9,11},{10,... | collective-permute-start | bytes 147464 | tf_op jit(solution)/shard_map/ppermute | solution.py:42
  128.7 6.9 %collective-permute-start.26 = (bf16[64,384]{1,0:T(8,128)(2,1)S(1)}, bf16[64,384]{1,0:T(8,128)(2,1)S(1)}, u32[]{:S(2)}, u32[]{:S(2)}) collective-permute-start(bf16[64,384]{1,0:T(8,128)(2,1)S(1)} %add_convert_fusion), channel_id=1, source_target_pairs={{0,4},{1,5},{2,6},{3,7},{4,0},{5,1},{6,2},{7,3},{8,12},{9,13},{10,... | collective-permute-start | bytes 147464 | tf_op jit(solution)/shard_map/ppermute | solution.py:42
  130.5 5.9 %collective-permute-start.27 = (bf16[64,384]{1,0:T(8,128)(2,1)S(1)}, bf16[64,384]{1,0:T(8,128)(2,1)S(1)}, u32[]{:S(2)}, u32[]{:S(2)}) collective-permute-start(bf16[64,384]{1,0:T(8,128)(2,1)S(1)} %add_convert_fusion), channel_id=1, source_target_pairs={{0,6},{1,7},{2,4},{3,5},{4,2},{5,3},{6,0},{7,1},{8,14},{9,15},{10,... | collective-permute-start | bytes 147464 | tf_op jit(solution)/shard_map/ppermute | solution.py:42
  154.5 15.8 %copy-start.7 = (f32[64]{0:T(128)}, f32[64]{0:T(128)S(1)}, u32[]{:S(2)}) copy-start(f32[64]{0:T(128)S(1)} %get-tuple-element.8) | copy-start | bytes 772
  154.5 3.6 %collective-permute-start.28 = (f32[64]{0:T(128)S(1)}, f32[64]{0:T(128)S(1)}, u32[]{:S(2)}, u32[]{:S(2)}) collective-permute-start(f32[64]{0:T(128)S(1)} %get-tuple-element.7), channel_id=1, source_target_pairs={{0,8},{8,0},{16,24},{24,16},{1,9},{9,1},{17,25},{25,17},{2,10},{10... | collective-permute-start | bytes 776 | tf_op jit(solution)/shard_map/ppermute | solution.py:70
  155.3 3.5 %collective-permute-start.29 = (f32[64]{0:T(128)S(1)}, f32[64]{0:T(128)S(1)}, u32[]{:S(2)}, u32[]{:S(2)}) collective-permute-start(f32[64]{0:T(128)S(1)} %get-tuple-element.7), channel_id=1, source_target_pairs={{0,16},{8,24},{16,0},{24,8},{1,17},{9,25},{17,1},{25,9},{2,18},{10... | collective-permute-start | bytes 776 | tf_op jit(solution)/shard_map/ppermute | solution.py:70
  155.8 4.4 %collective-permute-start.30 = (f32[64]{0:T(128)S(1)}, f32[64]{0:T(128)S(1)}, u32[]{:S(2)}, u32[]{:S(2)}) collective-permute-start(f32[64]{0:T(128)S(1)} %get-tuple-element.7), channel_id=1, source_target_pairs={{0,24},{8,16},{16,8},{24,0},{1,25},{9,17},{17,9},{25,1},{2,26},{10... | collective-permute-start | bytes 776 | tf_op jit(solution)/shard_map/ppermute | solution.py:70
  160.3 1.1 collective-permute-start.31
  161.4 5.1 %collective-permute-start.32 = (f32[64]{0:T(128)S(1)}, f32[64]{0:T(128)S(1)}, u32[]{:S(2)}, u32[]{:S(2)}) collective-permute-start(f32[64]{0:T(128)S(1)} %max.129), channel_id=1, source_target_pairs={{0,2},{1,3},{2,0},{3,1},{4,6},{5,7},{6,4},{7,5},{8,10},{9,11},{10,... | collective-permute-start | bytes 776 | tf_op jit(solution)/shard_map/ppermute | solution.py:42
  161.5 5.0 %collective-permute-start.33 = (f32[64]{0:T(128)S(1)}, f32[64]{0:T(128)S(1)}, u32[]{:S(2)}, u32[]{:S(2)}) collective-permute-start(f32[64]{0:T(128)S(1)} %max.129), channel_id=1, source_target_pairs={{0,4},{1,5},{2,6},{3,7},{4,0},{5,1},{6,2},{7,3},{8,12},{9,13},{10,... | collective-permute-start | bytes 776 | tf_op jit(solution)/shard_map/ppermute | solution.py:42
  164.4 5.3 %collective-permute-start.34 = (f32[64]{0:T(128)S(1)}, f32[64]{0:T(128)S(1)}, u32[]{:S(2)}, u32[]{:S(2)}) collective-permute-start(f32[64]{0:T(128)S(1)} %max.129), channel_id=1, source_target_pairs={{0,6},{1,7},{2,4},{3,5},{4,2},{5,3},{6,0},{7,1},{8,14},{9,15},{10,... | collective-permute-start | bytes 776 | tf_op jit(solution)/shard_map/ppermute | solution.py:42

commit v14 on v13

--- a/solution.py
+++ b/solution.py
@@ -146,9 +146,9 @@
     )
     page_out = mixed[:, :, HEAD:]
     member_f = member.astype(jnp.float32)
-    row_sum = jnp.einsum("rp,ph->rh", member_f, page_sum, precision=lax.Precision.HIGHEST)
-    row_out = jnp.einsum("rp,phd->rhd", member_f, page_out, precision=lax.Precision.HIGHEST)
-    return row_peak, row_sum, row_out
+    packed = jnp.concatenate([page_sum[:, :, None], page_out], axis=2)
+    row_all = jnp.einsum("rp,phd->rhd", member_f, packed, precision=lax.Precision.HIGHEST)
+    return row_peak, row_all[:, :, 0], row_all[:, :, 1:]
 
 
 def merge_pages(row_peak, row_sum, row_out):

time: 171 us -> 173 us (1.012)
  local copies, waits for them, and re-layouts: 4.67 us -> 6.48 us
    broadcast_in_dim x0 -> x2, local copies, waits for them, and re-layouts: none -> 1.78 us  [local_attention(): packed = jnp.concatenate([page_sum[:, :, None], page_out], axis=2)]
where the time goes in v14:
time: 173 us; the launch traced here: 172 us
  starting transfers between devices  41.2 us (24%)
  waiting for transfers between devices  37.2 us (22%)
  blocking collectives  35 us (20%)
  matrix products  31.6 us (18%)
  Pallas kernels  11.4 us (7%)
  other arithmetic  7.7 us (4%)
  local copies, waits for them, and re-layouts  6.48 us (4%)
    ppermute x26, waiting for transfers between devices, exchange(): return lax.ppermute(value, axis, [(i, i ^ partner) for i in range(count)])  34.9 us
    ppermute x26, starting transfers between devices, exchange(): return lax.ppermute(value, axis, [(i, i ^ partner) for i in range(count)])  29.6 us
    all_gather x2, blocking collectives, gather_sum(): return jnp.sum(lax.all_gather(value, axis).astype(jnp.float32), axis=0)  21.3 us
    all_to_all x1, blocking collectives, local(): pieces = lax.all_to_all(pieces, 'gx', 1, 1, tiled=True).astype(jnp.float32)  13.8 us
    dot_general x2, matrix products, local_attention(): jnp.einsum('pthc,pkhc->pkt', kv_layer, query_block, preferred_element_typ...  11.7 us
    pallas_call x2, Pallas kernels, layer_slice(): pl.pallas_call(copy_block, grid=(slots // block,), in_specs=[pl.BlockSpec...  11.4 us
    dot_general x2, matrix products, local_attention(): jnp.einsum('pkth,pthc->pkc', weight_block, kv_layer, preferred_element_ty...  9.34 us
    ppermute x6, starting transfers between devices, xor_sum(): lax.ppermute(value, axis, [(i, i ^ k) for i in range(count)])  8.1 us
  transfers between devices with their start and end apart: 35, of which 25 were waited for; matrix products, arithmetic and copies ran while one was open for 2% of the time, Pallas kernels for 7%

profile of v14, /device:TPU:0, one launch (start us, length us, event | category | flops | bytes accessed | tf_op | source)
XLA Modules:
  0.0 172.0 jit_solution(12260341004468687757)
XLA Ops:
  2.3 1.3 convolution_convert_fusion.2
  4.6 3.0 %collective-permute-start = (bf16[64,388]{0,1:T(8,128)(2,1)S(1)}, bf16[64,388]{0,1:T(8,128)(2,1)S(1)}, u32[]{:S(2)}, u32[]{:S(2)}) collective-permute-start(bf16[64,388]{0,1:T(8,128)(2,1)S(1)} %pad_maximum_fusion.3), channel_id=1, source_target_pairs={{0,8},{8,0},{16,24},{24,16},{1,9},{9,1},{17,25},{25,17},{2,10},{10... | collective-permute-start | bytes 149000 | tf_op jit(solution)/shard_map/ppermute | solution.py:25
  7.6 1.5 collective-permute-start.1
  12.6 5.7 %shard_map.175 = bf16[128,128,2,128]{3,2,1,0:T(2,128)(2,1)} custom-call(bf16[2,128,128,2,128]{4,3,2,1,0:T(2,128)(2,1)} %source.3), custom_call_target="tpu_custom_call" | custom-call | bytes 16777216 | tf_op jit(solution)/shard_map/pallas_call | solution.py:84
  19.1 5.9 %fusion.231 = (f32[128,2]{1,0:T(8,128)S(1)}, f32[128,2,128]{2,1,0:T(2,128)S(1)}) fusion(f32[128,2]{1,0:T(8,128)S(1)} %fusion.136, f32[2,128,2,128]{3,2,1,0:T(2,128)S(1)} %copy-done.10, bf16[128,128,2,128]{3,2,1,0:T(2,128)(2,1)} %shard_map.175, bf16[128,2,128]{2,1,0:T(2,128)(2,1)S(1)} %concatenate.41.clone, bf16[2,2]{0,1:T(2,128)(2,1)S(1)} %compare_convert_fusion, ...), kind=kOutput, calls=%fused_computation.344 | convolution fusion | flops 17202944 | bytes 8734728 | tf_op jit(solution)/shard_map/pthc,pkhc->pkt/dot_general | solution.py:132
  25.9 4.7 %fusion.11 = f32[128,2,128]{2,1,0:T(2,128)S(1)} fusion(bf16[128,128,2,128]{3,2,1,0:T(2,128)(2,1)} %shard_map.175, bf16[128,2,128]{2,1,0:T(2,128)(2,1)S(1)} %get-tuple-element.28, bf16[2,2]{0,1:T(2,128)(2,1)S(1)} %compare_convert_fusion), kind=kOutput, calls=%fused_computation.15 | convolution fusion | flops 17039360 | bytes 8585224 | tf_op jit(solution)/shard_map/pkth,pthc->pkc/dot_general | solution.py:144
  32.2 2.0 %collective-permute-start.3 = (f32[64,2,66]{0,1,2:T(2,128)S(1)}, f32[64,2,66]{0,1,2:T(2,128)S(1)}, u32[]{:S(2)}, u32[]{:S(2)}) collective-permute-start(f32[64,2,66]{0,1,2:T(2,128)S(1)} %pad_maximum_fusion.5), channel_id=1, source_target_pairs={{0,8},{8,0},{16,24},{24,16},{1,9},{9,1},{17,25},{25,17},{2,10},{10... | collective-permute-start | bytes 101384 | tf_op jit(solution)/shard_map/ppermute | solution.py:42
  34.2 1.5 collective-permute-start.4
  36.6 2.6 %collective-permute-done.4 = f32[64,2,66]{0,1,2:T(2,128)S(1)} collective-permute-done((f32[64,2,66]{0,1,2:T(2,128)S(1)}, f32[64,2,66]{0,1,2:T(2,128)S(1)}, u32[]{:S(2)}, u32[]{:S(2)}) %collective-permute-start.4) | collective-permute-done | bytes 33824 | tf_op jit(solution)/shard_map/ppermute | solution.py:42
  39.2 1.8 %collective-permute-done.5 = f32[64,2,66]{0,1,2:T(2,128)S(1)} collective-permute-done((f32[64,2,66]{0,1,2:T(2,128)S(1)}, f32[64,2,66]{0,1,2:T(2,128)S(1)}, u32[]{:S(2)}, u32[]{:S(2)}) %collective-permute-start.5) | collective-permute-done | bytes 33824 | tf_op jit(solution)/shard_map/ppermute | solution.py:42
  41.6 1.2 collective-permute-done.6
  42.8 1.6 collective-permute-start.7
  44.5 2.6 %collective-permute-start.8 = (bf16[64,384]{1,0:T(8,128)(2,1)S(1)}, bf16[64,384]{1,0:T(8,128)(2,1)S(1)}, u32[]{:S(2)}, u32[]{:S(2)}) collective-permute-start(bf16[64,384]{1,0:T(8,128)(2,1)S(1)} %add_convert_fusion.3), channel_id=1, source_target_pairs={{0,4},{1,5},{2,6},{3,7},{4,0},{5,1},{6,2},{7,3},{8,12},{9,13},{10,... | collective-permute-start | bytes 147464 | tf_op jit(solution)/shard_map/ppermute | solution.py:42
  47.3 3.1 %collective-permute-done.8 = bf16[64,384]{1,0:T(8,128)(2,1)S(1)} collective-permute-done((bf16[64,384]{1,0:T(8,128)(2,1)S(1)}, bf16[64,384]{1,0:T(8,128)(2,1)S(1)}, u32[]{:S(2)}, u32[]{:S(2)}) %collective-permute-start.8) | collective-permute-done | bytes 49184 | tf_op jit(solution)/shard_map/ppermute | solution.py:42
  50.4 2.6 %collective-permute-done.9 = bf16[64,384]{1,0:T(8,128)(2,1)S(1)} collective-permute-done((bf16[64,384]{1,0:T(8,128)(2,1)S(1)}, bf16[64,384]{1,0:T(8,128)(2,1)S(1)}, u32[]{:S(2)}, u32[]{:S(2)}) %collective-permute-start.9) | collective-permute-done | bytes 49184 | tf_op jit(solution)/shard_map/ppermute | solution.py:42
  53.8 9.9 %all-gather = bf16[256,1026]{1,0:T(8,128)(2,1)S(1)} all-gather(bf16[64,1026]{1,0:T(8,128)(2,1)S(1)} %concatenate.44), channel_id=2, replica_groups=mesh['gx'=4,'gy'=8] {'gx'}, dimensions={0}, use_global_device_ids=true | all-gather | bytes 656640 | tf_op jit(solution)/shard_map/all_gather | solution.py:19
  64.1 1.3 convolution_convert_fusion.10
  65.5 1.2 collective-permute-done.10
  66.8 1.7 collective-permute-start.12
  68.5 2.7 %collective-permute-start.13 = (bf16[64,384]{1,0:T(8,128)(2,1)S(1)}, bf16[64,384]{1,0:T(8,128)(2,1)S(1)}, u32[]{:S(2)}, u32[]{:S(2)}) collective-permute-start(bf16[64,384]{1,0:T(8,128)(2,1)S(1)} %add_convert_fusion.2), channel_id=1, source_target_pairs={{0,6},{1,7},{2,4},{3,5},{4,2},{5,3},{6,0},{7,1},{8,14},{9,15},{10,... | collective-permute-start | bytes 147464 | tf_op jit(solution)/shard_map/ppermute | solution.py:42
  71.6 2.2 %collective-permute-done.12 = bf16[64,384]{1,0:T(8,128)(2,1)S(1)} collective-permute-done((bf16[64,384]{1,0:T(8,128)(2,1)S(1)}, bf16[64,384]{1,0:T(8,128)(2,1)S(1)}, u32[]{:S(2)}, u32[]{:S(2)}) %collective-permute-start.12) | collective-permute-done | bytes 49184 | tf_op jit(solution)/shard_map/ppermute | solution.py:42
  75.1 1.8 %collective-permute-start.14 = (bf16[64,388]{0,1:T(8,128)(2,1)S(1)}, bf16[64,388]{0,1:T(8,128)(2,1)S(1)}, u32[]{:S(2)}, u32[]{:S(2)}) collective-permute-start(bf16[64,388]{0,1:T(8,128)(2,1)S(1)} %pad_maximum_fusion.4), channel_id=1, source_target_pairs={{0,8},{8,0},{16,24},{24,16},{1,9},{9,1},{17,25},{25,17},{2,10},{10... | collective-permute-start | bytes 149000 | tf_op jit(solution)/shard_map/ppermute | solution.py:25
  77.2 1.5 collective-permute-start.16
  78.6 5.7 %shard_map.176 = bf16[128,128,2,128]{3,2,1,0:T(2,128)(2,1)} custom-call(bf16[2,128,128,2,128]{4,3,2,1,0:T(2,128)(2,1)} %source.3), custom_call_target="tpu_custom_call" | custom-call | bytes 16777216 | tf_op jit(solution)/shard_map/pallas_call | solution.py:84
  85.1 5.8 %fusion.232 = (f32[128,2]{1,0:T(8,128)S(1)}, f32[128,2,128]{2,1,0:T(2,128)S(1)}) fusion(f32[128,2]{1,0:T(8,128)S(1)} %fusion.132, f32[2,128,2,128]{3,2,1,0:T(2,128)S(1)} %copy-done.10, bf16[128,128,2,128]{3,2,1,0:T(2,128)(2,1)} %shard_map.176, bf16[128,2,128]{2,1,0:T(2,128)(2,1)S(1)} %concatenate.46.clone, bf16[2,2]{0,1:T(2,128)(2,1)S(1)} %compare_convert_fusion, ...), kind=kOutput, calls=%fused_computation.345 | convolution fusion | flops 17202944 | bytes 8734728 | tf_op jit(solution)/shard_map/pthc,pkhc->pkt/dot_general | solution.py:132
  91.7 4.6 %fusion.17 = f32[128,2,128]{2,1,0:T(2,128)S(1)} fusion(bf16[128,128,2,128]{3,2,1,0:T(2,128)(2,1)} %shard_map.176, bf16[128,2,128]{2,1,0:T(2,128)(2,1)S(1)} %get-tuple-element.26, bf16[2,2]{0,1:T(2,128)(2,1)S(1)} %compare_convert_fusion), kind=kOutput, calls=%fused_computation.17 | convolution fusion | flops 17039360 | bytes 8585224 | tf_op jit(solution)/shard_map/pkth,pthc->pkc/dot_general | solution.py:144
  98.0 1.8 %collective-permute-start.17 = (f32[64,2,66]{0,1,2:T(2,128)S(1)}, f32[64,2,66]{0,1,2:T(2,128)S(1)}, u32[]{:S(2)}, u32[]{:S(2)}) collective-permute-start(f32[64,2,66]{0,1,2:T(2,128)S(1)} %pad_maximum_fusion.6), channel_id=1, source_target_pairs={{0,8},{8,0},{16,24},{24,16},{1,9},{9,1},{17,25},{25,17},{2,10},{10... | collective-permute-start | bytes 101384 | tf_op jit(solution)/shard_map/ppermute | solution.py:42
  100.1 1.5 collective-permute-start.19
  102.5 1.6 collective-permute-done.18
  104.1 1.2 collective-permute-done.19
  105.9 1.2 collective-permute-done.20
  107.2 1.2 collective-permute-start.21
  108.4 2.0 %collective-permute-start.22 = (bf16[64,384]{1,0:T(8,128)(2,1)S(1)}, bf16[64,384]{1,0:T(8,128)(2,1)S(1)}, u32[]{:S(2)}, u32[]{:S(2)}) collective-permute-start(bf16[64,384]{1,0:T(8,128)(2,1)S(1)} %add_convert_fusion.1), channel_id=1, source_target_pairs={{0,4},{1,5},{2,6},{3,7},{4,0},{5,1},{6,2},{7,3},{8,12},{9,13},{10,... | collective-permute-start | bytes 147464 | tf_op jit(solution)/shard_map/ppermute | solution.py:42
  110.4 1.2 collective-permute-start.23
  111.6 2.7 %collective-permute-done.22 = bf16[64,384]{1,0:T(8,128)(2,1)S(1)} collective-permute-done((bf16[64,384]{1,0:T(8,128)(2,1)S(1)}, bf16[64,384]{1,0:T(8,128)(2,1)S(1)}, u32[]{:S(2)}, u32[]{:S(2)}) %collective-permute-start.22) | collective-permute-done | bytes 49184 | tf_op jit(solution)/shard_map/ppermute | solution.py:42
  114.4 1.9 %collective-permute-done.23 = bf16[64,384]{1,0:T(8,128)(2,1)S(1)} collective-permute-done((bf16[64,384]{1,0:T(8,128)(2,1)S(1)}, bf16[64,384]{1,0:T(8,128)(2,1)S(1)}, u32[]{:S(2)}, u32[]{:S(2)}) %collective-permute-start.23) | collective-permute-done | bytes 49184 | tf_op jit(solution)/shard_map/ppermute | solution.py:42
  117.2 11.3 %all-gather.1 = bf16[256,1026]{1,0:T(8,128)(2,1)S(1)} all-gather(bf16[64,1026]{1,0:T(8,128)(2,1)S(1)} %concatenate.49), channel_id=3, replica_groups=mesh['gx'=4,'gy'=8] {'gx'}, dimensions={0}, use_global_device_ids=true | all-gather | bytes 656640 | tf_op jit(solution)/shard_map/all_gather | solution.py:19
  129.2 1.2 collective-permute-done.24
  130.5 1.7 collective-permute-start.26
  132.2 2.7 %collective-permute-start.27 = (bf16[64,384]{1,0:T(8,128)(2,1)S(1)}, bf16[64,384]{1,0:T(8,128)(2,1)S(1)}, u32[]{:S(2)}, u32[]{:S(2)}) collective-permute-start(bf16[64,384]{1,0:T(8,128)(2,1)S(1)} %add_convert_fusion), channel_id=1, source_target_pairs={{0,6},{1,7},{2,4},{3,5},{4,2},{5,3},{6,0},{7,1},{8,14},{9,15},{10,... | collective-permute-start | bytes 147464 | tf_op jit(solution)/shard_map/ppermute | solution.py:42
  135.2 2.2 %collective-permute-done.26 = bf16[64,384]{1,0:T(8,128)(2,1)S(1)} collective-permute-done((bf16[64,384]{1,0:T(8,128)(2,1)S(1)}, bf16[64,384]{1,0:T(8,128)(2,1)S(1)}, u32[]{:S(2)}, u32[]{:S(2)}) %collective-permute-start.26) | collective-permute-done | bytes 49184 | tf_op jit(solution)/shard_map/ppermute | solution.py:42
  138.3 3.3 %convolution_convert_fusion = bf16[64,6144]{1,0:T(8,128)(2,1)S(1)} fusion(bf16[384,6144]{1,0:T(8,128)(2,1)} %param.27, f32[64,384]{1,0:T(8,128)S(1)} %get-tuple-element.10, f32[384]{0:T(512)S(1)} %copy-done.5), kind=kOutput, calls=%fused_computation.8 | convolution fusion | flops 302432256 | bytes 5604864 | tf_op jit(solution)/shard_map/dot_general | solution.py:266
  141.9 13.8 %all_to_all.5 = bf16[64,4,1538]{2,0,1:T(8,128)(2,1)S(1)} all-to-all(bf16[64,4,1538]{2,0,1:T(8,128)(2,1)S(1)} %pad_maximum_fusion), channel_id=1, replica_groups=mesh['gx'=4,'gy'=8] {'gx'}, dimensions={1} | all-to-all | bytes 1574912 | tf_op jit(solution)/shard_map/all_to_all | solution.py:277
  157.6 2.2 %collective-permute-start.30 = (f32[64]{0:T(128)S(1)}, f32[64]{0:T(128)S(1)}, u32[]{:S(2)}, u32[]{:S(2)}) collective-permute-start(f32[64]{0:T(128)S(1)} %get-tuple-element.7), channel_id=1, source_target_pairs={{0,24},{8,16},{16,8},{24,0},{1,25},{9,17},{17,9},{25,1},{2,26},{10... | collective-permute-start | bytes 776 | tf_op jit(solution)/shard_map/ppermute | solution.py:70
  160.6 1.5 collective-permute-done.30
  163.3 2.9 %collective-permute-start.33 = (f32[64]{0:T(128)S(1)}, f32[64]{0:T(128)S(1)}, u32[]{:S(2)}, u32[]{:S(2)}) collective-permute-start(f32[64]{0:T(128)S(1)} %max.139), channel_id=1, source_target_pairs={{0,4},{1,5},{2,6},{3,7},{4,0},{5,1},{6,2},{7,3},{8,12},{9,13},{10,... | collective-permute-start | bytes 776 | tf_op jit(solution)/shard_map/ppermute | solution.py:42
  166.2 1.4 collective-permute-start.34
  168.3 3.2 %collective-permute-done.34 = f32[64]{0:T(128)S(1)} collective-permute-done((f32[64]{0:T(128)S(1)}, f32[64]{0:T(128)S(1)}, u32[]{:S(2)}, u32[]{:S(2)}) %collective-permute-start.34) | collective-permute-done | bytes 288 | tf_op jit(solution)/shard_map/ppermute | solution.py:42
  (189 shorter events, 27.4 us)
Async XLA Ops:
  4.6 13.7 %collective-permute-start = (bf16[64,388]{0,1:T(8,128)(2,1)S(1)}, bf16[64,388]{0,1:T(8,128)(2,1)S(1)}, u32[]{:S(2)}, u32[]{:S(2)}) collective-permute-start(bf16[64,388]{0,1:T(8,128)(2,1)S(1)} %pad_maximum_fusion.3), channel_id=1, source_target_pairs={{0,8},{8,0},{16,24},{24,16},{1,9},{9,1},{17,25},{25,17},{2,10},{10... | collective-permute-start | bytes 149000 | tf_op jit(solution)/shard_map/ppermute | solution.py:25
  7.6 10.7 %collective-permute-start.1 = (bf16[64,388]{0,1:T(8,128)(2,1)S(1)}, bf16[64,388]{0,1:T(8,128)(2,1)S(1)}, u32[]{:S(2)}, u32[]{:S(2)}) collective-permute-start(bf16[64,388]{0,1:T(8,128)(2,1)S(1)} %pad_maximum_fusion.3), channel_id=1, source_target_pairs={{0,16},{8,24},{16,0},{24,8},{1,17},{9,25},{17,1},{25,9},{2,18},{10... | collective-permute-start | bytes 149000 | tf_op jit(solution)/shard_map/ppermute | solution.py:25
  9.1 9.2 %collective-permute-start.2 = (bf16[64,388]{0,1:T(8,128)(2,1)S(1)}, bf16[64,388]{0,1:T(8,128)(2,1)S(1)}, u32[]{:S(2)}, u32[]{:S(2)}) collective-permute-start(bf16[64,388]{0,1:T(8,128)(2,1)S(1)} %pad_maximum_fusion.3), channel_id=1, source_target_pairs={{0,24},{8,16},{16,8},{24,0},{1,25},{9,17},{17,9},{25,1},{2,26},{10... | collective-permute-start | bytes 149000 | tf_op jit(solution)/shard_map/ppermute | solution.py:25
  12.6 6.5 %copy-start.10 = (f32[2,128,2,128]{3,2,1,0:T(2,128)S(1)}, f32[2,128,2,128]{3,2,1,0:T(2,128)}, u32[]{:S(2)}) copy-start(f32[2,128,2,128]{3,2,1,0:T(2,128)} %param.29) | copy-start | bytes 786436
  19.1 22.3 %copy-start.4 = (bf16[2,128,384]{2,1,0:T(8,128)(2,1)S(1)}, bf16[2,128,384]{2,1,0:T(8,128)(2,1)}, u32[]{:S(2)}) copy-start(bf16[2,128,384]{2,1,0:T(8,128)(2,1)} %param.23) | copy-start | bytes 589828
  19.1 28.2 %copy-start.6 = (f32[2,384]{1,0:T(2,128)S(1)}, f32[2,384]{1,0:T(2,128)}, u32[]{:S(2)}) copy-start(f32[2,384]{1,0:T(2,128)} %param.18) | copy-start | bytes 9220
  19.1 33.8 %copy-start.3 = (bf16[64,384]{1,0:T(8,128)(2,1)S(1)}, bf16[64,384]{1,0:T(8,128)(2,1)}, u32[]{:S(2)}) copy-start(bf16[64,384]{1,0:T(8,128)(2,1)} %param.16) | copy-start | bytes 147460
  19.1 34.0 %copy-start = (bf16[2,384,512]{2,1,0:T(8,128)(2,1)S(1)}, bf16[2,384,512]{2,1,0:T(8,128)(2,1)}, u32[]{:S(2)}) copy-start(bf16[2,384,512]{2,1,0:T(8,128)(2,1)} %param.25) | copy-start | bytes 2359300
  25.0 28.3 %copy-start.1 = (bf16[2,384,512]{2,1,0:T(8,128)(2,1)S(1)}, bf16[2,384,512]{2,1,0:T(8,128)(2,1)}, u32[]{:S(2)}) copy-start(bf16[2,384,512]{2,1,0:T(8,128)(2,1)} %param.24) | copy-start | bytes 2359300
  25.9 48.7 %copy-start.2 = (bf16[2,384,384]{2,1,0:T(8,128)(2,1)S(1)}, bf16[2,384,384]{2,1,0:T(8,128)(2,1)}, u32[]{:S(2)}) copy-start(bf16[2,384,384]{2,1,0:T(8,128)(2,1)} %param.20) | copy-start | bytes 1769476
  25.9 49.0 %copy-start.8 = (bf16[2,384,2]{1,2,0:T(2,128)(2,1)S(1)}, bf16[2,384,2]{1,2,0:T(2,128)(2,1)}, u32[]{:S(2)}) copy-start(bf16[2,384,2]{1,2,0:T(2,128)(2,1)} %param.21) | copy-start | bytes 9220
  32.2 4.4 %collective-permute-start.3 = (f32[64,2,66]{0,1,2:T(2,128)S(1)}, f32[64,2,66]{0,1,2:T(2,128)S(1)}, u32[]{:S(2)}, u32[]{:S(2)}) collective-permute-start(f32[64,2,66]{0,1,2:T(2,128)S(1)} %pad_maximum_fusion.5), channel_id=1, source_target_pairs={{0,8},{8,0},{16,24},{24,16},{1,9},{9,1},{17,25},{25,17},{2,10},{10... | collective-permute-start | bytes 101384 | tf_op jit(solution)/shard_map/ppermute | solution.py:42
  34.2 4.9 %collective-permute-start.4 = (f32[64,2,66]{0,1,2:T(2,128)S(1)}, f32[64,2,66]{0,1,2:T(2,128)S(1)}, u32[]{:S(2)}, u32[]{:S(2)}) collective-permute-start(f32[64,2,66]{0,1,2:T(2,128)S(1)} %pad_maximum_fusion.5), channel_id=1, source_target_pairs={{0,16},{8,24},{16,0},{24,8},{1,17},{9,25},{17,1},{25,9},{2,18},{10... | collective-permute-start | bytes 101384 | tf_op jit(solution)/shard_map/ppermute | solution.py:42
  35.8 5.2 %collective-permute-start.5 = (f32[64,2,66]{0,1,2:T(2,128)S(1)}, f32[64,2,66]{0,1,2:T(2,128)S(1)}, u32[]{:S(2)}, u32[]{:S(2)}) collective-permute-start(f32[64,2,66]{0,1,2:T(2,128)S(1)} %pad_maximum_fusion.5), channel_id=1, source_target_pairs={{0,24},{8,16},{16,8},{24,0},{1,25},{9,17},{17,9},{25,1},{2,26},{10... | collective-permute-start | bytes 101384 | tf_op jit(solution)/shard_map/ppermute | solution.py:42
  41.5 1.3 collective-permute-start.6
  42.8 4.5 %collective-permute-start.7 = (bf16[64,384]{1,0:T(8,128)(2,1)S(1)}, bf16[64,384]{1,0:T(8,128)(2,1)S(1)}, u32[]{:S(2)}, u32[]{:S(2)}) collective-permute-start(bf16[64,384]{1,0:T(8,128)(2,1)S(1)} %add_convert_fusion.3), channel_id=1, source_target_pairs={{0,2},{1,3},{2,0},{3,1},{4,6},{5,7},{6,4},{7,5},{8,10},{9,11},{10,... | collective-permute-start | bytes 147464 | tf_op jit(solution)/shard_map/ppermute | solution.py:42
  44.5 5.9 %collective-permute-start.8 = (bf16[64,384]{1,0:T(8,128)(2,1)S(1)}, bf16[64,384]{1,0:T(8,128)(2,1)S(1)}, u32[]{:S(2)}, u32[]{:S(2)}) collective-permute-start(bf16[64,384]{1,0:T(8,128)(2,1)S(1)} %add_convert_fusion.3), channel_id=1, source_target_pairs={{0,4},{1,5},{2,6},{3,7},{4,0},{5,1},{6,2},{7,3},{8,12},{9,13},{10,... | collective-permute-start | bytes 147464 | tf_op jit(solution)/shard_map/ppermute | solution.py:42
  47.1 5.9 %collective-permute-start.9 = (bf16[64,384]{1,0:T(8,128)(2,1)S(1)}, bf16[64,384]{1,0:T(8,128)(2,1)S(1)}, u32[]{:S(2)}, u32[]{:S(2)}) collective-permute-start(bf16[64,384]{1,0:T(8,128)(2,1)S(1)} %add_convert_fusion.3), channel_id=1, source_target_pairs={{0,6},{1,7},{2,4},{3,5},{4,2},{5,3},{6,0},{7,1},{8,14},{9,15},{10,... | collective-permute-start | bytes 147464 | tf_op jit(solution)/shard_map/ppermute | solution.py:42
  65.4 1.3 collective-permute-start.10
  66.7 4.9 %collective-permute-start.11 = (bf16[64,384]{1,0:T(8,128)(2,1)S(1)}, bf16[64,384]{1,0:T(8,128)(2,1)S(1)}, u32[]{:S(2)}, u32[]{:S(2)}) collective-permute-start(bf16[64,384]{1,0:T(8,128)(2,1)S(1)} %add_convert_fusion.2), channel_id=1, source_target_pairs={{0,2},{1,3},{2,0},{3,1},{4,6},{5,7},{6,4},{7,5},{8,10},{9,11},{10,... | collective-permute-start | bytes 147464 | tf_op jit(solution)/shard_map/ppermute | solution.py:42
  66.8 7.0 %collective-permute-start.12 = (bf16[64,384]{1,0:T(8,128)(2,1)S(1)}, bf16[64,384]{1,0:T(8,128)(2,1)S(1)}, u32[]{:S(2)}, u32[]{:S(2)}) collective-permute-start(bf16[64,384]{1,0:T(8,128)(2,1)S(1)} %add_convert_fusion.2), channel_id=1, source_target_pairs={{0,4},{1,5},{2,6},{3,7},{4,0},{5,1},{6,2},{7,3},{8,12},{9,13},{10,... | collective-permute-start | bytes 147464 | tf_op jit(solution)/shard_map/ppermute | solution.py:42
  68.5 5.9 %collective-permute-start.13 = (bf16[64,384]{1,0:T(8,128)(2,1)S(1)}, bf16[64,384]{1,0:T(8,128)(2,1)S(1)}, u32[]{:S(2)}, u32[]{:S(2)}) collective-permute-start(bf16[64,384]{1,0:T(8,128)(2,1)S(1)} %add_convert_fusion.2), channel_id=1, source_target_pairs={{0,6},{1,7},{2,4},{3,5},{4,2},{5,3},{6,0},{7,1},{8,14},{9,15},{10,... | collective-permute-start | bytes 147464 | tf_op jit(solution)/shard_map/ppermute | solution.py:42
  75.1 9.3 %collective-permute-start.14 = (bf16[64,388]{0,1:T(8,128)(2,1)S(1)}, bf16[64,388]{0,1:T(8,128)(2,1)S(1)}, u32[]{:S(2)}, u32[]{:S(2)}) collective-permute-start(bf16[64,388]{0,1:T(8,128)(2,1)S(1)} %pad_maximum_fusion.4), channel_id=1, source_target_pairs={{0,8},{8,0},{16,24},{24,16},{1,9},{9,1},{17,25},{25,17},{2,10},{10... | collective-permute-start | bytes 149000 | tf_op jit(solution)/shard_map/ppermute | solution.py:25
  76.9 7.5 %collective-permute-start.15 = (bf16[64,388]{0,1:T(8,128)(2,1)S(1)}, bf16[64,388]{0,1:T(8,128)(2,1)S(1)}, u32[]{:S(2)}, u32[]{:S(2)}) collective-permute-start(bf16[64,388]{0,1:T(8,128)(2,1)S(1)} %pad_maximum_fusion.4), channel_id=1, source_target_pairs={{0,16},{8,24},{16,0},{24,8},{1,17},{9,25},{17,1},{25,9},{2,18},{10... | collective-permute-start | bytes 149000 | tf_op jit(solution)/shard_map/ppermute | solution.py:25
  77.2 7.2 %collective-permute-start.16 = (bf16[64,388]{0,1:T(8,128)(2,1)S(1)}, bf16[64,388]{0,1:T(8,128)(2,1)S(1)}, u32[]{:S(2)}, u32[]{:S(2)}) collective-permute-start(bf16[64,388]{0,1:T(8,128)(2,1)S(1)} %pad_maximum_fusion.4), channel_id=1, source_target_pairs={{0,24},{8,16},{16,8},{24,0},{1,25},{9,17},{17,9},{25,1},{2,26},{10... | collective-permute-start | bytes 149000 | tf_op jit(solution)/shard_map/ppermute | solution.py:25
  90.9 37.9 %copy-start.9 = (bf16[2,512,384]{2,1,0:T(8,128)(2,1)S(1)}, bf16[2,512,384]{2,1,0:T(8,128)(2,1)}, u32[]{:S(2)}) copy-start(bf16[2,512,384]{2,1,0:T(8,128)(2,1)} %param.26) | copy-start | bytes 2359300
  91.7 46.6 %copy-start.5 = (f32[384]{0:T(512)S(1)}, f32[384]{0:T(512)}, u32[]{:S(2)}) copy-start(f32[384]{0:T(512)} %param.19) | copy-start | bytes 4612
  98.0 4.5 %collective-permute-start.17 = (f32[64,2,66]{0,1,2:T(2,128)S(1)}, f32[64,2,66]{0,1,2:T(2,128)S(1)}, u32[]{:S(2)}, u32[]{:S(2)}) collective-permute-start(f32[64,2,66]{0,1,2:T(2,128)S(1)} %pad_maximum_fusion.6), channel_id=1, source_target_pairs={{0,8},{8,0},{16,24},{24,16},{1,9},{9,1},{17,25},{25,17},{2,10},{10... | collective-permute-start | bytes 101384 | tf_op jit(solution)/shard_map/ppermute | solution.py:42
  99.8 4.3 %collective-permute-start.18 = (f32[64,2,66]{0,1,2:T(2,128)S(1)}, f32[64,2,66]{0,1,2:T(2,128)S(1)}, u32[]{:S(2)}, u32[]{:S(2)}) collective-permute-start(f32[64,2,66]{0,1,2:T(2,128)S(1)} %pad_maximum_fusion.6), channel_id=1, source_target_pairs={{0,16},{8,24},{16,0},{24,8},{1,17},{9,25},{17,1},{25,9},{2,18},{10... | collective-permute-start | bytes 101384 | tf_op jit(solution)/shard_map/ppermute | solution.py:42
  100.1 5.2 %collective-permute-start.19 = (f32[64,2,66]{0,1,2:T(2,128)S(1)}, f32[64,2,66]{0,1,2:T(2,128)S(1)}, u32[]{:S(2)}, u32[]{:S(2)}) collective-permute-start(f32[64,2,66]{0,1,2:T(2,128)S(1)} %pad_maximum_fusion.6), channel_id=1, source_target_pairs={{0,24},{8,16},{16,8},{24,0},{1,25},{9,17},{17,9},{25,1},{2,26},{10... | collective-permute-start | bytes 101384 | tf_op jit(solution)/shard_map/ppermute | solution.py:42
  105.9 1.3 collective-permute-start.20
  107.2 4.5 %collective-permute-start.21 = (bf16[64,384]{1,0:T(8,128)(2,1)S(1)}, bf16[64,384]{1,0:T(8,128)(2,1)S(1)}, u32[]{:S(2)}, u32[]{:S(2)}) collective-permute-start(bf16[64,384]{1,0:T(8,128)(2,1)S(1)} %add_convert_fusion.1), channel_id=1, source_target_pairs={{0,2},{1,3},{2,0},{3,1},{4,6},{5,7},{6,4},{7,5},{8,10},{9,11},{10,... | collective-permute-start | bytes 147464 | tf_op jit(solution)/shard_map/ppermute | solution.py:42
  108.4 6.0 %collective-permute-start.22 = (bf16[64,384]{1,0:T(8,128)(2,1)S(1)}, bf16[64,384]{1,0:T(8,128)(2,1)S(1)}, u32[]{:S(2)}, u32[]{:S(2)}) collective-permute-start(bf16[64,384]{1,0:T(8,128)(2,1)S(1)} %add_convert_fusion.1), channel_id=1, source_target_pairs={{0,4},{1,5},{2,6},{3,7},{4,0},{5,1},{6,2},{7,3},{8,12},{9,13},{10,... | collective-permute-start | bytes 147464 | tf_op jit(solution)/shard_map/ppermute | solution.py:42
  110.4 5.9 %collective-permute-start.23 = (bf16[64,384]{1,0:T(8,128)(2,1)S(1)}, bf16[64,384]{1,0:T(8,128)(2,1)S(1)}, u32[]{:S(2)}, u32[]{:S(2)}) collective-permute-start(bf16[64,384]{1,0:T(8,128)(2,1)S(1)} %add_convert_fusion.1), channel_id=1, source_target_pairs={{0,6},{1,7},{2,4},{3,5},{4,2},{5,3},{6,0},{7,1},{8,14},{9,15},{10,... | collective-permute-start | bytes 147464 | tf_op jit(solution)/shard_map/ppermute | solution.py:42
  129.1 1.3 collective-permute-start.24
  130.4 4.8 %collective-permute-start.25 = (bf16[64,384]{1,0:T(8,128)(2,1)S(1)}, bf16[64,384]{1,0:T(8,128)(2,1)S(1)}, u32[]{:S(2)}, u32[]{:S(2)}) collective-permute-start(bf16[64,384]{1,0:T(8,128)(2,1)S(1)} %add_convert_fusion), channel_id=1, source_target_pairs={{0,2},{1,3},{2,0},{3,1},{4,6},{5,7},{6,4},{7,5},{8,10},{9,11},{10,... | collective-permute-start | bytes 147464 | tf_op jit(solution)/shard_map/ppermute | solution.py:42
  130.5 6.9 %collective-permute-start.26 = (bf16[64,384]{1,0:T(8,128)(2,1)S(1)}, bf16[64,384]{1,0:T(8,128)(2,1)S(1)}, u32[]{:S(2)}, u32[]{:S(2)}) collective-permute-start(bf16[64,384]{1,0:T(8,128)(2,1)S(1)} %add_convert_fusion), channel_id=1, source_target_pairs={{0,4},{1,5},{2,6},{3,7},{4,0},{5,1},{6,2},{7,3},{8,12},{9,13},{10,... | collective-permute-start | bytes 147464 | tf_op jit(solution)/shard_map/ppermute | solution.py:42
  132.2 5.9 %collective-permute-start.27 = (bf16[64,384]{1,0:T(8,128)(2,1)S(1)}, bf16[64,384]{1,0:T(8,128)(2,1)S(1)}, u32[]{:S(2)}, u32[]{:S(2)}) collective-permute-start(bf16[64,384]{1,0:T(8,128)(2,1)S(1)} %add_convert_fusion), channel_id=1, source_target_pairs={{0,6},{1,7},{2,4},{3,5},{4,2},{5,3},{6,0},{7,1},{8,14},{9,15},{10,... | collective-permute-start | bytes 147464 | tf_op jit(solution)/shard_map/ppermute | solution.py:42
  156.2 15.8 %copy-start.7 = (f32[64]{0:T(128)}, f32[64]{0:T(128)S(1)}, u32[]{:S(2)}) copy-start(f32[64]{0:T(128)S(1)} %get-tuple-element.8) | copy-start | bytes 772
  156.2 3.6 %collective-permute-start.28 = (f32[64]{0:T(128)S(1)}, f32[64]{0:T(128)S(1)}, u32[]{:S(2)}, u32[]{:S(2)}) collective-permute-start(f32[64]{0:T(128)S(1)} %get-tuple-element.7), channel_id=1, source_target_pairs={{0,8},{8,0},{16,24},{24,16},{1,9},{9,1},{17,25},{25,17},{2,10},{10... | collective-permute-start | bytes 776 | tf_op jit(solution)/shard_map/ppermute | solution.py:70
  157.1 3.5 %collective-permute-start.29 = (f32[64]{0:T(128)S(1)}, f32[64]{0:T(128)S(1)}, u32[]{:S(2)}, u32[]{:S(2)}) collective-permute-start(f32[64]{0:T(128)S(1)} %get-tuple-element.7), channel_id=1, source_target_pairs={{0,16},{8,24},{16,0},{24,8},{1,17},{9,25},{17,1},{25,9},{2,18},{10... | collective-permute-start | bytes 776 | tf_op jit(solution)/shard_map/ppermute | solution.py:70
  157.6 4.4 %collective-permute-start.30 = (f32[64]{0:T(128)S(1)}, f32[64]{0:T(128)S(1)}, u32[]{:S(2)}, u32[]{:S(2)}) collective-permute-start(f32[64]{0:T(128)S(1)} %get-tuple-element.7), channel_id=1, source_target_pairs={{0,24},{8,16},{16,8},{24,0},{1,25},{9,17},{17,9},{25,1},{2,26},{10... | collective-permute-start | bytes 776 | tf_op jit(solution)/shard_map/ppermute | solution.py:70
  162.1 1.1 collective-permute-start.31
  163.2 5.1 %collective-permute-start.32 = (f32[64]{0:T(128)S(1)}, f32[64]{0:T(128)S(1)}, u32[]{:S(2)}, u32[]{:S(2)}) collective-permute-start(f32[64]{0:T(128)S(1)} %max.139), channel_id=1, source_target_pairs={{0,2},{1,3},{2,0},{3,1},{4,6},{5,7},{6,4},{7,5},{8,10},{9,11},{10,... | collective-permute-start | bytes 776 | tf_op jit(solution)/shard_map/ppermute | solution.py:42
  163.3 5.0 %collective-permute-start.33 = (f32[64]{0:T(128)S(1)}, f32[64]{0:T(128)S(1)}, u32[]{:S(2)}, u32[]{:S(2)}) collective-permute-start(f32[64]{0:T(128)S(1)} %max.139), channel_id=1, source_target_pairs={{0,4},{1,5},{2,6},{3,7},{4,0},{5,1},{6,2},{7,3},{8,12},{9,13},{10,... | collective-permute-start | bytes 776 | tf_op jit(solution)/shard_map/ppermute | solution.py:42
  166.2 5.3 %collective-permute-start.34 = (f32[64]{0:T(128)S(1)}, f32[64]{0:T(128)S(1)}, u32[]{:S(2)}, u32[]{:S(2)}) collective-permute-start(f32[64]{0:T(128)S(1)} %max.139), channel_id=1, source_target_pairs={{0,6},{1,7},{2,4},{3,5},{4,2},{5,3},{6,0},{7,1},{8,14},{9,15},{10,... | collective-permute-start | bytes 776 | tf_op jit(solution)/shard_map/ppermute | solution.py:42
